TPU v7x, 128 devices: a whole 4x4x4 slice. The times are simulated.
128 devices in a mesh: blk: 64 (over z, x_lo, y, core), split: 2 (over x_hi).
Axes of the slice: x: 4 (x_hi: 2, x_lo: 2; x = x_hi * 2 + x_lo), y: 4, z: 4, core: 2. Of those that a mesh axis runs over, the one named last changes fastest.
Arguments:
- queries: bfloat16 [16384, 1024], P('blk'), may hold values from -400 to 400
- keys: bfloat16 [16384, 64], P(('blk', 'split')), may hold values from -5 to 5
- values: bfloat16 [16384, 64], P(('blk', 'split')), may hold values from -5 to 5
- out_grad: bfloat16 [16384, 1024], P('blk'), may hold values from -5 to 5
- block_lists: int32 [128, 48], P('blk'), may hold values from 0 to 127, as said below
Outputs:
- attended: bfloat16 [16384, 1024], P('blk')
- query_grad: bfloat16 [16384, 1024], P('blk')
- key_grad: bfloat16 [16384, 64], P(('blk', 'split'))
- value_grad: bfloat16 [16384, 64], P(('blk', 'split'))
Inputs may be any that keep to these rules, and one draw needn't show every extreme that they name: `block_lists`: row a names blocks a, a - 1 and a + 1 (modulo 128); a block named twice in a row counts once.
All inputs are finite; a program needn't handle non-finite values.
Results may differ from a plain program's by a relative error of at most 0.019.
Values may be sent and summed in bfloat16 or wider, within the bound.
No kernel may reach another device: no remote copies, remote signals or barrier semaphores. Data moves between devices by JAX's collectives and lax.ppermute only.
A program may use at most 64 MiB of HBM per device.

v0:
```python
from functools import partial
import math

import jax
import jax.numpy as jnp
from jax import lax
from jax.sharding import PartitionSpec as P

HEADS = 16
HEAD_DIM = 64
BLOCK = 128


lowest_score = -1e30


def passed_along(value, axis, steps):
    count = lax.axis_size(axis)
    pairs = [(source, (source + steps) % count) for source in range(count)]
    return lax.ppermute(value, axis, pairs)


def keep_state(state_in):
    return state_in


def local(queries, keys, values, out_grad, block_lists):
    query_count = block_lists.shape[0]
    cycle_size = lax.axis_size("blk")
    own_half = keys.shape[0] // BLOCK
    split_place = lax.axis_index("split")
    cycle_place = lax.axis_index("blk")
    row_count = BLOCK * HEADS
    scale_value = 1.0 / math.sqrt(HEAD_DIM)
    query_rows = queries.reshape(query_count, row_count, HEAD_DIM)
    grad_rows = out_grad.reshape(query_count, row_count, HEAD_DIM)
    every_block = jnp.arange(cycle_size * query_count, dtype=jnp.int32)
    listed = jnp.any(block_lists[:, :, None] == every_block[None, None, :], axis=1)

    def block_label(first_row, offset):
        gathered = first_row // BLOCK + offset
        return gathered // own_half * query_count + split_place * own_half + gathered % own_half

    def forward_tile(target, key_tile, value_tile, state_in):
        maxima, totals, accum = state_in
        scores = (
            lax.dot_general(
                query_rows[target],
                key_tile,
                (((1,), (1,)), ((), ())),
                preferred_element_type=jnp.float32,
            )
            * scale_value
        )
        old_max = maxima[target]
        new_max = jnp.maximum(old_max, jnp.max(scores, axis=1))
        factor = jnp.exp(old_max - new_max)
        numerator = jnp.exp(scores - new_max[:, None])
        new_total = totals[target] * factor + jnp.sum(numerator, axis=1)
        weighted = jnp.dot(
            numerator.astype(jnp.bfloat16), value_tile, preferred_element_type=jnp.float32
        )
        new_accum = accum[target] * factor[:, None] + weighted
        return (
            maxima.at[target].set(new_max),
            totals.at[target].set(new_total),
            accum.at[target].set(new_accum),
        )

    def forward_piece(state_in, kv_piece, first_row):
        key_piece, value_piece = kv_piece
        block_count = key_piece.shape[0] // BLOCK
        key_stack = key_piece.reshape(block_count, BLOCK, HEAD_DIM)
        value_stack = value_piece.reshape(block_count, BLOCK, HEAD_DIM)

        def forward_visit_block(running, tile_item):
            key_tile, value_tile, offset = tile_item
            key_label = block_label(first_row, offset)
            for target in range(query_count):
                running = lax.cond(
                    listed[target, key_label],
                    partial(forward_tile, target, key_tile, value_tile),
                    keep_state,
                    running,
                )
            return (running, None)

        result, unused = lax.scan(
            forward_visit_block,
            state_in,
            (key_stack, value_stack, jnp.arange(block_count, dtype=jnp.int32)),
        )
        return result

    start_state = (
        jnp.full((query_count, row_count), lowest_score, jnp.float32),
        jnp.zeros((query_count, row_count), jnp.float32),
        jnp.zeros((query_count, row_count, HEAD_DIM), jnp.float32),
    )

    def cycle_turn(turn_index, running):
        state_in, moving = running
        anchor = (cycle_place - turn_index) % cycle_size
        state_in = forward_piece(state_in, moving, anchor * own_half * BLOCK)
        moving = passed_along((moving[0], moving[1]), "blk", 1)
        return (state_in, moving)

    state_out, moving = lax.fori_loop(0, cycle_size - 1, cycle_turn, (start_state, (keys, values)))
    anchor = (cycle_place - (cycle_size - 1)) % cycle_size
    state_out = forward_piece(state_out, moving, anchor * own_half * BLOCK)
    maxima, totals, accum = state_out
    joined_max = lax.pmax(maxima, "split")
    factor = jnp.exp(maxima - joined_max)
    totals, accum = lax.psum((totals * factor, accum * factor[:, :, None]), "split")
    maxima = joined_max
    outputs = accum / totals[:, :, None]
    log_total = maxima + jnp.log(totals)
    row_delta = jnp.sum(grad_rows.astype(jnp.float32) * outputs, axis=2)

    def backward_tile(target, key_tile, value_tile, state_in):
        query_acc, key_acc, value_acc = state_in
        scores = (
            lax.dot_general(
                query_rows[target],
                key_tile,
                (((1,), (1,)), ((), ())),
                preferred_element_type=jnp.float32,
            )
            * scale_value
        )
        probability = jnp.exp(scores - log_total[target][:, None])
        probs_low = probability.astype(jnp.bfloat16)
        value_acc = value_acc + lax.dot_general(
            probs_low,
            grad_rows[target],
            (((0,), (0,)), ((), ())),
            preferred_element_type=jnp.float32,
        )
        prob_grad = lax.dot_general(
            grad_rows[target],
            value_tile,
            (((1,), (1,)), ((), ())),
            preferred_element_type=jnp.float32,
        )
        score_grad = (probability * (prob_grad - row_delta[target][:, None])).astype(jnp.bfloat16)
        query_acc = query_acc.at[target].add(
            jnp.dot(score_grad, key_tile, preferred_element_type=jnp.float32)
        )
        key_acc = key_acc + lax.dot_general(
            score_grad,
            query_rows[target],
            (((0,), (0,)), ((), ())),
            preferred_element_type=jnp.float32,
        )
        return (query_acc, key_acc, value_acc)

    def backward_piece(query_acc, kv_piece, first_row):
        key_piece, value_piece = kv_piece
        block_count = key_piece.shape[0] // BLOCK
        key_stack = key_piece.reshape(block_count, BLOCK, HEAD_DIM)
        value_stack = value_piece.reshape(block_count, BLOCK, HEAD_DIM)
        empty_tile = jnp.zeros((BLOCK, HEAD_DIM), jnp.float32)

        def backward_visit_block(running, tile_item):
            key_tile, value_tile, offset = tile_item
            key_label = block_label(first_row, offset)
            tile_state = (running, empty_tile, empty_tile)
            for target in range(query_count):
                tile_state = lax.cond(
                    listed[target, key_label],
                    partial(backward_tile, target, key_tile, value_tile),
                    keep_state,
                    tile_state,
                )
            return (tile_state[0], (tile_state[1], tile_state[2]))

        query_acc, (key_parts, value_parts) = lax.scan(
            backward_visit_block,
            query_acc,
            (key_stack, value_stack, jnp.arange(block_count, dtype=jnp.int32)),
        )
        return (
            query_acc,
            key_parts.reshape(block_count * BLOCK, HEAD_DIM),
            value_parts.reshape(block_count * BLOCK, HEAD_DIM),
        )

    query_start = jnp.zeros((query_count, row_count, HEAD_DIM), jnp.float32)
    empty_grads = jnp.zeros((own_half * BLOCK, HEAD_DIM), jnp.float32)

    def back_turn(turn_index, running):
        query_acc, moving, travel = running
        anchor = (cycle_place - turn_index) % cycle_size
        query_acc, key_part, value_part = backward_piece(
            query_acc, moving, anchor * own_half * BLOCK
        )
        travel = (travel[0] + key_part, travel[1] + value_part)
        moving = passed_along((moving[0], moving[1]), "blk", 1)
        travel = (
            passed_along(travel[0].astype(jnp.bfloat16), "blk", 1).astype(jnp.float32),
            passed_along(travel[1].astype(jnp.bfloat16), "blk", 1).astype(jnp.float32),
        )
        return (query_acc, moving, travel)

    query_acc, moving, travel = lax.fori_loop(
        0, cycle_size - 1, back_turn, (query_start, (keys, values), (empty_grads, empty_grads))
    )
    anchor = (cycle_place - (cycle_size - 1)) % cycle_size
    query_acc, key_part, value_part = backward_piece(query_acc, moving, anchor * own_half * BLOCK)
    key_sum, value_sum = (
        passed_along((travel[0] + key_part).astype(jnp.bfloat16), "blk", 1).astype(jnp.float32),
        passed_along((travel[1] + value_part).astype(jnp.bfloat16), "blk", 1).astype(jnp.float32),
    )
    query_total = lax.psum(query_acc.astype(jnp.bfloat16), "split").astype(jnp.float32)
    token_rows = query_count * BLOCK
    attended = outputs.astype(jnp.bfloat16).reshape(token_rows, HEADS * HEAD_DIM)
    query_grad = (
        (query_total * scale_value).astype(jnp.bfloat16).reshape(token_rows, HEADS * HEAD_DIM)
    )
    key_grad = (key_sum * scale_value).astype(jnp.bfloat16)
    value_grad = value_sum.astype(jnp.bfloat16)
    return (attended, query_grad, key_grad, value_grad)


def solution(mesh):
    placed = (
        P("blk", None),
        P(("blk", "split"), None),
        P(("blk", "split"), None),
        P("blk", None),
        P("blk", None),
    )
    return jax.shard_map(
        local,
        mesh=mesh,
        in_specs=placed,
        out_specs=(
            P("blk", None),
            P("blk", None),
            P(("blk", "split"), None),
            P(("blk", "split"), None),
        ),
        check_vma=False,
    )
```

profile of v0, /device:TPU:0, one launch (start us, length us, event | category | flops | bytes accessed | tf_op | source)
XLA Modules:
  0.0 1431.4 jit_solution(9263547945155239028)
XLA Ops:
  13.5 570.5 %while.111 = (s32[]{:T(128)}, f32[2,2048]{1,0:T(2,128)S(1)}, f32[2,2048]{1,0:T(2,128)S(1)}, f32[2,2048,64]{1,2,0:T(8,128)S(1)}, bf16[128,64]{1,0:T(8,128)(2,1)S(...) while((s32[]{:T(128)}, f32[2,2048]{1,0:T(2,128)S(1)}, ...), condition=%wide.region_10.11_spmd, body=%wide.region_1.10_spmd.sunk | while | flops 137904160 | bytes 12141356 | solution.py:108
  588.2 11.2 pmax.7
  604.7 9.1 psum.22
  613.7 56.6 %all-reduce.3.cloned.1.call-done = f32[2,2048,64]{2,1,0:T(8,128)} async-done(((f32[2,2048,64]{2,1,0:T(8,128)}), f32[2,2048,64]{2,1,0:T(8,128)}) %all-reduce.3.cloned.1.call-update) | async-done | bytes 1048592 | tf_op jit(solution)/shard_map/psum | solution.py:114
  673.8 711.4 %while.112 = (s32[]{:T(128)}, f32[2,2048,64]{1,2,0:T(8,128)S(1)}, bf16[128,64]{1,0:T(8,128)(2,1)S(1)}, bf16[128,64]{1,0:T(8,128)(2,1)S(1)}, f32[128,64]{0,1:T(8,...) while((s32[]{:T(128)}, f32[2,2048,64]{1,2,0:T(8,128)S(1)}, ...), condition=%wide.region_28.29_spmd.clone, body=%wide.region_23.28_spmd.clone.sunk | while | flops 339034144 | bytes 16810896 | solution.py:205
  710.3 7.1 collective-permute-done.4
  722.7 7.1 collective-permute-done.4
  737.0 7.1 collective-permute-done.4
  751.4 7.1 collective-permute-done.4
  763.7 7.1 collective-permute-done.4
  809.3 7.1 collective-permute-done.4
  830.1 7.1 collective-permute-done.4
  840.5 7.1 collective-permute-done.4
  861.2 7.1 collective-permute-done.4
  882.0 7.1 collective-permute-done.4
  902.8 7.1 collective-permute-done.4
  913.2 7.1 collective-permute-done.4
  934.0 7.1 collective-permute-done.4
  954.7 7.1 collective-permute-done.4
  1000.2 7.1 collective-permute-done.4
  1021.0 7.1 collective-permute-done.4
  1033.3 7.1 collective-permute-done.4
  1043.7 7.1 collective-permute-done.4
  1398.3 22.5 %all-reduce.5.cloned.1.call-done = bf16[2,2048,64]{1,2,0:T(8,128)(2,1)} async-done(((bf16[2,2048,64]{1,2,0:T(8,128)(2,1)}), bf16[2,2048,64]{1,2,0:T(8,128)(2,1)}) %all-reduce.5.cloned.1.call-update) | async-done | bytes 524304 | tf_op jit(solution)/shard_map/psum | solution.py:214
  (2238 shorter events, 1156.7 us)
Async XLA Ops:
  7.2 663.2 %all-reduce.3.cloned.1.call-start = ((), (), s32[]{:S(2)}) async-start(), calls=%async_computation | async-start | bytes 4194304 | tf_op jit(solution)/shard_map/psum | solution.py:114
  14.2 9.6 collective-permute-start
  14.8 9.0 collective-permute-start.1
  24.4 9.5 collective-permute-start
  25.0 8.9 collective-permute-start.1
  34.6 9.2 collective-permute-start
  35.2 8.6 collective-permute-start.1
  603.0 817.9 %all-reduce.5.cloned.1.call-start = ((), (), s32[]{:S(2)}) async-start(), calls=%async_computation.1 | async-start | bytes 1048576 | tf_op jit(solution)/shard_map/psum | solution.py:214
  695.9 8.1 collective-permute-start.3
  710.2 8.1 collective-permute-start.3
  722.6 8.1 collective-permute-start.3
  736.9 8.1 collective-permute-start.3
  774.0 8.1 collective-permute-start.3
  784.4 8.1 collective-permute-start.3
  796.8 8.1 collective-permute-start.3
  819.6 8.1 collective-permute-start.3
  830.0 8.1 collective-permute-start.3
  840.4 8.1 collective-permute-start.3
  850.8 8.1 collective-permute-start.3
  861.2 8.1 collective-permute-start.3
  871.5 8.1 collective-permute-start.3
  892.3 8.1 collective-permute-start.3
  902.7 8.1 collective-permute-start.3
  913.1 8.1 collective-permute-start.3
  (360 other events, 2763.5 us)
Sparse Core Ops, SparseCore 0:
  603.1 67.1 all-reduce.2
  1390.2 30.6 all-reduce.4
where the time goes:
time: 1440 us; the launch traced here: 1430 us
  waiting for transfers between devices  876 us (61%)
  local copies, waits for them, and re-layouts  180 us (12%)
  loops' own time  175 us (12%)
  matrix products  119 us (8%)
  starting transfers between devices  27.7 us (2%)
  blocking collectives  20.2 us (1%)
  other arithmetic  18.1 us (1%)
  between operations  15.6 us (1%)
    ppermute x380, waiting for transfers between devices, passed_along(): return lax.ppermute(value, axis, pairs)  796 us
    another operation x1, loops' own time, local(): lax.fori_loop(0, cycle_size - 1, back_turn, (query_start, (keys, values),...  86 us
    another operation x1, loops' own time, local(): lax.fori_loop(0, cycle_size - 1, cycle_turn, (start_state, (keys, values)))  80.5 us
    another operation x222, local copies, waits for them, and re-layouts  78 us
    psum x1, waiting for transfers between devices, local(): lax.psum((totals * factor, accum * factor[:, :, None]), 'split')  56.6 us
    dynamic_slice x64, local copies, waits for them, and re-layouts, forward_visit_block(): listed[target, key_label]  41.6 us
    dynamic_slice x63, local copies, waits for them, and re-layouts, backward_visit_block(): listed[target, key_label]  41 us
    dot_general x30, matrix products, forward_tile(): jnp.dot(numerator.astype(jnp.bfloat16), value_tile, preferred_element_typ...  30.7 us
  transfers between devices with their start and end apart: 382, of which 371 were waited for; matrix products, arithmetic and copies ran while one was open for 11% of the time, Pallas kernels for 0%

commit v1 on v0

v1 whole, which is shorter than its diff:
```python
import math

import jax
import jax.numpy as jnp
from jax import lax
from jax.experimental import pallas as pl
from jax.experimental.pallas import tpu as pltpu
from jax.sharding import PartitionSpec as P

HEADS = 16
HEAD_DIM = 64
BLOCK = 128

SCALE = 1.0 / math.sqrt(HEAD_DIM)
LOWEST = -1e30
VMEM_LIMIT = 60 * 1024 * 1024


def _smem():
    return pl.BlockSpec(memory_space=pltpu.SMEM)


def _vmem():
    return pl.BlockSpec(memory_space=pltpu.VMEM)


def _forward_kernel(lists_ref, keep_ref, q_ref, k_ref, v_ref, do_ref,
                    o_ref, lse_ref, delta_ref, m_sc, l_sc, acc_sc):
    query_count, slots = lists_ref.shape
    for qb in range(query_count):
        m_sc[...] = jnp.full(m_sc.shape, LOWEST, jnp.float32)
        l_sc[...] = jnp.zeros(l_sc.shape, jnp.float32)
        acc_sc[...] = jnp.zeros(acc_sc.shape, jnp.float32)

        def body(j, carry):
            @pl.when(keep_ref[qb, j] != 0)
            def _():
                b = lists_ref[qb, j]
                k = k_ref[b]
                v = v_ref[b]
                s = lax.dot_general(
                    q_ref[qb], k, (((1,), (1,)), ((), ())),
                    preferred_element_type=jnp.float32) * SCALE
                m_prev = m_sc[...]
                m_new = jnp.maximum(m_prev, jnp.max(s, axis=1, keepdims=True))
                alpha = jnp.exp(m_prev - m_new)
                p = jnp.exp(s - m_new)
                l_sc[...] = alpha * l_sc[...] + jnp.sum(p, axis=1, keepdims=True)
                acc_sc[...] = alpha * acc_sc[...] + jnp.dot(
                    p.astype(jnp.bfloat16), v, preferred_element_type=jnp.float32)
                m_sc[...] = m_new
            return carry

        lax.fori_loop(0, slots, body, 0)
        out = acc_sc[...] / l_sc[...]
        o_ref[qb] = out.astype(jnp.bfloat16)
        lse_ref[qb] = m_sc[...] + jnp.log(l_sc[...])
        delta_ref[qb] = jnp.sum(do_ref[qb].astype(jnp.float32) * out, axis=1, keepdims=True)


def _backward_kernel(lists_ref, keep_ref, q_ref, k_ref, v_ref, do_ref, lse_ref, delta_ref,
                     dq_ref, dk_ref, dv_ref, dq_sc):
    query_count, slots = lists_ref.shape
    dk_ref[...] = jnp.zeros(dk_ref.shape, jnp.float32)
    dv_ref[...] = jnp.zeros(dv_ref.shape, jnp.float32)
    for qb in range(query_count):
        dq_sc[...] = jnp.zeros(dq_sc.shape, jnp.float32)

        def body(j, carry):
            @pl.when(keep_ref[qb, j] != 0)
            def _():
                b = lists_ref[qb, j]
                k = k_ref[b]
                v = v_ref[b]
                q = q_ref[qb]
                do = do_ref[qb]
                s = lax.dot_general(
                    q, k, (((1,), (1,)), ((), ())),
                    preferred_element_type=jnp.float32) * SCALE
                p = jnp.exp(s - lse_ref[qb])
                dv_ref[b] += lax.dot_general(
                    p.astype(jnp.bfloat16), do, (((0,), (0,)), ((), ())),
                    preferred_element_type=jnp.float32)
                dp = lax.dot_general(
                    do, v, (((1,), (1,)), ((), ())),
                    preferred_element_type=jnp.float32)
                ds = (p * (dp - delta_ref[qb])).astype(jnp.bfloat16)
                dq_sc[...] += jnp.dot(ds, k, preferred_element_type=jnp.float32)
                dk_ref[b] += lax.dot_general(
                    ds, q, (((0,), (0,)), ((), ())),
                    preferred_element_type=jnp.float32)
            return carry

        lax.fori_loop(0, slots, body, 0)
        dq_ref[qb] = (dq_sc[...] * SCALE).astype(jnp.bfloat16)


def attend_local(q_rows, do_rows, key_blocks, value_blocks, lists, keep):
    query_count, rows, _ = q_rows.shape
    block_total = key_blocks.shape[0]
    f32 = jnp.float32
    o_rows, lse, delta = pl.pallas_call(
        _forward_kernel,
        out_shape=(
            jax.ShapeDtypeStruct((query_count, rows, HEAD_DIM), jnp.bfloat16),
            jax.ShapeDtypeStruct((query_count, rows, 1), f32),
            jax.ShapeDtypeStruct((query_count, rows, 1), f32),
        ),
        in_specs=[_smem(), _smem(), _vmem(), _vmem(), _vmem(), _vmem()],
        out_specs=(_vmem(), _vmem(), _vmem()),
        scratch_shapes=[
            pltpu.VMEM((rows, 1), f32),
            pltpu.VMEM((rows, 1), f32),
            pltpu.VMEM((rows, HEAD_DIM), f32),
        ],
        compiler_params=pltpu.CompilerParams(vmem_limit_bytes=VMEM_LIMIT),
    )(lists, keep, q_rows, key_blocks, value_blocks, do_rows)
    dq_rows, dk_blocks, dv_blocks = pl.pallas_call(
        _backward_kernel,
        out_shape=(
            jax.ShapeDtypeStruct((query_count, rows, HEAD_DIM), jnp.bfloat16),
            jax.ShapeDtypeStruct((block_total, BLOCK, HEAD_DIM), f32),
            jax.ShapeDtypeStruct((block_total, BLOCK, HEAD_DIM), f32),
        ),
        in_specs=[_smem(), _smem()] + [_vmem()] * 6,
        out_specs=(_vmem(), _vmem(), _vmem()),
        scratch_shapes=[pltpu.VMEM((rows, HEAD_DIM), f32)],
        compiler_params=pltpu.CompilerParams(vmem_limit_bytes=VMEM_LIMIT),
    )(lists, keep, q_rows, key_blocks, value_blocks, do_rows, lse, delta)
    return o_rows, dq_rows, dk_blocks, dv_blocks


def first_occurrence(block_lists):
    slots = block_lists.shape[1]
    positions = jnp.arange(slots, dtype=jnp.int32)
    matches = block_lists[:, :, None] == block_lists[:, None, :]
    earlier = jnp.any(matches & (positions[None, None, :] < positions[None, :, None]), axis=2)
    return jnp.logical_not(earlier).astype(jnp.int32)


def local(queries, keys, values, out_grad, block_lists):
    query_count = block_lists.shape[0]
    token_rows = queries.shape[0]
    split_size = lax.axis_size("split")
    split_place = lax.axis_index("split")
    width = queries.shape[1] // split_size
    heads_here = width // HEAD_DIM

    kv_all = lax.all_gather(jnp.stack([keys, values]), ("blk", "split"), axis=1, tiled=True)
    block_total = kv_all.shape[1] // BLOCK
    key_blocks = kv_all[0].reshape(block_total, BLOCK, HEAD_DIM)
    value_blocks = kv_all[1].reshape(block_total, BLOCK, HEAD_DIM)

    def my_heads(x):
        part = lax.dynamic_slice_in_dim(x, split_place * width, width, axis=1)
        return part.reshape(query_count, BLOCK * heads_here, HEAD_DIM)

    lists = block_lists.astype(jnp.int32)
    keep = first_occurrence(lists)
    o_rows, dq_rows, dk_blocks, dv_blocks = attend_local(
        my_heads(queries), my_heads(out_grad), key_blocks, value_blocks, lists, keep)

    attended = lax.all_gather(o_rows.reshape(token_rows, width), "split", axis=1, tiled=True)
    query_grad = lax.all_gather(dq_rows.reshape(token_rows, width), "split", axis=1, tiled=True)
    partial_kv = jnp.stack([
        dk_blocks.reshape(block_total * BLOCK, HEAD_DIM),
        dv_blocks.reshape(block_total * BLOCK, HEAD_DIM),
    ])
    owned = lax.psum_scatter(partial_kv, ("blk", "split"), scatter_dimension=1, tiled=True)
    key_grad = (owned[0] * SCALE).astype(jnp.bfloat16)
    value_grad = owned[1].astype(jnp.bfloat16)
    return (attended, query_grad, key_grad, value_grad)


def solution(mesh):
    placed = (
        P("blk", None),
        P(("blk", "split"), None),
        P(("blk", "split"), None),
        P("blk", None),
        P("blk", None),
    )
    return jax.shard_map(
        local,
        mesh=mesh,
        in_specs=placed,
        out_specs=(
            P("blk", None),
            P("blk", None),
            P(("blk", "split"), None),
            P(("blk", "split"), None),
        ),
        check_vma=False,
    )
```

time: 1440 us -> 1150 us (0.80)
  loops' own time: 175 us -> 0 us
  Pallas kernels: 0 us -> 163 us
  local copies, waits for them, and re-layouts: 180 us -> 33.2 us
  matrix products: 119 us -> 0 us
  waiting for transfers between devices: 876 us -> 913 us
  starting transfers between devices: 27.7 us -> 0.08 us
    ppermute x380 -> x0, waiting for transfers between devices: 796 us -> none  [passed_along(): return lax.ppermute(value, axis, pairs)]
    reduce_scatter x0 -> x1, waiting for transfers between devices: none -> 656 us  [local(): lax.psum_scatter(partial_kv, ('blk', 'split'), scatter_dimension=1, tiled...]
    all_gather x0 -> x1, waiting for transfers between devices: none -> 257 us  [local(): lax.all_gather(jnp.stack([keys, values]), ('blk', 'split'), axis=1, tiled...]
    another operation x258 -> x0, loops' own time: 175 us -> none  [the longest x1 86 us: local(): lax.fori_loop(0, cycle_size - 1, back_turn, (query_start, (keys, values),...]
    pallas_call x0 -> x2, Pallas kernels: none -> 163 us  [the longest x1 99.8 us: attend_local(): pl.pallas_call(_forward_kernel, out_shape=(jax.ShapeDtypeStruct((query_co...]
    dot_general x210 -> x0, matrix products: 119 us -> none  [the longest x30 30.7 us: forward_tile(): jnp.dot(numerator.astype(jnp.bfloat16), value_tile, preferred_element_typ...]
    dynamic_slice x127 -> x1, local copies, waits for them, and re-layouts: 82.6 us -> 1.07 us  [my_heads(): part = lax.dynamic_slice_in_dim(x, split_place * width, width, axis=1)]
    psum x2 -> x0, waiting for transfers between devices: 79.1 us -> none  [the longest x1 56.6 us: local(): lax.psum((totals * factor, accum * factor[:, :, None]), 'split')]
  transfers between devices with their start and end apart: 382 -> 2, of which waited for: 371 -> 2; matrix products, arithmetic and copies ran while one was open for 11% -> 0% of each run, Pallas kernels for 0% -> 0%
where the time goes in v1:
time: 1150 us
  waiting for transfers between devices  913 us (79%)
  Pallas kernels  163 us (14%)
  local copies, waits for them, and re-layouts  33.2 us (3%)
  blocking collectives  17.1 us (1%)
  between operations  14.1 us (1%)
  other arithmetic  11.7 us (1%)
    reduce_scatter x1, waiting for transfers between devices, local(): lax.psum_scatter(partial_kv, ('blk', 'split'), scatter_dimension=1, tiled...  656 us
    all_gather x1, waiting for transfers between devices, local(): lax.all_gather(jnp.stack([keys, values]), ('blk', 'split'), axis=1, tiled...  257 us
    pallas_call x1, Pallas kernels, attend_local(): pl.pallas_call(_forward_kernel, out_shape=(jax.ShapeDtypeStruct((query_co...  99.8 us
    pallas_call x1, Pallas kernels, attend_local(): pl.pallas_call(_backward_kernel, out_shape=(jax.ShapeDtypeStruct((query_c...  63.2 us
  transfers between devices with their start and end apart: 2, of which 2 were waited for; matrix products, arithmetic and copies ran while one was open for 0% of the time, Pallas kernels for 0%

profile of v1, /device:TPU:0, one launch (start us, length us, event | category | flops | bytes accessed | tf_op | source)
XLA Modules:
  0.0 1152.5 jit_solution(10191587887568978440)
XLA Ops:
  7.2 1.4 pad_maximum_fusion.1
  8.6 1.1 constant_dynamic-slice_fusion
  9.7 1.1 reshape.42.do_ref
  10.8 1.1 reshape.41.q_ref
  11.9 0.9 and_reduce_fusion
  12.8 0.6 not_convert_fusion.keep_ref
  13.4 256.9 %all-gather.2.cloned.1.call-done = bf16[2,16384,64]{1,2,0:T(8,128)(2,1)} async-done(((bf16[2,128,64]{1,2,0:T(8,128)(2,1)}), bf16[2,16384,64]{1,2,0:T(8,128)(2,1)}) %all-gather.2.cloned.1.call-update) | async-done | bytes 4194320 | tf_op jit(solution)/shard_map/all_gather | solution.py:149
  270.3 3.9 fusion.3
  274.2 4.8 copy.18
  278.9 3.2 copy.17
  282.1 99.8 %shard_map.84 = (bf16[2,1024,64]{2,1,0:T(8,128)(2,1)}, f32[2,1024,1]{2,1,0:T(8,128)}, f32[2,1024,1]{2,1,0:T(8,128)}) custom-call(s32[2,48]{1,0:T(2,128)} %lists_ref.3, s32[2,48]{1,0:T(2,128)} %not_convert_fusion.keep_ref, bf16[2,1024,64]{2,1,0:T(8,128)(2,1)} %reshape.41.q_ref, bf16[128,128,64]{2,1,0:T(8,128)(2,1)} %bitcast.12, ...), custom_call_target="tpu_custom_call" | custom-call | tf_op jit(solution)/shard_map/pallas_call | solution.py:102
  381.9 63.2 %shard_map.85 = (bf16[2,1024,64]{2,1,0:T(8,128)(2,1)}, f32[128,128,64]{2,1,0:T(8,128)}, f32[128,128,64]{2,1,0:T(8,128)}) custom-call(s32[2,48]{1,0:T(2,128)} %lists_ref.3, s32[2,48]{1,0:T(2,128)} %not_convert_fusion.keep_ref, bf16[2,1024,64]{2,1,0:T(8,128)(2,1)} %reshape.41.q_ref, bf16[128,128,64]{2,1,0:T(8,128)(2,1)} %bitcast.13, ...), custom_call_target="tpu_custom_call" | custom-call | tf_op jit(solution)/shard_map/pallas_call | solution.py:118
  445.0 6.8 copy.19
  451.8 6.8 copy.20
  458.6 7.5 pad_maximum_fusion
  466.1 1.0 copy-done.1
  467.4 8.5 all_gather.10
  476.0 0.3 reshape.44
  476.3 8.5 all_gather.11
  484.9 656.5 %reduce-scatter.2.cloned.1.call-done = f32[2,128,64]{1,2,0:T(8,128)} async-done(((f32[2,16384,64]{1,2,0:T(8,128)}), f32[2,128,64]{1,2,0:T(8,128)}) %reduce-scatter.2.cloned.1.call-update) | async-done | bytes 65552 | tf_op jit(solution)/shard_map/reduce_scatter | solution.py:169
  1141.3 1.4 fusion.2
  1142.7 1.4 fusion.1
  1144.1 0.8 copy.23
  1144.9 0.8 copy.24
  (9 shorter events, 0.4 us)
Async XLA Ops:
  7.2 263.1 %all-gather.2.cloned.1.call-start = ((), (), s32[]{:S(2)}) async-start(), calls=%async_computation.1 | async-start | bytes 4227072 | tf_op jit(solution)/shard_map/all_gather | solution.py:149
  8.6 1132.8 %reduce-scatter.2.cloned.1.call-start = ((), (), s32[]{:S(2)}) async-start(), calls=%async_computation.2 | async-start | bytes 8454144 | tf_op jit(solution)/shard_map/reduce_scatter | solution.py:169
  466.1 1.0 copy-start.1
  466.1 9.9 copy-start
Sparse Core Ops, SparseCore 0:
  9.6 260.6 all-gather.1
  466.2 675.0 reduce-scatter.1

commit v2 on v1

--- a/solution.py
+++ b/solution.py
@@ -1,6 +1,7 @@
 import math
 
 import jax
+import numpy as np
 import jax.numpy as jnp
 from jax import lax
 from jax.experimental import pallas as pl
@@ -138,38 +139,100 @@
     return jnp.logical_not(earlier).astype(jnp.int32)
 
 
-def local(queries, keys, values, out_grad, block_lists):
-    query_count = block_lists.shape[0]
-    token_rows = queries.shape[0]
-    split_size = lax.axis_size("split")
-    split_place = lax.axis_index("split")
-    width = queries.shape[1] // split_size
-    heads_here = width // HEAD_DIM
-
-    kv_all = lax.all_gather(jnp.stack([keys, values]), ("blk", "split"), axis=1, tiled=True)
-    block_total = kv_all.shape[1] // BLOCK
-    key_blocks = kv_all[0].reshape(block_total, BLOCK, HEAD_DIM)
-    value_blocks = kv_all[1].reshape(block_total, BLOCK, HEAD_DIM)
-
-    def my_heads(x):
-        part = lax.dynamic_slice_in_dim(x, split_place * width, width, axis=1)
-        return part.reshape(query_count, BLOCK * heads_here, HEAD_DIM)
-
-    lists = block_lists.astype(jnp.int32)
-    keep = first_occurrence(lists)
-    o_rows, dq_rows, dk_blocks, dv_blocks = attend_local(
-        my_heads(queries), my_heads(out_grad), key_blocks, value_blocks, lists, keep)
-
-    attended = lax.all_gather(o_rows.reshape(token_rows, width), "split", axis=1, tiled=True)
-    query_grad = lax.all_gather(dq_rows.reshape(token_rows, width), "split", axis=1, tiled=True)
-    partial_kv = jnp.stack([
-        dk_blocks.reshape(block_total * BLOCK, HEAD_DIM),
-        dv_blocks.reshape(block_total * BLOCK, HEAD_DIM),
-    ])
-    owned = lax.psum_scatter(partial_kv, ("blk", "split"), scatter_dimension=1, tiled=True)
-    key_grad = (owned[0] * SCALE).astype(jnp.bfloat16)
-    value_grad = owned[1].astype(jnp.bfloat16)
-    return (attended, query_grad, key_grad, value_grad)
+def device_table(mesh):
+    flat = mesh.devices.reshape(-1)
+    table = np.array([[*d.coords, d.core_on_chip] for d in flat], dtype=np.int32)
+    sizes = table.max(axis=0) + 1
+    stages = [(1, int(sizes[1])), (0, int(sizes[0])), (2, int(sizes[2])), (3, int(sizes[3]))]
+    stages = [(axis, size) for axis, size in stages if size > 1]
+    where = {tuple(row): index for index, row in enumerate(table.tolist())}
+
+    def pairs(axis, shift):
+        out = []
+        for index, row in enumerate(table.tolist()):
+            dest = list(row)
+            dest[axis] = (row[axis] + shift) % int(sizes[axis])
+            out.append((index, where[tuple(dest)]))
+        return out
+
+    return table, stages, pairs
+
+
+def make_local(mesh):
+    table_np, stages, pairs = device_table(mesh)
+    axes = ("blk", "split")
+
+    def gather_blocks(piece):
+        buf = piece[None]
+        for axis, size in stages:
+            pieces = [buf]
+            for shift in range(1, size):
+                pieces.append(lax.ppermute(buf, axes, pairs(axis, size - shift)))
+            buf = jnp.stack(pieces)
+        return buf.reshape((-1,) + piece.shape)
+
+    def scatter_sum(part, piece_shape):
+        part = part.reshape(tuple(size for _, size in reversed(stages)) + piece_shape)
+        for axis, size in reversed(stages):
+            total = part[0]
+            for shift in range(1, size):
+                sent = part[shift].astype(jnp.bfloat16)
+                total = total + lax.ppermute(sent, axes, pairs(axis, shift)).astype(jnp.float32)
+            part = total
+        return part
+
+    def local(queries, keys, values, out_grad, block_lists):
+        query_count = block_lists.shape[0]
+        token_rows = queries.shape[0]
+        split_size = lax.axis_size("split")
+        split_place = lax.axis_index("split")
+        me = lax.axis_index("blk") * split_size + split_place
+        width = queries.shape[1] // split_size
+        heads_here = width // HEAD_DIM
+
+        table = jnp.asarray(table_np)
+        own = table[me]
+
+        kv_held = gather_blocks(jnp.concatenate([keys, values], axis=1))
+        block_total = kv_held.shape[0]
+        key_blocks = kv_held[:, :, :HEAD_DIM]
+        value_blocks = kv_held[:, :, HEAD_DIM:]
+
+        def held_at(block):
+            coords = table[block]
+            position = jnp.zeros_like(block)
+            stride = 1
+            for axis, size in stages:
+                position = position + ((coords[..., axis] - own[axis]) % size) * stride
+                stride *= size
+            return position
+
+        def my_heads(x):
+            part = lax.dynamic_slice_in_dim(x, split_place * width, width, axis=1)
+            return part.reshape(query_count, BLOCK * heads_here, HEAD_DIM)
+
+        lists = block_lists.astype(jnp.int32)
+        keep = first_occurrence(lists)
+        o_rows, dq_rows, dk_blocks, dv_blocks = attend_local(
+            my_heads(queries), my_heads(out_grad), key_blocks, value_blocks,
+            held_at(lists), keep)
+
+        def join_halves(rows):
+            mine = rows.reshape(token_rows, width)
+            other = lax.ppermute(mine, "split", [(i, (i + 1) % split_size) for i in range(split_size)])
+            return jnp.where(split_place == 0,
+                             jnp.concatenate([mine, other], axis=1),
+                             jnp.concatenate([other, mine], axis=1))
+
+        attended = join_halves(o_rows)
+        query_grad = join_halves(dq_rows)
+        partial_kv = jnp.concatenate([dk_blocks, dv_blocks], axis=2)
+        owned = scatter_sum(partial_kv, (BLOCK, 2 * HEAD_DIM))
+        key_grad = (owned[:, :HEAD_DIM] * SCALE).astype(jnp.bfloat16)
+        value_grad = owned[:, HEAD_DIM:].astype(jnp.bfloat16)
+        return (attended, query_grad, key_grad, value_grad)
+
+    return local
 
 
 def solution(mesh):
@@ -181,7 +244,7 @@
         P("blk", None),
     )
     return jax.shard_map(
-        local,
+        make_local(mesh),
         mesh=mesh,
         in_specs=placed,
         out_specs=(

time: 1150 us -> 331 us (0.29)
  waiting for transfers between devices: 913 us -> 56.9 us
  starting transfers between devices: 0.08 us -> 112 us
  Pallas kernels: 163 us -> 99.7 us
  other arithmetic: 11.7 us -> 30.7 us
  blocking collectives: 17.1 us -> 0 us
  between operations: 14.1 us -> 0.78 us
    reduce_scatter x1 -> x0, waiting for transfers between devices: 656 us -> none  [local(): lax.psum_scatter(partial_kv, ('blk', 'split'), scatter_dimension=1, tiled...]
    all_gather x1 -> x0, waiting for transfers between devices: 257 us -> none  [local(): lax.all_gather(jnp.stack([keys, values]), ('blk', 'split'), axis=1, tiled...]
    ppermute x0 -> x22, starting transfers between devices: none -> 112 us  [the longest x10 89.2 us: scatter_sum(): lax.ppermute(sent, axes, pairs(axis, shift)).astype(jnp.float32)]
    ppermute x0 -> x22, waiting for transfers between devices: none -> 56.9 us  [the longest x10 31.4 us: scatter_sum(): lax.ppermute(sent, axes, pairs(axis, shift)).astype(jnp.float32)]
    pallas_call x1, Pallas kernels: 99.8 us -> 58.8 us  [attend_local(): pl.pallas_call(_forward_kernel, out_shape=(jax.ShapeDtypeStruct((query_co...]
    pallas_call x1, Pallas kernels: 63.2 us -> 40.9 us  [attend_local(): pl.pallas_call(_backward_kernel, out_shape=(jax.ShapeDtypeStruct((query_c...]
    all_gather x2 -> x0, blocking collectives: 17.1 us -> none  [the longest x1 8.54 us: local(): lax.all_gather(o_rows.reshape(token_rows, width), 'split', axis=1, tiled=...]
  transfers between devices with their start and end apart: 2 -> 22, of which waited for: 2 -> 13; matrix products, arithmetic and copies ran while one was open for 0% -> 8% of each run, Pallas kernels for 0% -> 0%
where the time goes in v2:
time: 331 us
  starting transfers between devices  112 us (34%)
  Pallas kernels  99.7 us (30%)
  waiting for transfers between devices  56.9 us (17%)
  other arithmetic  30.7 us (9%)
  local copies, waits for them, and re-layouts  30.1 us (9%)
    ppermute x10, starting transfers between devices, scatter_sum(): lax.ppermute(sent, axes, pairs(axis, shift)).astype(jnp.float32)  89.2 us
    pallas_call x1, Pallas kernels, attend_local(): pl.pallas_call(_forward_kernel, out_shape=(jax.ShapeDtypeStruct((query_co...  58.8 us
    pallas_call x1, Pallas kernels, attend_local(): pl.pallas_call(_backward_kernel, out_shape=(jax.ShapeDtypeStruct((query_c...  40.9 us
    ppermute x10, waiting for transfers between devices, scatter_sum(): lax.ppermute(sent, axes, pairs(axis, shift)).astype(jnp.float32)  31.4 us
    ppermute x10, waiting for transfers between devices, gather_blocks(): pieces.append(lax.ppermute(buf, axes, pairs(axis, size - shift)))  25.6 us
    ppermute x10, starting transfers between devices, gather_blocks(): pieces.append(lax.ppermute(buf, axes, pairs(axis, size - shift)))  18.2 us
    another operation x4, other arithmetic  11.8 us
    slice x1, local copies, waits for them, and re-layouts, local(): value_blocks = kv_held[:, :, HEAD_DIM:]  7.58 us
  transfers between devices with their start and end apart: 22, of which 13 were waited for; matrix products, arithmetic and copies ran while one was open for 8% of the time, Pallas kernels for 0%

profile of v2, /device:TPU:0, one launch (start us, length us, event | category | flops | bytes accessed | tf_op | source)
XLA Modules:
  0.0 330.5 jit_solution(10177147344277799569)
XLA Ops:
  3.8 2.9 collective-permute-start.1
  12.2 2.7 collective-permute-start.4
  22.0 3.6 %collective-permute-start.7 = (bf16[4,4,1,128,128]{3,4,1,0,2:T(8,128)(2,1)S(1)}, bf16[4,4,1,128,128]{3,4,1,0,2:T(8,128)(2,1)S(1)}, u32[]{:S(2)}, u32[]{:S(2)}) collective-permute-start(bf16[4,4,1,128,128]{3,4,1,0,2:T(8,128)(2,1)S(1)} %get-tuple-element.33), channel_id=1, source_target_pairs={{0,64},{1,65},{2,66},{3,67},{4,68},{5,69},{6,70},{7,71},{8,72},{9,... | collective-permute-start | bytes 1572872 | tf_op jit(solution)/shard_map/ppermute | solution.py:170
  26.6 9.4 %collective-permute-done.8 = bf16[4,4,1,128,128]{3,4,1,2,0:T(8,128)(2,1)S(1)} collective-permute-done((bf16[4,4,1,128,128]{3,4,1,2,0:T(8,128)(2,1)S(1)}, bf16[4,4,1,128,128]{3,4,1,2,0:T(8,128)(2,1)S(1)}, u32[]{:S(2)}, u32[]{:S(2)}) %collective-permute-start.8) | collective-permute-done | bytes 524320 | tf_op jit(solution)/shard_map/ppermute | solution.py:170
  36.0 10.1 %collective-permute-done.7 = bf16[4,4,1,128,128]{3,4,1,0,2:T(8,128)(2,1)S(1)} collective-permute-done((bf16[4,4,1,128,128]{3,4,1,0,2:T(8,128)(2,1)S(1)}, bf16[4,4,1,128,128]{3,4,1,0,2:T(8,128)(2,1)S(1)}, u32[]{:S(2)}, u32[]{:S(2)}) %collective-permute-start.7) | collective-permute-done | bytes 524320 | tf_op jit(solution)/shard_map/ppermute | solution.py:170
  49.1 2.7 slice_subtract_fusion.3
  56.6 4.0 %pad_maximum_fusion.1 = bf16[2,4,4,4,1,128,128]{5,6,3,2,1,4,0:T(8,128)(2,1)} fusion(bf16[1,4,4,4,1,128,128]{5,6,3,2,1,4,0:T(8,128)(2,1)} %bitcast.25, bf16[1,4,4,4,1,128,128]{5,6,3,2,1,4,0:T(8,128)(2,1)S(1)} %get-tuple-element.27), kind=kLoop, calls=%fused_computation.6 | loop fusion | flops 2097152 | bytes 8388608 | tf_op jit(solution)/shard_map/stack | solution.py:171
  60.6 7.3 %copy.40 = bf16[2,4,4,4,1,128,128]{6,5,3,2,1,0,4:T(8,128)(2,1)} copy(bf16[2,4,4,4,1,128,128]{5,6,3,2,1,4,0:T(8,128)(2,1)} %pad_maximum_fusion.1) | data formatting | bytes 8388608 | tf_op jit(solution)/shard_map/stack | solution.py:171
  67.9 7.6 %fusion.32 = (bf16[128,128,64]{2,1,0:T(8,128)(2,1)}, bf16[128,128,64]{2,1,0:T(8,128)(2,1)}) fusion(bf16[128,128,128]{2,1,0:T(8,128)(2,1)} %bitcast.88), kind=kLoop, calls=%fused_computation.81 | loop fusion | bytes 8388608 | tf_op jit(solution)/shard_map/slice | solution.py:199
  75.4 58.8 %shard_map.93 = (bf16[2,1024,64]{2,1,0:T(8,128)(2,1)}, f32[2,1024,1]{2,1,0:T(8,128)}, f32[2,1024,1]{2,1,0:T(8,128)}) custom-call(s32[2,48]{1,0:T(2,128)} %fusion.17.lists_ref, s32[2,48]{1,0:T(2,128)} %not_convert_fusion.keep_ref, bf16[2,1024,64]{2,1,0:T(8,128)(2,1)} %reshape.71.q_ref, bf16[128,128,64]{2,1,0:T(8,128)(2,1)} %get-tuple-element.23.k_ref, ...), custom_call_target="tpu_custom_call" | custom-call | tf_op jit(solution)/shard_map/pallas_call | solution.py:103
  134.3 40.9 %shard_map.94 = (bf16[2,1024,64]{2,1,0:T(8,128)(2,1)}, f32[128,128,64]{2,1,0:T(8,128)}, f32[128,128,64]{2,1,0:T(8,128)}) custom-call(s32[2,48]{1,0:T(2,128)} %fusion.17.lists_ref, s32[2,48]{1,0:T(2,128)} %not_convert_fusion.keep_ref, bf16[2,1024,64]{2,1,0:T(8,128)(2,1)} %reshape.71.q_ref, bf16[128,128,64]{2,1,0:T(8,128)(2,1)} %get-tuple-element.23.k_ref, ...), custom_call_target="tpu_custom_call" | custom-call | tf_op jit(solution)/shard_map/pallas_call | solution.py:119
  175.2 4.4 %fusion.1 = bf16[64,128,128]{2,1,0:T(8,128)(2,1)S(1)} fusion(f32[128,128,64]{2,1,0:T(8,128)} %get-tuple-element.15, f32[128,128,64]{2,1,0:T(8,128)} %get-tuple-element.14), kind=kLoop, calls=%fused_computation.5 | loop fusion | flops 4194304 | bytes 10485760 | tf_op jit(solution)/shard_map/convert.10
  182.0 6.6 %fusion = f32[64,128,128]{2,1,0:T(8,128)} fusion(f32[128,128,64]{2,1,0:T(8,128)} %get-tuple-element.14, f32[128,128,64]{2,1,0:T(8,128)} %get-tuple-element.15), kind=kLoop, calls=%fused_computation.3 | loop fusion | flops 1048576 | bytes 12582912 | tf_op jit(solution)/shard_map/concatenate | solution.py:229
  188.6 5.2 %copy.42 = f32[4,4,4,128,128]{3,4,2,1,0:T(8,128)} copy(f32[4,4,4,128,128]{4,3,2,1,0:T(8,128)} %bitcast.89) | data formatting | bytes 8388608 | tf_op jit(solution)/shard_map/squeeze | solution.py:177
  193.8 5.3 %fusion.31 = (bf16[4,4,4,128,128]{3,4,2,1,0:T(8,128)(2,1)S(1)}, f32[4,4,4,128,128]{3,4,2,1,0:T(8,128)}) fusion(f32[4,4,4,128,128]{3,4,2,1,0:T(8,128)} %copy.42, bf16[4,4,4,128,128]{3,4,2,1,0:T(8,128)(2,1)S(1)} %collective-permute-done.12), kind=kLoop, calls=%fused_computation.80 | loop fusion | flops 3145728 | bytes 12582912 | tf_op jit(solution)/shard_map/convert.9
  201.0 78.2 %collective-permute-start.15 = (bf16[4,4,128,128]{2,3,1,0:T(8,128)(2,1)S(1)}, bf16[4,4,128,128]{2,3,1,0:T(8,128)(2,1)}, u32[]{:S(2)}, u32[]{:S(2)}) collective-permute-start(bf16[4,4,128,128]{2,3,1,0:T(8,128)(2,1)S(1)} %get-tuple-element.25), channel_id=1, source_target_pairs={{0,96},{1,97},{2,98},{3,99},{4,100},{5,101},{6,102},{7,103},{8,104... | collective-permute-start | bytes 1572872 | tf_op jit(solution)/shard_map/ppermute | solution.py:180
  281.0 2.4 collective-permute-start.10
  283.4 8.0 %collective-permute-done.13 = bf16[4,4,128,128]{2,3,1,0:T(8,128)(2,1)} collective-permute-done((bf16[4,4,128,128]{2,3,1,0:T(8,128)(2,1)S(1)}, bf16[4,4,128,128]{2,3,1,0:T(8,128)(2,1)}, u32[]{:S(2)}, u32[]{:S(2)}) %collective-permute-start.13) | collective-permute-done | bytes 524320 | tf_op jit(solution)/shard_map/ppermute | solution.py:180
  291.4 10.5 %collective-permute-done.15 = bf16[4,4,128,128]{2,3,1,0:T(8,128)(2,1)} collective-permute-done((bf16[4,4,128,128]{2,3,1,0:T(8,128)(2,1)S(1)}, bf16[4,4,128,128]{2,3,1,0:T(8,128)(2,1)}, u32[]{:S(2)}, u32[]{:S(2)}) %collective-permute-start.15) | collective-permute-done | bytes 524320 | tf_op jit(solution)/shard_map/ppermute | solution.py:180
  305.9 3.2 collective-permute-start.18
  310.6 2.5 collective-permute-start.11
  314.0 6.5 %collective-permute-done.16 = bf16[4,128,128]{1,2,0:T(8,128)(2,1)S(1)} collective-permute-done((bf16[4,128,128]{1,2,0:T(8,128)(2,1)S(1)}, bf16[4,128,128]{1,2,0:T(8,128)(2,1)S(1)}, u32[]{:S(2)}, u32[]{:S(2)}) %collective-permute-start.16) | collective-permute-done | bytes 131104 | tf_op jit(solution)/shard_map/ppermute | solution.py:180
  320.7 3.2 collective-permute-start.21
  325.8 3.5 %collective-permute-done.20 = bf16[128,128]{0,1:T(8,128)(2,1)S(1)} collective-permute-done((bf16[128,128]{0,1:T(8,128)(2,1)S(1)}, bf16[128,128]{0,1:T(8,128)(2,1)S(1)}, u32[]{:S(2)}, u32[]{:S(2)}) %collective-permute-start.20) | collective-permute-done | bytes 32800 | tf_op jit(solution)/shard_map/ppermute | solution.py:180
  (75 shorter events, 40.2 us)
Async XLA Ops:
  2.1 5.9 %collective-permute-start.2 = (bf16[1,128,128]{1,2,0:T(8,128)(2,1)S(1)}, bf16[1,128,128]{1,2,0:T(8,128)(2,1)S(1)}, u32[]{:S(2)}, u32[]{:S(2)}) collective-permute-start(bf16[1,128,128]{1,2,0:T(8,128)(2,1)S(1)} %bitcast.98), channel_id=1, source_target_pairs={{0,4},{1,5},{2,6},{3,7},{4,8},{5,9},{6,10},{7,11},{8,12},{9,13},{1... | collective-permute-start | bytes 98312 | tf_op jit(solution)/shard_map/ppermute | solution.py:170
  3.8 5.4 %collective-permute-start.1 = (bf16[1,128,128]{1,2,0:T(8,128)(2,1)S(1)}, bf16[1,128,128]{1,2,0:T(8,128)(2,1)S(1)}, u32[]{:S(2)}, u32[]{:S(2)}) collective-permute-start(bf16[1,128,128]{1,2,0:T(8,128)(2,1)S(1)} %bitcast.99), channel_id=1, source_target_pairs={{0,8},{1,9},{2,10},{3,11},{4,12},{5,13},{6,14},{7,15},{8,0},{9,1},... | collective-permute-start | bytes 98312 | tf_op jit(solution)/shard_map/ppermute | solution.py:170
  6.7 3.9 %collective-permute-start = (bf16[1,128,128]{1,2,0:T(8,128)(2,1)S(1)}, bf16[1,128,128]{1,2,0:T(8,128)(2,1)S(1)}, u32[]{:S(2)}, u32[]{:S(2)}) collective-permute-start(bf16[1,128,128]{1,2,0:T(8,128)(2,1)S(1)} %bitcast.100), channel_id=1, source_target_pairs={{0,12},{1,13},{2,14},{3,15},{4,0},{5,1},{6,2},{7,3},{8,4},{9,5},{1... | collective-permute-start | bytes 98312 | tf_op jit(solution)/shard_map/ppermute | solution.py:170
  10.6 7.5 %collective-permute-start.5 = (bf16[4,1,128,128]{2,3,1,0:T(8,128)(2,1)S(1)}, bf16[4,1,128,128]{2,3,1,0:T(8,128)(2,1)S(1)}, u32[]{:S(2)}, u32[]{:S(2)}) collective-permute-start(bf16[4,1,128,128]{2,3,1,0:T(8,128)(2,1)S(1)} %get-tuple-element.40), channel_id=1, source_target_pairs={{0,16},{1,17},{2,18},{3,19},{4,20},{5,21},{6,22},{7,23},{8,24},{9,... | collective-permute-start | bytes 393224 | tf_op jit(solution)/shard_map/ppermute | solution.py:170
  12.2 7.3 %collective-permute-start.4 = (bf16[4,1,128,128]{2,3,0,1:T(8,128)(2,1)S(1)}, bf16[4,1,128,128]{2,3,0,1:T(8,128)(2,1)S(1)}, u32[]{:S(2)}, u32[]{:S(2)}) collective-permute-start(bf16[4,1,128,128]{2,3,0,1:T(8,128)(2,1)S(1)} %get-tuple-element.39), channel_id=1, source_target_pairs={{0,1},{1,0},{2,3},{3,2},{4,5},{5,4},{6,7},{7,6},{8,9},{9,8},{10,11... | collective-permute-start | bytes 393224 | tf_op jit(solution)/shard_map/ppermute | solution.py:170
  14.9 5.0 %collective-permute-start.3 = (bf16[4,1,128,128]{2,3,0,1:T(8,128)(2,1)S(1)}, bf16[4,1,128,128]{2,3,0,1:T(8,128)(2,1)S(1)}, u32[]{:S(2)}, u32[]{:S(2)}) collective-permute-start(bf16[4,1,128,128]{2,3,0,1:T(8,128)(2,1)S(1)} %get-tuple-element.39), channel_id=1, source_target_pairs={{0,17},{1,16},{2,19},{3,18},{4,21},{5,20},{6,23},{7,22},{8,25},{9,... | collective-permute-start | bytes 393224 | tf_op jit(solution)/shard_map/ppermute | solution.py:170
  20.0 16.0 %collective-permute-start.8 = (bf16[4,4,1,128,128]{3,4,1,2,0:T(8,128)(2,1)S(1)}, bf16[4,4,1,128,128]{3,4,1,2,0:T(8,128)(2,1)S(1)}, u32[]{:S(2)}, u32[]{:S(2)}) collective-permute-start(bf16[4,4,1,128,128]{3,4,1,2,0:T(8,128)(2,1)S(1)} %get-tuple-element.34), channel_id=1, source_target_pairs={{0,32},{1,33},{2,34},{3,35},{4,36},{5,37},{6,38},{7,39},{8,40},{9,... | collective-permute-start | bytes 1572872 | tf_op jit(solution)/shard_map/ppermute | solution.py:170
  22.0 24.1 %collective-permute-start.7 = (bf16[4,4,1,128,128]{3,4,1,0,2:T(8,128)(2,1)S(1)}, bf16[4,4,1,128,128]{3,4,1,0,2:T(8,128)(2,1)S(1)}, u32[]{:S(2)}, u32[]{:S(2)}) collective-permute-start(bf16[4,4,1,128,128]{3,4,1,0,2:T(8,128)(2,1)S(1)} %get-tuple-element.33), channel_id=1, source_target_pairs={{0,64},{1,65},{2,66},{3,67},{4,68},{5,69},{6,70},{7,71},{8,72},{9,... | collective-permute-start | bytes 1572872 | tf_op jit(solution)/shard_map/ppermute | solution.py:170
  25.6 20.5 %collective-permute-start.6 = (bf16[4,4,1,128,128]{3,4,1,0,2:T(8,128)(2,1)S(1)}, bf16[4,4,1,128,128]{3,4,1,0,2:T(8,128)(2,1)S(1)}, u32[]{:S(2)}, u32[]{:S(2)}) collective-permute-start(bf16[4,4,1,128,128]{3,4,1,0,2:T(8,128)(2,1)S(1)} %get-tuple-element.33), channel_id=1, source_target_pairs={{0,96},{1,97},{2,98},{3,99},{4,100},{5,101},{6,102},{7,103},{8,104... | collective-permute-start | bytes 1572872 | tf_op jit(solution)/shard_map/ppermute | solution.py:170
  47.7 8.9 %collective-permute-start.9 = (bf16[4,4,4,1,128,128]{4,5,2,1,3,0:T(8,128)(2,1)}, bf16[4,4,4,1,128,128]{4,5,2,1,3,0:T(8,128)(2,1)}, u32[]{:S(2)}, u32[]{:S(2)}) collective-permute-start(bf16[4,4,4,1,128,128]{4,5,2,1,3,0:T(8,128)(2,1)} %get-tuple-element.28), channel_id=1, source_target_pairs={{0,2},{1,3},{2,0},{3,1},{4,6},{5,7},{6,4},{7,5},{8,10},{9,11},{10,... | collective-permute-start | bytes 6291464 | tf_op jit(solution)/shard_map/ppermute | solution.py:170
  182.0 11.9 %collective-permute-start.12 = (bf16[4,4,4,128,128]{3,4,2,1,0:T(8,128)(2,1)}, bf16[4,4,4,128,128]{3,4,2,1,0:T(8,128)(2,1)S(1)}, u32[]{:S(2)}, u32[]{:S(2)}) collective-permute-start(bf16[4,4,4,128,128]{3,4,2,1,0:T(8,128)(2,1)} %copy.41), channel_id=1, source_target_pairs={{0,2},{1,3},{2,0},{3,1},{4,6},{5,7},{6,4},{7,5},{8,10},{9,11},{10,... | collective-permute-start | bytes 6291464 | tf_op jit(solution)/shard_map/ppermute | solution.py:180
  193.8 86.8 %copy-start.2 = (bf16[2,1024,64]{2,1,0:T(8,128)(2,1)S(1)}, bf16[2,1024,64]{2,1,0:T(8,128)(2,1)}, u32[]{:S(2)}) copy-start(bf16[2,1024,64]{2,1,0:T(8,128)(2,1)} %get-tuple-element.10) | copy-start | bytes 786436
  199.1 111.2 %copy-start.1 = (bf16[2,1024,64]{2,1,0:T(8,128)(2,1)S(1)}, bf16[2,1024,64]{2,1,0:T(8,128)(2,1)}, u32[]{:S(2)}) copy-start(bf16[2,1024,64]{2,1,0:T(8,128)(2,1)} %get-tuple-element.13) | copy-start | bytes 786436
  199.2 92.2 %collective-permute-start.13 = (bf16[4,4,128,128]{2,3,1,0:T(8,128)(2,1)S(1)}, bf16[4,4,128,128]{2,3,1,0:T(8,128)(2,1)}, u32[]{:S(2)}, u32[]{:S(2)}) collective-permute-start(bf16[4,4,128,128]{2,3,1,0:T(8,128)(2,1)S(1)} %get-tuple-element.24), channel_id=1, source_target_pairs={{0,32},{1,33},{2,34},{3,35},{4,36},{5,37},{6,38},{7,39},{8,40},{9,... | collective-permute-start | bytes 1572872 | tf_op jit(solution)/shard_map/ppermute | solution.py:180
  201.0 100.8 %collective-permute-start.15 = (bf16[4,4,128,128]{2,3,1,0:T(8,128)(2,1)S(1)}, bf16[4,4,128,128]{2,3,1,0:T(8,128)(2,1)}, u32[]{:S(2)}, u32[]{:S(2)}) collective-permute-start(bf16[4,4,128,128]{2,3,1,0:T(8,128)(2,1)S(1)} %get-tuple-element.25), channel_id=1, source_target_pairs={{0,96},{1,97},{2,98},{3,99},{4,100},{5,101},{6,102},{7,103},{8,104... | collective-permute-start | bytes 1572872 | tf_op jit(solution)/shard_map/ppermute | solution.py:180
  279.2 24.5 %collective-permute-start.14 = (bf16[4,4,128,128]{2,3,1,0:T(8,128)(2,1)S(1)}, bf16[4,4,128,128]{2,3,1,0:T(8,128)(2,1)}, u32[]{:S(2)}, u32[]{:S(2)}) collective-permute-start(bf16[4,4,128,128]{2,3,1,0:T(8,128)(2,1)S(1)} %get-tuple-element.26), channel_id=1, source_target_pairs={{0,64},{1,65},{2,66},{3,67},{4,68},{5,69},{6,70},{7,71},{8,72},{9,... | collective-permute-start | bytes 1572872 | tf_op jit(solution)/shard_map/ppermute | solution.py:180
  281.0 32.1 %collective-permute-start.10 = (bf16[256,512]{1,0:T(8,128)(2,1)S(1)}, bf16[256,512]{1,0:T(8,128)(2,1)S(1)}, u32[]{:S(2)}, u32[]{:S(2)}) collective-permute-start(bf16[256,512]{1,0:T(8,128)(2,1)S(1)} %reshape.74), channel_id=1, source_target_pairs={{0,1},{1,0},{2,3},{3,2},{4,5},{5,4},{6,7},{7,6},{8,9},{9,8},{10,11... | collective-permute-start | bytes 786440 | tf_op jit(solution)/shard_map/ppermute | solution.py:222
  305.8 14.7 %collective-permute-start.16 = (bf16[4,128,128]{1,2,0:T(8,128)(2,1)S(1)}, bf16[4,128,128]{1,2,0:T(8,128)(2,1)S(1)}, u32[]{:S(2)}, u32[]{:S(2)}) collective-permute-start(bf16[4,128,128]{1,2,0:T(8,128)(2,1)S(1)} %get-tuple-element.29), channel_id=1, source_target_pairs={{0,16},{1,17},{2,18},{3,19},{4,20},{5,21},{6,22},{7,23},{8,24},{9,... | collective-permute-start | bytes 393224 | tf_op jit(solution)/shard_map/ppermute | solution.py:180
  305.9 14.6 %collective-permute-start.18 = (bf16[4,128,128]{1,2,0:T(8,128)(2,1)S(1)}, bf16[4,128,128]{1,2,0:T(8,128)(2,1)S(1)}, u32[]{:S(2)}, u32[]{:S(2)}) collective-permute-start(bf16[4,128,128]{1,2,0:T(8,128)(2,1)S(1)} %get-tuple-element.30), channel_id=1, source_target_pairs={{0,17},{1,16},{2,19},{3,18},{4,21},{5,20},{6,23},{7,22},{8,25},{9,... | collective-permute-start | bytes 393224 | tf_op jit(solution)/shard_map/ppermute | solution.py:180
  309.1 11.4 %collective-permute-start.17 = (bf16[4,128,128]{1,2,0:T(8,128)(2,1)S(1)}, bf16[4,128,128]{1,2,0:T(8,128)(2,1)S(1)}, u32[]{:S(2)}, u32[]{:S(2)}) collective-permute-start(bf16[4,128,128]{1,2,0:T(8,128)(2,1)S(1)} %get-tuple-element.31), channel_id=1, source_target_pairs={{0,1},{1,0},{2,3},{3,2},{4,5},{5,4},{6,7},{7,6},{8,9},{9,8},{10,11... | collective-permute-start | bytes 393224 | tf_op jit(solution)/shard_map/ppermute | solution.py:180
  310.6 13.3 %collective-permute-start.11 = (bf16[256,512]{1,0:T(8,128)(2,1)S(1)}, bf16[256,512]{1,0:T(8,128)(2,1)S(1)}, u32[]{:S(2)}, u32[]{:S(2)}) collective-permute-start(bf16[256,512]{1,0:T(8,128)(2,1)S(1)} %reshape.75), channel_id=1, source_target_pairs={{0,1},{1,0},{2,3},{3,2},{4,5},{5,4},{6,7},{7,6},{8,9},{9,8},{10,11... | collective-permute-start | bytes 786440 | tf_op jit(solution)/shard_map/ppermute | solution.py:222
  320.6 5.2 %collective-permute-start.19 = (bf16[128,128]{0,1:T(8,128)(2,1)S(1)}, bf16[128,128]{0,1:T(8,128)(2,1)S(1)}, u32[]{:S(2)}, u32[]{:S(2)}) collective-permute-start(bf16[128,128]{0,1:T(8,128)(2,1)S(1)} %get-tuple-element.35), channel_id=1, source_target_pairs={{0,4},{1,5},{2,6},{3,7},{4,8},{5,9},{6,10},{7,11},{8,12},{9,13},{1... | collective-permute-start | bytes 98312 | tf_op jit(solution)/shard_map/ppermute | solution.py:180
  320.7 5.1 %collective-permute-start.21 = (bf16[128,128]{0,1:T(8,128)(2,1)S(1)}, bf16[128,128]{0,1:T(8,128)(2,1)S(1)}, u32[]{:S(2)}, u32[]{:S(2)}) collective-permute-start(bf16[128,128]{0,1:T(8,128)(2,1)S(1)} %get-tuple-element.36), channel_id=1, source_target_pairs={{0,12},{1,13},{2,14},{3,15},{4,0},{5,1},{6,2},{7,3},{8,4},{9,5},{1... | collective-permute-start | bytes 98312 | tf_op jit(solution)/shard_map/ppermute | solution.py:180
  323.9 5.4 %collective-permute-start.20 = (bf16[128,128]{0,1:T(8,128)(2,1)S(1)}, bf16[128,128]{0,1:T(8,128)(2,1)S(1)}, u32[]{:S(2)}, u32[]{:S(2)}) collective-permute-start(bf16[128,128]{0,1:T(8,128)(2,1)S(1)} %get-tuple-element.37), channel_id=1, source_target_pairs={{0,8},{1,9},{2,10},{3,11},{4,12},{5,13},{6,14},{7,15},{8,0},{9,1},... | collective-permute-start | bytes 98312 | tf_op jit(solution)/shard_map/ppermute | solution.py:180
  (3 other events, 87.9 us)

commit v3 on v2

--- a/solution.py
+++ b/solution.py
@@ -25,8 +25,16 @@
     return pl.BlockSpec(memory_space=pltpu.VMEM)
 
 
-def _forward_kernel(lists_ref, keep_ref, q_ref, k_ref, v_ref, do_ref,
-                    o_ref, lse_ref, delta_ref, m_sc, l_sc, acc_sc):
+def _nn(a, b):
+    return jnp.dot(a, b, preferred_element_type=jnp.float32)
+
+
+def _nt(a, b):
+    return lax.dot_general(a, b, (((1,), (1,)), ((), ())), preferred_element_type=jnp.float32)
+
+
+def _forward_kernel(lists_ref, keep_ref, q_ref, k_ref, vt_ref, dot_ref,
+                    ot_ref, lse_ref, delta_ref, m_sc, l_sc, acc_sc):
     query_count, slots = lists_ref.shape
     for qb in range(query_count):
         m_sc[...] = jnp.full(m_sc.shape, LOWEST, jnp.float32)
@@ -37,30 +45,25 @@
             @pl.when(keep_ref[qb, j] != 0)
             def _():
                 b = lists_ref[qb, j]
-                k = k_ref[b]
-                v = v_ref[b]
-                s = lax.dot_general(
-                    q_ref[qb], k, (((1,), (1,)), ((), ())),
-                    preferred_element_type=jnp.float32) * SCALE
+                st = _nt(k_ref[b], q_ref[qb]) * SCALE
                 m_prev = m_sc[...]
-                m_new = jnp.maximum(m_prev, jnp.max(s, axis=1, keepdims=True))
+                m_new = jnp.maximum(m_prev, jnp.max(st, axis=0, keepdims=True))
                 alpha = jnp.exp(m_prev - m_new)
-                p = jnp.exp(s - m_new)
-                l_sc[...] = alpha * l_sc[...] + jnp.sum(p, axis=1, keepdims=True)
-                acc_sc[...] = alpha * acc_sc[...] + jnp.dot(
-                    p.astype(jnp.bfloat16), v, preferred_element_type=jnp.float32)
+                pt = jnp.exp(st - m_new)
+                l_sc[...] = alpha * l_sc[...] + jnp.sum(pt, axis=0, keepdims=True)
+                acc_sc[...] = alpha * acc_sc[...] + _nn(vt_ref[b], pt.astype(jnp.bfloat16))
                 m_sc[...] = m_new
             return carry
 
         lax.fori_loop(0, slots, body, 0)
         out = acc_sc[...] / l_sc[...]
-        o_ref[qb] = out.astype(jnp.bfloat16)
+        ot_ref[qb] = out.astype(jnp.bfloat16)
         lse_ref[qb] = m_sc[...] + jnp.log(l_sc[...])
-        delta_ref[qb] = jnp.sum(do_ref[qb].astype(jnp.float32) * out, axis=1, keepdims=True)
-
-
-def _backward_kernel(lists_ref, keep_ref, q_ref, k_ref, v_ref, do_ref, lse_ref, delta_ref,
-                     dq_ref, dk_ref, dv_ref, dq_sc):
+        delta_ref[qb] = jnp.sum(dot_ref[qb].astype(jnp.float32) * out, axis=0, keepdims=True)
+
+
+def _backward_kernel(lists_ref, keep_ref, q_ref, k_ref, kt_ref, v_ref, do_ref, lse_ref, delta_ref,
+                     dqt_ref, dk_ref, dv_ref, dq_sc):
     query_count, slots = lists_ref.shape
     dk_ref[...] = jnp.zeros(dk_ref.shape, jnp.float32)
     dv_ref[...] = jnp.zeros(dv_ref.shape, jnp.float32)
@@ -71,64 +74,57 @@
             @pl.when(keep_ref[qb, j] != 0)
             def _():
                 b = lists_ref[qb, j]
-                k = k_ref[b]
-                v = v_ref[b]
                 q = q_ref[qb]
                 do = do_ref[qb]
-                s = lax.dot_general(
-                    q, k, (((1,), (1,)), ((), ())),
-                    preferred_element_type=jnp.float32) * SCALE
-                p = jnp.exp(s - lse_ref[qb])
-                dv_ref[b] += lax.dot_general(
-                    p.astype(jnp.bfloat16), do, (((0,), (0,)), ((), ())),
-                    preferred_element_type=jnp.float32)
-                dp = lax.dot_general(
-                    do, v, (((1,), (1,)), ((), ())),
-                    preferred_element_type=jnp.float32)
-                ds = (p * (dp - delta_ref[qb])).astype(jnp.bfloat16)
-                dq_sc[...] += jnp.dot(ds, k, preferred_element_type=jnp.float32)
-                dk_ref[b] += lax.dot_general(
-                    ds, q, (((0,), (0,)), ((), ())),
-                    preferred_element_type=jnp.float32)
+                st = _nt(k_ref[b], q) * SCALE
+                pt = jnp.exp(st - lse_ref[qb])
+                dv_ref[b] += _nn(pt.astype(jnp.bfloat16), do)
+                dpt = _nt(v_ref[b], do)
+                dst = (pt * (dpt - delta_ref[qb])).astype(jnp.bfloat16)
+                dq_sc[...] += _nn(kt_ref[b], dst)
+                dk_ref[b] += _nn(dst, q)
             return carry
 
         lax.fori_loop(0, slots, body, 0)
-        dq_ref[qb] = (dq_sc[...] * SCALE).astype(jnp.bfloat16)
+        dqt_ref[qb] = (dq_sc[...] * SCALE).astype(jnp.bfloat16)
 
 
 def attend_local(q_rows, do_rows, key_blocks, value_blocks, lists, keep):
     query_count, rows, _ = q_rows.shape
     block_total = key_blocks.shape[0]
     f32 = jnp.float32
-    o_rows, lse, delta = pl.pallas_call(
+    key_t = jnp.swapaxes(key_blocks, 1, 2)
+    value_t = jnp.swapaxes(value_blocks, 1, 2)
+    do_t = jnp.swapaxes(do_rows, 1, 2)
+    o_t, lse, delta = pl.pallas_call(
         _forward_kernel,
         out_shape=(
-            jax.ShapeDtypeStruct((query_count, rows, HEAD_DIM), jnp.bfloat16),
-            jax.ShapeDtypeStruct((query_count, rows, 1), f32),
-            jax.ShapeDtypeStruct((query_count, rows, 1), f32),
+            jax.ShapeDtypeStruct((query_count, HEAD_DIM, rows), jnp.bfloat16),
+            jax.ShapeDtypeStruct((query_count, 1, rows), f32),
+            jax.ShapeDtypeStruct((query_count, 1, rows), f32),
         ),
         in_specs=[_smem(), _smem(), _vmem(), _vmem(), _vmem(), _vmem()],
         out_specs=(_vmem(), _vmem(), _vmem()),
         scratch_shapes=[
-            pltpu.VMEM((rows, 1), f32),
-            pltpu.VMEM((rows, 1), f32),
-            pltpu.VMEM((rows, HEAD_DIM), f32),
+            pltpu.VMEM((1, rows), f32),
+            pltpu.VMEM((1, rows), f32),
+            pltpu.VMEM((HEAD_DIM, rows), f32),
         ],
         compiler_params=pltpu.CompilerParams(vmem_limit_bytes=VMEM_LIMIT),
-    )(lists, keep, q_rows, key_blocks, value_blocks, do_rows)
-    dq_rows, dk_blocks, dv_blocks = pl.pallas_call(
+    )(lists, keep, q_rows, key_blocks, value_t, do_t)
+    dq_t, dk_blocks, dv_blocks = pl.pallas_call(
         _backward_kernel,
         out_shape=(
-            jax.ShapeDtypeStruct((query_count, rows, HEAD_DIM), jnp.bfloat16),
+            jax.ShapeDtypeStruct((query_count, HEAD_DIM, rows), jnp.bfloat16),
             jax.ShapeDtypeStruct((block_total, BLOCK, HEAD_DIM), f32),
             jax.ShapeDtypeStruct((block_total, BLOCK, HEAD_DIM), f32),
         ),
-        in_specs=[_smem(), _smem()] + [_vmem()] * 6,
+        in_specs=[_smem(), _smem()] + [_vmem()] * 7,
         out_specs=(_vmem(), _vmem(), _vmem()),
-        scratch_shapes=[pltpu.VMEM((rows, HEAD_DIM), f32)],
+        scratch_shapes=[pltpu.VMEM((HEAD_DIM, rows), f32)],
         compiler_params=pltpu.CompilerParams(vmem_limit_bytes=VMEM_LIMIT),
-    )(lists, keep, q_rows, key_blocks, value_blocks, do_rows, lse, delta)
-    return o_rows, dq_rows, dk_blocks, dv_blocks
+    )(lists, keep, q_rows, key_blocks, key_t, value_blocks, do_rows, lse, delta)
+    return jnp.swapaxes(o_t, 1, 2), jnp.swapaxes(dq_t, 1, 2), dk_blocks, dv_blocks
 
 
 def first_occurrence(block_lists):

time: 331 us -> 264 us (0.80)
  starting transfers between devices: 112 us -> 38.5 us
  local copies, waits for them, and re-layouts: 30.1 us -> 45.9 us
  Pallas kernels: 99.7 us -> 87.4 us
    ppermute x10, starting transfers between devices: 89.2 us -> 20.2 us  [scatter_sum(): lax.ppermute(sent, axes, pairs(axis, shift)).astype(jnp.float32)]
    pallas_call x1, Pallas kernels: 58.8 us -> 34.2 us  [attend_local(): pl.pallas_call(_forward_kernel, out_shape=(jax.ShapeDtypeStruct((query_co...]
    pallas_call x1, Pallas kernels: 40.9 us -> 53.2 us  [attend_local(): pl.pallas_call(_backward_kernel, out_shape=(jax.ShapeDtypeStruct((query_c...]
    transpose x0 -> x4, local copies, waits for them, and re-layouts: none -> 11.1 us  [the longest x1 4.84 us: attend_local(): key_t = jnp.swapaxes(key_blocks, 1, 2)]
    ppermute x10, waiting for transfers between devices: 25.6 us -> 32.1 us  [gather_blocks(): pieces.append(lax.ppermute(buf, axes, pairs(axis, size - shift)))]
    slice x1, local copies, waits for them, and re-layouts: 7.58 us -> 12 us  [local(): value_blocks = kv_held[:, :, HEAD_DIM:]]
    ppermute x10, starting transfers between devices: 18.2 us -> 14.6 us  [gather_blocks(): pieces.append(lax.ppermute(buf, axes, pairs(axis, size - shift)))]
    ppermute x10, waiting for transfers between devices: 31.4 us -> 28 us  [scatter_sum(): lax.ppermute(sent, axes, pairs(axis, shift)).astype(jnp.float32)]
  transfers between devices with their start and end apart: 22 -> 22, of which waited for: 13 -> 13; matrix products, arithmetic and copies ran while one was open for 8% -> 10% of each run, Pallas kernels for 0% -> 0%
where the time goes in v3:
time: 264 us
  Pallas kernels  87.4 us (33%)
  waiting for transfers between devices  60.1 us (23%)
  local copies, waits for them, and re-layouts  45.9 us (17%)
  starting transfers between devices  38.5 us (15%)
  other arithmetic  31.3 us (12%)
    pallas_call x1, Pallas kernels, attend_local(): pl.pallas_call(_backward_kernel, out_shape=(jax.ShapeDtypeStruct((query_c...  53.2 us
    pallas_call x1, Pallas kernels, attend_local(): pl.pallas_call(_forward_kernel, out_shape=(jax.ShapeDtypeStruct((query_co...  34.2 us
    ppermute x10, waiting for transfers between devices, gather_blocks(): pieces.append(lax.ppermute(buf, axes, pairs(axis, size - shift)))  32.1 us
    ppermute x10, waiting for transfers between devices, scatter_sum(): lax.ppermute(sent, axes, pairs(axis, shift)).astype(jnp.float32)  28 us
    ppermute x10, starting transfers between devices, scatter_sum(): lax.ppermute(sent, axes, pairs(axis, shift)).astype(jnp.float32)  20.2 us
    ppermute x10, starting transfers between devices, gather_blocks(): pieces.append(lax.ppermute(buf, axes, pairs(axis, size - shift)))  14.6 us
    slice x1, local copies, waits for them, and re-layouts, local(): value_blocks = kv_held[:, :, HEAD_DIM:]  12 us
    another operation x4, other arithmetic  11.4 us
  transfers between devices with their start and end apart: 22, of which 13 were waited for; matrix products, arithmetic and copies ran while one was open for 10% of the time, Pallas kernels for 0%

profile of v3, /device:TPU:0, one launch (start us, length us, event | category | flops | bytes accessed | tf_op | source)
XLA Modules:
  0.0 264.0 jit_solution(9078134506937107605)
XLA Ops:
  2.1 3.1 %collective-permute-start = (bf16[1,128,128]{1,2,0:T(8,128)(2,1)S(1)}, bf16[1,128,128]{1,2,0:T(8,128)(2,1)S(1)}, u32[]{:S(2)}, u32[]{:S(2)}) collective-permute-start(bf16[1,128,128]{1,2,0:T(8,128)(2,1)S(1)} %bitcast.108), channel_id=1, source_target_pairs={{0,12},{1,13},{2,14},{3,15},{4,0},{5,1},{6,2},{7,3},{8,4},{9,5},{1... | collective-permute-start | bytes 98312 | tf_op jit(solution)/shard_map/ppermute | solution.py:166
  6.8 3.8 %collective-permute-done.1 = bf16[1,128,128]{1,2,0:T(8,128)(2,1)S(1)} collective-permute-done((bf16[1,128,128]{1,2,0:T(8,128)(2,1)S(1)}, bf16[1,128,128]{1,2,0:T(8,128)(2,1)S(1)}, u32[]{:S(2)}, u32[]{:S(2)}) %collective-permute-start.1) | collective-permute-done | bytes 32800 | tf_op jit(solution)/shard_map/ppermute | solution.py:166
  11.0 2.8 %collective-permute-start.3 = (bf16[4,1,128,128]{2,3,0,1:T(8,128)(2,1)S(1)}, bf16[4,1,128,128]{2,3,0,1:T(8,128)(2,1)S(1)}, u32[]{:S(2)}, u32[]{:S(2)}) collective-permute-start(bf16[4,1,128,128]{2,3,0,1:T(8,128)(2,1)S(1)} %get-tuple-element.41), channel_id=1, source_target_pairs={{0,17},{1,16},{2,19},{3,18},{4,21},{5,20},{6,23},{7,22},{8,25},{9,... | collective-permute-start | bytes 393224 | tf_op jit(solution)/shard_map/ppermute | solution.py:166
  21.8 4.1 %collective-permute-start.6 = (bf16[4,4,1,128,128]{3,4,1,0,2:T(8,128)(2,1)S(1)}, bf16[4,4,1,128,128]{3,4,1,0,2:T(8,128)(2,1)S(1)}, u32[]{:S(2)}, u32[]{:S(2)}) collective-permute-start(bf16[4,4,1,128,128]{3,4,1,0,2:T(8,128)(2,1)S(1)} %get-tuple-element.35), channel_id=1, source_target_pairs={{0,96},{1,97},{2,98},{3,99},{4,100},{5,101},{6,102},{7,103},{8,104... | collective-permute-start | bytes 1572872 | tf_op jit(solution)/shard_map/ppermute | solution.py:166
  27.2 18.3 %collective-permute-done.6 = bf16[4,4,1,128,128]{3,4,1,0,2:T(8,128)(2,1)S(1)} collective-permute-done((bf16[4,4,1,128,128]{3,4,1,0,2:T(8,128)(2,1)S(1)}, bf16[4,4,1,128,128]{3,4,1,0,2:T(8,128)(2,1)S(1)}, u32[]{:S(2)}, u32[]{:S(2)}) %collective-permute-start.6) | collective-permute-done | bytes 524320 | tf_op jit(solution)/shard_map/ppermute | solution.py:166
  45.5 3.4 %collective-permute-done.8 = bf16[4,4,1,128,128]{3,4,1,2,0:T(8,128)(2,1)S(1)} collective-permute-done((bf16[4,4,1,128,128]{3,4,1,2,0:T(8,128)(2,1)S(1)}, bf16[4,4,1,128,128]{3,4,1,2,0:T(8,128)(2,1)S(1)}, u32[]{:S(2)}, u32[]{:S(2)}) %collective-permute-start.8) | collective-permute-done | bytes 524320 | tf_op jit(solution)/shard_map/ppermute | solution.py:166
  59.7 3.9 %pad_maximum_fusion.1 = bf16[2,4,4,4,1,128,128]{5,6,3,2,1,4,0:T(8,128)(2,1)} fusion(bf16[1,4,4,4,1,128,128]{5,6,3,2,1,4,0:T(8,128)(2,1)} %bitcast.25, bf16[1,4,4,4,1,128,128]{5,6,3,2,1,4,0:T(8,128)(2,1)S(1)} %get-tuple-element.29), kind=kLoop, calls=%fused_computation.6 | loop fusion | flops 2097152 | bytes 8388608 | tf_op jit(solution)/shard_map/stack | solution.py:167
  63.6 7.3 %copy.48 = bf16[2,4,4,4,1,128,128]{6,5,3,2,1,0,4:T(8,128)(2,1)} copy(bf16[2,4,4,4,1,128,128]{5,6,3,2,1,4,0:T(8,128)(2,1)} %pad_maximum_fusion.1) | data formatting | bytes 8388608 | tf_op jit(solution)/shard_map/stack | solution.py:167
  70.9 12.0 %fusion.32 = (bf16[128,128,64]{2,1,0:T(8,128)(2,1)}, bf16[128,64,128]{1,2,0:T(8,128)(2,1)}, bf16[128,64,128]{1,2,0:T(8,128)(2,1)}, bf16[128,128,64]{2,1,0:T(8,128)(2,1)}) fusion(bf16[128,128,128]{2,1,0:T(8,128)(2,1)} %bitcast.95), kind=kLoop, calls=%fused_computation.83 | loop fusion | bytes 12582912 | tf_op jit(solution)/shard_map/slice | solution.py:195
  82.9 4.8 %copy.50.vt_ref = bf16[128,64,128]{2,1,0:T(8,128)(2,1)} copy(bf16[128,64,128]{1,2,0:T(8,128)(2,1)} %get-tuple-element.24) | data formatting | bytes 4194304 | tf_op jit(solution)/shard_map/transpose | solution.py:97
  87.7 4.8 %copy.52.kt_ref = bf16[128,64,128]{2,1,0:T(8,128)(2,1)} copy(bf16[128,64,128]{1,2,0:T(8,128)(2,1)} %get-tuple-element.23) | data formatting | bytes 4194304 | tf_op jit(solution)/shard_map/transpose | solution.py:96
  92.6 34.2 %shard_map.93 = (bf16[2,64,1024]{2,1,0:T(8,128)(2,1)}, f32[2,1,1024]{2,1,0:T(1,128)}, f32[2,1,1024]{2,1,0:T(1,128)}) custom-call(s32[2,48]{1,0:T(2,128)} %fusion.17.lists_ref, s32[2,48]{1,0:T(2,128)} %not_convert_fusion.keep_ref, bf16[2,1024,64]{2,1,0:T(8,128)(2,1)} %reshape.71.q_ref, bf16[128,128,64]{2,1,0:T(8,128)(2,1)} %get-tuple-element.25.k_ref, ...), custom_call_target="tpu_custom_call" | custom-call | tf_op jit(solution)/shard_map/pallas_call | solution.py:99
  126.8 53.2 %shard_map.94 = (bf16[2,64,1024]{2,1,0:T(8,128)(2,1)}, f32[128,128,64]{2,1,0:T(8,128)}, f32[128,128,64]{2,1,0:T(8,128)}) custom-call(s32[2,48]{1,0:T(2,128)} %fusion.17.lists_ref, s32[2,48]{1,0:T(2,128)} %not_convert_fusion.keep_ref, bf16[2,1024,64]{2,1,0:T(8,128)(2,1)} %reshape.71.q_ref, bf16[128,128,64]{2,1,0:T(8,128)(2,1)} %get-tuple-element.25.k_ref, ...), custom_call_target="tpu_custom_call" | custom-call | tf_op jit(solution)/shard_map/pallas_call | solution.py:115
  180.0 4.4 %fusion.1 = bf16[64,128,128]{2,1,0:T(8,128)(2,1)S(1)} fusion(f32[128,128,64]{2,1,0:T(8,128)} %get-tuple-element.15, f32[128,128,64]{2,1,0:T(8,128)} %get-tuple-element.14), kind=kLoop, calls=%fused_computation.5 | loop fusion | flops 4194304 | bytes 10485760 | tf_op jit(solution)/shard_map/convert.10
  186.8 6.6 %fusion = f32[64,128,128]{2,1,0:T(8,128)} fusion(f32[128,128,64]{2,1,0:T(8,128)} %get-tuple-element.14, f32[128,128,64]{2,1,0:T(8,128)} %get-tuple-element.15), kind=kLoop, calls=%fused_computation.3 | loop fusion | flops 1048576 | bytes 12582912 | tf_op jit(solution)/shard_map/concatenate | solution.py:225
  193.4 5.2 %copy.55 = f32[4,4,4,128,128]{3,4,2,1,0:T(8,128)} copy(f32[4,4,4,128,128]{4,3,2,1,0:T(8,128)} %bitcast.96) | data formatting | bytes 8388608 | tf_op jit(solution)/shard_map/squeeze | solution.py:173
  198.6 5.2 %fusion.31 = (bf16[4,4,4,128,128]{3,4,2,1,0:T(8,128)(2,1)S(1)}, f32[4,4,4,128,128]{3,4,2,1,0:T(8,128)}) fusion(f32[4,4,4,128,128]{3,4,2,1,0:T(8,128)} %copy.55, bf16[4,4,4,128,128]{3,4,2,1,0:T(8,128)(2,1)S(1)} %collective-permute-done.12), kind=kLoop, calls=%fused_computation.82 | loop fusion | flops 3145728 | bytes 12582912 | tf_op jit(solution)/shard_map/convert.9
  204.0 7.3 %collective-permute-start.13 = (bf16[4,4,128,128]{2,3,1,0:T(8,128)(2,1)S(1)}, bf16[4,4,128,128]{2,3,1,0:T(8,128)(2,1)S(1)}, u32[]{:S(2)}, u32[]{:S(2)}) collective-permute-start(bf16[4,4,128,128]{2,3,1,0:T(8,128)(2,1)S(1)} %get-tuple-element.26), channel_id=1, source_target_pairs={{0,32},{1,33},{2,34},{3,35},{4,36},{5,37},{6,38},{7,39},{8,40},{9,... | collective-permute-start | bytes 1572872 | tf_op jit(solution)/shard_map/ppermute | solution.py:176
  211.2 2.8 %collective-permute-start.15 = (bf16[4,4,128,128]{2,3,1,0:T(8,128)(2,1)S(1)}, bf16[4,4,128,128]{2,3,1,0:T(8,128)(2,1)}, u32[]{:S(2)}, u32[]{:S(2)}) collective-permute-start(bf16[4,4,128,128]{2,3,1,0:T(8,128)(2,1)S(1)} %get-tuple-element.27), channel_id=1, source_target_pairs={{0,96},{1,97},{2,98},{3,99},{4,100},{5,101},{6,102},{7,103},{8,104... | collective-permute-start | bytes 1572872 | tf_op jit(solution)/shard_map/ppermute | solution.py:176
  216.4 14.4 %collective-permute-done.13 = bf16[4,4,128,128]{2,3,1,0:T(8,128)(2,1)S(1)} collective-permute-done((bf16[4,4,128,128]{2,3,1,0:T(8,128)(2,1)S(1)}, bf16[4,4,128,128]{2,3,1,0:T(8,128)(2,1)S(1)}, u32[]{:S(2)}, u32[]{:S(2)}) %collective-permute-start.13) | collective-permute-done | bytes 524320 | tf_op jit(solution)/shard_map/ppermute | solution.py:176
  230.8 3.5 %collective-permute-done.14 = bf16[4,4,128,128]{2,3,1,0:T(8,128)(2,1)S(1)} collective-permute-done((bf16[4,4,128,128]{2,3,1,0:T(8,128)(2,1)S(1)}, bf16[4,4,128,128]{2,3,1,0:T(8,128)(2,1)S(1)}, u32[]{:S(2)}, u32[]{:S(2)}) %collective-permute-start.14) | collective-permute-done | bytes 524320 | tf_op jit(solution)/shard_map/ppermute | solution.py:176
  241.1 2.8 %collective-permute-start.10 = (bf16[256,512]{1,0:T(8,128)(2,1)S(1)}, bf16[256,512]{1,0:T(8,128)(2,1)S(1)}, u32[]{:S(2)}, u32[]{:S(2)}) collective-permute-start(bf16[256,512]{1,0:T(8,128)(2,1)S(1)} %reshape.74), channel_id=1, source_target_pairs={{0,1},{1,0},{2,3},{3,2},{4,5},{5,4},{6,7},{7,6},{8,9},{9,8},{10,11... | collective-permute-start | bytes 786440 | tf_op jit(solution)/shard_map/ppermute | solution.py:218
  245.9 6.1 %collective-permute-done.16 = bf16[4,128,128]{1,2,0:T(8,128)(2,1)S(1)} collective-permute-done((bf16[4,128,128]{1,2,0:T(8,128)(2,1)S(1)}, bf16[4,128,128]{1,2,0:T(8,128)(2,1)S(1)}, u32[]{:S(2)}, u32[]{:S(2)}) %collective-permute-start.16) | collective-permute-done | bytes 131104 | tf_op jit(solution)/shard_map/ppermute | solution.py:176
  252.2 6.6 %collective-permute-start.20 = (bf16[128,128]{0,1:T(8,128)(2,1)S(1)}, bf16[128,128]{0,1:T(8,128)(2,1)S(1)}, u32[]{:S(2)}, u32[]{:S(2)}) collective-permute-start(bf16[128,128]{0,1:T(8,128)(2,1)S(1)} %get-tuple-element.39), channel_id=1, source_target_pairs={{0,8},{1,9},{2,10},{3,11},{4,12},{5,13},{6,14},{7,15},{8,0},{9,1},... | collective-permute-start | bytes 98312 | tf_op jit(solution)/shard_map/ppermute | solution.py:176
  (78 shorter events, 42.4 us)
Async XLA Ops:
  2.1 4.7 %collective-permute-start = (bf16[1,128,128]{1,2,0:T(8,128)(2,1)S(1)}, bf16[1,128,128]{1,2,0:T(8,128)(2,1)S(1)}, u32[]{:S(2)}, u32[]{:S(2)}) collective-permute-start(bf16[1,128,128]{1,2,0:T(8,128)(2,1)S(1)} %bitcast.108), channel_id=1, source_target_pairs={{0,12},{1,13},{2,14},{3,15},{4,0},{5,1},{6,2},{7,3},{8,4},{9,5},{1... | collective-permute-start | bytes 98312 | tf_op jit(solution)/shard_map/ppermute | solution.py:166
  5.2 5.4 %collective-permute-start.1 = (bf16[1,128,128]{1,2,0:T(8,128)(2,1)S(1)}, bf16[1,128,128]{1,2,0:T(8,128)(2,1)S(1)}, u32[]{:S(2)}, u32[]{:S(2)}) collective-permute-start(bf16[1,128,128]{1,2,0:T(8,128)(2,1)S(1)} %bitcast.109), channel_id=1, source_target_pairs={{0,8},{1,9},{2,10},{3,11},{4,12},{5,13},{6,14},{7,15},{8,0},{9,1},... | collective-permute-start | bytes 98312 | tf_op jit(solution)/shard_map/ppermute | solution.py:166
  5.8 5.1 %collective-permute-start.2 = (bf16[1,128,128]{1,2,0:T(8,128)(2,1)S(1)}, bf16[1,128,128]{1,2,0:T(8,128)(2,1)S(1)}, u32[]{:S(2)}, u32[]{:S(2)}) collective-permute-start(bf16[1,128,128]{1,2,0:T(8,128)(2,1)S(1)} %bitcast.110), channel_id=1, source_target_pairs={{0,4},{1,5},{2,6},{3,7},{4,8},{5,9},{6,10},{7,11},{8,12},{9,13},{1... | collective-permute-start | bytes 98312 | tf_op jit(solution)/shard_map/ppermute | solution.py:166
  11.0 7.1 %collective-permute-start.3 = (bf16[4,1,128,128]{2,3,0,1:T(8,128)(2,1)S(1)}, bf16[4,1,128,128]{2,3,0,1:T(8,128)(2,1)S(1)}, u32[]{:S(2)}, u32[]{:S(2)}) collective-permute-start(bf16[4,1,128,128]{2,3,0,1:T(8,128)(2,1)S(1)} %get-tuple-element.41), channel_id=1, source_target_pairs={{0,17},{1,16},{2,19},{3,18},{4,21},{5,20},{6,23},{7,22},{8,25},{9,... | collective-permute-start | bytes 393224 | tf_op jit(solution)/shard_map/ppermute | solution.py:166
  13.8 6.6 %collective-permute-start.4 = (bf16[4,1,128,128]{2,3,0,1:T(8,128)(2,1)S(1)}, bf16[4,1,128,128]{2,3,0,1:T(8,128)(2,1)S(1)}, u32[]{:S(2)}, u32[]{:S(2)}) collective-permute-start(bf16[4,1,128,128]{2,3,0,1:T(8,128)(2,1)S(1)} %get-tuple-element.41), channel_id=1, source_target_pairs={{0,1},{1,0},{2,3},{3,2},{4,5},{5,4},{6,7},{7,6},{8,9},{9,8},{10,11... | collective-permute-start | bytes 393224 | tf_op jit(solution)/shard_map/ppermute | solution.py:166
  14.6 7.1 %collective-permute-start.5 = (bf16[4,1,128,128]{2,3,1,0:T(8,128)(2,1)S(1)}, bf16[4,1,128,128]{2,3,1,0:T(8,128)(2,1)S(1)}, u32[]{:S(2)}, u32[]{:S(2)}) collective-permute-start(bf16[4,1,128,128]{2,3,1,0:T(8,128)(2,1)S(1)} %get-tuple-element.42), channel_id=1, source_target_pairs={{0,16},{1,17},{2,18},{3,19},{4,20},{5,21},{6,22},{7,23},{8,24},{9,... | collective-permute-start | bytes 393224 | tf_op jit(solution)/shard_map/ppermute | solution.py:166
  21.7 28.9 %copy-start.3 = (s32[2,48]{1,0:T(2,128)S(1)}, s32[2,48]{1,0:T(2,128)}, u32[]{:S(2)}) copy-start(s32[2,48]{1,0:T(2,128)} %param.10) | copy-start | bytes 1156
  21.7 29.0 %copy-start.1 = (s32[128,4]{1,0:T(8,128)S(1)}, s32[128,4]{1,0:T(8,128)}, u32[]{:S(2)}) copy-start(s32[128,4]{1,0:T(8,128)} %constant.64.clone) | copy-start | bytes 6148
  21.8 23.7 %collective-permute-start.6 = (bf16[4,4,1,128,128]{3,4,1,0,2:T(8,128)(2,1)S(1)}, bf16[4,4,1,128,128]{3,4,1,0,2:T(8,128)(2,1)S(1)}, u32[]{:S(2)}, u32[]{:S(2)}) collective-permute-start(bf16[4,4,1,128,128]{3,4,1,0,2:T(8,128)(2,1)S(1)} %get-tuple-element.35), channel_id=1, source_target_pairs={{0,96},{1,97},{2,98},{3,99},{4,100},{5,101},{6,102},{7,103},{8,104... | collective-permute-start | bytes 1572872 | tf_op jit(solution)/shard_map/ppermute | solution.py:166
  25.9 19.6 %collective-permute-start.7 = (bf16[4,4,1,128,128]{3,4,1,0,2:T(8,128)(2,1)S(1)}, bf16[4,4,1,128,128]{3,4,1,0,2:T(8,128)(2,1)S(1)}, u32[]{:S(2)}, u32[]{:S(2)}) collective-permute-start(bf16[4,4,1,128,128]{3,4,1,0,2:T(8,128)(2,1)S(1)} %get-tuple-element.35), channel_id=1, source_target_pairs={{0,64},{1,65},{2,66},{3,67},{4,68},{5,69},{6,70},{7,71},{8,72},{9,... | collective-permute-start | bytes 1572872 | tf_op jit(solution)/shard_map/ppermute | solution.py:166
  25.9 23.0 %collective-permute-start.8 = (bf16[4,4,1,128,128]{3,4,1,2,0:T(8,128)(2,1)S(1)}, bf16[4,4,1,128,128]{3,4,1,2,0:T(8,128)(2,1)S(1)}, u32[]{:S(2)}, u32[]{:S(2)}) collective-permute-start(bf16[4,4,1,128,128]{3,4,1,2,0:T(8,128)(2,1)S(1)} %get-tuple-element.36), channel_id=1, source_target_pairs={{0,32},{1,33},{2,34},{3,35},{4,36},{5,37},{6,38},{7,39},{8,40},{9,... | collective-permute-start | bytes 1572872 | tf_op jit(solution)/shard_map/ppermute | solution.py:166
  50.6 9.1 %collective-permute-start.9 = (bf16[4,4,4,1,128,128]{4,5,2,1,3,0:T(8,128)(2,1)}, bf16[4,4,4,1,128,128]{4,5,2,1,3,0:T(8,128)(2,1)}, u32[]{:S(2)}, u32[]{:S(2)}) collective-permute-start(bf16[4,4,4,1,128,128]{4,5,2,1,3,0:T(8,128)(2,1)} %get-tuple-element.30), channel_id=1, source_target_pairs={{0,2},{1,3},{2,0},{3,1},{4,6},{5,7},{6,4},{7,5},{8,10},{9,11},{10,... | collective-permute-start | bytes 6291464 | tf_op jit(solution)/shard_map/ppermute | solution.py:166
  186.8 11.8 %collective-permute-start.12 = (bf16[4,4,4,128,128]{3,4,2,1,0:T(8,128)(2,1)}, bf16[4,4,4,128,128]{3,4,2,1,0:T(8,128)(2,1)S(1)}, u32[]{:S(2)}, u32[]{:S(2)}) collective-permute-start(bf16[4,4,4,128,128]{3,4,2,1,0:T(8,128)(2,1)} %copy.54), channel_id=1, source_target_pairs={{0,2},{1,3},{2,0},{3,1},{4,6},{5,7},{6,4},{7,5},{8,10},{9,11},{10,... | collective-permute-start | bytes 6291464 | tf_op jit(solution)/shard_map/ppermute | solution.py:176
  204.0 26.9 %collective-permute-start.13 = (bf16[4,4,128,128]{2,3,1,0:T(8,128)(2,1)S(1)}, bf16[4,4,128,128]{2,3,1,0:T(8,128)(2,1)S(1)}, u32[]{:S(2)}, u32[]{:S(2)}) collective-permute-start(bf16[4,4,128,128]{2,3,1,0:T(8,128)(2,1)S(1)} %get-tuple-element.26), channel_id=1, source_target_pairs={{0,32},{1,33},{2,34},{3,35},{4,36},{5,37},{6,38},{7,39},{8,40},{9,... | collective-permute-start | bytes 1572872 | tf_op jit(solution)/shard_map/ppermute | solution.py:176
  211.2 23.1 %collective-permute-start.14 = (bf16[4,4,128,128]{2,3,1,0:T(8,128)(2,1)S(1)}, bf16[4,4,128,128]{2,3,1,0:T(8,128)(2,1)S(1)}, u32[]{:S(2)}, u32[]{:S(2)}) collective-permute-start(bf16[4,4,128,128]{2,3,1,0:T(8,128)(2,1)S(1)} %get-tuple-element.28), channel_id=1, source_target_pairs={{0,64},{1,65},{2,66},{3,67},{4,68},{5,69},{6,70},{7,71},{8,72},{9,... | collective-permute-start | bytes 1572872 | tf_op jit(solution)/shard_map/ppermute | solution.py:176
  211.2 24.1 %collective-permute-start.15 = (bf16[4,4,128,128]{2,3,1,0:T(8,128)(2,1)S(1)}, bf16[4,4,128,128]{2,3,1,0:T(8,128)(2,1)}, u32[]{:S(2)}, u32[]{:S(2)}) collective-permute-start(bf16[4,4,128,128]{2,3,1,0:T(8,128)(2,1)S(1)} %get-tuple-element.27), channel_id=1, source_target_pairs={{0,96},{1,97},{2,98},{3,99},{4,100},{5,101},{6,102},{7,103},{8,104... | collective-permute-start | bytes 1572872 | tf_op jit(solution)/shard_map/ppermute | solution.py:176
  215.6 28.4 %collective-permute-start.11 = (bf16[256,512]{1,0:T(8,128)(2,1)S(1)}, bf16[256,512]{1,0:T(8,128)(2,1)}, u32[]{:S(2)}, u32[]{:S(2)}) collective-permute-start(bf16[256,512]{1,0:T(8,128)(2,1)S(1)} %reshape.75), channel_id=1, source_target_pairs={{0,1},{1,0},{2,3},{3,2},{4,5},{5,4},{6,7},{7,6},{8,9},{9,8},{10,11... | collective-permute-start | bytes 786440 | tf_op jit(solution)/shard_map/ppermute | solution.py:218
  237.0 15.0 %collective-permute-start.16 = (bf16[4,128,128]{1,2,0:T(8,128)(2,1)S(1)}, bf16[4,128,128]{1,2,0:T(8,128)(2,1)S(1)}, u32[]{:S(2)}, u32[]{:S(2)}) collective-permute-start(bf16[4,128,128]{1,2,0:T(8,128)(2,1)S(1)} %get-tuple-element.31), channel_id=1, source_target_pairs={{0,16},{1,17},{2,18},{3,19},{4,20},{5,21},{6,22},{7,23},{8,24},{9,... | collective-permute-start | bytes 393224 | tf_op jit(solution)/shard_map/ppermute | solution.py:176
  237.1 15.0 %collective-permute-start.17 = (bf16[4,128,128]{1,2,0:T(8,128)(2,1)S(1)}, bf16[4,128,128]{1,2,0:T(8,128)(2,1)S(1)}, u32[]{:S(2)}, u32[]{:S(2)}) collective-permute-start(bf16[4,128,128]{1,2,0:T(8,128)(2,1)S(1)} %get-tuple-element.33), channel_id=1, source_target_pairs={{0,1},{1,0},{2,3},{3,2},{4,5},{5,4},{6,7},{7,6},{8,9},{9,8},{10,11... | collective-permute-start | bytes 393224 | tf_op jit(solution)/shard_map/ppermute | solution.py:176
  239.4 12.7 %collective-permute-start.18 = (bf16[4,128,128]{1,2,0:T(8,128)(2,1)S(1)}, bf16[4,128,128]{1,2,0:T(8,128)(2,1)S(1)}, u32[]{:S(2)}, u32[]{:S(2)}) collective-permute-start(bf16[4,128,128]{1,2,0:T(8,128)(2,1)S(1)} %get-tuple-element.32), channel_id=1, source_target_pairs={{0,17},{1,16},{2,19},{3,18},{4,21},{5,20},{6,23},{7,22},{8,25},{9,... | collective-permute-start | bytes 393224 | tf_op jit(solution)/shard_map/ppermute | solution.py:176
  241.1 17.7 %collective-permute-start.10 = (bf16[256,512]{1,0:T(8,128)(2,1)S(1)}, bf16[256,512]{1,0:T(8,128)(2,1)S(1)}, u32[]{:S(2)}, u32[]{:S(2)}) collective-permute-start(bf16[256,512]{1,0:T(8,128)(2,1)S(1)} %reshape.74), channel_id=1, source_target_pairs={{0,1},{1,0},{2,3},{3,2},{4,5},{5,4},{6,7},{7,6},{8,9},{9,8},{10,11... | collective-permute-start | bytes 786440 | tf_op jit(solution)/shard_map/ppermute | solution.py:218
  252.2 7.6 %collective-permute-start.19 = (bf16[128,128]{0,1:T(8,128)(2,1)S(1)}, bf16[128,128]{0,1:T(8,128)(2,1)S(1)}, u32[]{:S(2)}, u32[]{:S(2)}) collective-permute-start(bf16[128,128]{0,1:T(8,128)(2,1)S(1)} %get-tuple-element.37), channel_id=1, source_target_pairs={{0,4},{1,5},{2,6},{3,7},{4,8},{5,9},{6,10},{7,11},{8,12},{9,13},{1... | collective-permute-start | bytes 98312 | tf_op jit(solution)/shard_map/ppermute | solution.py:176
  252.2 8.9 %collective-permute-start.20 = (bf16[128,128]{0,1:T(8,128)(2,1)S(1)}, bf16[128,128]{0,1:T(8,128)(2,1)S(1)}, u32[]{:S(2)}, u32[]{:S(2)}) collective-permute-start(bf16[128,128]{0,1:T(8,128)(2,1)S(1)} %get-tuple-element.39), channel_id=1, source_target_pairs={{0,8},{1,9},{2,10},{3,11},{4,12},{5,13},{6,14},{7,15},{8,0},{9,1},... | collective-permute-start | bytes 98312 | tf_op jit(solution)/shard_map/ppermute | solution.py:176
  258.9 3.9 %collective-permute-start.21 = (bf16[128,128]{0,1:T(8,128)(2,1)S(1)}, bf16[128,128]{0,1:T(8,128)(2,1)S(1)}, u32[]{:S(2)}, u32[]{:S(2)}) collective-permute-start(bf16[128,128]{0,1:T(8,128)(2,1)S(1)} %get-tuple-element.38), channel_id=1, source_target_pairs={{0,12},{1,13},{2,14},{3,15},{4,0},{5,1},{6,2},{7,3},{8,4},{9,5},{1... | collective-permute-start | bytes 98312 | tf_op jit(solution)/shard_map/ppermute | solution.py:176
  (2 other events, 17.0 us)

commit v4 on v3

--- a/solution.py
+++ b/solution.py
@@ -33,7 +33,12 @@
     return lax.dot_general(a, b, (((1,), (1,)), ((), ())), preferred_element_type=jnp.float32)
 
 
-def _forward_kernel(lists_ref, keep_ref, q_ref, k_ref, vt_ref, dot_ref,
+def _rows_of(kvt_ref, b, first):
+    tile = kvt_ref[b, first:first + HEAD_DIM, :].astype(jnp.float32)
+    return jnp.transpose(tile).astype(jnp.bfloat16)
+
+
+def _forward_kernel(lists_ref, keep_ref, q_ref, kvt_ref, dot_ref,
                     ot_ref, lse_ref, delta_ref, m_sc, l_sc, acc_sc):
     query_count, slots = lists_ref.shape
     for qb in range(query_count):
@@ -45,13 +50,14 @@
             @pl.when(keep_ref[qb, j] != 0)
             def _():
                 b = lists_ref[qb, j]
-                st = _nt(k_ref[b], q_ref[qb]) * SCALE
+                st = _nt(_rows_of(kvt_ref, b, 0), q_ref[qb]) * SCALE
                 m_prev = m_sc[...]
                 m_new = jnp.maximum(m_prev, jnp.max(st, axis=0, keepdims=True))
                 alpha = jnp.exp(m_prev - m_new)
                 pt = jnp.exp(st - m_new)
                 l_sc[...] = alpha * l_sc[...] + jnp.sum(pt, axis=0, keepdims=True)
-                acc_sc[...] = alpha * acc_sc[...] + _nn(vt_ref[b], pt.astype(jnp.bfloat16))
+                acc_sc[...] = alpha * acc_sc[...] + _nn(
+                    kvt_ref[b, HEAD_DIM:, :], pt.astype(jnp.bfloat16))
                 m_sc[...] = m_new
             return carry
 
@@ -62,7 +68,7 @@
         delta_ref[qb] = jnp.sum(dot_ref[qb].astype(jnp.float32) * out, axis=0, keepdims=True)
 
 
-def _backward_kernel(lists_ref, keep_ref, q_ref, k_ref, kt_ref, v_ref, do_ref, lse_ref, delta_ref,
+def _backward_kernel(lists_ref, keep_ref, q_ref, kvt_ref, do_ref, lse_ref, delta_ref,
                      dqt_ref, dk_ref, dv_ref, dq_sc):
     query_count, slots = lists_ref.shape
     dk_ref[...] = jnp.zeros(dk_ref.shape, jnp.float32)
@@ -76,12 +82,12 @@
                 b = lists_ref[qb, j]
                 q = q_ref[qb]
                 do = do_ref[qb]
-                st = _nt(k_ref[b], q) * SCALE
+                st = _nt(_rows_of(kvt_ref, b, 0), q) * SCALE
                 pt = jnp.exp(st - lse_ref[qb])
                 dv_ref[b] += _nn(pt.astype(jnp.bfloat16), do)
-                dpt = _nt(v_ref[b], do)
+                dpt = _nt(_rows_of(kvt_ref, b, HEAD_DIM), do)
                 dst = (pt * (dpt - delta_ref[qb])).astype(jnp.bfloat16)
-                dq_sc[...] += _nn(kt_ref[b], dst)
+                dq_sc[...] += _nn(kvt_ref[b, :HEAD_DIM, :], dst)
                 dk_ref[b] += _nn(dst, q)
             return carry
 
@@ -89,12 +95,10 @@
         dqt_ref[qb] = (dq_sc[...] * SCALE).astype(jnp.bfloat16)
 
 
-def attend_local(q_rows, do_rows, key_blocks, value_blocks, lists, keep):
+def attend_local(q_rows, do_rows, kv_t, lists, keep):
     query_count, rows, _ = q_rows.shape
-    block_total = key_blocks.shape[0]
+    block_total = kv_t.shape[0]
     f32 = jnp.float32
-    key_t = jnp.swapaxes(key_blocks, 1, 2)
-    value_t = jnp.swapaxes(value_blocks, 1, 2)
     do_t = jnp.swapaxes(do_rows, 1, 2)
     o_t, lse, delta = pl.pallas_call(
         _forward_kernel,
@@ -103,7 +107,7 @@
             jax.ShapeDtypeStruct((query_count, 1, rows), f32),
             jax.ShapeDtypeStruct((query_count, 1, rows), f32),
         ),
-        in_specs=[_smem(), _smem(), _vmem(), _vmem(), _vmem(), _vmem()],
+        in_specs=[_smem(), _smem(), _vmem(), _vmem(), _vmem()],
         out_specs=(_vmem(), _vmem(), _vmem()),
         scratch_shapes=[
             pltpu.VMEM((1, rows), f32),
@@ -111,7 +115,7 @@
             pltpu.VMEM((HEAD_DIM, rows), f32),
         ],
         compiler_params=pltpu.CompilerParams(vmem_limit_bytes=VMEM_LIMIT),
-    )(lists, keep, q_rows, key_blocks, value_t, do_t)
+    )(lists, keep, q_rows, kv_t, do_t)
     dq_t, dk_blocks, dv_blocks = pl.pallas_call(
         _backward_kernel,
         out_shape=(
@@ -119,11 +123,11 @@
             jax.ShapeDtypeStruct((block_total, BLOCK, HEAD_DIM), f32),
             jax.ShapeDtypeStruct((block_total, BLOCK, HEAD_DIM), f32),
         ),
-        in_specs=[_smem(), _smem()] + [_vmem()] * 7,
+        in_specs=[_smem(), _smem()] + [_vmem()] * 5,
         out_specs=(_vmem(), _vmem(), _vmem()),
         scratch_shapes=[pltpu.VMEM((HEAD_DIM, rows), f32)],
         compiler_params=pltpu.CompilerParams(vmem_limit_bytes=VMEM_LIMIT),
-    )(lists, keep, q_rows, key_blocks, key_t, value_blocks, do_rows, lse, delta)
+    )(lists, keep, q_rows, kv_t, do_rows, lse, delta)
     return jnp.swapaxes(o_t, 1, 2), jnp.swapaxes(dq_t, 1, 2), dk_blocks, dv_blocks
 
 
@@ -164,8 +168,8 @@
             pieces = [buf]
             for shift in range(1, size):
                 pieces.append(lax.ppermute(buf, axes, pairs(axis, size - shift)))
-            buf = jnp.stack(pieces)
-        return buf.reshape((-1,) + piece.shape)
+            buf = jnp.concatenate(pieces, axis=0)
+        return buf
 
     def scatter_sum(part, piece_shape):
         part = part.reshape(tuple(size for _, size in reversed(stages)) + piece_shape)
@@ -189,10 +193,8 @@
         table = jnp.asarray(table_np)
         own = table[me]
 
-        kv_held = gather_blocks(jnp.concatenate([keys, values], axis=1))
-        block_total = kv_held.shape[0]
-        key_blocks = kv_held[:, :, :HEAD_DIM]
-        value_blocks = kv_held[:, :, HEAD_DIM:]
+        kv_t = gather_blocks(jnp.concatenate([keys.T, values.T], axis=0))
+        block_total = kv_t.shape[0]
 
         def held_at(block):
             coords = table[block]
@@ -210,8 +212,7 @@
         lists = block_lists.astype(jnp.int32)
         keep = first_occurrence(lists)
         o_rows, dq_rows, dk_blocks, dv_blocks = attend_local(
-            my_heads(queries), my_heads(out_grad), key_blocks, value_blocks,
-            held_at(lists), keep)
+            my_heads(queries), my_heads(out_grad), kv_t, held_at(lists), keep)
 
         def join_halves(rows):
             mine = rows.reshape(token_rows, width)

time: 264 us -> 234 us (0.89)
  starting transfers between devices: 38.5 us -> 82.1 us
  Pallas kernels: 87.4 us -> 50.3 us
  local copies, waits for them, and re-layouts: 45.9 us -> 25.4 us
  waiting for transfers between devices: 60.1 us -> 49 us
  other arithmetic: 31.3 us -> 27.7 us
    ppermute x10, starting transfers between devices: 20.2 us -> 63.8 us  [scatter_sum(): lax.ppermute(sent, axes, pairs(axis, shift)).astype(jnp.float32)]
    pallas_call x1, Pallas kernels: 53.2 us -> 31 us  [attend_local(): pl.pallas_call(_backward_kernel, out_shape=(jax.ShapeDtypeStruct((query_c...]
    pallas_call x1, Pallas kernels: 34.2 us -> 19.4 us  [attend_local(): pl.pallas_call(_forward_kernel, out_shape=(jax.ShapeDtypeStruct((query_co...]
    slice x1 -> x0, local copies, waits for them, and re-layouts: 12 us -> none  [local(): value_blocks = kv_held[:, :, HEAD_DIM:]]
    transpose x2 -> x0, local copies, waits for them, and re-layouts: 9.64 us -> none  [the longest x1 4.84 us: attend_local(): key_t = jnp.swapaxes(key_blocks, 1, 2)]
    ppermute x10, waiting for transfers between devices: 32.1 us -> 24.4 us  [gather_blocks(): pieces.append(lax.ppermute(buf, axes, pairs(axis, size - shift)))]
    another operation x1 -> x0, local copies, waits for them, and re-layouts: 7.29 us -> none  [gather_blocks(): buf = jnp.stack(pieces)]
    unnamed x13 -> x20, local copies, waits for them, and re-layouts: 1.06 us -> 7.39 us
  transfers between devices with their start and end apart: 22 -> 22, of which waited for: 13 -> 10; matrix products, arithmetic and copies ran while one was open for 10% -> 15% of each run, Pallas kernels for 0% -> 0%
where the time goes in v4:
time: 234 us; the launch traced here: 235 us
  starting transfers between devices  82.1 us (35%)
  Pallas kernels  50.3 us (21%)
  waiting for transfers between devices  49 us (21%)
  other arithmetic  27.7 us (12%)
  local copies, waits for them, and re-layouts  25.4 us (11%)
    ppermute x10, starting transfers between devices, scatter_sum(): lax.ppermute(sent, axes, pairs(axis, shift)).astype(jnp.float32)  63.8 us
    pallas_call x1, Pallas kernels, attend_local(): pl.pallas_call(_backward_kernel, out_shape=(jax.ShapeDtypeStruct((query_c...  31 us
    ppermute x10, waiting for transfers between devices, scatter_sum(): lax.ppermute(sent, axes, pairs(axis, shift)).astype(jnp.float32)  24.6 us
    ppermute x10, waiting for transfers between devices, gather_blocks(): pieces.append(lax.ppermute(buf, axes, pairs(axis, size - shift)))  24.4 us
    pallas_call x1, Pallas kernels, attend_local(): pl.pallas_call(_forward_kernel, out_shape=(jax.ShapeDtypeStruct((query_co...  19.4 us
    ppermute x10, starting transfers between devices, gather_blocks(): pieces.append(lax.ppermute(buf, axes, pairs(axis, size - shift)))  14.5 us
    another operation x4, other arithmetic  11.4 us
    unnamed x20, local copies, waits for them, and re-layouts  7.39 us
  transfers between devices with their start and end apart: 22, of which 10 were waited for; matrix products, arithmetic and copies ran while one was open for 15% of the time, Pallas kernels for 0%

profile of v4, /device:TPU:0, one launch (start us, length us, event | category | flops | bytes accessed | tf_op | source)
XLA Modules:
  0.0 235.3 jit_solution(13155724400459634578)
XLA Ops:
  1.4 3.1 %collective-permute-start = (bf16[1,128,128]{2,1,0:T(8,128)(2,1)S(1)}, bf16[1,128,128]{2,1,0:T(8,128)(2,1)S(1)}, u32[]{:S(2)}, u32[]{:S(2)}) collective-permute-start(bf16[1,128,128]{2,1,0:T(8,128)(2,1)S(1)} %maximum_bitcast_fusion), channel_id=1, source_target_pairs={{0,12},{1,13},{2,14},{3,15},{4,0},{5,1},{6,2},{7,3},{8,4},{9,5},{1... | collective-permute-start | bytes 98312 | tf_op jit(solution)/shard_map/ppermute | solution.py:170
  7.6 2.4 %collective-permute-done.1 = bf16[1,128,128]{2,1,0:T(8,128)(2,1)S(1)} collective-permute-done((bf16[1,128,128]{2,1,0:T(8,128)(2,1)S(1)}, bf16[1,128,128]{2,1,0:T(8,128)(2,1)S(1)}, u32[]{:S(2)}, u32[]{:S(2)}) %collective-permute-start.1) | collective-permute-done | bytes 32800 | tf_op jit(solution)/shard_map/ppermute | solution.py:170
  10.3 2.8 %collective-permute-start.3 = (bf16[4,128,128]{2,1,0:T(8,128)(2,1)S(1)}, bf16[4,128,128]{2,1,0:T(8,128)(2,1)S(1)}, u32[]{:S(2)}, u32[]{:S(2)}) collective-permute-start(bf16[4,128,128]{2,1,0:T(8,128)(2,1)S(1)} %pad_maximum_fusion.1), channel_id=1, source_target_pairs={{0,17},{1,16},{2,19},{3,18},{4,21},{5,20},{6,23},{7,22},{8,25},{9,... | collective-permute-start | bytes 393224 | tf_op jit(solution)/shard_map/ppermute | solution.py:170
  21.8 4.0 %collective-permute-start.6 = (bf16[16,128,128]{2,1,0:T(8,128)(2,1)S(1)}, bf16[16,128,128]{2,1,0:T(8,128)(2,1)S(1)}, u32[]{:S(2)}, u32[]{:S(2)}) collective-permute-start(bf16[16,128,128]{2,1,0:T(8,128)(2,1)S(1)} %get-tuple-element.39), channel_id=1, source_target_pairs={{0,96},{1,97},{2,98},{3,99},{4,100},{5,101},{6,102},{7,103},{8,104... | collective-permute-start | bytes 1572872 | tf_op jit(solution)/shard_map/ppermute | solution.py:170
  27.1 18.3 %collective-permute-done.6 = bf16[16,128,128]{2,1,0:T(8,128)(2,1)S(1)} collective-permute-done((bf16[16,128,128]{2,1,0:T(8,128)(2,1)S(1)}, bf16[16,128,128]{2,1,0:T(8,128)(2,1)S(1)}, u32[]{:S(2)}, u32[]{:S(2)}) %collective-permute-start.6) | collective-permute-done | bytes 524320 | tf_op jit(solution)/shard_map/ppermute | solution.py:170
  51.5 2.7 %slice_subtract_fusion.3 = (s32[2,48,1]{2,1,0:T(8,128)S(1)}, s32[2,48,1]{2,1,0:T(8,128)S(1)}, s32[2,48,1]{2,1,0:T(8,128)S(1)}, s32[2,48,1]{2,1,0:T(8,128)S(1)}) fusion(s32[2,48,4]{2,1,0:T(8,128)S(1)} %bitcast.80, s32[]{:T(128)} %bitcast.1, s32[]{:T(128)} %bitcast.5, s32[]{:T(128)} %bitcast.3, s32[]{:T(128)} %bitcast.7), kind=kLoop, calls=%fused_computation.59 | loop fusion | flops 384 | bytes 3088 | tf_op jit(solution)/shard_map/sub | solution.py:204
  60.7 19.4 %shard_map.93 = (bf16[2,64,1024]{2,1,0:T(8,128)(2,1)}, f32[2,1,1024]{2,1,0:T(1,128)}, f32[2,1,1024]{2,1,0:T(1,128)}) custom-call(s32[2,48]{1,0:T(2,128)} %fusion.17.lists_ref, s32[2,48]{1,0:T(2,128)} %not_convert_fusion.keep_ref, bf16[2,1024,64]{2,1,0:T(8,128)(2,1)} %reshape.68.q_ref, bf16[128,128,128]{2,1,0:T(8,128)(2,1)} %constant_dynamic-update-slice_fusion.17.kvt_ref, ...), custom_call_target="tpu_custom_call" | custom-call | tf_op jit(solution)/shard_map/pallas_call | solution.py:103
  80.1 31.0 %shard_map.94 = (bf16[2,64,1024]{2,1,0:T(8,128)(2,1)}, f32[128,128,64]{2,1,0:T(8,128)}, f32[128,128,64]{2,1,0:T(8,128)}) custom-call(s32[2,48]{1,0:T(2,128)} %fusion.17.lists_ref, s32[2,48]{1,0:T(2,128)} %not_convert_fusion.keep_ref, bf16[2,1024,64]{2,1,0:T(8,128)(2,1)} %reshape.68.q_ref, ...), custom_call_target="tpu_custom_call" | custom-call | tf_op jit(solution)/shard_map/pallas_call | solution.py:119
  111.1 4.4 %fusion.1 = bf16[64,128,128]{2,1,0:T(8,128)(2,1)S(1)} fusion(f32[128,128,64]{2,1,0:T(8,128)} %get-tuple-element.15, f32[128,128,64]{2,1,0:T(8,128)} %get-tuple-element.14), kind=kLoop, calls=%fused_computation.5 | loop fusion | flops 4194304 | bytes 10485760 | tf_op jit(solution)/shard_map/convert.10
  115.5 2.4 %copy.33 = bf16[4,4,4,128,128]{3,4,2,1,0:T(8,128)(2,1)} copy(bf16[4,4,4,128,128]{4,3,2,1,0:T(8,128)(2,1)S(1)} %bitcast.79) | data formatting | bytes 4194304 | tf_op jit(solution)/shard_map/convert_element_type | solution.py:179
  117.9 6.6 %fusion = f32[64,128,128]{2,1,0:T(8,128)} fusion(f32[128,128,64]{2,1,0:T(8,128)} %get-tuple-element.14, f32[128,128,64]{2,1,0:T(8,128)} %get-tuple-element.15), kind=kLoop, calls=%fused_computation.3 | loop fusion | flops 1048576 | bytes 12582912 | tf_op jit(solution)/shard_map/concatenate | solution.py:226
  124.5 5.2 %copy.34 = f32[4,4,4,128,128]{3,4,2,1,0:T(8,128)} copy(f32[4,4,4,128,128]{4,3,2,1,0:T(8,128)} %bitcast.78) | data formatting | bytes 8388608 | tf_op jit(solution)/shard_map/squeeze | solution.py:177
  129.7 5.2 %fusion.26 = (bf16[4,4,4,128,128]{3,4,2,1,0:T(8,128)(2,1)S(1)}, f32[4,4,4,128,128]{3,4,2,1,0:T(8,128)}) fusion(f32[4,4,4,128,128]{3,4,2,1,0:T(8,128)} %copy.34, bf16[4,4,4,128,128]{3,4,2,1,0:T(8,128)(2,1)S(1)} %collective-permute-done.12), kind=kLoop, calls=%fused_computation.99 | loop fusion | flops 3145728 | bytes 12582912 | tf_op jit(solution)/shard_map/convert.9
  135.0 8.4 %collective-permute-start.13 = (bf16[4,4,128,128]{2,3,1,0:T(8,128)(2,1)S(1)}, bf16[4,4,128,128]{2,3,1,0:T(8,128)(2,1)S(1)}, u32[]{:S(2)}, u32[]{:S(2)}) collective-permute-start(bf16[4,4,128,128]{2,3,1,0:T(8,128)(2,1)S(1)} %get-tuple-element.22), channel_id=1, source_target_pairs={{0,32},{1,33},{2,34},{3,35},{4,36},{5,37},{6,38},{7,39},{8,40},{9,... | collective-permute-start | bytes 1572872 | tf_op jit(solution)/shard_map/ppermute | solution.py:180
  143.4 40.1 %collective-permute-start.14 = (bf16[4,4,128,128]{2,3,1,0:T(8,128)(2,1)S(1)}, bf16[4,4,128,128]{2,3,1,0:T(8,128)(2,1)S(1)}, u32[]{:S(2)}, u32[]{:S(2)}) collective-permute-start(bf16[4,4,128,128]{2,3,1,0:T(8,128)(2,1)S(1)} %get-tuple-element.24), channel_id=1, source_target_pairs={{0,64},{1,65},{2,66},{3,67},{4,68},{5,69},{6,70},{7,71},{8,72},{9,... | collective-permute-start | bytes 1572872 | tf_op jit(solution)/shard_map/ppermute | solution.py:180
  183.5 2.5 %collective-permute-start.15 = (bf16[4,4,128,128]{2,3,1,0:T(8,128)(2,1)S(1)}, bf16[4,4,128,128]{2,3,1,0:T(8,128)(2,1)}, u32[]{:S(2)}, u32[]{:S(2)}) collective-permute-start(bf16[4,4,128,128]{2,3,1,0:T(8,128)(2,1)S(1)} %get-tuple-element.23), channel_id=1, source_target_pairs={{0,96},{1,97},{2,98},{3,99},{4,100},{5,101},{6,102},{7,103},{8,104... | collective-permute-start | bytes 1572872 | tf_op jit(solution)/shard_map/ppermute | solution.py:180
  188.5 18.3 %collective-permute-done.14 = bf16[4,4,128,128]{2,3,1,0:T(8,128)(2,1)S(1)} collective-permute-done((bf16[4,4,128,128]{2,3,1,0:T(8,128)(2,1)S(1)}, bf16[4,4,128,128]{2,3,1,0:T(8,128)(2,1)S(1)}, u32[]{:S(2)}, u32[]{:S(2)}) %collective-permute-start.14) | collective-permute-done | bytes 524320 | tf_op jit(solution)/shard_map/ppermute | solution.py:180
  206.7 1.7 fusion.24
  209.4 2.5 %collective-permute-start.18 = (bf16[4,128,128]{1,2,0:T(8,128)(2,1)S(1)}, bf16[4,128,128]{1,2,0:T(8,128)(2,1)S(1)}, u32[]{:S(2)}, u32[]{:S(2)}) collective-permute-start(bf16[4,128,128]{1,2,0:T(8,128)(2,1)S(1)} %get-tuple-element.26), channel_id=1, source_target_pairs={{0,17},{1,16},{2,19},{3,18},{4,21},{5,20},{6,23},{7,22},{8,25},{9,... | collective-permute-start | bytes 393224 | tf_op jit(solution)/shard_map/ppermute | solution.py:180
  212.6 2.8 %collective-permute-start.10 = (bf16[256,512]{1,0:T(8,128)(2,1)S(1)}, bf16[256,512]{1,0:T(8,128)(2,1)S(1)}, u32[]{:S(2)}, u32[]{:S(2)}) collective-permute-start(bf16[256,512]{1,0:T(8,128)(2,1)S(1)} %reshape.70), channel_id=1, source_target_pairs={{0,1},{1,0},{2,3},{3,2},{4,5},{5,4},{6,7},{7,6},{8,9},{9,8},{10,11... | collective-permute-start | bytes 786440 | tf_op jit(solution)/shard_map/ppermute | solution.py:219
  215.4 2.0 maximum_select_fusion.1
  217.4 5.6 %collective-permute-done.16 = bf16[4,128,128]{1,2,0:T(8,128)(2,1)S(1)} collective-permute-done((bf16[4,128,128]{1,2,0:T(8,128)(2,1)S(1)}, bf16[4,128,128]{1,2,0:T(8,128)(2,1)S(1)}, u32[]{:S(2)}, u32[]{:S(2)}) %collective-permute-start.16) | collective-permute-done | bytes 131104 | tf_op jit(solution)/shard_map/ppermute | solution.py:180
  223.2 6.7 %collective-permute-start.20 = (bf16[128,128]{0,1:T(8,128)(2,1)S(1)}, bf16[128,128]{0,1:T(8,128)(2,1)S(1)}, u32[]{:S(2)}, u32[]{:S(2)}) collective-permute-start(bf16[128,128]{0,1:T(8,128)(2,1)S(1)} %get-tuple-element.36), channel_id=1, source_target_pairs={{0,8},{1,9},{2,10},{3,11},{4,12},{5,13},{6,14},{7,15},{8,0},{9,1},... | collective-permute-start | bytes 98312 | tf_op jit(solution)/shard_map/ppermute | solution.py:180
  229.9 2.5 %collective-permute-start.21 = (bf16[128,128]{0,1:T(8,128)(2,1)S(1)}, bf16[128,128]{0,1:T(8,128)(2,1)S(1)}, u32[]{:S(2)}, u32[]{:S(2)}) collective-permute-start(bf16[128,128]{0,1:T(8,128)(2,1)S(1)} %get-tuple-element.35), channel_id=1, source_target_pairs={{0,12},{1,13},{2,14},{3,15},{4,0},{5,1},{6,2},{7,3},{8,4},{9,5},{1... | collective-permute-start | bytes 98312 | tf_op jit(solution)/shard_map/ppermute | solution.py:180
  (81 shorter events, 33.7 us)
Async XLA Ops:
  0.6 49.7 %copy-start.1 = (s32[128,4]{1,0:T(8,128)S(1)}, s32[128,4]{1,0:T(8,128)}, u32[]{:S(2)}) copy-start(s32[128,4]{1,0:T(8,128)} %constant.64.clone) | copy-start | bytes 6148
  0.6 49.6 %copy-start.3 = (s32[2,48]{1,0:T(2,128)S(1)}, s32[2,48]{1,0:T(2,128)}, u32[]{:S(2)}) copy-start(s32[2,48]{1,0:T(2,128)} %param.10) | copy-start | bytes 1156
  1.4 6.1 %collective-permute-start = (bf16[1,128,128]{2,1,0:T(8,128)(2,1)S(1)}, bf16[1,128,128]{2,1,0:T(8,128)(2,1)S(1)}, u32[]{:S(2)}, u32[]{:S(2)}) collective-permute-start(bf16[1,128,128]{2,1,0:T(8,128)(2,1)S(1)} %maximum_bitcast_fusion), channel_id=1, source_target_pairs={{0,12},{1,13},{2,14},{3,15},{4,0},{5,1},{6,2},{7,3},{8,4},{9,5},{1... | collective-permute-start | bytes 98312 | tf_op jit(solution)/shard_map/ppermute | solution.py:170
  4.6 5.4 %collective-permute-start.1 = (bf16[1,128,128]{2,1,0:T(8,128)(2,1)S(1)}, bf16[1,128,128]{2,1,0:T(8,128)(2,1)S(1)}, u32[]{:S(2)}, u32[]{:S(2)}) collective-permute-start(bf16[1,128,128]{2,1,0:T(8,128)(2,1)S(1)} %maximum_bitcast_fusion), channel_id=1, source_target_pairs={{0,8},{1,9},{2,10},{3,11},{4,12},{5,13},{6,14},{7,15},{8,0},{9,1},... | collective-permute-start | bytes 98312 | tf_op jit(solution)/shard_map/ppermute | solution.py:170
  5.2 5.1 %collective-permute-start.2 = (bf16[1,128,128]{2,1,0:T(8,128)(2,1)S(1)}, bf16[1,128,128]{2,1,0:T(8,128)(2,1)S(1)}, u32[]{:S(2)}, u32[]{:S(2)}) collective-permute-start(bf16[1,128,128]{2,1,0:T(8,128)(2,1)S(1)} %maximum_bitcast_fusion), channel_id=1, source_target_pairs={{0,4},{1,5},{2,6},{3,7},{4,8},{5,9},{6,10},{7,11},{8,12},{9,13},{1... | collective-permute-start | bytes 98312 | tf_op jit(solution)/shard_map/ppermute | solution.py:170
  10.3 7.1 %collective-permute-start.3 = (bf16[4,128,128]{2,1,0:T(8,128)(2,1)S(1)}, bf16[4,128,128]{2,1,0:T(8,128)(2,1)S(1)}, u32[]{:S(2)}, u32[]{:S(2)}) collective-permute-start(bf16[4,128,128]{2,1,0:T(8,128)(2,1)S(1)} %pad_maximum_fusion.1), channel_id=1, source_target_pairs={{0,17},{1,16},{2,19},{3,18},{4,21},{5,20},{6,23},{7,22},{8,25},{9,... | collective-permute-start | bytes 393224 | tf_op jit(solution)/shard_map/ppermute | solution.py:170
  13.2 6.6 %collective-permute-start.4 = (bf16[4,128,128]{2,1,0:T(8,128)(2,1)S(1)}, bf16[4,128,128]{2,1,0:T(8,128)(2,1)S(1)}, u32[]{:S(2)}, u32[]{:S(2)}) collective-permute-start(bf16[4,128,128]{2,1,0:T(8,128)(2,1)S(1)} %pad_maximum_fusion.1), channel_id=1, source_target_pairs={{0,1},{1,0},{2,3},{3,2},{4,5},{5,4},{6,7},{7,6},{8,9},{9,8},{10,11... | collective-permute-start | bytes 393224 | tf_op jit(solution)/shard_map/ppermute | solution.py:170
  14.0 7.1 %collective-permute-start.5 = (bf16[4,128,128]{2,1,0:T(8,128)(2,1)S(1)}, bf16[4,128,128]{2,1,0:T(8,128)(2,1)S(1)}, u32[]{:S(2)}, u32[]{:S(2)}) collective-permute-start(bf16[4,128,128]{2,1,0:T(8,128)(2,1)S(1)} %pad_maximum_fusion.1), channel_id=1, source_target_pairs={{0,16},{1,17},{2,18},{3,19},{4,20},{5,21},{6,22},{7,23},{8,24},{9,... | collective-permute-start | bytes 393224 | tf_op jit(solution)/shard_map/ppermute | solution.py:170
  21.8 23.6 %collective-permute-start.6 = (bf16[16,128,128]{2,1,0:T(8,128)(2,1)S(1)}, bf16[16,128,128]{2,1,0:T(8,128)(2,1)S(1)}, u32[]{:S(2)}, u32[]{:S(2)}) collective-permute-start(bf16[16,128,128]{2,1,0:T(8,128)(2,1)S(1)} %get-tuple-element.39), channel_id=1, source_target_pairs={{0,96},{1,97},{2,98},{3,99},{4,100},{5,101},{6,102},{7,103},{8,104... | collective-permute-start | bytes 1572872 | tf_op jit(solution)/shard_map/ppermute | solution.py:170
  25.9 20.9 %collective-permute-start.7 = (bf16[16,128,128]{2,1,0:T(8,128)(2,1)S(1)}, bf16[16,128,128]{2,1,0:T(8,128)(2,1)S(1)}, u32[]{:S(2)}, u32[]{:S(2)}) collective-permute-start(bf16[16,128,128]{2,1,0:T(8,128)(2,1)S(1)} %get-tuple-element.39), channel_id=1, source_target_pairs={{0,64},{1,65},{2,66},{3,67},{4,68},{5,69},{6,70},{7,71},{8,72},{9,... | collective-permute-start | bytes 1572872 | tf_op jit(solution)/shard_map/ppermute | solution.py:170
  25.9 23.0 %collective-permute-start.8 = (bf16[16,128,128]{2,1,0:T(8,128)(2,1)S(1)}, bf16[16,128,128]{2,1,0:T(8,128)(2,1)S(1)}, u32[]{:S(2)}, u32[]{:S(2)}) collective-permute-start(bf16[16,128,128]{2,1,0:T(8,128)(2,1)S(1)} %get-tuple-element.39), channel_id=1, source_target_pairs={{0,32},{1,33},{2,34},{3,35},{4,36},{5,37},{6,38},{7,39},{8,40},{9,... | collective-permute-start | bytes 1572872 | tf_op jit(solution)/shard_map/ppermute | solution.py:170
  50.2 9.1 %collective-permute-start.9 = (bf16[64,128,128]{2,1,0:T(8,128)(2,1)}, bf16[64,128,128]{2,1,0:T(8,128)(2,1)S(1)}, u32[]{:S(2)}, u32[]{:S(2)}) collective-permute-start(bf16[64,128,128]{2,1,0:T(8,128)(2,1)} %get-tuple-element.28), channel_id=1, source_target_pairs={{0,2},{1,3},{2,0},{3,1},{4,6},{5,7},{6,4},{7,5},{8,10},{9,11},{10,... | collective-permute-start | bytes 6291464 | tf_op jit(solution)/shard_map/ppermute | solution.py:170
  117.9 11.8 %collective-permute-start.12 = (bf16[4,4,4,128,128]{3,4,2,1,0:T(8,128)(2,1)}, bf16[4,4,4,128,128]{3,4,2,1,0:T(8,128)(2,1)S(1)}, u32[]{:S(2)}, u32[]{:S(2)}) collective-permute-start(bf16[4,4,4,128,128]{3,4,2,1,0:T(8,128)(2,1)} %copy.33), channel_id=1, source_target_pairs={{0,2},{1,3},{2,0},{3,1},{4,6},{5,7},{6,4},{7,5},{8,10},{9,11},{10,... | collective-permute-start | bytes 6291464 | tf_op jit(solution)/shard_map/ppermute | solution.py:180
  135.0 53.4 %collective-permute-start.13 = (bf16[4,4,128,128]{2,3,1,0:T(8,128)(2,1)S(1)}, bf16[4,4,128,128]{2,3,1,0:T(8,128)(2,1)S(1)}, u32[]{:S(2)}, u32[]{:S(2)}) collective-permute-start(bf16[4,4,128,128]{2,3,1,0:T(8,128)(2,1)S(1)} %get-tuple-element.22), channel_id=1, source_target_pairs={{0,32},{1,33},{2,34},{3,35},{4,36},{5,37},{6,38},{7,39},{8,40},{9,... | collective-permute-start | bytes 1572872 | tf_op jit(solution)/shard_map/ppermute | solution.py:180
  143.4 63.3 %collective-permute-start.14 = (bf16[4,4,128,128]{2,3,1,0:T(8,128)(2,1)S(1)}, bf16[4,4,128,128]{2,3,1,0:T(8,128)(2,1)S(1)}, u32[]{:S(2)}, u32[]{:S(2)}) collective-permute-start(bf16[4,4,128,128]{2,3,1,0:T(8,128)(2,1)S(1)} %get-tuple-element.24), channel_id=1, source_target_pairs={{0,64},{1,65},{2,66},{3,67},{4,68},{5,69},{6,70},{7,71},{8,72},{9,... | collective-permute-start | bytes 1572872 | tf_op jit(solution)/shard_map/ppermute | solution.py:180
  183.5 23.2 %collective-permute-start.15 = (bf16[4,4,128,128]{2,3,1,0:T(8,128)(2,1)S(1)}, bf16[4,4,128,128]{2,3,1,0:T(8,128)(2,1)}, u32[]{:S(2)}, u32[]{:S(2)}) collective-permute-start(bf16[4,4,128,128]{2,3,1,0:T(8,128)(2,1)S(1)} %get-tuple-element.23), channel_id=1, source_target_pairs={{0,96},{1,97},{2,98},{3,99},{4,100},{5,101},{6,102},{7,103},{8,104... | collective-permute-start | bytes 1572872 | tf_op jit(solution)/shard_map/ppermute | solution.py:180
  187.6 27.8 %collective-permute-start.11 = (bf16[256,512]{1,0:T(8,128)(2,1)S(1)}, bf16[256,512]{1,0:T(8,128)(2,1)}, u32[]{:S(2)}, u32[]{:S(2)}) collective-permute-start(bf16[256,512]{1,0:T(8,128)(2,1)S(1)} %reshape.71), channel_id=1, source_target_pairs={{0,1},{1,0},{2,3},{3,2},{4,5},{5,4},{6,7},{7,6},{8,9},{9,8},{10,11... | collective-permute-start | bytes 786440 | tf_op jit(solution)/shard_map/ppermute | solution.py:219
  208.5 14.5 %collective-permute-start.16 = (bf16[4,128,128]{1,2,0:T(8,128)(2,1)S(1)}, bf16[4,128,128]{1,2,0:T(8,128)(2,1)S(1)}, u32[]{:S(2)}, u32[]{:S(2)}) collective-permute-start(bf16[4,128,128]{1,2,0:T(8,128)(2,1)S(1)} %get-tuple-element.25), channel_id=1, source_target_pairs={{0,16},{1,17},{2,18},{3,19},{4,20},{5,21},{6,22},{7,23},{8,24},{9,... | collective-permute-start | bytes 393224 | tf_op jit(solution)/shard_map/ppermute | solution.py:180
  208.5 14.5 %collective-permute-start.17 = (bf16[4,128,128]{1,2,0:T(8,128)(2,1)S(1)}, bf16[4,128,128]{1,2,0:T(8,128)(2,1)S(1)}, u32[]{:S(2)}, u32[]{:S(2)}) collective-permute-start(bf16[4,128,128]{1,2,0:T(8,128)(2,1)S(1)} %get-tuple-element.27), channel_id=1, source_target_pairs={{0,1},{1,0},{2,3},{3,2},{4,5},{5,4},{6,7},{7,6},{8,9},{9,8},{10,11... | collective-permute-start | bytes 393224 | tf_op jit(solution)/shard_map/ppermute | solution.py:180
  209.4 13.6 %collective-permute-start.18 = (bf16[4,128,128]{1,2,0:T(8,128)(2,1)S(1)}, bf16[4,128,128]{1,2,0:T(8,128)(2,1)S(1)}, u32[]{:S(2)}, u32[]{:S(2)}) collective-permute-start(bf16[4,128,128]{1,2,0:T(8,128)(2,1)S(1)} %get-tuple-element.26), channel_id=1, source_target_pairs={{0,17},{1,16},{2,19},{3,18},{4,21},{5,20},{6,23},{7,22},{8,25},{9,... | collective-permute-start | bytes 393224 | tf_op jit(solution)/shard_map/ppermute | solution.py:180
  212.6 19.9 %collective-permute-start.10 = (bf16[256,512]{1,0:T(8,128)(2,1)S(1)}, bf16[256,512]{1,0:T(8,128)(2,1)S(1)}, u32[]{:S(2)}, u32[]{:S(2)}) collective-permute-start(bf16[256,512]{1,0:T(8,128)(2,1)S(1)} %reshape.70), channel_id=1, source_target_pairs={{0,1},{1,0},{2,3},{3,2},{4,5},{5,4},{6,7},{7,6},{8,9},{9,8},{10,11... | collective-permute-start | bytes 786440 | tf_op jit(solution)/shard_map/ppermute | solution.py:219
  223.1 10.3 %collective-permute-start.19 = (bf16[128,128]{0,1:T(8,128)(2,1)S(1)}, bf16[128,128]{0,1:T(8,128)(2,1)S(1)}, u32[]{:S(2)}, u32[]{:S(2)}) collective-permute-start(bf16[128,128]{0,1:T(8,128)(2,1)S(1)} %get-tuple-element.34), channel_id=1, source_target_pairs={{0,4},{1,5},{2,6},{3,7},{4,8},{5,9},{6,10},{7,11},{8,12},{9,13},{1... | collective-permute-start | bytes 98312 | tf_op jit(solution)/shard_map/ppermute | solution.py:180
  223.2 10.2 %collective-permute-start.20 = (bf16[128,128]{0,1:T(8,128)(2,1)S(1)}, bf16[128,128]{0,1:T(8,128)(2,1)S(1)}, u32[]{:S(2)}, u32[]{:S(2)}) collective-permute-start(bf16[128,128]{0,1:T(8,128)(2,1)S(1)} %get-tuple-element.36), channel_id=1, source_target_pairs={{0,8},{1,9},{2,10},{3,11},{4,12},{5,13},{6,14},{7,15},{8,0},{9,1},... | collective-permute-start | bytes 98312 | tf_op jit(solution)/shard_map/ppermute | solution.py:180
  229.9 4.1 %collective-permute-start.21 = (bf16[128,128]{0,1:T(8,128)(2,1)S(1)}, bf16[128,128]{0,1:T(8,128)(2,1)S(1)}, u32[]{:S(2)}, u32[]{:S(2)}) collective-permute-start(bf16[128,128]{0,1:T(8,128)(2,1)S(1)} %get-tuple-element.35), channel_id=1, source_target_pairs={{0,12},{1,13},{2,14},{3,15},{4,0},{5,1},{6,2},{7,3},{8,4},{9,5},{1... | collective-permute-start | bytes 98312 | tf_op jit(solution)/shard_map/ppermute | solution.py:180
  (2 other events, 47.7 us)

commit v5 on v4

--- a/solution.py
+++ b/solution.py
@@ -69,10 +69,9 @@
 
 
 def _backward_kernel(lists_ref, keep_ref, q_ref, kvt_ref, do_ref, lse_ref, delta_ref,
-                     dqt_ref, dk_ref, dv_ref, dq_sc):
+                     dqt_ref, dkvt_ref, dq_sc):
     query_count, slots = lists_ref.shape
-    dk_ref[...] = jnp.zeros(dk_ref.shape, jnp.float32)
-    dv_ref[...] = jnp.zeros(dv_ref.shape, jnp.float32)
+    dkvt_ref[...] = jnp.zeros(dkvt_ref.shape, jnp.float32)
     for qb in range(query_count):
         dq_sc[...] = jnp.zeros(dq_sc.shape, jnp.float32)
 
@@ -84,11 +83,11 @@
                 do = do_ref[qb]
                 st = _nt(_rows_of(kvt_ref, b, 0), q) * SCALE
                 pt = jnp.exp(st - lse_ref[qb])
-                dv_ref[b] += _nn(pt.astype(jnp.bfloat16), do)
+                dkvt_ref[b, HEAD_DIM:, :] += jnp.transpose(_nn(pt.astype(jnp.bfloat16), do))
                 dpt = _nt(_rows_of(kvt_ref, b, HEAD_DIM), do)
                 dst = (pt * (dpt - delta_ref[qb])).astype(jnp.bfloat16)
                 dq_sc[...] += _nn(kvt_ref[b, :HEAD_DIM, :], dst)
-                dk_ref[b] += _nn(dst, q)
+                dkvt_ref[b, :HEAD_DIM, :] += jnp.transpose(_nn(dst, q))
             return carry
 
         lax.fori_loop(0, slots, body, 0)
@@ -116,19 +115,18 @@
         ],
         compiler_params=pltpu.CompilerParams(vmem_limit_bytes=VMEM_LIMIT),
     )(lists, keep, q_rows, kv_t, do_t)
-    dq_t, dk_blocks, dv_blocks = pl.pallas_call(
+    dq_t, dkv_t = pl.pallas_call(
         _backward_kernel,
         out_shape=(
             jax.ShapeDtypeStruct((query_count, HEAD_DIM, rows), jnp.bfloat16),
-            jax.ShapeDtypeStruct((block_total, BLOCK, HEAD_DIM), f32),
-            jax.ShapeDtypeStruct((block_total, BLOCK, HEAD_DIM), f32),
+            jax.ShapeDtypeStruct((block_total, 2 * HEAD_DIM, BLOCK), f32),
         ),
         in_specs=[_smem(), _smem()] + [_vmem()] * 5,
-        out_specs=(_vmem(), _vmem(), _vmem()),
+        out_specs=(_vmem(), _vmem()),
         scratch_shapes=[pltpu.VMEM((HEAD_DIM, rows), f32)],
         compiler_params=pltpu.CompilerParams(vmem_limit_bytes=VMEM_LIMIT),
     )(lists, keep, q_rows, kv_t, do_rows, lse, delta)
-    return jnp.swapaxes(o_t, 1, 2), jnp.swapaxes(dq_t, 1, 2), dk_blocks, dv_blocks
+    return jnp.swapaxes(o_t, 1, 2), jnp.swapaxes(dq_t, 1, 2), dkv_t
 
 
 def first_occurrence(block_lists):
@@ -211,7 +209,7 @@
 
         lists = block_lists.astype(jnp.int32)
         keep = first_occurrence(lists)
-        o_rows, dq_rows, dk_blocks, dv_blocks = attend_local(
+        o_rows, dq_rows, dkv_t = attend_local(
             my_heads(queries), my_heads(out_grad), kv_t, held_at(lists), keep)
 
         def join_halves(rows):
@@ -223,10 +221,9 @@
 
         attended = join_halves(o_rows)
         query_grad = join_halves(dq_rows)
-        partial_kv = jnp.concatenate([dk_blocks, dv_blocks], axis=2)
-        owned = scatter_sum(partial_kv, (BLOCK, 2 * HEAD_DIM))
-        key_grad = (owned[:, :HEAD_DIM] * SCALE).astype(jnp.bfloat16)
-        value_grad = owned[:, HEAD_DIM:].astype(jnp.bfloat16)
+        owned = scatter_sum(dkv_t, (2 * HEAD_DIM, BLOCK))
+        key_grad = (owned[:HEAD_DIM].T * SCALE).astype(jnp.bfloat16)
+        value_grad = owned[HEAD_DIM:].T.astype(jnp.bfloat16)
         return (attended, query_grad, key_grad, value_grad)
 
     return local

time: 234 us -> 217 us (0.927)
  Pallas kernels: 50.3 us -> 30.6 us
  starting transfers between devices: 82.1 us -> 101 us
  other arithmetic: 27.7 us -> 14.5 us
  local copies, waits for them, and re-layouts: 25.4 us -> 21.5 us
    ppermute x10, starting transfers between devices: 63.8 us -> 84 us  [scatter_sum(): lax.ppermute(sent, axes, pairs(axis, shift)).astype(jnp.float32)]
    pallas_call x1, Pallas kernels: 31 us -> 18.6 us  [attend_local(): pl.pallas_call(_backward_kernel, out_shape=(jax.ShapeDtypeStruct((query_c...]
    pallas_call x1, Pallas kernels: 19.4 us -> 12 us  [attend_local(): pl.pallas_call(_forward_kernel, out_shape=(jax.ShapeDtypeStruct((query_co...]
    another operation x4 -> x3, other arithmetic: 11.4 us -> 4.71 us
    concatenate x1 -> x0, other arithmetic: 6.59 us -> none  [local(): partial_kv = jnp.concatenate([dk_blocks, dv_blocks], axis=2)]
    squeeze x1 -> x0, local copies, waits for them, and re-layouts: 5.23 us -> none  [scatter_sum(): total = part[0]]
    slice x1 -> x2, local copies, waits for them, and re-layouts: 0.61 us -> 5.01 us  [the longest x1 2.55 us: scatter_sum(): sent = part[shift].astype(jnp.bfloat16)]
    convert_element_type x4 -> x3, local copies, waits for them, and re-layouts: 2.54 us -> 0.14 us  [scatter_sum(): sent = part[shift].astype(jnp.bfloat16)]
  transfers between devices with their start and end apart: 22 -> 22, of which waited for: 10 -> 12; matrix products, arithmetic and copies ran while one was open for 15% -> 11% of each run, Pallas kernels for 0% -> 0%
where the time goes in v5:
time: 217 us; the launch traced here: 218 us
  starting transfers between devices  101 us (47%)
  waiting for transfers between devices  49.2 us (23%)
  Pallas kernels  30.6 us (14%)
  local copies, waits for them, and re-layouts  21.5 us (10%)
  other arithmetic  14.5 us (7%)
    ppermute x10, starting transfers between devices, scatter_sum(): lax.ppermute(sent, axes, pairs(axis, shift)).astype(jnp.float32)  84 us
    ppermute x10, waiting for transfers between devices, gather_blocks(): pieces.append(lax.ppermute(buf, axes, pairs(axis, size - shift)))  24.7 us
    ppermute x10, waiting for transfers between devices, scatter_sum(): lax.ppermute(sent, axes, pairs(axis, shift)).astype(jnp.float32)  24.5 us
    pallas_call x1, Pallas kernels, attend_local(): pl.pallas_call(_backward_kernel, out_shape=(jax.ShapeDtypeStruct((query_c...  18.6 us
    ppermute x10, starting transfers between devices, gather_blocks(): pieces.append(lax.ppermute(buf, axes, pairs(axis, size - shift)))  14.5 us
    pallas_call x1, Pallas kernels, attend_local(): pl.pallas_call(_forward_kernel, out_shape=(jax.ShapeDtypeStruct((query_co...  12 us
    unnamed x22, local copies, waits for them, and re-layouts  7.08 us
    another operation x3, other arithmetic  4.71 us
  transfers between devices with their start and end apart: 22, of which 12 were waited for; matrix products, arithmetic and copies ran while one was open for 11% of the time, Pallas kernels for 0%

profile of v5, /device:TPU:0, one launch (start us, length us, event | category | flops | bytes accessed | tf_op | source)
XLA Modules:
  0.0 217.7 jit_solution(9612339409571990949)
XLA Ops:
  1.4 3.1 %collective-permute-start = (bf16[1,128,128]{2,1,0:T(8,128)(2,1)S(1)}, bf16[1,128,128]{2,1,0:T(8,128)(2,1)S(1)}, u32[]{:S(2)}, u32[]{:S(2)}) collective-permute-start(bf16[1,128,128]{2,1,0:T(8,128)(2,1)S(1)} %maximum_bitcast_fusion), channel_id=1, source_target_pairs={{0,12},{1,13},{2,14},{3,15},{4,0},{5,1},{6,2},{7,3},{8,4},{9,5},{1... | collective-permute-start | bytes 98312 | tf_op jit(solution)/shard_map/ppermute | solution.py:168
  7.5 2.4 %collective-permute-done.1 = bf16[1,128,128]{2,1,0:T(8,128)(2,1)S(1)} collective-permute-done((bf16[1,128,128]{2,1,0:T(8,128)(2,1)S(1)}, bf16[1,128,128]{2,1,0:T(8,128)(2,1)S(1)}, u32[]{:S(2)}, u32[]{:S(2)}) %collective-permute-start.1) | collective-permute-done | bytes 32800 | tf_op jit(solution)/shard_map/ppermute | solution.py:168
  10.3 2.8 %collective-permute-start.3 = (bf16[4,128,128]{2,1,0:T(8,128)(2,1)S(1)}, bf16[4,128,128]{2,1,0:T(8,128)(2,1)S(1)}, u32[]{:S(2)}, u32[]{:S(2)}) collective-permute-start(bf16[4,128,128]{2,1,0:T(8,128)(2,1)S(1)} %pad_maximum_fusion), channel_id=1, source_target_pairs={{0,17},{1,16},{2,19},{3,18},{4,21},{5,20},{6,23},{7,22},{8,25},{9,... | collective-permute-start | bytes 393224 | tf_op jit(solution)/shard_map/ppermute | solution.py:168
  21.8 4.0 %collective-permute-start.6 = (bf16[16,128,128]{2,1,0:T(8,128)(2,1)S(1)}, bf16[16,128,128]{2,1,0:T(8,128)(2,1)S(1)}, u32[]{:S(2)}, u32[]{:S(2)}) collective-permute-start(bf16[16,128,128]{2,1,0:T(8,128)(2,1)S(1)} %get-tuple-element.37), channel_id=1, source_target_pairs={{0,96},{1,97},{2,98},{3,99},{4,100},{5,101},{6,102},{7,103},{8,104... | collective-permute-start | bytes 1572872 | tf_op jit(solution)/shard_map/ppermute | solution.py:168
  27.1 18.3 %collective-permute-done.6 = bf16[16,128,128]{2,1,0:T(8,128)(2,1)S(1)} collective-permute-done((bf16[16,128,128]{2,1,0:T(8,128)(2,1)S(1)}, bf16[16,128,128]{2,1,0:T(8,128)(2,1)S(1)}, u32[]{:S(2)}, u32[]{:S(2)}) %collective-permute-start.6) | collective-permute-done | bytes 524320 | tf_op jit(solution)/shard_map/ppermute | solution.py:168
  51.5 2.7 %slice_subtract_fusion.3 = (s32[2,48,1]{2,1,0:T(8,128)S(1)}, s32[2,48,1]{2,1,0:T(8,128)S(1)}, s32[2,48,1]{2,1,0:T(8,128)S(1)}, s32[2,48,1]{2,1,0:T(8,128)S(1)}) fusion(s32[2,48,4]{2,1,0:T(8,128)S(1)} %bitcast.84, s32[]{:T(128)} %bitcast.1, s32[]{:T(128)} %bitcast.5, s32[]{:T(128)} %bitcast.3, s32[]{:T(128)} %bitcast.7), kind=kLoop, calls=%fused_computation.55 | loop fusion | flops 384 | bytes 3088 | tf_op jit(solution)/shard_map/sub | solution.py:202
  60.8 12.0 %shard_map.93 = (bf16[2,64,1024]{2,1,0:T(8,128)(2,1)}, f32[2,1,1024]{2,1,0:T(1,128)}, f32[2,1,1024]{2,1,0:T(1,128)}) custom-call(s32[2,48]{1,0:T(2,128)} %fusion.17.lists_ref, s32[2,48]{1,0:T(2,128)} %not_convert_fusion.keep_ref, bf16[2,1024,64]{2,1,0:T(8,128)(2,1)} %reshape.68.q_ref, bf16[128,128,128]{2,1,0:T(8,128)(2,1)} %constant_dynamic-update-slice_fusion.17.kvt_ref, ...), custom_call_target="tpu_custom_call" | custom-call | tf_op jit(solution)/shard_map/pallas_call | solution.py:102
  72.8 18.6 %shard_map.94 = (bf16[2,64,1024]{2,1,0:T(8,128)(2,1)}, f32[128,128,128]{2,1,0:T(8,128)}) custom-call(s32[2,48]{1,0:T(2,128)} %fusion.17.lists_ref, s32[2,48]{1,0:T(2,128)} %not_convert_fusion.keep_ref, bf16[2,1024,64]{2,1,0:T(8,128)(2,1)} %reshape.68.q_ref, bf16[128,128,128]{2,1,0:T(8,128)(2,1)} %constant_dynamic-update-slice_fusion.17.kvt_ref, ...), custom_call_target="tpu_custom_call" | custom-call | tf_op jit(solution)/shard_map/pallas_call | solution.py:118
  91.3 2.6 %slice.177 = bf16[64,128,128]{2,1,0:T(8,128)(2,1)S(1)} slice(f32[128,128,128]{2,1,0:T(8,128)} %get-tuple-element.13), slice={[64:128], [0:128], [0:128]} | slice | bytes 4194304 | tf_op jit(solution)/shard_map/slice | solution.py:177
  93.9 27.7 %collective-permute-start.12 = (bf16[4,4,4,128,128]{4,3,2,1,0:T(8,128)(2,1)S(1)}, bf16[4,4,4,128,128]{4,3,2,1,0:T(8,128)(2,1)S(1)}, u32[]{:S(2)}, u32[]{:S(2)}) collective-permute-start(bf16[4,4,4,128,128]{4,3,2,1,0:T(8,128)(2,1)S(1)} %bitcast.83), channel_id=1, source_target_pairs={{0,2},{1,3},{2,0},{3,1},{4,6},{5,7},{6,4},{7,5},{8,10},{9,11},{10,... | collective-permute-start | bytes 6291464 | tf_op jit(solution)/shard_map/ppermute | solution.py:178
  121.6 2.5 %slice.97 = f32[64,128,128]{2,1,0:T(8,128)S(1)} slice(f32[128,128,128]{2,1,0:T(8,128)} %get-tuple-element.13), slice={[0:64], [0:128], [0:128]} | slice | bytes 8388608 | tf_op jit(solution)/shard_map/slice | solution.py:175
  125.4 3.0 %fusion.26 = (bf16[4,4,4,128,128]{4,3,2,1,0:T(8,128)(2,1)S(1)}, f32[4,4,4,128,128]{4,3,2,1,0:T(8,128)}) fusion(f32[4,4,4,128,128]{4,3,2,1,0:T(8,128)S(1)} %bitcast.82, bf16[4,4,4,128,128]{4,3,2,1,0:T(8,128)(2,1)S(1)} %collective-permute-done.12), kind=kLoop, calls=%fused_computation.97 | loop fusion | flops 3145728 | bytes 12582912 | tf_op jit(solution)/shard_map/convert.9
  128.5 21.5 %collective-permute-start.13 = (bf16[4,4,128,128]{3,2,1,0:T(8,128)(2,1)S(1)}, bf16[4,4,128,128]{3,2,1,0:T(8,128)(2,1)S(1)}, u32[]{:S(2)}, u32[]{:S(2)}) collective-permute-start(bf16[4,4,128,128]{3,2,1,0:T(8,128)(2,1)S(1)} %get-tuple-element.20), channel_id=1, source_target_pairs={{0,32},{1,33},{2,34},{3,35},{4,36},{5,37},{6,38},{7,39},{8,40},{9,... | collective-permute-start | bytes 1572872 | tf_op jit(solution)/shard_map/ppermute | solution.py:178
  149.9 5.1 %collective-permute-start.14 = (bf16[4,4,128,128]{3,2,1,0:T(8,128)(2,1)S(1)}, bf16[4,4,128,128]{3,2,1,0:T(8,128)(2,1)S(1)}, u32[]{:S(2)}, u32[]{:S(2)}) collective-permute-start(bf16[4,4,128,128]{3,2,1,0:T(8,128)(2,1)S(1)} %get-tuple-element.22), channel_id=1, source_target_pairs={{0,64},{1,65},{2,66},{3,67},{4,68},{5,69},{6,70},{7,71},{8,72},{9,... | collective-permute-start | bytes 1572872 | tf_op jit(solution)/shard_map/ppermute | solution.py:178
  155.1 2.5 %collective-permute-start.15 = (bf16[4,4,128,128]{3,2,1,0:T(8,128)(2,1)S(1)}, bf16[4,4,128,128]{3,2,1,0:T(8,128)(2,1)}, u32[]{:S(2)}, u32[]{:S(2)}) collective-permute-start(bf16[4,4,128,128]{3,2,1,0:T(8,128)(2,1)S(1)} %get-tuple-element.21), channel_id=1, source_target_pairs={{0,96},{1,97},{2,98},{3,99},{4,100},{5,101},{6,102},{7,103},{8,104... | collective-permute-start | bytes 1572872 | tf_op jit(solution)/shard_map/ppermute | solution.py:178
  159.1 3.2 %collective-permute-done.13 = bf16[4,4,128,128]{3,2,1,0:T(8,128)(2,1)S(1)} collective-permute-done((bf16[4,4,128,128]{3,2,1,0:T(8,128)(2,1)S(1)}, bf16[4,4,128,128]{3,2,1,0:T(8,128)(2,1)S(1)}, u32[]{:S(2)}, u32[]{:S(2)}) %collective-permute-start.13) | collective-permute-done | bytes 524320 | tf_op jit(solution)/shard_map/ppermute | solution.py:178
  162.3 16.4 %collective-permute-done.14 = bf16[4,4,128,128]{3,2,1,0:T(8,128)(2,1)S(1)} collective-permute-done((bf16[4,4,128,128]{3,2,1,0:T(8,128)(2,1)S(1)}, bf16[4,4,128,128]{3,2,1,0:T(8,128)(2,1)S(1)}, u32[]{:S(2)}, u32[]{:S(2)}) %collective-permute-start.14) | collective-permute-done | bytes 524320 | tf_op jit(solution)/shard_map/ppermute | solution.py:178
  178.7 1.7 fusion.24
  180.4 14.3 %collective-permute-start.16 = (bf16[4,128,128]{2,1,0:T(8,128)(2,1)S(1)}, bf16[4,128,128]{2,1,0:T(8,128)(2,1)S(1)}, u32[]{:S(2)}, u32[]{:S(2)}) collective-permute-start(bf16[4,128,128]{2,1,0:T(8,128)(2,1)S(1)} %get-tuple-element.23), channel_id=1, source_target_pairs={{0,16},{1,17},{2,18},{3,19},{4,20},{5,21},{6,22},{7,23},{8,24},{9,... | collective-permute-start | bytes 393224 | tf_op jit(solution)/shard_map/ppermute | solution.py:178
  194.7 3.0 %collective-permute-start.17 = (bf16[4,128,128]{2,1,0:T(8,128)(2,1)S(1)}, bf16[4,128,128]{2,1,0:T(8,128)(2,1)S(1)}, u32[]{:S(2)}, u32[]{:S(2)}) collective-permute-start(bf16[4,128,128]{2,1,0:T(8,128)(2,1)S(1)} %get-tuple-element.25), channel_id=1, source_target_pairs={{0,1},{1,0},{2,3},{3,2},{4,5},{5,4},{6,7},{7,6},{8,9},{9,8},{10,11... | collective-permute-start | bytes 393224 | tf_op jit(solution)/shard_map/ppermute | solution.py:178
  199.9 2.0 maximum_select_fusion.1
  201.9 2.9 %collective-permute-done.17 = bf16[4,128,128]{2,1,0:T(8,128)(2,1)S(1)} collective-permute-done((bf16[4,128,128]{2,1,0:T(8,128)(2,1)S(1)}, bf16[4,128,128]{2,1,0:T(8,128)(2,1)S(1)}, u32[]{:S(2)}, u32[]{:S(2)}) %collective-permute-start.17) | collective-permute-done | bytes 131104 | tf_op jit(solution)/shard_map/ppermute | solution.py:178
  205.0 7.3 %collective-permute-start.20 = (bf16[128,128]{1,0:T(8,128)(2,1)S(1)}, bf16[128,128]{1,0:T(8,128)(2,1)S(1)}, u32[]{:S(2)}, u32[]{:S(2)}) collective-permute-start(bf16[128,128]{1,0:T(8,128)(2,1)S(1)} %get-tuple-element.34), channel_id=1, source_target_pairs={{0,8},{1,9},{2,10},{3,11},{4,12},{5,13},{6,14},{7,15},{8,0},{9,1},... | collective-permute-start | bytes 98312 | tf_op jit(solution)/shard_map/ppermute | solution.py:178
  212.3 2.5 %collective-permute-start.21 = (bf16[128,128]{1,0:T(8,128)(2,1)S(1)}, bf16[128,128]{1,0:T(8,128)(2,1)S(1)}, u32[]{:S(2)}, u32[]{:S(2)}) collective-permute-start(bf16[128,128]{1,0:T(8,128)(2,1)S(1)} %get-tuple-element.33), channel_id=1, source_target_pairs={{0,12},{1,13},{2,14},{3,15},{4,0},{5,1},{6,2},{7,3},{8,4},{9,5},{1... | collective-permute-start | bytes 98312 | tf_op jit(solution)/shard_map/ppermute | solution.py:178
  (81 shorter events, 34.8 us)
Async XLA Ops:
  0.6 49.6 %copy-start.1 = (s32[128,4]{1,0:T(8,128)S(1)}, s32[128,4]{1,0:T(8,128)}, u32[]{:S(2)}) copy-start(s32[128,4]{1,0:T(8,128)} %constant.64.clone) | copy-start | bytes 6148
  0.6 49.5 %copy-start.4 = (s32[2,48]{1,0:T(2,128)S(1)}, s32[2,48]{1,0:T(2,128)}, u32[]{:S(2)}) copy-start(s32[2,48]{1,0:T(2,128)} %param.10) | copy-start | bytes 1156
  1.4 6.1 %collective-permute-start = (bf16[1,128,128]{2,1,0:T(8,128)(2,1)S(1)}, bf16[1,128,128]{2,1,0:T(8,128)(2,1)S(1)}, u32[]{:S(2)}, u32[]{:S(2)}) collective-permute-start(bf16[1,128,128]{2,1,0:T(8,128)(2,1)S(1)} %maximum_bitcast_fusion), channel_id=1, source_target_pairs={{0,12},{1,13},{2,14},{3,15},{4,0},{5,1},{6,2},{7,3},{8,4},{9,5},{1... | collective-permute-start | bytes 98312 | tf_op jit(solution)/shard_map/ppermute | solution.py:168
  4.6 5.4 %collective-permute-start.1 = (bf16[1,128,128]{2,1,0:T(8,128)(2,1)S(1)}, bf16[1,128,128]{2,1,0:T(8,128)(2,1)S(1)}, u32[]{:S(2)}, u32[]{:S(2)}) collective-permute-start(bf16[1,128,128]{2,1,0:T(8,128)(2,1)S(1)} %maximum_bitcast_fusion), channel_id=1, source_target_pairs={{0,8},{1,9},{2,10},{3,11},{4,12},{5,13},{6,14},{7,15},{8,0},{9,1},... | collective-permute-start | bytes 98312 | tf_op jit(solution)/shard_map/ppermute | solution.py:168
  5.2 5.1 %collective-permute-start.2 = (bf16[1,128,128]{2,1,0:T(8,128)(2,1)S(1)}, bf16[1,128,128]{2,1,0:T(8,128)(2,1)S(1)}, u32[]{:S(2)}, u32[]{:S(2)}) collective-permute-start(bf16[1,128,128]{2,1,0:T(8,128)(2,1)S(1)} %maximum_bitcast_fusion), channel_id=1, source_target_pairs={{0,4},{1,5},{2,6},{3,7},{4,8},{5,9},{6,10},{7,11},{8,12},{9,13},{1... | collective-permute-start | bytes 98312 | tf_op jit(solution)/shard_map/ppermute | solution.py:168
  10.3 7.1 %collective-permute-start.3 = (bf16[4,128,128]{2,1,0:T(8,128)(2,1)S(1)}, bf16[4,128,128]{2,1,0:T(8,128)(2,1)S(1)}, u32[]{:S(2)}, u32[]{:S(2)}) collective-permute-start(bf16[4,128,128]{2,1,0:T(8,128)(2,1)S(1)} %pad_maximum_fusion), channel_id=1, source_target_pairs={{0,17},{1,16},{2,19},{3,18},{4,21},{5,20},{6,23},{7,22},{8,25},{9,... | collective-permute-start | bytes 393224 | tf_op jit(solution)/shard_map/ppermute | solution.py:168
  13.2 6.6 %collective-permute-start.4 = (bf16[4,128,128]{2,1,0:T(8,128)(2,1)S(1)}, bf16[4,128,128]{2,1,0:T(8,128)(2,1)S(1)}, u32[]{:S(2)}, u32[]{:S(2)}) collective-permute-start(bf16[4,128,128]{2,1,0:T(8,128)(2,1)S(1)} %pad_maximum_fusion), channel_id=1, source_target_pairs={{0,1},{1,0},{2,3},{3,2},{4,5},{5,4},{6,7},{7,6},{8,9},{9,8},{10,11... | collective-permute-start | bytes 393224 | tf_op jit(solution)/shard_map/ppermute | solution.py:168
  14.0 7.1 %collective-permute-start.5 = (bf16[4,128,128]{2,1,0:T(8,128)(2,1)S(1)}, bf16[4,128,128]{2,1,0:T(8,128)(2,1)S(1)}, u32[]{:S(2)}, u32[]{:S(2)}) collective-permute-start(bf16[4,128,128]{2,1,0:T(8,128)(2,1)S(1)} %pad_maximum_fusion), channel_id=1, source_target_pairs={{0,16},{1,17},{2,18},{3,19},{4,20},{5,21},{6,22},{7,23},{8,24},{9,... | collective-permute-start | bytes 393224 | tf_op jit(solution)/shard_map/ppermute | solution.py:168
  21.8 23.6 %collective-permute-start.6 = (bf16[16,128,128]{2,1,0:T(8,128)(2,1)S(1)}, bf16[16,128,128]{2,1,0:T(8,128)(2,1)S(1)}, u32[]{:S(2)}, u32[]{:S(2)}) collective-permute-start(bf16[16,128,128]{2,1,0:T(8,128)(2,1)S(1)} %get-tuple-element.37), channel_id=1, source_target_pairs={{0,96},{1,97},{2,98},{3,99},{4,100},{5,101},{6,102},{7,103},{8,104... | collective-permute-start | bytes 1572872 | tf_op jit(solution)/shard_map/ppermute | solution.py:168
  25.9 20.8 %collective-permute-start.7 = (bf16[16,128,128]{2,1,0:T(8,128)(2,1)S(1)}, bf16[16,128,128]{2,1,0:T(8,128)(2,1)S(1)}, u32[]{:S(2)}, u32[]{:S(2)}) collective-permute-start(bf16[16,128,128]{2,1,0:T(8,128)(2,1)S(1)} %get-tuple-element.37), channel_id=1, source_target_pairs={{0,64},{1,65},{2,66},{3,67},{4,68},{5,69},{6,70},{7,71},{8,72},{9,... | collective-permute-start | bytes 1572872 | tf_op jit(solution)/shard_map/ppermute | solution.py:168
  25.9 23.0 %collective-permute-start.8 = (bf16[16,128,128]{2,1,0:T(8,128)(2,1)S(1)}, bf16[16,128,128]{2,1,0:T(8,128)(2,1)S(1)}, u32[]{:S(2)}, u32[]{:S(2)}) collective-permute-start(bf16[16,128,128]{2,1,0:T(8,128)(2,1)S(1)} %get-tuple-element.37), channel_id=1, source_target_pairs={{0,32},{1,33},{2,34},{3,35},{4,36},{5,37},{6,38},{7,39},{8,40},{9,... | collective-permute-start | bytes 1572872 | tf_op jit(solution)/shard_map/ppermute | solution.py:168
  50.1 9.1 %collective-permute-start.9 = (bf16[64,128,128]{2,1,0:T(8,128)(2,1)}, bf16[64,128,128]{2,1,0:T(8,128)(2,1)S(1)}, u32[]{:S(2)}, u32[]{:S(2)}) collective-permute-start(bf16[64,128,128]{2,1,0:T(8,128)(2,1)} %get-tuple-element.26), channel_id=1, source_target_pairs={{0,2},{1,3},{2,0},{3,1},{4,6},{5,7},{6,4},{7,5},{8,10},{9,11},{10,... | collective-permute-start | bytes 6291464 | tf_op jit(solution)/shard_map/ppermute | solution.py:168
  93.9 31.5 %collective-permute-start.12 = (bf16[4,4,4,128,128]{4,3,2,1,0:T(8,128)(2,1)S(1)}, bf16[4,4,4,128,128]{4,3,2,1,0:T(8,128)(2,1)S(1)}, u32[]{:S(2)}, u32[]{:S(2)}) collective-permute-start(bf16[4,4,4,128,128]{4,3,2,1,0:T(8,128)(2,1)S(1)} %bitcast.83), channel_id=1, source_target_pairs={{0,2},{1,3},{2,0},{3,1},{4,6},{5,7},{6,4},{7,5},{8,10},{9,11},{10,... | collective-permute-start | bytes 6291464 | tf_op jit(solution)/shard_map/ppermute | solution.py:178
  128.5 33.8 %collective-permute-start.13 = (bf16[4,4,128,128]{3,2,1,0:T(8,128)(2,1)S(1)}, bf16[4,4,128,128]{3,2,1,0:T(8,128)(2,1)S(1)}, u32[]{:S(2)}, u32[]{:S(2)}) collective-permute-start(bf16[4,4,128,128]{3,2,1,0:T(8,128)(2,1)S(1)} %get-tuple-element.20), channel_id=1, source_target_pairs={{0,32},{1,33},{2,34},{3,35},{4,36},{5,37},{6,38},{7,39},{8,40},{9,... | collective-permute-start | bytes 1572872 | tf_op jit(solution)/shard_map/ppermute | solution.py:178
  149.9 28.7 %collective-permute-start.14 = (bf16[4,4,128,128]{3,2,1,0:T(8,128)(2,1)S(1)}, bf16[4,4,128,128]{3,2,1,0:T(8,128)(2,1)S(1)}, u32[]{:S(2)}, u32[]{:S(2)}) collective-permute-start(bf16[4,4,128,128]{3,2,1,0:T(8,128)(2,1)S(1)} %get-tuple-element.22), channel_id=1, source_target_pairs={{0,64},{1,65},{2,66},{3,67},{4,68},{5,69},{6,70},{7,71},{8,72},{9,... | collective-permute-start | bytes 1572872 | tf_op jit(solution)/shard_map/ppermute | solution.py:178
  155.1 23.6 %collective-permute-start.15 = (bf16[4,4,128,128]{3,2,1,0:T(8,128)(2,1)S(1)}, bf16[4,4,128,128]{3,2,1,0:T(8,128)(2,1)}, u32[]{:S(2)}, u32[]{:S(2)}) collective-permute-start(bf16[4,4,128,128]{3,2,1,0:T(8,128)(2,1)S(1)} %get-tuple-element.21), channel_id=1, source_target_pairs={{0,96},{1,97},{2,98},{3,99},{4,100},{5,101},{6,102},{7,103},{8,104... | collective-permute-start | bytes 1572872 | tf_op jit(solution)/shard_map/ppermute | solution.py:178
  158.2 41.7 %collective-permute-start.11 = (bf16[256,512]{1,0:T(8,128)(2,1)S(1)}, bf16[256,512]{1,0:T(8,128)(2,1)}, u32[]{:S(2)}, u32[]{:S(2)}) collective-permute-start(bf16[256,512]{1,0:T(8,128)(2,1)S(1)} %reshape.71), channel_id=1, source_target_pairs={{0,1},{1,0},{2,3},{3,2},{4,5},{5,4},{6,7},{7,6},{8,9},{9,8},{10,11... | collective-permute-start | bytes 786440 | tf_op jit(solution)/shard_map/ppermute | solution.py:217
  180.4 21.5 %collective-permute-start.16 = (bf16[4,128,128]{2,1,0:T(8,128)(2,1)S(1)}, bf16[4,128,128]{2,1,0:T(8,128)(2,1)S(1)}, u32[]{:S(2)}, u32[]{:S(2)}) collective-permute-start(bf16[4,128,128]{2,1,0:T(8,128)(2,1)S(1)} %get-tuple-element.23), channel_id=1, source_target_pairs={{0,16},{1,17},{2,18},{3,19},{4,20},{5,21},{6,22},{7,23},{8,24},{9,... | collective-permute-start | bytes 393224 | tf_op jit(solution)/shard_map/ppermute | solution.py:178
  194.7 10.2 %collective-permute-start.17 = (bf16[4,128,128]{2,1,0:T(8,128)(2,1)S(1)}, bf16[4,128,128]{2,1,0:T(8,128)(2,1)S(1)}, u32[]{:S(2)}, u32[]{:S(2)}) collective-permute-start(bf16[4,128,128]{2,1,0:T(8,128)(2,1)S(1)} %get-tuple-element.25), channel_id=1, source_target_pairs={{0,1},{1,0},{2,3},{3,2},{4,5},{5,4},{6,7},{7,6},{8,9},{9,8},{10,11... | collective-permute-start | bytes 393224 | tf_op jit(solution)/shard_map/ppermute | solution.py:178
  197.7 7.2 %collective-permute-start.18 = (bf16[4,128,128]{2,1,0:T(8,128)(2,1)S(1)}, bf16[4,128,128]{2,1,0:T(8,128)(2,1)S(1)}, u32[]{:S(2)}, u32[]{:S(2)}) collective-permute-start(bf16[4,128,128]{2,1,0:T(8,128)(2,1)S(1)} %get-tuple-element.24), channel_id=1, source_target_pairs={{0,17},{1,16},{2,19},{3,18},{4,21},{5,20},{6,23},{7,22},{8,25},{9,... | collective-permute-start | bytes 393224 | tf_op jit(solution)/shard_map/ppermute | solution.py:178
  198.3 16.5 %collective-permute-start.10 = (bf16[256,512]{1,0:T(8,128)(2,1)S(1)}, bf16[256,512]{1,0:T(8,128)(2,1)S(1)}, u32[]{:S(2)}, u32[]{:S(2)}) collective-permute-start(bf16[256,512]{1,0:T(8,128)(2,1)S(1)} %reshape.70), channel_id=1, source_target_pairs={{0,1},{1,0},{2,3},{3,2},{4,5},{5,4},{6,7},{7,6},{8,9},{9,8},{10,11... | collective-permute-start | bytes 786440 | tf_op jit(solution)/shard_map/ppermute | solution.py:217
  204.9 10.9 %collective-permute-start.19 = (bf16[128,128]{1,0:T(8,128)(2,1)S(1)}, bf16[128,128]{1,0:T(8,128)(2,1)S(1)}, u32[]{:S(2)}, u32[]{:S(2)}) collective-permute-start(bf16[128,128]{1,0:T(8,128)(2,1)S(1)} %get-tuple-element.32), channel_id=1, source_target_pairs={{0,4},{1,5},{2,6},{3,7},{4,8},{5,9},{6,10},{7,11},{8,12},{9,13},{1... | collective-permute-start | bytes 98312 | tf_op jit(solution)/shard_map/ppermute | solution.py:178
  205.0 10.8 %collective-permute-start.20 = (bf16[128,128]{1,0:T(8,128)(2,1)S(1)}, bf16[128,128]{1,0:T(8,128)(2,1)S(1)}, u32[]{:S(2)}, u32[]{:S(2)}) collective-permute-start(bf16[128,128]{1,0:T(8,128)(2,1)S(1)} %get-tuple-element.34), channel_id=1, source_target_pairs={{0,8},{1,9},{2,10},{3,11},{4,12},{5,13},{6,14},{7,15},{8,0},{9,1},... | collective-permute-start | bytes 98312 | tf_op jit(solution)/shard_map/ppermute | solution.py:178
  212.3 4.1 %collective-permute-start.21 = (bf16[128,128]{1,0:T(8,128)(2,1)S(1)}, bf16[128,128]{1,0:T(8,128)(2,1)S(1)}, u32[]{:S(2)}, u32[]{:S(2)}) collective-permute-start(bf16[128,128]{1,0:T(8,128)(2,1)S(1)} %get-tuple-element.33), channel_id=1, source_target_pairs={{0,12},{1,13},{2,14},{3,15},{4,0},{5,1},{6,2},{7,3},{8,4},{9,5},{1... | collective-permute-start | bytes 98312 | tf_op jit(solution)/shard_map/ppermute | solution.py:178
  (3 other events, 84.5 us)

commit v6 on v5

--- a/solution.py
+++ b/solution.py
@@ -38,7 +38,7 @@
     return jnp.transpose(tile).astype(jnp.bfloat16)
 
 
-def _forward_kernel(lists_ref, keep_ref, q_ref, kvt_ref, dot_ref,
+def _forward_kernel(lists_ref, keep_ref, qt_ref, kvt_ref, dot_ref,
                     ot_ref, lse_ref, delta_ref, m_sc, l_sc, acc_sc):
     query_count, slots = lists_ref.shape
     for qb in range(query_count):
@@ -50,7 +50,7 @@
             @pl.when(keep_ref[qb, j] != 0)
             def _():
                 b = lists_ref[qb, j]
-                st = _nt(_rows_of(kvt_ref, b, 0), q_ref[qb]) * SCALE
+                st = _nn(_rows_of(kvt_ref, b, 0), qt_ref[qb]) * SCALE
                 m_prev = m_sc[...]
                 m_new = jnp.maximum(m_prev, jnp.max(st, axis=0, keepdims=True))
                 alpha = jnp.exp(m_prev - m_new)
@@ -68,7 +68,7 @@
         delta_ref[qb] = jnp.sum(dot_ref[qb].astype(jnp.float32) * out, axis=0, keepdims=True)
 
 
-def _backward_kernel(lists_ref, keep_ref, q_ref, kvt_ref, do_ref, lse_ref, delta_ref,
+def _backward_kernel(lists_ref, keep_ref, q_ref, qt_ref, kvt_ref, do_ref, dot_ref, lse_ref, delta_ref,
                      dqt_ref, dkvt_ref, dq_sc):
     query_count, slots = lists_ref.shape
     dkvt_ref[...] = jnp.zeros(dkvt_ref.shape, jnp.float32)
@@ -81,10 +81,10 @@
                 b = lists_ref[qb, j]
                 q = q_ref[qb]
                 do = do_ref[qb]
-                st = _nt(_rows_of(kvt_ref, b, 0), q) * SCALE
+                st = _nn(_rows_of(kvt_ref, b, 0), qt_ref[qb]) * SCALE
                 pt = jnp.exp(st - lse_ref[qb])
                 dkvt_ref[b, HEAD_DIM:, :] += jnp.transpose(_nn(pt.astype(jnp.bfloat16), do))
-                dpt = _nt(_rows_of(kvt_ref, b, HEAD_DIM), do)
+                dpt = _nn(_rows_of(kvt_ref, b, HEAD_DIM), dot_ref[qb])
                 dst = (pt * (dpt - delta_ref[qb])).astype(jnp.bfloat16)
                 dq_sc[...] += _nn(kvt_ref[b, :HEAD_DIM, :], dst)
                 dkvt_ref[b, :HEAD_DIM, :] += jnp.transpose(_nn(dst, q))
@@ -99,6 +99,7 @@
     block_total = kv_t.shape[0]
     f32 = jnp.float32
     do_t = jnp.swapaxes(do_rows, 1, 2)
+    q_t = jnp.swapaxes(q_rows, 1, 2)
     o_t, lse, delta = pl.pallas_call(
         _forward_kernel,
         out_shape=(
@@ -114,18 +115,18 @@
             pltpu.VMEM((HEAD_DIM, rows), f32),
         ],
         compiler_params=pltpu.CompilerParams(vmem_limit_bytes=VMEM_LIMIT),
-    )(lists, keep, q_rows, kv_t, do_t)
+    )(lists, keep, q_t, kv_t, do_t)
     dq_t, dkv_t = pl.pallas_call(
         _backward_kernel,
         out_shape=(
             jax.ShapeDtypeStruct((query_count, HEAD_DIM, rows), jnp.bfloat16),
             jax.ShapeDtypeStruct((block_total, 2 * HEAD_DIM, BLOCK), f32),
         ),
-        in_specs=[_smem(), _smem()] + [_vmem()] * 5,
+        in_specs=[_smem(), _smem()] + [_vmem()] * 7,
         out_specs=(_vmem(), _vmem()),
         scratch_shapes=[pltpu.VMEM((HEAD_DIM, rows), f32)],
         compiler_params=pltpu.CompilerParams(vmem_limit_bytes=VMEM_LIMIT),
-    )(lists, keep, q_rows, kv_t, do_rows, lse, delta)
+    )(lists, keep, q_rows, q_t, kv_t, do_rows, do_t, lse, delta)
     return jnp.swapaxes(o_t, 1, 2), jnp.swapaxes(dq_t, 1, 2), dkv_t
 
 

time: 217 us -> 222 us (1.023); the launches traced: 218 us -> 220 us
  starting transfers between devices: 101 us -> 60.4 us
  Pallas kernels: 30.6 us -> 70.7 us
  waiting for transfers between devices: 49.2 us -> 51.7 us
    ppermute x10, starting transfers between devices: 84 us -> 43.4 us  [scatter_sum(): lax.ppermute(sent, axes, pairs(axis, shift)).astype(jnp.float32)]
    pallas_call x1, Pallas kernels: 18.6 us -> 42.6 us  [attend_local(): pl.pallas_call(_backward_kernel, out_shape=(jax.ShapeDtypeStruct((query_c...]
    pallas_call x1, Pallas kernels: 12 us -> 28.1 us  [attend_local(): pl.pallas_call(_forward_kernel, out_shape=(jax.ShapeDtypeStruct((query_co...]
    ppermute x10, waiting for transfers between devices: 24.5 us -> 27 us  [scatter_sum(): lax.ppermute(sent, axes, pairs(axis, shift)).astype(jnp.float32)]
    unnamed x22 -> x24, local copies, waits for them, and re-layouts: 7.08 us -> 7.13 us
  transfers between devices with their start and end apart: 22 -> 22, of which waited for: 12 -> 14; matrix products, arithmetic and copies ran while one was open for 11% -> 11% of each run, Pallas kernels for 0% -> 0%
where the time goes in v6:
time: 222 us; the launch traced here: 220 us
  Pallas kernels  70.7 us (32%)
  starting transfers between devices  60.4 us (27%)
  waiting for transfers between devices  51.7 us (23%)
  local copies, waits for them, and re-layouts  21.7 us (10%)
  other arithmetic  14.5 us (7%)
    ppermute x10, starting transfers between devices, scatter_sum(): lax.ppermute(sent, axes, pairs(axis, shift)).astype(jnp.float32)  43.4 us
    pallas_call x1, Pallas kernels, attend_local(): pl.pallas_call(_backward_kernel, out_shape=(jax.ShapeDtypeStruct((query_c...  42.6 us
    pallas_call x1, Pallas kernels, attend_local(): pl.pallas_call(_forward_kernel, out_shape=(jax.ShapeDtypeStruct((query_co...  28.1 us
    ppermute x10, waiting for transfers between devices, scatter_sum(): lax.ppermute(sent, axes, pairs(axis, shift)).astype(jnp.float32)  27 us
    ppermute x10, waiting for transfers between devices, gather_blocks(): pieces.append(lax.ppermute(buf, axes, pairs(axis, size - shift)))  24.7 us
    ppermute x10, starting transfers between devices, gather_blocks(): pieces.append(lax.ppermute(buf, axes, pairs(axis, size - shift)))  14.5 us
    unnamed x24, local copies, waits for them, and re-layouts  7.13 us
    another operation x3, other arithmetic  4.69 us
  transfers between devices with their start and end apart: 22, of which 14 were waited for; matrix products, arithmetic and copies ran while one was open for 11% of the time, Pallas kernels for 0%

profile of v6, /device:TPU:0, one launch (start us, length us, event | category | flops | bytes accessed | tf_op | source)
XLA Modules:
  0.0 219.8 jit_solution(9060313525707458649)
XLA Ops:
  1.4 3.1 %collective-permute-start = (bf16[1,128,128]{2,1,0:T(8,128)(2,1)S(1)}, bf16[1,128,128]{2,1,0:T(8,128)(2,1)S(1)}, u32[]{:S(2)}, u32[]{:S(2)}) collective-permute-start(bf16[1,128,128]{2,1,0:T(8,128)(2,1)S(1)} %maximum_bitcast_fusion), channel_id=1, source_target_pairs={{0,12},{1,13},{2,14},{3,15},{4,0},{5,1},{6,2},{7,3},{8,4},{9,5},{1... | collective-permute-start | bytes 98312 | tf_op jit(solution)/shard_map/ppermute | solution.py:169
  7.5 2.4 %collective-permute-done.1 = bf16[1,128,128]{2,1,0:T(8,128)(2,1)S(1)} collective-permute-done((bf16[1,128,128]{2,1,0:T(8,128)(2,1)S(1)}, bf16[1,128,128]{2,1,0:T(8,128)(2,1)S(1)}, u32[]{:S(2)}, u32[]{:S(2)}) %collective-permute-start.1) | collective-permute-done | bytes 32800 | tf_op jit(solution)/shard_map/ppermute | solution.py:169
  10.3 2.8 %collective-permute-start.3 = (bf16[4,128,128]{2,1,0:T(8,128)(2,1)S(1)}, bf16[4,128,128]{2,1,0:T(8,128)(2,1)S(1)}, u32[]{:S(2)}, u32[]{:S(2)}) collective-permute-start(bf16[4,128,128]{2,1,0:T(8,128)(2,1)S(1)} %pad_maximum_fusion), channel_id=1, source_target_pairs={{0,17},{1,16},{2,19},{3,18},{4,21},{5,20},{6,23},{7,22},{8,25},{9,... | collective-permute-start | bytes 393224 | tf_op jit(solution)/shard_map/ppermute | solution.py:169
  21.8 4.0 %collective-permute-start.6 = (bf16[16,128,128]{2,1,0:T(8,128)(2,1)S(1)}, bf16[16,128,128]{2,1,0:T(8,128)(2,1)S(1)}, u32[]{:S(2)}, u32[]{:S(2)}) collective-permute-start(bf16[16,128,128]{2,1,0:T(8,128)(2,1)S(1)} %get-tuple-element.37), channel_id=1, source_target_pairs={{0,96},{1,97},{2,98},{3,99},{4,100},{5,101},{6,102},{7,103},{8,104... | collective-permute-start | bytes 1572872 | tf_op jit(solution)/shard_map/ppermute | solution.py:169
  27.1 18.3 %collective-permute-done.6 = bf16[16,128,128]{2,1,0:T(8,128)(2,1)S(1)} collective-permute-done((bf16[16,128,128]{2,1,0:T(8,128)(2,1)S(1)}, bf16[16,128,128]{2,1,0:T(8,128)(2,1)S(1)}, u32[]{:S(2)}, u32[]{:S(2)}) %collective-permute-start.6) | collective-permute-done | bytes 524320 | tf_op jit(solution)/shard_map/ppermute | solution.py:169
  51.4 2.7 %slice_subtract_fusion.3 = (s32[2,48,1]{2,1,0:T(8,128)S(1)}, s32[2,48,1]{2,1,0:T(8,128)S(1)}, s32[2,48,1]{2,1,0:T(8,128)S(1)}, s32[2,48,1]{2,1,0:T(8,128)S(1)}) fusion(s32[2,48,4]{2,1,0:T(8,128)S(1)} %bitcast.89, s32[]{:T(128)} %bitcast.1, s32[]{:T(128)} %bitcast.5, s32[]{:T(128)} %bitcast.3, s32[]{:T(128)} %bitcast.7), kind=kLoop, calls=%fused_computation.55 | loop fusion | flops 384 | bytes 3088 | tf_op jit(solution)/shard_map/sub | solution.py:203
  60.9 28.1 %shard_map.93 = (bf16[2,64,1024]{2,1,0:T(8,128)(2,1)}, f32[2,1,1024]{2,1,0:T(1,128)}, f32[2,1,1024]{2,1,0:T(1,128)}) custom-call(s32[2,48]{1,0:T(2,128)} %fusion.17.lists_ref, s32[2,48]{1,0:T(2,128)} %not_convert_fusion.keep_ref, bf16[2,64,1024]{2,1,0:T(8,128)(2,1)} %bitcast.86, bf16[128,128,128]{2,1,0:T(8,128)(2,1)} %constant_dynamic-update-slice_fusion.17.kvt_ref, ...), custom_call_target="tpu_custom_call" | custom-call | tf_op jit(solution)/shard_map/pallas_call | solution.py:103
  89.0 42.6 %shard_map.94 = (bf16[2,64,1024]{2,1,0:T(8,128)(2,1)}, f32[128,128,128]{2,1,0:T(8,128)}) custom-call(s32[2,48]{1,0:T(2,128)} %fusion.17.lists_ref, s32[2,48]{1,0:T(2,128)} %not_convert_fusion.keep_ref, bf16[2,1024,64]{2,1,0:T(8,128)(2,1)} %copy-done.1, bf16[2,64,1024]{2,1,0:T(8,128)(2,1)} %bitcast.87, ...), custom_call_target="tpu_custom_call" | custom-call | tf_op jit(solution)/shard_map/pallas_call | solution.py:119
  131.6 2.6 %slice.177 = bf16[64,128,128]{2,1,0:T(8,128)(2,1)S(1)} slice(f32[128,128,128]{2,1,0:T(8,128)} %get-tuple-element.13), slice={[64:128], [0:128], [0:128]} | slice | bytes 4194304 | tf_op jit(solution)/shard_map/slice | solution.py:178
  134.2 2.5 %slice.97 = f32[64,128,128]{2,1,0:T(8,128)S(1)} slice(f32[128,128,128]{2,1,0:T(8,128)} %get-tuple-element.13), slice={[0:64], [0:128], [0:128]} | slice | bytes 8388608 | tf_op jit(solution)/shard_map/slice | solution.py:176
  136.7 1.7 collective-permute-done.12
  138.4 3.0 %fusion.26 = (bf16[4,4,4,128,128]{4,3,2,1,0:T(8,128)(2,1)S(1)}, f32[4,4,4,128,128]{4,3,2,1,0:T(8,128)}) fusion(f32[4,4,4,128,128]{4,3,2,1,0:T(8,128)S(1)} %bitcast.83, bf16[4,4,4,128,128]{4,3,2,1,0:T(8,128)(2,1)S(1)} %collective-permute-done.12), kind=kLoop, calls=%fused_computation.97 | loop fusion | flops 3145728 | bytes 12582912 | tf_op jit(solution)/shard_map/convert.9
  141.4 24.2 %collective-permute-start.13 = (bf16[4,4,128,128]{3,2,1,0:T(8,128)(2,1)S(1)}, bf16[4,4,128,128]{3,2,1,0:T(8,128)(2,1)S(1)}, u32[]{:S(2)}, u32[]{:S(2)}) collective-permute-start(bf16[4,4,128,128]{3,2,1,0:T(8,128)(2,1)S(1)} %get-tuple-element.20), channel_id=1, source_target_pairs={{0,32},{1,33},{2,34},{3,35},{4,36},{5,37},{6,38},{7,39},{8,40},{9,... | collective-permute-start | bytes 1572872 | tf_op jit(solution)/shard_map/ppermute | solution.py:179
  165.6 2.8 %collective-permute-start.15 = (bf16[4,4,128,128]{3,2,1,0:T(8,128)(2,1)S(1)}, bf16[4,4,128,128]{3,2,1,0:T(8,128)(2,1)}, u32[]{:S(2)}, u32[]{:S(2)}) collective-permute-start(bf16[4,4,128,128]{3,2,1,0:T(8,128)(2,1)S(1)} %get-tuple-element.21), channel_id=1, source_target_pairs={{0,96},{1,97},{2,98},{3,99},{4,100},{5,101},{6,102},{7,103},{8,104... | collective-permute-start | bytes 1572872 | tf_op jit(solution)/shard_map/ppermute | solution.py:179
  169.9 8.1 %collective-permute-done.13 = bf16[4,4,128,128]{3,2,1,0:T(8,128)(2,1)S(1)} collective-permute-done((bf16[4,4,128,128]{3,2,1,0:T(8,128)(2,1)S(1)}, bf16[4,4,128,128]{3,2,1,0:T(8,128)(2,1)S(1)}, u32[]{:S(2)}, u32[]{:S(2)}) %collective-permute-start.13) | collective-permute-done | bytes 524320 | tf_op jit(solution)/shard_map/ppermute | solution.py:179
  177.9 10.4 %collective-permute-done.14 = bf16[4,4,128,128]{3,2,1,0:T(8,128)(2,1)S(1)} collective-permute-done((bf16[4,4,128,128]{3,2,1,0:T(8,128)(2,1)S(1)}, bf16[4,4,128,128]{3,2,1,0:T(8,128)(2,1)S(1)}, u32[]{:S(2)}, u32[]{:S(2)}) %collective-permute-start.14) | collective-permute-done | bytes 524320 | tf_op jit(solution)/shard_map/ppermute | solution.py:179
  189.3 1.7 fusion.24
  191.0 2.5 %collective-permute-start.16 = (bf16[4,128,128]{2,1,0:T(8,128)(2,1)S(1)}, bf16[4,128,128]{2,1,0:T(8,128)(2,1)S(1)}, u32[]{:S(2)}, u32[]{:S(2)}) collective-permute-start(bf16[4,128,128]{2,1,0:T(8,128)(2,1)S(1)} %get-tuple-element.23), channel_id=1, source_target_pairs={{0,16},{1,17},{2,18},{3,19},{4,20},{5,21},{6,22},{7,23},{8,24},{9,... | collective-permute-start | bytes 393224 | tf_op jit(solution)/shard_map/ppermute | solution.py:179
  193.5 3.0 %collective-permute-start.17 = (bf16[4,128,128]{2,1,0:T(8,128)(2,1)S(1)}, bf16[4,128,128]{2,1,0:T(8,128)(2,1)S(1)}, u32[]{:S(2)}, u32[]{:S(2)}) collective-permute-start(bf16[4,128,128]{2,1,0:T(8,128)(2,1)S(1)} %get-tuple-element.25), channel_id=1, source_target_pairs={{0,1},{1,0},{2,3},{3,2},{4,5},{5,4},{6,7},{7,6},{8,9},{9,8},{10,11... | collective-permute-start | bytes 393224 | tf_op jit(solution)/shard_map/ppermute | solution.py:179
  198.8 2.0 maximum_select_fusion.1
  200.8 2.9 %collective-permute-done.17 = bf16[4,128,128]{2,1,0:T(8,128)(2,1)S(1)} collective-permute-done((bf16[4,128,128]{2,1,0:T(8,128)(2,1)S(1)}, bf16[4,128,128]{2,1,0:T(8,128)(2,1)S(1)}, u32[]{:S(2)}, u32[]{:S(2)}) %collective-permute-start.17) | collective-permute-done | bytes 131104 | tf_op jit(solution)/shard_map/ppermute | solution.py:179
  203.7 3.0 %collective-permute-start.19 = (bf16[128,128]{1,0:T(8,128)(2,1)S(1)}, bf16[128,128]{1,0:T(8,128)(2,1)S(1)}, u32[]{:S(2)}, u32[]{:S(2)}) collective-permute-start(bf16[128,128]{1,0:T(8,128)(2,1)S(1)} %get-tuple-element.32), channel_id=1, source_target_pairs={{0,4},{1,5},{2,6},{3,7},{4,8},{5,9},{6,10},{7,11},{8,12},{9,13},{1... | collective-permute-start | bytes 98312 | tf_op jit(solution)/shard_map/ppermute | solution.py:179
  206.8 7.8 %collective-permute-start.20 = (bf16[128,128]{1,0:T(8,128)(2,1)S(1)}, bf16[128,128]{1,0:T(8,128)(2,1)S(1)}, u32[]{:S(2)}, u32[]{:S(2)}) collective-permute-start(bf16[128,128]{1,0:T(8,128)(2,1)S(1)} %get-tuple-element.34), channel_id=1, source_target_pairs={{0,8},{1,9},{2,10},{3,11},{4,12},{5,13},{6,14},{7,15},{8,0},{9,1},... | collective-permute-start | bytes 98312 | tf_op jit(solution)/shard_map/ppermute | solution.py:179
  216.9 1.7 collective-permute-done.21
  (84 shorter events, 35.2 us)
Async XLA Ops:
  0.6 49.6 %copy-start.2 = (s32[128,4]{1,0:T(8,128)S(1)}, s32[128,4]{1,0:T(8,128)}, u32[]{:S(2)}) copy-start(s32[128,4]{1,0:T(8,128)} %constant.64.clone) | copy-start | bytes 6148
  0.6 49.5 %copy-start.5 = (s32[2,48]{1,0:T(2,128)S(1)}, s32[2,48]{1,0:T(2,128)}, u32[]{:S(2)}) copy-start(s32[2,48]{1,0:T(2,128)} %param.10) | copy-start | bytes 1156
  1.4 6.1 %collective-permute-start = (bf16[1,128,128]{2,1,0:T(8,128)(2,1)S(1)}, bf16[1,128,128]{2,1,0:T(8,128)(2,1)S(1)}, u32[]{:S(2)}, u32[]{:S(2)}) collective-permute-start(bf16[1,128,128]{2,1,0:T(8,128)(2,1)S(1)} %maximum_bitcast_fusion), channel_id=1, source_target_pairs={{0,12},{1,13},{2,14},{3,15},{4,0},{5,1},{6,2},{7,3},{8,4},{9,5},{1... | collective-permute-start | bytes 98312 | tf_op jit(solution)/shard_map/ppermute | solution.py:169
  4.6 5.4 %collective-permute-start.1 = (bf16[1,128,128]{2,1,0:T(8,128)(2,1)S(1)}, bf16[1,128,128]{2,1,0:T(8,128)(2,1)S(1)}, u32[]{:S(2)}, u32[]{:S(2)}) collective-permute-start(bf16[1,128,128]{2,1,0:T(8,128)(2,1)S(1)} %maximum_bitcast_fusion), channel_id=1, source_target_pairs={{0,8},{1,9},{2,10},{3,11},{4,12},{5,13},{6,14},{7,15},{8,0},{9,1},... | collective-permute-start | bytes 98312 | tf_op jit(solution)/shard_map/ppermute | solution.py:169
  5.2 5.1 %collective-permute-start.2 = (bf16[1,128,128]{2,1,0:T(8,128)(2,1)S(1)}, bf16[1,128,128]{2,1,0:T(8,128)(2,1)S(1)}, u32[]{:S(2)}, u32[]{:S(2)}) collective-permute-start(bf16[1,128,128]{2,1,0:T(8,128)(2,1)S(1)} %maximum_bitcast_fusion), channel_id=1, source_target_pairs={{0,4},{1,5},{2,6},{3,7},{4,8},{5,9},{6,10},{7,11},{8,12},{9,13},{1... | collective-permute-start | bytes 98312 | tf_op jit(solution)/shard_map/ppermute | solution.py:169
  10.3 7.1 %collective-permute-start.3 = (bf16[4,128,128]{2,1,0:T(8,128)(2,1)S(1)}, bf16[4,128,128]{2,1,0:T(8,128)(2,1)S(1)}, u32[]{:S(2)}, u32[]{:S(2)}) collective-permute-start(bf16[4,128,128]{2,1,0:T(8,128)(2,1)S(1)} %pad_maximum_fusion), channel_id=1, source_target_pairs={{0,17},{1,16},{2,19},{3,18},{4,21},{5,20},{6,23},{7,22},{8,25},{9,... | collective-permute-start | bytes 393224 | tf_op jit(solution)/shard_map/ppermute | solution.py:169
  13.2 6.6 %collective-permute-start.4 = (bf16[4,128,128]{2,1,0:T(8,128)(2,1)S(1)}, bf16[4,128,128]{2,1,0:T(8,128)(2,1)S(1)}, u32[]{:S(2)}, u32[]{:S(2)}) collective-permute-start(bf16[4,128,128]{2,1,0:T(8,128)(2,1)S(1)} %pad_maximum_fusion), channel_id=1, source_target_pairs={{0,1},{1,0},{2,3},{3,2},{4,5},{5,4},{6,7},{7,6},{8,9},{9,8},{10,11... | collective-permute-start | bytes 393224 | tf_op jit(solution)/shard_map/ppermute | solution.py:169
  14.0 7.1 %collective-permute-start.5 = (bf16[4,128,128]{2,1,0:T(8,128)(2,1)S(1)}, bf16[4,128,128]{2,1,0:T(8,128)(2,1)S(1)}, u32[]{:S(2)}, u32[]{:S(2)}) collective-permute-start(bf16[4,128,128]{2,1,0:T(8,128)(2,1)S(1)} %pad_maximum_fusion), channel_id=1, source_target_pairs={{0,16},{1,17},{2,18},{3,19},{4,20},{5,21},{6,22},{7,23},{8,24},{9,... | collective-permute-start | bytes 393224 | tf_op jit(solution)/shard_map/ppermute | solution.py:169
  21.8 23.6 %collective-permute-start.6 = (bf16[16,128,128]{2,1,0:T(8,128)(2,1)S(1)}, bf16[16,128,128]{2,1,0:T(8,128)(2,1)S(1)}, u32[]{:S(2)}, u32[]{:S(2)}) collective-permute-start(bf16[16,128,128]{2,1,0:T(8,128)(2,1)S(1)} %get-tuple-element.37), channel_id=1, source_target_pairs={{0,96},{1,97},{2,98},{3,99},{4,100},{5,101},{6,102},{7,103},{8,104... | collective-permute-start | bytes 1572872 | tf_op jit(solution)/shard_map/ppermute | solution.py:169
  25.9 20.8 %collective-permute-start.7 = (bf16[16,128,128]{2,1,0:T(8,128)(2,1)S(1)}, bf16[16,128,128]{2,1,0:T(8,128)(2,1)S(1)}, u32[]{:S(2)}, u32[]{:S(2)}) collective-permute-start(bf16[16,128,128]{2,1,0:T(8,128)(2,1)S(1)} %get-tuple-element.37), channel_id=1, source_target_pairs={{0,64},{1,65},{2,66},{3,67},{4,68},{5,69},{6,70},{7,71},{8,72},{9,... | collective-permute-start | bytes 1572872 | tf_op jit(solution)/shard_map/ppermute | solution.py:169
  25.9 23.0 %collective-permute-start.8 = (bf16[16,128,128]{2,1,0:T(8,128)(2,1)S(1)}, bf16[16,128,128]{2,1,0:T(8,128)(2,1)S(1)}, u32[]{:S(2)}, u32[]{:S(2)}) collective-permute-start(bf16[16,128,128]{2,1,0:T(8,128)(2,1)S(1)} %get-tuple-element.37), channel_id=1, source_target_pairs={{0,32},{1,33},{2,34},{3,35},{4,36},{5,37},{6,38},{7,39},{8,40},{9,... | collective-permute-start | bytes 1572872 | tf_op jit(solution)/shard_map/ppermute | solution.py:169
  50.1 9.2 %collective-permute-start.9 = (bf16[64,128,128]{2,1,0:T(8,128)(2,1)}, bf16[64,128,128]{2,1,0:T(8,128)(2,1)S(1)}, u32[]{:S(2)}, u32[]{:S(2)}) collective-permute-start(bf16[64,128,128]{2,1,0:T(8,128)(2,1)} %get-tuple-element.26), channel_id=1, source_target_pairs={{0,2},{1,3},{2,0},{3,1},{4,6},{5,7},{6,4},{7,5},{8,10},{9,11},{10,... | collective-permute-start | bytes 6291464 | tf_op jit(solution)/shard_map/ppermute | solution.py:169
  134.1 4.2 %collective-permute-start.12 = (bf16[4,4,4,128,128]{4,3,2,1,0:T(8,128)(2,1)S(1)}, bf16[4,4,4,128,128]{4,3,2,1,0:T(8,128)(2,1)S(1)}, u32[]{:S(2)}, u32[]{:S(2)}) collective-permute-start(bf16[4,4,4,128,128]{4,3,2,1,0:T(8,128)(2,1)S(1)} %bitcast.88), channel_id=1, source_target_pairs={{0,2},{1,3},{2,0},{3,1},{4,6},{5,7},{6,4},{7,5},{8,10},{9,11},{10,... | collective-permute-start | bytes 6291464 | tf_op jit(solution)/shard_map/ppermute | solution.py:179
  141.4 36.5 %collective-permute-start.13 = (bf16[4,4,128,128]{3,2,1,0:T(8,128)(2,1)S(1)}, bf16[4,4,128,128]{3,2,1,0:T(8,128)(2,1)S(1)}, u32[]{:S(2)}, u32[]{:S(2)}) collective-permute-start(bf16[4,4,128,128]{3,2,1,0:T(8,128)(2,1)S(1)} %get-tuple-element.20), channel_id=1, source_target_pairs={{0,32},{1,33},{2,34},{3,35},{4,36},{5,37},{6,38},{7,39},{8,40},{9,... | collective-permute-start | bytes 1572872 | tf_op jit(solution)/shard_map/ppermute | solution.py:179
  165.6 22.7 %collective-permute-start.14 = (bf16[4,4,128,128]{3,2,1,0:T(8,128)(2,1)S(1)}, bf16[4,4,128,128]{3,2,1,0:T(8,128)(2,1)S(1)}, u32[]{:S(2)}, u32[]{:S(2)}) collective-permute-start(bf16[4,4,128,128]{3,2,1,0:T(8,128)(2,1)S(1)} %get-tuple-element.22), channel_id=1, source_target_pairs={{0,64},{1,65},{2,66},{3,67},{4,68},{5,69},{6,70},{7,71},{8,72},{9,... | collective-permute-start | bytes 1572872 | tf_op jit(solution)/shard_map/ppermute | solution.py:179
  165.6 23.7 %collective-permute-start.15 = (bf16[4,4,128,128]{3,2,1,0:T(8,128)(2,1)S(1)}, bf16[4,4,128,128]{3,2,1,0:T(8,128)(2,1)}, u32[]{:S(2)}, u32[]{:S(2)}) collective-permute-start(bf16[4,4,128,128]{3,2,1,0:T(8,128)(2,1)S(1)} %get-tuple-element.21), channel_id=1, source_target_pairs={{0,96},{1,97},{2,98},{3,99},{4,100},{5,101},{6,102},{7,103},{8,104... | collective-permute-start | bytes 1572872 | tf_op jit(solution)/shard_map/ppermute | solution.py:179
  169.0 29.8 %collective-permute-start.11 = (bf16[256,512]{1,0:T(8,128)(2,1)S(1)}, bf16[256,512]{1,0:T(8,128)(2,1)}, u32[]{:S(2)}, u32[]{:S(2)}) collective-permute-start(bf16[256,512]{1,0:T(8,128)(2,1)S(1)} %reshape.71), channel_id=1, source_target_pairs={{0,1},{1,0},{2,3},{3,2},{4,5},{5,4},{6,7},{7,6},{8,9},{9,8},{10,11... | collective-permute-start | bytes 786440 | tf_op jit(solution)/shard_map/ppermute | solution.py:218
  191.0 9.8 %collective-permute-start.16 = (bf16[4,128,128]{2,1,0:T(8,128)(2,1)S(1)}, bf16[4,128,128]{2,1,0:T(8,128)(2,1)S(1)}, u32[]{:S(2)}, u32[]{:S(2)}) collective-permute-start(bf16[4,128,128]{2,1,0:T(8,128)(2,1)S(1)} %get-tuple-element.23), channel_id=1, source_target_pairs={{0,16},{1,17},{2,18},{3,19},{4,20},{5,21},{6,22},{7,23},{8,24},{9,... | collective-permute-start | bytes 393224 | tf_op jit(solution)/shard_map/ppermute | solution.py:179
  193.5 10.1 %collective-permute-start.17 = (bf16[4,128,128]{2,1,0:T(8,128)(2,1)S(1)}, bf16[4,128,128]{2,1,0:T(8,128)(2,1)S(1)}, u32[]{:S(2)}, u32[]{:S(2)}) collective-permute-start(bf16[4,128,128]{2,1,0:T(8,128)(2,1)S(1)} %get-tuple-element.25), channel_id=1, source_target_pairs={{0,1},{1,0},{2,3},{3,2},{4,5},{5,4},{6,7},{7,6},{8,9},{9,8},{10,11... | collective-permute-start | bytes 393224 | tf_op jit(solution)/shard_map/ppermute | solution.py:179
  196.5 7.2 %collective-permute-start.18 = (bf16[4,128,128]{2,1,0:T(8,128)(2,1)S(1)}, bf16[4,128,128]{2,1,0:T(8,128)(2,1)S(1)}, u32[]{:S(2)}, u32[]{:S(2)}) collective-permute-start(bf16[4,128,128]{2,1,0:T(8,128)(2,1)S(1)} %get-tuple-element.24), channel_id=1, source_target_pairs={{0,17},{1,16},{2,19},{3,18},{4,21},{5,20},{6,23},{7,22},{8,25},{9,... | collective-permute-start | bytes 393224 | tf_op jit(solution)/shard_map/ppermute | solution.py:179
  197.1 17.5 %collective-permute-start.10 = (bf16[256,512]{1,0:T(8,128)(2,1)S(1)}, bf16[256,512]{1,0:T(8,128)(2,1)S(1)}, u32[]{:S(2)}, u32[]{:S(2)}) collective-permute-start(bf16[256,512]{1,0:T(8,128)(2,1)S(1)} %reshape.70), channel_id=1, source_target_pairs={{0,1},{1,0},{2,3},{3,2},{4,5},{5,4},{6,7},{7,6},{8,9},{9,8},{10,11... | collective-permute-start | bytes 786440 | tf_op jit(solution)/shard_map/ppermute | solution.py:218
  203.7 11.8 %collective-permute-start.19 = (bf16[128,128]{1,0:T(8,128)(2,1)S(1)}, bf16[128,128]{1,0:T(8,128)(2,1)S(1)}, u32[]{:S(2)}, u32[]{:S(2)}) collective-permute-start(bf16[128,128]{1,0:T(8,128)(2,1)S(1)} %get-tuple-element.32), channel_id=1, source_target_pairs={{0,4},{1,5},{2,6},{3,7},{4,8},{5,9},{6,10},{7,11},{8,12},{9,13},{1... | collective-permute-start | bytes 98312 | tf_op jit(solution)/shard_map/ppermute | solution.py:179
  206.8 10.1 %collective-permute-start.20 = (bf16[128,128]{1,0:T(8,128)(2,1)S(1)}, bf16[128,128]{1,0:T(8,128)(2,1)S(1)}, u32[]{:S(2)}, u32[]{:S(2)}) collective-permute-start(bf16[128,128]{1,0:T(8,128)(2,1)S(1)} %get-tuple-element.34), channel_id=1, source_target_pairs={{0,8},{1,9},{2,10},{3,11},{4,12},{5,13},{6,14},{7,15},{8,0},{9,1},... | collective-permute-start | bytes 98312 | tf_op jit(solution)/shard_map/ppermute | solution.py:179
  214.6 3.9 %collective-permute-start.21 = (bf16[128,128]{1,0:T(8,128)(2,1)S(1)}, bf16[128,128]{1,0:T(8,128)(2,1)S(1)}, u32[]{:S(2)}, u32[]{:S(2)}) collective-permute-start(bf16[128,128]{1,0:T(8,128)(2,1)S(1)} %get-tuple-element.33), channel_id=1, source_target_pairs={{0,12},{1,13},{2,14},{3,15},{4,0},{5,1},{6,2},{7,3},{8,4},{9,5},{1... | collective-permute-start | bytes 98312 | tf_op jit(solution)/shard_map/ppermute | solution.py:179
  (4 other events, 113.7 us)

commit v7 on v6

--- a/solution.py
+++ b/solution.py
@@ -38,63 +38,87 @@
     return jnp.transpose(tile).astype(jnp.bfloat16)
 
 
-def _forward_kernel(lists_ref, keep_ref, qt_ref, kvt_ref, dot_ref,
+def _pair_rows(kvt_ref, blocks, first):
+    return jnp.concatenate([_rows_of(kvt_ref, b, first) for b in blocks], axis=0)
+
+
+def _pair_cols(kvt_ref, blocks, first):
+    return jnp.concatenate([kvt_ref[b, first:first + HEAD_DIM, :] for b in blocks], axis=1)
+
+
+def _visit_slots(count_ref, qb, visit):
+    count = count_ref[qb, 0]
+    pairs = count // 2
+
+    def body(i, carry):
+        @pl.when(i < pairs)
+        def _():
+            visit((2 * i, 2 * i + 1))
+        return carry
+
+    lax.fori_loop(0, count_ref.shape[1] // 2, body, 0)
+
+    @pl.when(count % 2 == 1)
+    def _():
+        visit((count - 1,))
+
+
+def _forward_kernel(lists_ref, count_ref, qt_ref, kvt_ref, dot_ref,
                     ot_ref, lse_ref, delta_ref, m_sc, l_sc, acc_sc):
-    query_count, slots = lists_ref.shape
+    query_count = lists_ref.shape[0]
     for qb in range(query_count):
         m_sc[...] = jnp.full(m_sc.shape, LOWEST, jnp.float32)
         l_sc[...] = jnp.zeros(l_sc.shape, jnp.float32)
         acc_sc[...] = jnp.zeros(acc_sc.shape, jnp.float32)
 
-        def body(j, carry):
-            @pl.when(keep_ref[qb, j] != 0)
-            def _():
-                b = lists_ref[qb, j]
-                st = _nn(_rows_of(kvt_ref, b, 0), qt_ref[qb]) * SCALE
-                m_prev = m_sc[...]
-                m_new = jnp.maximum(m_prev, jnp.max(st, axis=0, keepdims=True))
-                alpha = jnp.exp(m_prev - m_new)
-                pt = jnp.exp(st - m_new)
-                l_sc[...] = alpha * l_sc[...] + jnp.sum(pt, axis=0, keepdims=True)
-                acc_sc[...] = alpha * acc_sc[...] + _nn(
-                    kvt_ref[b, HEAD_DIM:, :], pt.astype(jnp.bfloat16))
-                m_sc[...] = m_new
-            return carry
-
-        lax.fori_loop(0, slots, body, 0)
+        def visit(slots, qb=qb):
+            blocks = [lists_ref[qb, j] for j in slots]
+            st = _nn(_pair_rows(kvt_ref, blocks, 0), qt_ref[qb]) * SCALE
+            m_prev = m_sc[...]
+            m_new = jnp.maximum(m_prev, jnp.max(st, axis=0, keepdims=True))
+            alpha = jnp.exp(m_prev - m_new)
+            pt = jnp.exp(st - m_new)
+            l_sc[...] = alpha * l_sc[...] + jnp.sum(pt, axis=0, keepdims=True)
+            acc_sc[...] = alpha * acc_sc[...] + _nn(
+                _pair_cols(kvt_ref, blocks, HEAD_DIM), pt.astype(jnp.bfloat16))
+            m_sc[...] = m_new
+
+        _visit_slots(count_ref, qb, visit)
         out = acc_sc[...] / l_sc[...]
         ot_ref[qb] = out.astype(jnp.bfloat16)
         lse_ref[qb] = m_sc[...] + jnp.log(l_sc[...])
         delta_ref[qb] = jnp.sum(dot_ref[qb].astype(jnp.float32) * out, axis=0, keepdims=True)
 
 
-def _backward_kernel(lists_ref, keep_ref, q_ref, qt_ref, kvt_ref, do_ref, dot_ref, lse_ref, delta_ref,
-                     dqt_ref, dkvt_ref, dq_sc):
-    query_count, slots = lists_ref.shape
+def _backward_kernel(lists_ref, count_ref, q_ref, qt_ref, kvt_ref, do_ref, dot_ref, lse_ref,
+                     delta_ref, dqt_ref, dkvt_ref, dq_sc):
+    query_count = lists_ref.shape[0]
     dkvt_ref[...] = jnp.zeros(dkvt_ref.shape, jnp.float32)
     for qb in range(query_count):
         dq_sc[...] = jnp.zeros(dq_sc.shape, jnp.float32)
 
-        def body(j, carry):
-            @pl.when(keep_ref[qb, j] != 0)
-            def _():
-                b = lists_ref[qb, j]
-                q = q_ref[qb]
-                do = do_ref[qb]
-                st = _nn(_rows_of(kvt_ref, b, 0), qt_ref[qb]) * SCALE
-                pt = jnp.exp(st - lse_ref[qb])
-                dkvt_ref[b, HEAD_DIM:, :] += jnp.transpose(_nn(pt.astype(jnp.bfloat16), do))
-                dpt = _nn(_rows_of(kvt_ref, b, HEAD_DIM), dot_ref[qb])
-                dst = (pt * (dpt - delta_ref[qb])).astype(jnp.bfloat16)
-                dq_sc[...] += _nn(kvt_ref[b, :HEAD_DIM, :], dst)
-                dkvt_ref[b, :HEAD_DIM, :] += jnp.transpose(_nn(dst, q))
-            return carry
-
-        lax.fori_loop(0, slots, body, 0)
+        def visit(slots, qb=qb):
+            blocks = [lists_ref[qb, j] for j in slots]
+            st = _nn(_pair_rows(kvt_ref, blocks, 0), qt_ref[qb]) * SCALE
+            pt = jnp.exp(st - lse_ref[qb])
+            dvt = jnp.transpose(_nn(pt.astype(jnp.bfloat16), do_ref[qb]))
+            dpt = _nn(_pair_rows(kvt_ref, blocks, HEAD_DIM), dot_ref[qb])
+            dst = (pt * (dpt - delta_ref[qb])).astype(jnp.bfloat16)
+            dq_sc[...] += _nn(_pair_cols(kvt_ref, blocks, 0), dst)
+            dkt = jnp.transpose(_nn(dst, q_ref[qb]))
+            for place, b in enumerate(blocks):
+                cols = slice(place * BLOCK, (place + 1) * BLOCK)
+                dkvt_ref[b, :HEAD_DIM, :] += dkt[:, cols]
+                dkvt_ref[b, HEAD_DIM:, :] += dvt[:, cols]
+
+        _visit_slots(count_ref, qb, visit)
         dqt_ref[qb] = (dq_sc[...] * SCALE).astype(jnp.bfloat16)
 
 
 def attend_local(q_rows, do_rows, kv_t, lists, keep):
+    order = jnp.argsort(1 - keep, axis=1, stable=True)
+    lists = jnp.take_along_axis(lists, order, axis=1)
+    keep = jnp.broadcast_to(jnp.sum(keep, axis=1, keepdims=True), lists.shape).astype(jnp.int32)
     query_count, rows, _ = q_rows.shape
     block_total = kv_t.shape[0]
     f32 = jnp.float32

time: 222 us -> 194 us (0.87); the launches traced: 220 us -> 195 us
  Pallas kernels: 70.7 us -> 49 us
  starting transfers between devices: 60.4 us -> 49.3 us
  waiting for transfers between devices: 51.7 us -> 56.7 us
  local copies, waits for them, and re-layouts: 21.7 us -> 24.1 us
    pallas_call x1, Pallas kernels: 42.6 us -> 28.8 us  [attend_local(): pl.pallas_call(_backward_kernel, out_shape=(jax.ShapeDtypeStruct((query_c...]
    ppermute x10, starting transfers between devices: 43.4 us -> 31.1 us  [scatter_sum(): lax.ppermute(sent, axes, pairs(axis, shift)).astype(jnp.float32)]
    pallas_call x1, Pallas kernels: 28.1 us -> 20.2 us  [attend_local(): pl.pallas_call(_forward_kernel, out_shape=(jax.ShapeDtypeStruct((query_co...]
    ppermute x10, waiting for transfers between devices: 27 us -> 31.9 us  [scatter_sum(): lax.ppermute(sent, axes, pairs(axis, shift)).astype(jnp.float32)]
  transfers between devices with their start and end apart: 22 -> 22, of which waited for: 14 -> 13; matrix products, arithmetic and copies ran while one was open for 11% -> 14% of each run, Pallas kernels for 0% -> 0%
where the time goes in v7:
time: 194 us; the launch traced here: 195 us
  waiting for transfers between devices  56.7 us (29%)
  starting transfers between devices  49.3 us (25%)
  Pallas kernels  49 us (25%)
  local copies, waits for them, and re-layouts  24.1 us (12%)
  other arithmetic  15 us (8%)
    ppermute x10, waiting for transfers between devices, scatter_sum(): lax.ppermute(sent, axes, pairs(axis, shift)).astype(jnp.float32)  31.9 us
    ppermute x10, starting transfers between devices, scatter_sum(): lax.ppermute(sent, axes, pairs(axis, shift)).astype(jnp.float32)  31.1 us
    pallas_call x1, Pallas kernels, attend_local(): pl.pallas_call(_backward_kernel, out_shape=(jax.ShapeDtypeStruct((query_c...  28.8 us
    ppermute x10, waiting for transfers between devices, gather_blocks(): pieces.append(lax.ppermute(buf, axes, pairs(axis, size - shift)))  24.7 us
    pallas_call x1, Pallas kernels, attend_local(): pl.pallas_call(_forward_kernel, out_shape=(jax.ShapeDtypeStruct((query_co...  20.2 us
    ppermute x10, starting transfers between devices, gather_blocks(): pieces.append(lax.ppermute(buf, axes, pairs(axis, size - shift)))  14.5 us
    unnamed x24, local copies, waits for them, and re-layouts  7.1 us
    another operation x3, other arithmetic  4.7 us
  transfers between devices with their start and end apart: 22, of which 13 were waited for; matrix products, arithmetic and copies ran while one was open for 14% of the time, Pallas kernels for 0%

profile of v7, /device:TPU:0, one launch (start us, length us, event | category | flops | bytes accessed | tf_op | source)
XLA Modules:
  0.0 195.0 jit_solution(9863861871508879974)
XLA Ops:
  1.4 3.1 %collective-permute-start = (bf16[1,128,128]{2,1,0:T(8,128)(2,1)S(1)}, bf16[1,128,128]{2,1,0:T(8,128)(2,1)S(1)}, u32[]{:S(2)}, u32[]{:S(2)}) collective-permute-start(bf16[1,128,128]{2,1,0:T(8,128)(2,1)S(1)} %maximum_bitcast_fusion), channel_id=1, source_target_pairs={{0,12},{1,13},{2,14},{3,15},{4,0},{5,1},{6,2},{7,3},{8,4},{9,5},{1... | collective-permute-start | bytes 98312 | tf_op jit(solution)/shard_map/ppermute | solution.py:193
  7.5 2.4 %collective-permute-done.1 = bf16[1,128,128]{2,1,0:T(8,128)(2,1)S(1)} collective-permute-done((bf16[1,128,128]{2,1,0:T(8,128)(2,1)S(1)}, bf16[1,128,128]{2,1,0:T(8,128)(2,1)S(1)}, u32[]{:S(2)}, u32[]{:S(2)}) %collective-permute-start.1) | collective-permute-done | bytes 32800 | tf_op jit(solution)/shard_map/ppermute | solution.py:193
  10.3 2.8 %collective-permute-start.3 = (bf16[4,128,128]{2,1,0:T(8,128)(2,1)S(1)}, bf16[4,128,128]{2,1,0:T(8,128)(2,1)S(1)}, u32[]{:S(2)}, u32[]{:S(2)}) collective-permute-start(bf16[4,128,128]{2,1,0:T(8,128)(2,1)S(1)} %pad_maximum_fusion), channel_id=1, source_target_pairs={{0,17},{1,16},{2,19},{3,18},{4,21},{5,20},{6,23},{7,22},{8,25},{9,... | collective-permute-start | bytes 393224 | tf_op jit(solution)/shard_map/ppermute | solution.py:193
  18.2 1.5 collective-permute-done.4
  21.8 4.0 %collective-permute-start.6 = (bf16[16,128,128]{2,1,0:T(8,128)(2,1)S(1)}, bf16[16,128,128]{2,1,0:T(8,128)(2,1)S(1)}, u32[]{:S(2)}, u32[]{:S(2)}) collective-permute-start(bf16[16,128,128]{2,1,0:T(8,128)(2,1)S(1)} %get-tuple-element.39), channel_id=1, source_target_pairs={{0,96},{1,97},{2,98},{3,99},{4,100},{5,101},{6,102},{7,103},{8,104... | collective-permute-start | bytes 1572872 | tf_op jit(solution)/shard_map/ppermute | solution.py:193
  27.1 18.3 %collective-permute-done.6 = bf16[16,128,128]{2,1,0:T(8,128)(2,1)S(1)} collective-permute-done((bf16[16,128,128]{2,1,0:T(8,128)(2,1)S(1)}, bf16[16,128,128]{2,1,0:T(8,128)(2,1)S(1)}, u32[]{:S(2)}, u32[]{:S(2)}) %collective-permute-start.6) | collective-permute-done | bytes 524320 | tf_op jit(solution)/shard_map/ppermute | solution.py:193
  51.5 2.7 %slice_subtract_fusion.3 = (s32[2,48,1]{2,1,0:T(8,128)S(1)}, s32[2,48,1]{2,1,0:T(8,128)S(1)}, s32[2,48,1]{2,1,0:T(8,128)S(1)}, s32[2,48,1]{2,1,0:T(8,128)S(1)}) fusion(s32[2,48,4]{2,1,0:T(8,128)S(1)} %bitcast.93, s32[]{:T(128)} %bitcast.1, s32[]{:T(128)} %bitcast.5, s32[]{:T(128)} %bitcast.3, s32[]{:T(128)} %bitcast.7), kind=kLoop, calls=%fused_computation.56 | loop fusion | flops 384 | bytes 3088 | tf_op jit(solution)/shard_map/sub | solution.py:227
  56.1 1.5 gather_fusion.1
  63.9 20.2 %shard_map.93 = (bf16[2,64,1024]{2,1,0:T(8,128)(2,1)}, f32[2,1,1024]{2,1,0:T(1,128)}, f32[2,1,1024]{2,1,0:T(1,128)}) custom-call(s32[2,48]{1,0:T(2,128)} %and_select_fusion.4.lists_ref, s32[2,48]{1,0:T(2,128)} %broadcast_in_dim.22.count_ref, bf16[2,64,1024]{2,1,0:T(8,128)(2,1)} %bitcast.88, ...), custom_call_target="tpu_custom_call" | custom-call | tf_op jit(solution)/shard_map/pallas_call | solution.py:127
  84.2 28.8 %shard_map.94 = (bf16[2,64,1024]{2,1,0:T(8,128)(2,1)}, f32[128,128,128]{2,1,0:T(8,128)}) custom-call(s32[2,48]{1,0:T(2,128)} %and_select_fusion.4.lists_ref, s32[2,48]{1,0:T(2,128)} %broadcast_in_dim.22.count_ref, bf16[2,1024,64]{2,1,0:T(8,128)(2,1)} %copy-done, bf16[2,64,1024]{2,1,0:T(8,128)(2,1)} %bitcast.89, ...), custom_call_target="tpu_custom_call" | custom-call | tf_op jit(solution)/shard_map/pallas_call | solution.py:143
  112.9 2.6 %slice.179 = bf16[64,128,128]{2,1,0:T(8,128)(2,1)S(1)} slice(f32[128,128,128]{2,1,0:T(8,128)} %get-tuple-element.15), slice={[64:128], [0:128], [0:128]} | slice | bytes 4194304 | tf_op jit(solution)/shard_map/slice | solution.py:202
  115.5 7.1 %collective-permute-start.12 = (bf16[4,4,4,128,128]{4,3,2,1,0:T(8,128)(2,1)S(1)}, bf16[4,4,4,128,128]{4,3,2,1,0:T(8,128)(2,1)S(1)}, u32[]{:S(2)}, u32[]{:S(2)}) collective-permute-start(bf16[4,4,4,128,128]{4,3,2,1,0:T(8,128)(2,1)S(1)} %bitcast.92), channel_id=1, source_target_pairs={{0,2},{1,3},{2,0},{3,1},{4,6},{5,7},{6,4},{7,5},{8,10},{9,11},{10,... | collective-permute-start | bytes 6291464 | tf_op jit(solution)/shard_map/ppermute | solution.py:203
  122.6 2.5 %slice.97 = f32[64,128,128]{2,1,0:T(8,128)S(1)} slice(f32[128,128,128]{2,1,0:T(8,128)} %get-tuple-element.15), slice={[0:64], [0:128], [0:128]} | slice | bytes 8388608 | tf_op jit(solution)/shard_map/slice | solution.py:200
  126.4 3.0 %fusion.28 = (bf16[4,4,4,128,128]{4,3,2,1,0:T(8,128)(2,1)S(1)}, f32[4,4,4,128,128]{4,3,2,1,0:T(8,128)}) fusion(f32[4,4,4,128,128]{4,3,2,1,0:T(8,128)S(1)} %bitcast.87, bf16[4,4,4,128,128]{4,3,2,1,0:T(8,128)(2,1)S(1)} %collective-permute-done.12), kind=kLoop, calls=%fused_computation.103 | loop fusion | flops 3145728 | bytes 12582912 | tf_op jit(solution)/shard_map/convert.9
  129.6 14.7 %collective-permute-start.14 = (bf16[4,4,128,128]{3,2,1,0:T(8,128)(2,1)S(1)}, bf16[4,4,128,128]{3,2,1,0:T(8,128)(2,1)S(1)}, u32[]{:S(2)}, u32[]{:S(2)}) collective-permute-start(bf16[4,4,128,128]{3,2,1,0:T(8,128)(2,1)S(1)} %get-tuple-element.24), channel_id=1, source_target_pairs={{0,64},{1,65},{2,66},{3,67},{4,68},{5,69},{6,70},{7,71},{8,72},{9,... | collective-permute-start | bytes 1572872 | tf_op jit(solution)/shard_map/ppermute | solution.py:203
  145.7 9.5 %collective-permute-done.13 = bf16[4,4,128,128]{3,2,1,0:T(8,128)(2,1)S(1)} collective-permute-done((bf16[4,4,128,128]{3,2,1,0:T(8,128)(2,1)S(1)}, bf16[4,4,128,128]{3,2,1,0:T(8,128)(2,1)S(1)}, u32[]{:S(2)}, u32[]{:S(2)}) %collective-permute-start.13) | collective-permute-done | bytes 524320 | tf_op jit(solution)/shard_map/ppermute | solution.py:203
  155.2 12.4 %collective-permute-done.14 = bf16[4,4,128,128]{3,2,1,0:T(8,128)(2,1)S(1)} collective-permute-done((bf16[4,4,128,128]{3,2,1,0:T(8,128)(2,1)S(1)}, bf16[4,4,128,128]{3,2,1,0:T(8,128)(2,1)S(1)}, u32[]{:S(2)}, u32[]{:S(2)}) %collective-permute-start.14) | collective-permute-done | bytes 524320 | tf_op jit(solution)/shard_map/ppermute | solution.py:203
  167.7 1.7 fusion.26
  170.3 2.5 %collective-permute-start.18 = (bf16[4,128,128]{2,1,0:T(8,128)(2,1)S(1)}, bf16[4,128,128]{2,1,0:T(8,128)(2,1)S(1)}, u32[]{:S(2)}, u32[]{:S(2)}) collective-permute-start(bf16[4,128,128]{2,1,0:T(8,128)(2,1)S(1)} %get-tuple-element.26), channel_id=1, source_target_pairs={{0,17},{1,16},{2,19},{3,18},{4,21},{5,20},{6,23},{7,22},{8,25},{9,... | collective-permute-start | bytes 393224 | tf_op jit(solution)/shard_map/ppermute | solution.py:203
  173.5 2.8 %collective-permute-start.10 = (bf16[256,512]{1,0:T(8,128)(2,1)S(1)}, bf16[256,512]{1,0:T(8,128)(2,1)S(1)}, u32[]{:S(2)}, u32[]{:S(2)}) collective-permute-start(bf16[256,512]{1,0:T(8,128)(2,1)S(1)} %reshape.81), channel_id=1, source_target_pairs={{0,1},{1,0},{2,3},{3,2},{4,5},{5,4},{6,7},{7,6},{8,9},{9,8},{10,11... | collective-permute-start | bytes 786440 | tf_op jit(solution)/shard_map/ppermute | solution.py:242
  176.3 2.0 %maximum_select_fusion.1 = bf16[256,1024]{1,0:T(8,128)(2,1)} fusion(bf16[256,512]{1,0:T(8,128)(2,1)} %collective-permute-done.11, bf16[256,512]{1,0:T(8,128)(2,1)S(1)} %reshape.82, pred[]{:T(512)S(6)} %eq.22), kind=kLoop, calls=%fused_computation.12 | loop fusion | flops 2359296 | bytes 1048577 | tf_op jit(solution)/shard_map/jit(_where)/select_n | solution.py:243
  178.3 5.7 %collective-permute-done.16 = bf16[4,128,128]{2,1,0:T(8,128)(2,1)S(1)} collective-permute-done((bf16[4,128,128]{2,1,0:T(8,128)(2,1)S(1)}, bf16[4,128,128]{2,1,0:T(8,128)(2,1)S(1)}, u32[]{:S(2)}, u32[]{:S(2)}) %collective-permute-start.16) | collective-permute-done | bytes 131104 | tf_op jit(solution)/shard_map/ppermute | solution.py:203
  184.2 5.6 %collective-permute-start.20 = (bf16[128,128]{1,0:T(8,128)(2,1)S(1)}, bf16[128,128]{1,0:T(8,128)(2,1)S(1)}, u32[]{:S(2)}, u32[]{:S(2)}) collective-permute-start(bf16[128,128]{1,0:T(8,128)(2,1)S(1)} %get-tuple-element.36), channel_id=1, source_target_pairs={{0,8},{1,9},{2,10},{3,11},{4,12},{5,13},{6,14},{7,15},{8,0},{9,1},... | collective-permute-start | bytes 98312 | tf_op jit(solution)/shard_map/ppermute | solution.py:203
  192.1 1.7 collective-permute-done.21
  (94 shorter events, 34.9 us)
Async XLA Ops:
  0.6 49.6 %copy-start.2 = (s32[128,4]{1,0:T(8,128)S(1)}, s32[128,4]{1,0:T(8,128)}, u32[]{:S(2)}) copy-start(s32[128,4]{1,0:T(8,128)} %constant.80.clone) | copy-start | bytes 6148
  0.6 49.5 %copy-start.5 = (s32[2,48]{1,0:T(2,128)S(1)}, s32[2,48]{1,0:T(2,128)}, u32[]{:S(2)}) copy-start(s32[2,48]{1,0:T(2,128)} %param.10) | copy-start | bytes 1156
  1.4 6.1 %collective-permute-start = (bf16[1,128,128]{2,1,0:T(8,128)(2,1)S(1)}, bf16[1,128,128]{2,1,0:T(8,128)(2,1)S(1)}, u32[]{:S(2)}, u32[]{:S(2)}) collective-permute-start(bf16[1,128,128]{2,1,0:T(8,128)(2,1)S(1)} %maximum_bitcast_fusion), channel_id=1, source_target_pairs={{0,12},{1,13},{2,14},{3,15},{4,0},{5,1},{6,2},{7,3},{8,4},{9,5},{1... | collective-permute-start | bytes 98312 | tf_op jit(solution)/shard_map/ppermute | solution.py:193
  4.6 5.4 %collective-permute-start.1 = (bf16[1,128,128]{2,1,0:T(8,128)(2,1)S(1)}, bf16[1,128,128]{2,1,0:T(8,128)(2,1)S(1)}, u32[]{:S(2)}, u32[]{:S(2)}) collective-permute-start(bf16[1,128,128]{2,1,0:T(8,128)(2,1)S(1)} %maximum_bitcast_fusion), channel_id=1, source_target_pairs={{0,8},{1,9},{2,10},{3,11},{4,12},{5,13},{6,14},{7,15},{8,0},{9,1},... | collective-permute-start | bytes 98312 | tf_op jit(solution)/shard_map/ppermute | solution.py:193
  5.2 5.1 %collective-permute-start.2 = (bf16[1,128,128]{2,1,0:T(8,128)(2,1)S(1)}, bf16[1,128,128]{2,1,0:T(8,128)(2,1)S(1)}, u32[]{:S(2)}, u32[]{:S(2)}) collective-permute-start(bf16[1,128,128]{2,1,0:T(8,128)(2,1)S(1)} %maximum_bitcast_fusion), channel_id=1, source_target_pairs={{0,4},{1,5},{2,6},{3,7},{4,8},{5,9},{6,10},{7,11},{8,12},{9,13},{1... | collective-permute-start | bytes 98312 | tf_op jit(solution)/shard_map/ppermute | solution.py:193
  10.3 7.1 %collective-permute-start.3 = (bf16[4,128,128]{2,1,0:T(8,128)(2,1)S(1)}, bf16[4,128,128]{2,1,0:T(8,128)(2,1)S(1)}, u32[]{:S(2)}, u32[]{:S(2)}) collective-permute-start(bf16[4,128,128]{2,1,0:T(8,128)(2,1)S(1)} %pad_maximum_fusion), channel_id=1, source_target_pairs={{0,17},{1,16},{2,19},{3,18},{4,21},{5,20},{6,23},{7,22},{8,25},{9,... | collective-permute-start | bytes 393224 | tf_op jit(solution)/shard_map/ppermute | solution.py:193
  13.2 6.6 %collective-permute-start.4 = (bf16[4,128,128]{2,1,0:T(8,128)(2,1)S(1)}, bf16[4,128,128]{2,1,0:T(8,128)(2,1)S(1)}, u32[]{:S(2)}, u32[]{:S(2)}) collective-permute-start(bf16[4,128,128]{2,1,0:T(8,128)(2,1)S(1)} %pad_maximum_fusion), channel_id=1, source_target_pairs={{0,1},{1,0},{2,3},{3,2},{4,5},{5,4},{6,7},{7,6},{8,9},{9,8},{10,11... | collective-permute-start | bytes 393224 | tf_op jit(solution)/shard_map/ppermute | solution.py:193
  14.0 7.1 %collective-permute-start.5 = (bf16[4,128,128]{2,1,0:T(8,128)(2,1)S(1)}, bf16[4,128,128]{2,1,0:T(8,128)(2,1)S(1)}, u32[]{:S(2)}, u32[]{:S(2)}) collective-permute-start(bf16[4,128,128]{2,1,0:T(8,128)(2,1)S(1)} %pad_maximum_fusion), channel_id=1, source_target_pairs={{0,16},{1,17},{2,18},{3,19},{4,20},{5,21},{6,22},{7,23},{8,24},{9,... | collective-permute-start | bytes 393224 | tf_op jit(solution)/shard_map/ppermute | solution.py:193
  21.8 23.6 %collective-permute-start.6 = (bf16[16,128,128]{2,1,0:T(8,128)(2,1)S(1)}, bf16[16,128,128]{2,1,0:T(8,128)(2,1)S(1)}, u32[]{:S(2)}, u32[]{:S(2)}) collective-permute-start(bf16[16,128,128]{2,1,0:T(8,128)(2,1)S(1)} %get-tuple-element.39), channel_id=1, source_target_pairs={{0,96},{1,97},{2,98},{3,99},{4,100},{5,101},{6,102},{7,103},{8,104... | collective-permute-start | bytes 1572872 | tf_op jit(solution)/shard_map/ppermute | solution.py:193
  25.9 20.8 %collective-permute-start.7 = (bf16[16,128,128]{2,1,0:T(8,128)(2,1)S(1)}, bf16[16,128,128]{2,1,0:T(8,128)(2,1)S(1)}, u32[]{:S(2)}, u32[]{:S(2)}) collective-permute-start(bf16[16,128,128]{2,1,0:T(8,128)(2,1)S(1)} %get-tuple-element.39), channel_id=1, source_target_pairs={{0,64},{1,65},{2,66},{3,67},{4,68},{5,69},{6,70},{7,71},{8,72},{9,... | collective-permute-start | bytes 1572872 | tf_op jit(solution)/shard_map/ppermute | solution.py:193
  25.9 23.0 %collective-permute-start.8 = (bf16[16,128,128]{2,1,0:T(8,128)(2,1)S(1)}, bf16[16,128,128]{2,1,0:T(8,128)(2,1)S(1)}, u32[]{:S(2)}, u32[]{:S(2)}) collective-permute-start(bf16[16,128,128]{2,1,0:T(8,128)(2,1)S(1)} %get-tuple-element.39), channel_id=1, source_target_pairs={{0,32},{1,33},{2,34},{3,35},{4,36},{5,37},{6,38},{7,39},{8,40},{9,... | collective-permute-start | bytes 1572872 | tf_op jit(solution)/shard_map/ppermute | solution.py:193
  50.1 11.6 %collective-permute-start.9 = (bf16[64,128,128]{2,1,0:T(8,128)(2,1)}, bf16[64,128,128]{2,1,0:T(8,128)(2,1)S(1)}, u32[]{:S(2)}, u32[]{:S(2)}) collective-permute-start(bf16[64,128,128]{2,1,0:T(8,128)(2,1)} %get-tuple-element.28), channel_id=1, source_target_pairs={{0,2},{1,3},{2,0},{3,1},{4,6},{5,7},{6,4},{7,5},{8,10},{9,11},{10,... | collective-permute-start | bytes 6291464 | tf_op jit(solution)/shard_map/ppermute | solution.py:193
  115.5 10.9 %collective-permute-start.12 = (bf16[4,4,4,128,128]{4,3,2,1,0:T(8,128)(2,1)S(1)}, bf16[4,4,4,128,128]{4,3,2,1,0:T(8,128)(2,1)S(1)}, u32[]{:S(2)}, u32[]{:S(2)}) collective-permute-start(bf16[4,4,4,128,128]{4,3,2,1,0:T(8,128)(2,1)S(1)} %bitcast.92), channel_id=1, source_target_pairs={{0,2},{1,3},{2,0},{3,1},{4,6},{5,7},{6,4},{7,5},{8,10},{9,11},{10,... | collective-permute-start | bytes 6291464 | tf_op jit(solution)/shard_map/ppermute | solution.py:203
  129.5 25.7 %collective-permute-start.13 = (bf16[4,4,128,128]{3,2,1,0:T(8,128)(2,1)S(1)}, bf16[4,4,128,128]{3,2,1,0:T(8,128)(2,1)S(1)}, u32[]{:S(2)}, u32[]{:S(2)}) collective-permute-start(bf16[4,4,128,128]{3,2,1,0:T(8,128)(2,1)S(1)} %get-tuple-element.22), channel_id=1, source_target_pairs={{0,32},{1,33},{2,34},{3,35},{4,36},{5,37},{6,38},{7,39},{8,40},{9,... | collective-permute-start | bytes 1572872 | tf_op jit(solution)/shard_map/ppermute | solution.py:203
  129.6 38.1 %collective-permute-start.14 = (bf16[4,4,128,128]{3,2,1,0:T(8,128)(2,1)S(1)}, bf16[4,4,128,128]{3,2,1,0:T(8,128)(2,1)S(1)}, u32[]{:S(2)}, u32[]{:S(2)}) collective-permute-start(bf16[4,4,128,128]{3,2,1,0:T(8,128)(2,1)S(1)} %get-tuple-element.24), channel_id=1, source_target_pairs={{0,64},{1,65},{2,66},{3,67},{4,68},{5,69},{6,70},{7,71},{8,72},{9,... | collective-permute-start | bytes 1572872 | tf_op jit(solution)/shard_map/ppermute | solution.py:203
  144.2 23.4 %collective-permute-start.15 = (bf16[4,4,128,128]{3,2,1,0:T(8,128)(2,1)S(1)}, bf16[4,4,128,128]{3,2,1,0:T(8,128)(2,1)}, u32[]{:S(2)}, u32[]{:S(2)}) collective-permute-start(bf16[4,4,128,128]{3,2,1,0:T(8,128)(2,1)S(1)} %get-tuple-element.23), channel_id=1, source_target_pairs={{0,96},{1,97},{2,98},{3,99},{4,100},{5,101},{6,102},{7,103},{8,104... | collective-permute-start | bytes 1572872 | tf_op jit(solution)/shard_map/ppermute | solution.py:203
  144.9 31.4 %collective-permute-start.11 = (bf16[256,512]{1,0:T(8,128)(2,1)S(1)}, bf16[256,512]{1,0:T(8,128)(2,1)}, u32[]{:S(2)}, u32[]{:S(2)}) collective-permute-start(bf16[256,512]{1,0:T(8,128)(2,1)S(1)} %reshape.82), channel_id=1, source_target_pairs={{0,1},{1,0},{2,3},{3,2},{4,5},{5,4},{6,7},{7,6},{8,9},{9,8},{10,11... | collective-permute-start | bytes 786440 | tf_op jit(solution)/shard_map/ppermute | solution.py:242
  169.4 14.6 %collective-permute-start.16 = (bf16[4,128,128]{2,1,0:T(8,128)(2,1)S(1)}, bf16[4,128,128]{2,1,0:T(8,128)(2,1)S(1)}, u32[]{:S(2)}, u32[]{:S(2)}) collective-permute-start(bf16[4,128,128]{2,1,0:T(8,128)(2,1)S(1)} %get-tuple-element.25), channel_id=1, source_target_pairs={{0,16},{1,17},{2,18},{3,19},{4,20},{5,21},{6,22},{7,23},{8,24},{9,... | collective-permute-start | bytes 393224 | tf_op jit(solution)/shard_map/ppermute | solution.py:203
  169.5 14.5 %collective-permute-start.17 = (bf16[4,128,128]{2,1,0:T(8,128)(2,1)S(1)}, bf16[4,128,128]{2,1,0:T(8,128)(2,1)S(1)}, u32[]{:S(2)}, u32[]{:S(2)}) collective-permute-start(bf16[4,128,128]{2,1,0:T(8,128)(2,1)S(1)} %get-tuple-element.27), channel_id=1, source_target_pairs={{0,1},{1,0},{2,3},{3,2},{4,5},{5,4},{6,7},{7,6},{8,9},{9,8},{10,11... | collective-permute-start | bytes 393224 | tf_op jit(solution)/shard_map/ppermute | solution.py:203
  170.3 13.7 %collective-permute-start.18 = (bf16[4,128,128]{2,1,0:T(8,128)(2,1)S(1)}, bf16[4,128,128]{2,1,0:T(8,128)(2,1)S(1)}, u32[]{:S(2)}, u32[]{:S(2)}) collective-permute-start(bf16[4,128,128]{2,1,0:T(8,128)(2,1)S(1)} %get-tuple-element.26), channel_id=1, source_target_pairs={{0,17},{1,16},{2,19},{3,18},{4,21},{5,20},{6,23},{7,22},{8,25},{9,... | collective-permute-start | bytes 393224 | tf_op jit(solution)/shard_map/ppermute | solution.py:203
  173.5 16.3 %collective-permute-start.10 = (bf16[256,512]{1,0:T(8,128)(2,1)S(1)}, bf16[256,512]{1,0:T(8,128)(2,1)S(1)}, u32[]{:S(2)}, u32[]{:S(2)}) collective-permute-start(bf16[256,512]{1,0:T(8,128)(2,1)S(1)} %reshape.81), channel_id=1, source_target_pairs={{0,1},{1,0},{2,3},{3,2},{4,5},{5,4},{6,7},{7,6},{8,9},{9,8},{10,11... | collective-permute-start | bytes 786440 | tf_op jit(solution)/shard_map/ppermute | solution.py:242
  184.1 6.7 %collective-permute-start.19 = (bf16[128,128]{1,0:T(8,128)(2,1)S(1)}, bf16[128,128]{1,0:T(8,128)(2,1)S(1)}, u32[]{:S(2)}, u32[]{:S(2)}) collective-permute-start(bf16[128,128]{1,0:T(8,128)(2,1)S(1)} %get-tuple-element.34), channel_id=1, source_target_pairs={{0,4},{1,5},{2,6},{3,7},{4,8},{5,9},{6,10},{7,11},{8,12},{9,13},{1... | collective-permute-start | bytes 98312 | tf_op jit(solution)/shard_map/ppermute | solution.py:203
  184.2 7.9 %collective-permute-start.20 = (bf16[128,128]{1,0:T(8,128)(2,1)S(1)}, bf16[128,128]{1,0:T(8,128)(2,1)S(1)}, u32[]{:S(2)}, u32[]{:S(2)}) collective-permute-start(bf16[128,128]{1,0:T(8,128)(2,1)S(1)} %get-tuple-element.36), channel_id=1, source_target_pairs={{0,8},{1,9},{2,10},{3,11},{4,12},{5,13},{6,14},{7,15},{8,0},{9,1},... | collective-permute-start | bytes 98312 | tf_op jit(solution)/shard_map/ppermute | solution.py:203
  189.8 3.9 %collective-permute-start.21 = (bf16[128,128]{1,0:T(8,128)(2,1)S(1)}, bf16[128,128]{1,0:T(8,128)(2,1)S(1)}, u32[]{:S(2)}, u32[]{:S(2)}) collective-permute-start(bf16[128,128]{1,0:T(8,128)(2,1)S(1)} %get-tuple-element.35), channel_id=1, source_target_pairs={{0,12},{1,13},{2,14},{3,15},{4,0},{5,1},{6,2},{7,3},{8,4},{9,5},{1... | collective-permute-start | bytes 98312 | tf_op jit(solution)/shard_map/ppermute | solution.py:203
  (4 other events, 84.3 us)

commit v8 on v7

--- a/solution.py
+++ b/solution.py
@@ -46,19 +46,25 @@
     return jnp.concatenate([kvt_ref[b, first:first + HEAD_DIM, :] for b in blocks], axis=1)
 
 
-def _visit_slots(count_ref, qb, visit):
+def _visit_slots(count_ref, qb, visit, group=4):
     count = count_ref[qb, 0]
-    pairs = count // 2
+    groups = count // group
 
     def body(i, carry):
-        @pl.when(i < pairs)
+        @pl.when(i < groups)
         def _():
-            visit((2 * i, 2 * i + 1))
+            visit(tuple(group * i + t for t in range(group)))
         return carry
 
-    lax.fori_loop(0, count_ref.shape[1] // 2, body, 0)
-
-    @pl.when(count % 2 == 1)
+    lax.fori_loop(0, count_ref.shape[1] // group, body, 0)
+    done = groups * group
+    rest = count - done
+
+    @pl.when(rest >= 2)
+    def _():
+        visit((done, done + 1))
+
+    @pl.when(rest % 2 == 1)
     def _():
         visit((count - 1,))
 

time: 194 us -> 186 us (0.959); the launches traced: 195 us -> 184 us
  starting transfers between devices: 49.3 us -> 30.3 us
  Pallas kernels: 49 us -> 59.7 us
  waiting for transfers between devices: 56.7 us -> 54.3 us
    ppermute x10, starting transfers between devices: 31.1 us -> 12.1 us  [scatter_sum(): lax.ppermute(sent, axes, pairs(axis, shift)).astype(jnp.float32)]
    pallas_call x1, Pallas kernels: 28.8 us -> 37.7 us  [attend_local(): pl.pallas_call(_backward_kernel, out_shape=(jax.ShapeDtypeStruct((query_c...]
    ppermute x10, waiting for transfers between devices: 31.9 us -> 29.6 us  [scatter_sum(): lax.ppermute(sent, axes, pairs(axis, shift)).astype(jnp.float32)]
  transfers between devices with their start and end apart: 22 -> 22, of which waited for: 13 -> 14; matrix products, arithmetic and copies ran while one was open for 14% -> 15% of each run, Pallas kernels for 0% -> 0%
where the time goes in v8:
time: 186 us; the launch traced here: 184 us
  Pallas kernels  59.7 us (32%)
  waiting for transfers between devices  54.3 us (29%)
  starting transfers between devices  30.3 us (16%)
  local copies, waits for them, and re-layouts  24.1 us (13%)
  other arithmetic  15 us (8%)
    pallas_call x1, Pallas kernels, attend_local(): pl.pallas_call(_backward_kernel, out_shape=(jax.ShapeDtypeStruct((query_c...  37.7 us
    ppermute x10, waiting for transfers between devices, scatter_sum(): lax.ppermute(sent, axes, pairs(axis, shift)).astype(jnp.float32)  29.6 us
    ppermute x10, waiting for transfers between devices, gather_blocks(): pieces.append(lax.ppermute(buf, axes, pairs(axis, size - shift)))  24.7 us
    pallas_call x1, Pallas kernels, attend_local(): pl.pallas_call(_forward_kernel, out_shape=(jax.ShapeDtypeStruct((query_co...  22 us
    ppermute x10, starting transfers between devices, gather_blocks(): pieces.append(lax.ppermute(buf, axes, pairs(axis, size - shift)))  14.5 us
    ppermute x10, starting transfers between devices, scatter_sum(): lax.ppermute(sent, axes, pairs(axis, shift)).astype(jnp.float32)  12.1 us
    unnamed x24, local copies, waits for them, and re-layouts  7.1 us
    another operation x3, other arithmetic  4.7 us
  transfers between devices with their start and end apart: 22, of which 14 were waited for; matrix products, arithmetic and copies ran while one was open for 15% of the time, Pallas kernels for 0%

profile of v8, /device:TPU:0, one launch (start us, length us, event | category | flops | bytes accessed | tf_op | source)
XLA Modules:
  0.0 184.3 jit_solution(1073401314703110127)
XLA Ops:
  1.4 3.1 %collective-permute-start = (bf16[1,128,128]{2,1,0:T(8,128)(2,1)S(1)}, bf16[1,128,128]{2,1,0:T(8,128)(2,1)S(1)}, u32[]{:S(2)}, u32[]{:S(2)}) collective-permute-start(bf16[1,128,128]{2,1,0:T(8,128)(2,1)S(1)} %maximum_bitcast_fusion), channel_id=1, source_target_pairs={{0,12},{1,13},{2,14},{3,15},{4,0},{5,1},{6,2},{7,3},{8,4},{9,5},{1... | collective-permute-start | bytes 98312 | tf_op jit(solution)/shard_map/ppermute | solution.py:199
  7.5 2.4 %collective-permute-done.1 = bf16[1,128,128]{2,1,0:T(8,128)(2,1)S(1)} collective-permute-done((bf16[1,128,128]{2,1,0:T(8,128)(2,1)S(1)}, bf16[1,128,128]{2,1,0:T(8,128)(2,1)S(1)}, u32[]{:S(2)}, u32[]{:S(2)}) %collective-permute-start.1) | collective-permute-done | bytes 32800 | tf_op jit(solution)/shard_map/ppermute | solution.py:199
  10.3 2.8 %collective-permute-start.3 = (bf16[4,128,128]{2,1,0:T(8,128)(2,1)S(1)}, bf16[4,128,128]{2,1,0:T(8,128)(2,1)S(1)}, u32[]{:S(2)}, u32[]{:S(2)}) collective-permute-start(bf16[4,128,128]{2,1,0:T(8,128)(2,1)S(1)} %pad_maximum_fusion), channel_id=1, source_target_pairs={{0,17},{1,16},{2,19},{3,18},{4,21},{5,20},{6,23},{7,22},{8,25},{9,... | collective-permute-start | bytes 393224 | tf_op jit(solution)/shard_map/ppermute | solution.py:199
  18.2 1.5 collective-permute-done.4
  21.8 4.0 %collective-permute-start.6 = (bf16[16,128,128]{2,1,0:T(8,128)(2,1)S(1)}, bf16[16,128,128]{2,1,0:T(8,128)(2,1)S(1)}, u32[]{:S(2)}, u32[]{:S(2)}) collective-permute-start(bf16[16,128,128]{2,1,0:T(8,128)(2,1)S(1)} %get-tuple-element.39), channel_id=1, source_target_pairs={{0,96},{1,97},{2,98},{3,99},{4,100},{5,101},{6,102},{7,103},{8,104... | collective-permute-start | bytes 1572872 | tf_op jit(solution)/shard_map/ppermute | solution.py:199
  27.1 18.3 %collective-permute-done.6 = bf16[16,128,128]{2,1,0:T(8,128)(2,1)S(1)} collective-permute-done((bf16[16,128,128]{2,1,0:T(8,128)(2,1)S(1)}, bf16[16,128,128]{2,1,0:T(8,128)(2,1)S(1)}, u32[]{:S(2)}, u32[]{:S(2)}) %collective-permute-start.6) | collective-permute-done | bytes 524320 | tf_op jit(solution)/shard_map/ppermute | solution.py:199
  51.5 2.7 %slice_subtract_fusion.3 = (s32[2,48,1]{2,1,0:T(8,128)S(1)}, s32[2,48,1]{2,1,0:T(8,128)S(1)}, s32[2,48,1]{2,1,0:T(8,128)S(1)}, s32[2,48,1]{2,1,0:T(8,128)S(1)}) fusion(s32[2,48,4]{2,1,0:T(8,128)S(1)} %bitcast.93, s32[]{:T(128)} %bitcast.1, s32[]{:T(128)} %bitcast.5, s32[]{:T(128)} %bitcast.3, s32[]{:T(128)} %bitcast.7), kind=kLoop, calls=%fused_computation.56 | loop fusion | flops 384 | bytes 3088 | tf_op jit(solution)/shard_map/sub | solution.py:233
  56.1 1.5 gather_fusion.1
  63.9 22.0 %shard_map.93 = (bf16[2,64,1024]{2,1,0:T(8,128)(2,1)}, f32[2,1,1024]{2,1,0:T(1,128)}, f32[2,1,1024]{2,1,0:T(1,128)}) custom-call(s32[2,48]{1,0:T(2,128)} %and_select_fusion.4.lists_ref, s32[2,48]{1,0:T(2,128)} %broadcast_in_dim.22.count_ref, bf16[2,64,1024]{2,1,0:T(8,128)(2,1)} %bitcast.88, ...), custom_call_target="tpu_custom_call" | custom-call | tf_op jit(solution)/shard_map/pallas_call | solution.py:133
  86.0 37.7 %shard_map.94 = (bf16[2,64,1024]{2,1,0:T(8,128)(2,1)}, f32[128,128,128]{2,1,0:T(8,128)}) custom-call(s32[2,48]{1,0:T(2,128)} %and_select_fusion.4.lists_ref, s32[2,48]{1,0:T(2,128)} %broadcast_in_dim.22.count_ref, bf16[2,1024,64]{2,1,0:T(8,128)(2,1)} %copy-done, bf16[2,64,1024]{2,1,0:T(8,128)(2,1)} %bitcast.89, ...), custom_call_target="tpu_custom_call" | custom-call | tf_op jit(solution)/shard_map/pallas_call | solution.py:149
  123.7 2.6 %slice.179 = bf16[64,128,128]{2,1,0:T(8,128)(2,1)S(1)} slice(f32[128,128,128]{2,1,0:T(8,128)} %get-tuple-element.15), slice={[64:128], [0:128], [0:128]} | slice | bytes 4194304 | tf_op jit(solution)/shard_map/slice | solution.py:208
  126.3 2.5 %slice.97 = f32[64,128,128]{2,1,0:T(8,128)S(1)} slice(f32[128,128,128]{2,1,0:T(8,128)} %get-tuple-element.15), slice={[0:64], [0:128], [0:128]} | slice | bytes 8388608 | tf_op jit(solution)/shard_map/slice | solution.py:206
  128.8 1.7 collective-permute-done.12
  130.5 3.0 %fusion.28 = (bf16[4,4,4,128,128]{4,3,2,1,0:T(8,128)(2,1)S(1)}, f32[4,4,4,128,128]{4,3,2,1,0:T(8,128)}) fusion(f32[4,4,4,128,128]{4,3,2,1,0:T(8,128)S(1)} %bitcast.87, bf16[4,4,4,128,128]{4,3,2,1,0:T(8,128)(2,1)S(1)} %collective-permute-done.12), kind=kLoop, calls=%fused_computation.103 | loop fusion | flops 3145728 | bytes 12582912 | tf_op jit(solution)/shard_map/convert.9
  133.6 2.0 %collective-permute-start.14 = (bf16[4,4,128,128]{3,2,1,0:T(8,128)(2,1)S(1)}, bf16[4,4,128,128]{3,2,1,0:T(8,128)(2,1)S(1)}, u32[]{:S(2)}, u32[]{:S(2)}) collective-permute-start(bf16[4,4,128,128]{3,2,1,0:T(8,128)(2,1)S(1)} %get-tuple-element.24), channel_id=1, source_target_pairs={{0,64},{1,65},{2,66},{3,67},{4,68},{5,69},{6,70},{7,71},{8,72},{9,... | collective-permute-start | bytes 1572872 | tf_op jit(solution)/shard_map/ppermute | solution.py:209
  135.6 2.5 %collective-permute-start.15 = (bf16[4,4,128,128]{3,2,1,0:T(8,128)(2,1)S(1)}, bf16[4,4,128,128]{3,2,1,0:T(8,128)(2,1)}, u32[]{:S(2)}, u32[]{:S(2)}) collective-permute-start(bf16[4,4,128,128]{3,2,1,0:T(8,128)(2,1)S(1)} %get-tuple-element.23), channel_id=1, source_target_pairs={{0,96},{1,97},{2,98},{3,99},{4,100},{5,101},{6,102},{7,103},{8,104... | collective-permute-start | bytes 1572872 | tf_op jit(solution)/shard_map/ppermute | solution.py:209
  139.6 20.4 %collective-permute-done.13 = bf16[4,4,128,128]{3,2,1,0:T(8,128)(2,1)S(1)} collective-permute-done((bf16[4,4,128,128]{3,2,1,0:T(8,128)(2,1)S(1)}, bf16[4,4,128,128]{3,2,1,0:T(8,128)(2,1)S(1)}, u32[]{:S(2)}, u32[]{:S(2)}) %collective-permute-start.13) | collective-permute-done | bytes 524320 | tf_op jit(solution)/shard_map/ppermute | solution.py:209
  160.7 1.7 fusion.26
  162.5 1.6 collective-permute-start.17
  164.2 1.8 collective-permute-start.18
  166.6 2.8 %collective-permute-start.10 = (bf16[256,512]{1,0:T(8,128)(2,1)S(1)}, bf16[256,512]{1,0:T(8,128)(2,1)S(1)}, u32[]{:S(2)}, u32[]{:S(2)}) collective-permute-start(bf16[256,512]{1,0:T(8,128)(2,1)S(1)} %reshape.81), channel_id=1, source_target_pairs={{0,1},{1,0},{2,3},{3,2},{4,5},{5,4},{6,7},{7,6},{8,9},{9,8},{10,11... | collective-permute-start | bytes 786440 | tf_op jit(solution)/shard_map/ppermute | solution.py:248
  169.4 2.0 %maximum_select_fusion.1 = bf16[256,1024]{1,0:T(8,128)(2,1)} fusion(bf16[256,512]{1,0:T(8,128)(2,1)} %collective-permute-done.11, bf16[256,512]{1,0:T(8,128)(2,1)S(1)} %reshape.82, pred[]{:T(512)S(6)} %eq.22), kind=kLoop, calls=%fused_computation.12 | loop fusion | flops 2359296 | bytes 1048577 | tf_op jit(solution)/shard_map/jit(_where)/select_n | solution.py:249
  171.4 5.2 %collective-permute-done.16 = bf16[4,128,128]{2,1,0:T(8,128)(2,1)S(1)} collective-permute-done((bf16[4,128,128]{2,1,0:T(8,128)(2,1)S(1)}, bf16[4,128,128]{2,1,0:T(8,128)(2,1)S(1)}, u32[]{:S(2)}, u32[]{:S(2)}) %collective-permute-start.16) | collective-permute-done | bytes 131104 | tf_op jit(solution)/shard_map/ppermute | solution.py:209
  178.2 2.4 %collective-permute-start.21 = (bf16[128,128]{1,0:T(8,128)(2,1)S(1)}, bf16[128,128]{1,0:T(8,128)(2,1)S(1)}, u32[]{:S(2)}, u32[]{:S(2)}) collective-permute-start(bf16[128,128]{1,0:T(8,128)(2,1)S(1)} %get-tuple-element.35), channel_id=1, source_target_pairs={{0,12},{1,13},{2,14},{3,15},{4,0},{5,1},{6,2},{7,3},{8,4},{9,5},{1... | collective-permute-start | bytes 98312 | tf_op jit(solution)/shard_map/ppermute | solution.py:209
  (94 shorter events, 35.2 us)
Async XLA Ops:
  0.6 49.6 %copy-start.2 = (s32[128,4]{1,0:T(8,128)S(1)}, s32[128,4]{1,0:T(8,128)}, u32[]{:S(2)}) copy-start(s32[128,4]{1,0:T(8,128)} %constant.80.clone) | copy-start | bytes 6148
  0.6 49.5 %copy-start.5 = (s32[2,48]{1,0:T(2,128)S(1)}, s32[2,48]{1,0:T(2,128)}, u32[]{:S(2)}) copy-start(s32[2,48]{1,0:T(2,128)} %param.10) | copy-start | bytes 1156
  1.4 6.1 %collective-permute-start = (bf16[1,128,128]{2,1,0:T(8,128)(2,1)S(1)}, bf16[1,128,128]{2,1,0:T(8,128)(2,1)S(1)}, u32[]{:S(2)}, u32[]{:S(2)}) collective-permute-start(bf16[1,128,128]{2,1,0:T(8,128)(2,1)S(1)} %maximum_bitcast_fusion), channel_id=1, source_target_pairs={{0,12},{1,13},{2,14},{3,15},{4,0},{5,1},{6,2},{7,3},{8,4},{9,5},{1... | collective-permute-start | bytes 98312 | tf_op jit(solution)/shard_map/ppermute | solution.py:199
  4.6 5.4 %collective-permute-start.1 = (bf16[1,128,128]{2,1,0:T(8,128)(2,1)S(1)}, bf16[1,128,128]{2,1,0:T(8,128)(2,1)S(1)}, u32[]{:S(2)}, u32[]{:S(2)}) collective-permute-start(bf16[1,128,128]{2,1,0:T(8,128)(2,1)S(1)} %maximum_bitcast_fusion), channel_id=1, source_target_pairs={{0,8},{1,9},{2,10},{3,11},{4,12},{5,13},{6,14},{7,15},{8,0},{9,1},... | collective-permute-start | bytes 98312 | tf_op jit(solution)/shard_map/ppermute | solution.py:199
  5.2 5.1 %collective-permute-start.2 = (bf16[1,128,128]{2,1,0:T(8,128)(2,1)S(1)}, bf16[1,128,128]{2,1,0:T(8,128)(2,1)S(1)}, u32[]{:S(2)}, u32[]{:S(2)}) collective-permute-start(bf16[1,128,128]{2,1,0:T(8,128)(2,1)S(1)} %maximum_bitcast_fusion), channel_id=1, source_target_pairs={{0,4},{1,5},{2,6},{3,7},{4,8},{5,9},{6,10},{7,11},{8,12},{9,13},{1... | collective-permute-start | bytes 98312 | tf_op jit(solution)/shard_map/ppermute | solution.py:199
  10.3 7.1 %collective-permute-start.3 = (bf16[4,128,128]{2,1,0:T(8,128)(2,1)S(1)}, bf16[4,128,128]{2,1,0:T(8,128)(2,1)S(1)}, u32[]{:S(2)}, u32[]{:S(2)}) collective-permute-start(bf16[4,128,128]{2,1,0:T(8,128)(2,1)S(1)} %pad_maximum_fusion), channel_id=1, source_target_pairs={{0,17},{1,16},{2,19},{3,18},{4,21},{5,20},{6,23},{7,22},{8,25},{9,... | collective-permute-start | bytes 393224 | tf_op jit(solution)/shard_map/ppermute | solution.py:199
  13.2 6.6 %collective-permute-start.4 = (bf16[4,128,128]{2,1,0:T(8,128)(2,1)S(1)}, bf16[4,128,128]{2,1,0:T(8,128)(2,1)S(1)}, u32[]{:S(2)}, u32[]{:S(2)}) collective-permute-start(bf16[4,128,128]{2,1,0:T(8,128)(2,1)S(1)} %pad_maximum_fusion), channel_id=1, source_target_pairs={{0,1},{1,0},{2,3},{3,2},{4,5},{5,4},{6,7},{7,6},{8,9},{9,8},{10,11... | collective-permute-start | bytes 393224 | tf_op jit(solution)/shard_map/ppermute | solution.py:199
  14.0 7.1 %collective-permute-start.5 = (bf16[4,128,128]{2,1,0:T(8,128)(2,1)S(1)}, bf16[4,128,128]{2,1,0:T(8,128)(2,1)S(1)}, u32[]{:S(2)}, u32[]{:S(2)}) collective-permute-start(bf16[4,128,128]{2,1,0:T(8,128)(2,1)S(1)} %pad_maximum_fusion), channel_id=1, source_target_pairs={{0,16},{1,17},{2,18},{3,19},{4,20},{5,21},{6,22},{7,23},{8,24},{9,... | collective-permute-start | bytes 393224 | tf_op jit(solution)/shard_map/ppermute | solution.py:199
  21.8 23.6 %collective-permute-start.6 = (bf16[16,128,128]{2,1,0:T(8,128)(2,1)S(1)}, bf16[16,128,128]{2,1,0:T(8,128)(2,1)S(1)}, u32[]{:S(2)}, u32[]{:S(2)}) collective-permute-start(bf16[16,128,128]{2,1,0:T(8,128)(2,1)S(1)} %get-tuple-element.39), channel_id=1, source_target_pairs={{0,96},{1,97},{2,98},{3,99},{4,100},{5,101},{6,102},{7,103},{8,104... | collective-permute-start | bytes 1572872 | tf_op jit(solution)/shard_map/ppermute | solution.py:199
  25.9 20.8 %collective-permute-start.7 = (bf16[16,128,128]{2,1,0:T(8,128)(2,1)S(1)}, bf16[16,128,128]{2,1,0:T(8,128)(2,1)S(1)}, u32[]{:S(2)}, u32[]{:S(2)}) collective-permute-start(bf16[16,128,128]{2,1,0:T(8,128)(2,1)S(1)} %get-tuple-element.39), channel_id=1, source_target_pairs={{0,64},{1,65},{2,66},{3,67},{4,68},{5,69},{6,70},{7,71},{8,72},{9,... | collective-permute-start | bytes 1572872 | tf_op jit(solution)/shard_map/ppermute | solution.py:199
  25.9 23.0 %collective-permute-start.8 = (bf16[16,128,128]{2,1,0:T(8,128)(2,1)S(1)}, bf16[16,128,128]{2,1,0:T(8,128)(2,1)S(1)}, u32[]{:S(2)}, u32[]{:S(2)}) collective-permute-start(bf16[16,128,128]{2,1,0:T(8,128)(2,1)S(1)} %get-tuple-element.39), channel_id=1, source_target_pairs={{0,32},{1,33},{2,34},{3,35},{4,36},{5,37},{6,38},{7,39},{8,40},{9,... | collective-permute-start | bytes 1572872 | tf_op jit(solution)/shard_map/ppermute | solution.py:199
  50.1 11.6 %collective-permute-start.9 = (bf16[64,128,128]{2,1,0:T(8,128)(2,1)}, bf16[64,128,128]{2,1,0:T(8,128)(2,1)S(1)}, u32[]{:S(2)}, u32[]{:S(2)}) collective-permute-start(bf16[64,128,128]{2,1,0:T(8,128)(2,1)} %get-tuple-element.28), channel_id=1, source_target_pairs={{0,2},{1,3},{2,0},{3,1},{4,6},{5,7},{6,4},{7,5},{8,10},{9,11},{10,... | collective-permute-start | bytes 6291464 | tf_op jit(solution)/shard_map/ppermute | solution.py:199
  126.2 4.2 %collective-permute-start.12 = (bf16[4,4,4,128,128]{4,3,2,1,0:T(8,128)(2,1)S(1)}, bf16[4,4,4,128,128]{4,3,2,1,0:T(8,128)(2,1)S(1)}, u32[]{:S(2)}, u32[]{:S(2)}) collective-permute-start(bf16[4,4,4,128,128]{4,3,2,1,0:T(8,128)(2,1)S(1)} %bitcast.92), channel_id=1, source_target_pairs={{0,2},{1,3},{2,0},{3,1},{4,6},{5,7},{6,4},{7,5},{8,10},{9,11},{10,... | collective-permute-start | bytes 6291464 | tf_op jit(solution)/shard_map/ppermute | solution.py:209
  133.5 26.5 %collective-permute-start.13 = (bf16[4,4,128,128]{3,2,1,0:T(8,128)(2,1)S(1)}, bf16[4,4,128,128]{3,2,1,0:T(8,128)(2,1)S(1)}, u32[]{:S(2)}, u32[]{:S(2)}) collective-permute-start(bf16[4,4,128,128]{3,2,1,0:T(8,128)(2,1)S(1)} %get-tuple-element.22), channel_id=1, source_target_pairs={{0,32},{1,33},{2,34},{3,35},{4,36},{5,37},{6,38},{7,39},{8,40},{9,... | collective-permute-start | bytes 1572872 | tf_op jit(solution)/shard_map/ppermute | solution.py:209
  133.6 26.4 %collective-permute-start.14 = (bf16[4,4,128,128]{3,2,1,0:T(8,128)(2,1)S(1)}, bf16[4,4,128,128]{3,2,1,0:T(8,128)(2,1)S(1)}, u32[]{:S(2)}, u32[]{:S(2)}) collective-permute-start(bf16[4,4,128,128]{3,2,1,0:T(8,128)(2,1)S(1)} %get-tuple-element.24), channel_id=1, source_target_pairs={{0,64},{1,65},{2,66},{3,67},{4,68},{5,69},{6,70},{7,71},{8,72},{9,... | collective-permute-start | bytes 1572872 | tf_op jit(solution)/shard_map/ppermute | solution.py:209
  135.6 25.2 %collective-permute-start.15 = (bf16[4,4,128,128]{3,2,1,0:T(8,128)(2,1)S(1)}, bf16[4,4,128,128]{3,2,1,0:T(8,128)(2,1)}, u32[]{:S(2)}, u32[]{:S(2)}) collective-permute-start(bf16[4,4,128,128]{3,2,1,0:T(8,128)(2,1)S(1)} %get-tuple-element.23), channel_id=1, source_target_pairs={{0,96},{1,97},{2,98},{3,99},{4,100},{5,101},{6,102},{7,103},{8,104... | collective-permute-start | bytes 1572872 | tf_op jit(solution)/shard_map/ppermute | solution.py:209
  138.7 30.7 %collective-permute-start.11 = (bf16[256,512]{1,0:T(8,128)(2,1)S(1)}, bf16[256,512]{1,0:T(8,128)(2,1)}, u32[]{:S(2)}, u32[]{:S(2)}) collective-permute-start(bf16[256,512]{1,0:T(8,128)(2,1)S(1)} %reshape.82), channel_id=1, source_target_pairs={{0,1},{1,0},{2,3},{3,2},{4,5},{5,4},{6,7},{7,6},{8,9},{9,8},{10,11... | collective-permute-start | bytes 786440 | tf_op jit(solution)/shard_map/ppermute | solution.py:248
  162.5 14.1 %collective-permute-start.16 = (bf16[4,128,128]{2,1,0:T(8,128)(2,1)S(1)}, bf16[4,128,128]{2,1,0:T(8,128)(2,1)S(1)}, u32[]{:S(2)}, u32[]{:S(2)}) collective-permute-start(bf16[4,128,128]{2,1,0:T(8,128)(2,1)S(1)} %get-tuple-element.25), channel_id=1, source_target_pairs={{0,16},{1,17},{2,18},{3,19},{4,20},{5,21},{6,22},{7,23},{8,24},{9,... | collective-permute-start | bytes 393224 | tf_op jit(solution)/shard_map/ppermute | solution.py:209
  162.5 14.0 %collective-permute-start.17 = (bf16[4,128,128]{2,1,0:T(8,128)(2,1)S(1)}, bf16[4,128,128]{2,1,0:T(8,128)(2,1)S(1)}, u32[]{:S(2)}, u32[]{:S(2)}) collective-permute-start(bf16[4,128,128]{2,1,0:T(8,128)(2,1)S(1)} %get-tuple-element.27), channel_id=1, source_target_pairs={{0,1},{1,0},{2,3},{3,2},{4,5},{5,4},{6,7},{7,6},{8,9},{9,8},{10,11... | collective-permute-start | bytes 393224 | tf_op jit(solution)/shard_map/ppermute | solution.py:209
  164.2 12.4 %collective-permute-start.18 = (bf16[4,128,128]{2,1,0:T(8,128)(2,1)S(1)}, bf16[4,128,128]{2,1,0:T(8,128)(2,1)S(1)}, u32[]{:S(2)}, u32[]{:S(2)}) collective-permute-start(bf16[4,128,128]{2,1,0:T(8,128)(2,1)S(1)} %get-tuple-element.26), channel_id=1, source_target_pairs={{0,17},{1,16},{2,19},{3,18},{4,21},{5,20},{6,23},{7,22},{8,25},{9,... | collective-permute-start | bytes 393224 | tf_op jit(solution)/shard_map/ppermute | solution.py:209
  166.6 14.0 %collective-permute-start.10 = (bf16[256,512]{1,0:T(8,128)(2,1)S(1)}, bf16[256,512]{1,0:T(8,128)(2,1)S(1)}, u32[]{:S(2)}, u32[]{:S(2)}) collective-permute-start(bf16[256,512]{1,0:T(8,128)(2,1)S(1)} %reshape.81), channel_id=1, source_target_pairs={{0,1},{1,0},{2,3},{3,2},{4,5},{5,4},{6,7},{7,6},{8,9},{9,8},{10,11... | collective-permute-start | bytes 786440 | tf_op jit(solution)/shard_map/ppermute | solution.py:248
  176.7 5.2 %collective-permute-start.19 = (bf16[128,128]{1,0:T(8,128)(2,1)S(1)}, bf16[128,128]{1,0:T(8,128)(2,1)S(1)}, u32[]{:S(2)}, u32[]{:S(2)}) collective-permute-start(bf16[128,128]{1,0:T(8,128)(2,1)S(1)} %get-tuple-element.34), channel_id=1, source_target_pairs={{0,4},{1,5},{2,6},{3,7},{4,8},{5,9},{6,10},{7,11},{8,12},{9,13},{1... | collective-permute-start | bytes 98312 | tf_op jit(solution)/shard_map/ppermute | solution.py:209
  176.7 5.5 %collective-permute-start.20 = (bf16[128,128]{1,0:T(8,128)(2,1)S(1)}, bf16[128,128]{1,0:T(8,128)(2,1)S(1)}, u32[]{:S(2)}, u32[]{:S(2)}) collective-permute-start(bf16[128,128]{1,0:T(8,128)(2,1)S(1)} %get-tuple-element.36), channel_id=1, source_target_pairs={{0,8},{1,9},{2,10},{3,11},{4,12},{5,13},{6,14},{7,15},{8,0},{9,1},... | collective-permute-start | bytes 98312 | tf_op jit(solution)/shard_map/ppermute | solution.py:209
  178.2 4.8 %collective-permute-start.21 = (bf16[128,128]{1,0:T(8,128)(2,1)S(1)}, bf16[128,128]{1,0:T(8,128)(2,1)S(1)}, u32[]{:S(2)}, u32[]{:S(2)}) collective-permute-start(bf16[128,128]{1,0:T(8,128)(2,1)S(1)} %get-tuple-element.35), channel_id=1, source_target_pairs={{0,12},{1,13},{2,14},{3,15},{4,0},{5,1},{6,2},{7,3},{8,4},{9,5},{1... | collective-permute-start | bytes 98312 | tf_op jit(solution)/shard_map/ppermute | solution.py:209
  (4 other events, 66.2 us)

commit v9 on v8

--- a/solution.py
+++ b/solution.py
@@ -72,7 +72,7 @@
 def _forward_kernel(lists_ref, count_ref, qt_ref, kvt_ref, dot_ref,
                     ot_ref, lse_ref, delta_ref, m_sc, l_sc, acc_sc):
     query_count = lists_ref.shape[0]
-    for qb in range(query_count):
+    def per_query(qb, carry):
         m_sc[...] = jnp.full(m_sc.shape, LOWEST, jnp.float32)
         l_sc[...] = jnp.zeros(l_sc.shape, jnp.float32)
         acc_sc[...] = jnp.zeros(acc_sc.shape, jnp.float32)
@@ -94,13 +94,16 @@
         ot_ref[qb] = out.astype(jnp.bfloat16)
         lse_ref[qb] = m_sc[...] + jnp.log(l_sc[...])
         delta_ref[qb] = jnp.sum(dot_ref[qb].astype(jnp.float32) * out, axis=0, keepdims=True)
+        return carry
+
+    lax.fori_loop(0, query_count, per_query, 0)
 
 
 def _backward_kernel(lists_ref, count_ref, q_ref, qt_ref, kvt_ref, do_ref, dot_ref, lse_ref,
                      delta_ref, dqt_ref, dkvt_ref, dq_sc):
     query_count = lists_ref.shape[0]
     dkvt_ref[...] = jnp.zeros(dkvt_ref.shape, jnp.float32)
-    for qb in range(query_count):
+    def per_query(qb, carry):
         dq_sc[...] = jnp.zeros(dq_sc.shape, jnp.float32)
 
         def visit(slots, qb=qb):
@@ -119,6 +122,9 @@
 
         _visit_slots(count_ref, qb, visit)
         dqt_ref[qb] = (dq_sc[...] * SCALE).astype(jnp.bfloat16)
+        return carry
+
+    lax.fori_loop(0, query_count, per_query, 0)
 
 
 def attend_local(q_rows, do_rows, kv_t, lists, keep):
@@ -172,8 +178,9 @@
     flat = mesh.devices.reshape(-1)
     table = np.array([[*d.coords, d.core_on_chip] for d in flat], dtype=np.int32)
     sizes = table.max(axis=0) + 1
-    stages = [(1, int(sizes[1])), (0, int(sizes[0])), (2, int(sizes[2])), (3, int(sizes[3]))]
-    stages = [(axis, size) for axis, size in stages if size > 1]
+    orders = [(1, 0, 2), (2, 1, 0), (0, 2, 1)]
+    stage_sets = [[(axis, int(sizes[axis])) for axis in order + (3,) if sizes[axis] > 1]
+                  for order in orders]
     where = {tuple(row): index for index, row in enumerate(table.tolist())}
 
     def pairs(axis, shift):
@@ -184,31 +191,66 @@
             out.append((index, where[tuple(dest)]))
         return out
 
-    return table, stages, pairs
+    return table, stage_sets, pairs
+
+
+CHUNK_ROWS = (48, 48, 32)
 
 
 def make_local(mesh):
-    table_np, stages, pairs = device_table(mesh)
+    table_np, stage_sets, pairs = device_table(mesh)
+    stages = stage_sets[0]
     axes = ("blk", "split")
 
-    def gather_blocks(piece):
+    def gather_blocks(piece, order):
         buf = piece[None]
-        for axis, size in stages:
+        for axis, size in order:
             pieces = [buf]
             for shift in range(1, size):
                 pieces.append(lax.ppermute(buf, axes, pairs(axis, size - shift)))
             buf = jnp.concatenate(pieces, axis=0)
         return buf
 
-    def scatter_sum(part, piece_shape):
-        part = part.reshape(tuple(size for _, size in reversed(stages)) + piece_shape)
-        for axis, size in reversed(stages):
+    def reorder(buf, order_from, order_to):
+        dims_from = [axis for axis, _ in reversed(order_from)]
+        dims_to = [axis for axis, _ in reversed(order_to)]
+        if dims_from == dims_to:
+            return buf
+        sizes = [size for _, size in reversed(order_from)]
+        inner = buf.shape[1:]
+        held = buf.reshape(tuple(sizes) + inner)
+        perm = [dims_from.index(axis) for axis in dims_to]
+        perm += list(range(len(sizes), len(sizes) + len(inner)))
+        return jnp.transpose(held, perm).reshape(buf.shape)
+
+    def scatter_sum(part, order):
+        piece_shape = part.shape[1:]
+        part = part.reshape(tuple(size for _, size in reversed(order)) + piece_shape)
+        for axis, size in reversed(order):
             total = part[0]
             for shift in range(1, size):
                 sent = part[shift].astype(jnp.bfloat16)
                 total = total + lax.ppermute(sent, axes, pairs(axis, shift)).astype(jnp.float32)
             part = total
         return part
+
+    def chunk_bounds():
+        first = 0
+        for rows in CHUNK_ROWS:
+            yield first, first + rows
+            first += rows
+
+    def gather_all(piece):
+        held = []
+        for (lo, hi), order in zip(chunk_bounds(), stage_sets):
+            held.append(reorder(gather_blocks(piece[lo:hi], order), order, stages))
+        return jnp.concatenate(held, axis=1)
+
+    def scatter_all(part):
+        owned = []
+        for (lo, hi), order in zip(chunk_bounds(), stage_sets):
+            owned.append(scatter_sum(reorder(part[:, lo:hi], stages, order), order))
+        return jnp.concatenate(owned, axis=0)
 
     def local(queries, keys, values, out_grad, block_lists):
         query_count = block_lists.shape[0]
@@ -222,7 +264,7 @@
         table = jnp.asarray(table_np)
         own = table[me]
 
-        kv_t = gather_blocks(jnp.concatenate([keys.T, values.T], axis=0))
+        kv_t = gather_all(jnp.concatenate([keys.T, values.T], axis=0))
         block_total = kv_t.shape[0]
 
         def held_at(block):
@@ -252,7 +294,7 @@
 
         attended = join_halves(o_rows)
         query_grad = join_halves(dq_rows)
-        owned = scatter_sum(dkv_t, (2 * HEAD_DIM, BLOCK))
+        owned = scatter_all(dkv_t)
         key_grad = (owned[:HEAD_DIM].T * SCALE).astype(jnp.bfloat16)
         value_grad = owned[HEAD_DIM:].T.astype(jnp.bfloat16)
         return (attended, query_grad, key_grad, value_grad)

time: 186 us -> 242 us (1.30)
  starting transfers between devices: 30.3 us -> 122 us
  Pallas kernels: 59.7 us -> 22.6 us
  waiting for transfers between devices: 54.3 us -> 22.9 us
  local copies, waits for them, and re-layouts: 24.1 us -> 55.4 us
    ppermute x10 -> x30, starting transfers between devices: 12.1 us -> 75.7 us  [scatter_sum(): lax.ppermute(sent, axes, pairs(axis, shift)).astype(jnp.float32)]
    ppermute x10 -> x30, starting transfers between devices: 14.5 us -> 43.1 us  [gather_blocks(): pieces.append(lax.ppermute(buf, axes, pairs(axis, size - shift)))]
    pallas_call x1, Pallas kernels: 37.7 us -> 14.3 us  [attend_local(): pl.pallas_call(_backward_kernel, out_shape=(jax.ShapeDtypeStruct((query_c...]
    ppermute x10 -> x30, waiting for transfers between devices: 24.7 us -> 6.55 us  [gather_blocks(): pieces.append(lax.ppermute(buf, axes, pairs(axis, size - shift)))]
    pallas_call x1, Pallas kernels: 22 us -> 8.29 us  [attend_local(): pl.pallas_call(_forward_kernel, out_shape=(jax.ShapeDtypeStruct((query_co...]
    unnamed x24 -> x46, local copies, waits for them, and re-layouts: 7.1 us -> 20.5 us
    ppermute x10 -> x30, waiting for transfers between devices: 29.6 us -> 16.4 us  [scatter_sum(): lax.ppermute(sent, axes, pairs(axis, shift)).astype(jnp.float32)]
    slice x0 -> x2, local copies, waits for them, and re-layouts: none -> 3.89 us  [scatter_all(): owned.append(scatter_sum(reorder(part[:, lo:hi], stages, order), order))]
  transfers between devices with their start and end apart: 22 -> 62, of which waited for: 14 -> 15; matrix products, arithmetic and copies ran while one was open for 15% -> 25% of each run, Pallas kernels for 0% -> 0%
where the time goes in v9:
time: 242 us; the launch traced here: 241 us
  starting transfers between devices  122 us (50%)
  local copies, waits for them, and re-layouts  55.4 us (23%)
  waiting for transfers between devices  22.9 us (9%)
  Pallas kernels  22.6 us (9%)
  other arithmetic  16.3 us (7%)
    ppermute x30, starting transfers between devices, scatter_sum(): lax.ppermute(sent, axes, pairs(axis, shift)).astype(jnp.float32)  75.7 us
    ppermute x30, starting transfers between devices, gather_blocks(): pieces.append(lax.ppermute(buf, axes, pairs(axis, size - shift)))  43.1 us
    unnamed x46, local copies, waits for them, and re-layouts  20.5 us
    ppermute x30, waiting for transfers between devices, scatter_sum(): lax.ppermute(sent, axes, pairs(axis, shift)).astype(jnp.float32)  16.4 us
    pallas_call x1, Pallas kernels, attend_local(): pl.pallas_call(_backward_kernel, out_shape=(jax.ShapeDtypeStruct((query_c...  14.3 us
    pallas_call x1, Pallas kernels, attend_local(): pl.pallas_call(_forward_kernel, out_shape=(jax.ShapeDtypeStruct((query_co...  8.29 us
    concatenate x6, local copies, waits for them, and re-layouts, gather_blocks(): buf = jnp.concatenate(pieces, axis=0)  6.67 us
    ppermute x30, waiting for transfers between devices, gather_blocks(): pieces.append(lax.ppermute(buf, axes, pairs(axis, size - shift)))  6.55 us
  transfers between devices with their start and end apart: 62, of which 15 were waited for; matrix products, arithmetic and copies ran while one was open for 25% of the time, Pallas kernels for 0%

profile of v9, /device:TPU:0, one launch (start us, length us, event | category | flops | bytes accessed | tf_op | source)
XLA Modules:
  0.0 240.8 jit_solution(609276735791261106)
XLA Ops:
  2.9 2.7 %collective-permute-start.21 = (bf16[1,32,128]{2,1,0:T(8,128)(2,1)S(1)}, bf16[1,32,128]{2,1,0:T(8,128)(2,1)S(1)}, u32[]{:S(2)}, u32[]{:S(2)}) collective-permute-start(bf16[1,32,128]{2,1,0:T(8,128)(2,1)S(1)} %slice_bitcast_fusion.39), channel_id=1, source_target_pairs={{0,1},{1,0},{2,3},{3,2},{4,5},{5,4},{6,7},{7,6},{8,9},{9,8},{10,11... | collective-permute-start | bytes 24584 | tf_op jit(solution)/shard_map/ppermute | solution.py:210
  9.4 2.9 %collective-permute-start.1 = (bf16[1,48,128]{2,1,0:T(8,128)(2,1)S(1)}, bf16[1,48,128]{2,1,0:T(8,128)(2,1)S(1)}, u32[]{:S(2)}, u32[]{:S(2)}) collective-permute-start(bf16[1,48,128]{2,1,0:T(8,128)(2,1)S(1)} %slice_bitcast_fusion.35), channel_id=1, source_target_pairs={{0,8},{1,9},{2,10},{3,11},{4,12},{5,13},{6,14},{7,15},{8,0},{9,1},... | collective-permute-start | bytes 36872 | tf_op jit(solution)/shard_map/ppermute | solution.py:210
  20.8 2.7 %slice_subtract_fusion.3 = (s32[2,48,1]{2,1,0:T(8,128)S(1)}, s32[2,48,1]{2,1,0:T(8,128)S(1)}, s32[2,48,1]{2,1,0:T(8,128)S(1)}, s32[2,48,1]{2,1,0:T(8,128)S(1)}) fusion(s32[2,48,4]{2,1,0:T(8,128)S(1)} %bitcast.233, s32[]{:T(128)} %bitcast.1, s32[]{:T(128)} %bitcast.5, s32[]{:T(128)} %bitcast.3, s32[]{:T(128)} %bitcast.7), kind=kLoop, calls=%fused_computation.143 | loop fusion | flops 384 | bytes 3088 | tf_op jit(solution)/shard_map/sub | solution.py:275
  27.8 3.6 %collective-permute-start.11 = (bf16[1,48,128]{2,1,0:T(8,128)(2,1)S(1)}, bf16[1,48,128]{2,1,0:T(8,128)(2,1)S(1)}, u32[]{:S(2)}, u32[]{:S(2)}) collective-permute-start(bf16[1,48,128]{2,1,0:T(8,128)(2,1)S(1)} %get-tuple-element.118), channel_id=1, source_target_pairs={{0,64},{1,65},{2,66},{3,67},{4,68},{5,69},{6,70},{7,71},{8,72},{9,... | collective-permute-start | bytes 36872 | tf_op jit(solution)/shard_map/ppermute | solution.py:210
  37.6 2.2 collective-permute-start.23
  55.2 2.6 %collective-permute-start.26 = (bf16[16,32,128]{2,1,0:T(8,128)(2,1)}, bf16[16,32,128]{2,1,0:T(8,128)(2,1)S(1)}, u32[]{:S(2)}, u32[]{:S(2)}) collective-permute-start(bf16[16,32,128]{2,1,0:T(8,128)(2,1)} %get-tuple-element.107), channel_id=1, source_target_pairs={{0,12},{1,13},{2,14},{3,15},{4,0},{5,1},{6,2},{7,3},{8,4},{9,5},{1... | collective-permute-start | bytes 393224 | tf_op jit(solution)/shard_map/ppermute | solution.py:210
  59.5 2.4 collective-permute-start.7
  62.6 2.2 collective-permute-start.6
  75.7 2.8 %collective-permute-done.18 = bf16[16,48,128]{2,1,0:T(8,128)(2,1)S(1)} collective-permute-done((bf16[16,48,128]{2,1,0:T(8,128)(2,1)}, bf16[16,48,128]{2,1,0:T(8,128)(2,1)S(1)}, u32[]{:S(2)}, u32[]{:S(2)}) %collective-permute-start.18) | collective-permute-done | bytes 196640 | tf_op jit(solution)/shard_map/ppermute | solution.py:210
  93.8 2.4 pad_maximum_fusion.kvt_ref
  96.8 8.3 %shard_map.93 = (bf16[2,64,1024]{2,1,0:T(8,128)(2,1)}, f32[2,1,1024]{2,1,0:T(1,128)}, f32[2,1,1024]{2,1,0:T(1,128)}) custom-call(s32[2,48]{1,0:T(2,128)} %and_select_fusion.4.lists_ref, s32[2,48]{1,0:T(2,128)} %broadcast_in_dim.28.count_ref, bf16[2,64,1024]{2,1,0:T(8,128)(2,1)} %bitcast.230, bf16[128,128,128]{2,1,0:T(8,128)(2,1)} %pad_maximum_fusion.kvt_ref, ...), custom_call_target="tpu_custom_call" | custom-call | tf_op jit(solution)/shard_map/pallas_call | solution.py:139
  105.1 14.3 %shard_map.94 = (bf16[2,64,1024]{2,1,0:T(8,128)(2,1)}, f32[128,128,128]{2,1,0:T(8,128)}) custom-call(s32[2,48]{1,0:T(2,128)} %and_select_fusion.4.lists_ref, s32[2,48]{1,0:T(2,128)} %broadcast_in_dim.28.count_ref, bf16[2,1024,64]{2,1,0:T(8,128)(2,1)} %copy-done.4, bf16[2,64,1024]{2,1,0:T(8,128)(2,1)} %bitcast.231, ...), custom_call_target="tpu_custom_call" | custom-call | tf_op jit(solution)/shard_map/pallas_call | solution.py:155
  123.6 2.8 %slice.224 = f32[64,48,128]{2,1,0:T(8,128)} slice(f32[128,128,128]{2,1,0:T(8,128)} %get-tuple-element.15), slice={[0:64], [0:48], [0:128]} | slice | bytes 3145728 | tf_op jit(solution)/shard_map/slice | solution.py:230
  141.5 34.9 %collective-permute-start.53 = (bf16[4,4,32,128]{3,2,1,0:T(8,128)(2,1)S(1)}, bf16[4,4,32,128]{3,2,1,0:T(8,128)(2,1)S(1)}, u32[]{:S(2)}, u32[]{:S(2)}) collective-permute-start(bf16[4,4,32,128]{3,2,1,0:T(8,128)(2,1)S(1)} %get-tuple-element.44), channel_id=1, source_target_pairs={{0,4},{1,5},{2,6},{3,7},{4,8},{5,9},{6,10},{7,11},{8,12},{9,13},{1... | collective-permute-start | bytes 393224 | tf_op jit(solution)/shard_map/ppermute | solution.py:233
  176.3 5.1 %collective-permute-start.54 = (bf16[4,4,32,128]{3,2,1,0:T(8,128)(2,1)S(1)}, bf16[4,4,32,128]{3,2,1,0:T(8,128)(2,1)S(1)}, u32[]{:S(2)}, u32[]{:S(2)}) collective-permute-start(bf16[4,4,32,128]{3,2,1,0:T(8,128)(2,1)S(1)} %get-tuple-element.46), channel_id=1, source_target_pairs={{0,8},{1,9},{2,10},{3,11},{4,12},{5,13},{6,14},{7,15},{8,0},{9,1},... | collective-permute-start | bytes 393224 | tf_op jit(solution)/shard_map/ppermute | solution.py:233
  185.5 6.4 %collective-permute-start.58 = (bf16[4,32,128]{2,1,0:T(8,128)(2,1)S(1)}, bf16[4,32,128]{2,1,0:T(8,128)(2,1)S(1)}, u32[]{:S(2)}, u32[]{:S(2)}) collective-permute-start(bf16[4,32,128]{2,1,0:T(8,128)(2,1)S(1)} %get-tuple-element.66), channel_id=1, source_target_pairs={{0,96},{1,97},{2,98},{3,99},{4,100},{5,101},{6,102},{7,103},{8,104... | collective-permute-start | bytes 98312 | tf_op jit(solution)/shard_map/ppermute | solution.py:233
  193.3 2.1 maximum_select_fusion
  197.4 3.2 %collective-permute-start.61 = (bf16[32,128]{1,0:T(8,128)(2,1)S(1)}, bf16[32,128]{1,0:T(8,128)(2,1)S(1)}, u32[]{:S(2)}, u32[]{:S(2)}) collective-permute-start(bf16[32,128]{1,0:T(8,128)(2,1)S(1)} %get-tuple-element.103), channel_id=1, source_target_pairs={{0,17},{1,16},{2,19},{3,18},{4,21},{5,20},{6,23},{7,22},{8,25},{9,... | collective-permute-start | bytes 24584 | tf_op jit(solution)/shard_map/ppermute | solution.py:233
  202.3 3.5 %collective-permute-done.60 = bf16[32,128]{1,0:T(8,128)(2,1)S(1)} collective-permute-done((bf16[32,128]{1,0:T(8,128)(2,1)S(1)}, bf16[32,128]{1,0:T(8,128)(2,1)S(1)}, u32[]{:S(2)}, u32[]{:S(2)}) %collective-permute-start.60) | collective-permute-done | bytes 8224 | tf_op jit(solution)/shard_map/ppermute | solution.py:233
  206.3 3.2 %collective-permute-start.35 = (bf16[4,4,48,128]{3,2,1,0:T(8,128)(2,1)S(1)}, bf16[4,4,48,128]{3,2,1,0:T(8,128)(2,1)S(1)}, u32[]{:S(2)}, u32[]{:S(2)}) collective-permute-start(bf16[4,4,48,128]{3,2,1,0:T(8,128)(2,1)S(1)} %get-tuple-element.39), channel_id=1, source_target_pairs={{0,96},{1,97},{2,98},{3,99},{4,100},{5,101},{6,102},{7,103},{8,104... | collective-permute-start | bytes 589832 | tf_op jit(solution)/shard_map/ppermute | solution.py:233
  210.1 3.2 %collective-permute-start.45 = (bf16[4,4,48,128]{3,2,1,0:T(8,128)(2,1)S(1)}, bf16[4,4,48,128]{3,2,1,0:T(8,128)(2,1)S(1)}, u32[]{:S(2)}, u32[]{:S(2)}) collective-permute-start(bf16[4,4,48,128]{3,2,1,0:T(8,128)(2,1)S(1)} %get-tuple-element.42), channel_id=1, source_target_pairs={{0,17},{1,16},{2,19},{3,18},{4,21},{5,20},{6,23},{7,22},{8,25},{9,... | collective-permute-start | bytes 589832 | tf_op jit(solution)/shard_map/ppermute | solution.py:233
  216.9 3.2 %collective-permute-start.38 = (bf16[4,48,128]{2,1,0:T(8,128)(2,1)S(1)}, bf16[4,48,128]{2,1,0:T(8,128)(2,1)S(1)}, u32[]{:S(2)}, u32[]{:S(2)}) collective-permute-start(bf16[4,48,128]{2,1,0:T(8,128)(2,1)S(1)} %get-tuple-element.48), channel_id=1, source_target_pairs={{0,17},{1,16},{2,19},{3,18},{4,21},{5,20},{6,23},{7,22},{8,25},{9,... | collective-permute-start | bytes 147464 | tf_op jit(solution)/shard_map/ppermute | solution.py:233
  231.4 3.0 %collective-permute-start.51 = (bf16[48,128]{1,0:T(8,128)(2,1)S(1)}, bf16[48,128]{1,0:T(8,128)(2,1)S(1)}, u32[]{:S(2)}, u32[]{:S(2)}) collective-permute-start(bf16[48,128]{1,0:T(8,128)(2,1)S(1)} %get-tuple-element.78), channel_id=1, source_target_pairs={{0,96},{1,97},{2,98},{3,99},{4,100},{5,101},{6,102},{7,103},{8,104... | collective-permute-start | bytes 36872 | tf_op jit(solution)/shard_map/ppermute | solution.py:233
  236.0 3.5 %collective-permute-done.50 = bf16[48,128]{1,0:T(8,128)(2,1)S(1)} collective-permute-done((bf16[48,128]{1,0:T(8,128)(2,1)S(1)}, bf16[48,128]{1,0:T(8,128)(2,1)S(1)}, u32[]{:S(2)}, u32[]{:S(2)}) %collective-permute-start.50) | collective-permute-done | bytes 12320 | tf_op jit(solution)/shard_map/ppermute | solution.py:233
  (226 shorter events, 116.4 us)
Async XLA Ops:
  1.3 23.2 %collective-permute-start.22 = (bf16[1,32,128]{2,1,0:T(8,128)(2,1)S(1)}, bf16[1,32,128]{2,1,0:T(8,128)(2,1)S(1)}, u32[]{:S(2)}, u32[]{:S(2)}) collective-permute-start(bf16[1,32,128]{2,1,0:T(8,128)(2,1)S(1)} %slice_bitcast_fusion.39), channel_id=1, source_target_pairs={{0,16},{1,17},{2,18},{3,19},{4,20},{5,21},{6,22},{7,23},{8,24},{9,... | collective-permute-start | bytes 24584 | tf_op jit(solution)/shard_map/ppermute | solution.py:210
  2.9 22.9 %collective-permute-start.21 = (bf16[1,32,128]{2,1,0:T(8,128)(2,1)S(1)}, bf16[1,32,128]{2,1,0:T(8,128)(2,1)S(1)}, u32[]{:S(2)}, u32[]{:S(2)}) collective-permute-start(bf16[1,32,128]{2,1,0:T(8,128)(2,1)S(1)} %slice_bitcast_fusion.39), channel_id=1, source_target_pairs={{0,1},{1,0},{2,3},{3,2},{4,5},{5,4},{6,7},{7,6},{8,9},{9,8},{10,11... | collective-permute-start | bytes 24584 | tf_op jit(solution)/shard_map/ppermute | solution.py:210
  5.7 22.1 %collective-permute-start.20 = (bf16[1,32,128]{2,1,0:T(8,128)(2,1)S(1)}, bf16[1,32,128]{2,1,0:T(8,128)(2,1)S(1)}, u32[]{:S(2)}, u32[]{:S(2)}) collective-permute-start(bf16[1,32,128]{2,1,0:T(8,128)(2,1)S(1)} %slice_bitcast_fusion.39), channel_id=1, source_target_pairs={{0,17},{1,16},{2,19},{3,18},{4,21},{5,20},{6,23},{7,22},{8,25},{9,... | collective-permute-start | bytes 24584 | tf_op jit(solution)/shard_map/ppermute | solution.py:210
  7.8 25.4 %collective-permute-start.2 = (bf16[1,48,128]{2,1,0:T(8,128)(2,1)S(1)}, bf16[1,48,128]{2,1,0:T(8,128)(2,1)S(1)}, u32[]{:S(2)}, u32[]{:S(2)}) collective-permute-start(bf16[1,48,128]{2,1,0:T(8,128)(2,1)S(1)} %slice_bitcast_fusion.35), channel_id=1, source_target_pairs={{0,4},{1,5},{2,6},{3,7},{4,8},{5,9},{6,10},{7,11},{8,12},{9,13},{1... | collective-permute-start | bytes 36872 | tf_op jit(solution)/shard_map/ppermute | solution.py:210
  9.4 24.8 %collective-permute-start.1 = (bf16[1,48,128]{2,1,0:T(8,128)(2,1)S(1)}, bf16[1,48,128]{2,1,0:T(8,128)(2,1)S(1)}, u32[]{:S(2)}, u32[]{:S(2)}) collective-permute-start(bf16[1,48,128]{2,1,0:T(8,128)(2,1)S(1)} %slice_bitcast_fusion.35), channel_id=1, source_target_pairs={{0,8},{1,9},{2,10},{3,11},{4,12},{5,13},{6,14},{7,15},{8,0},{9,1},... | collective-permute-start | bytes 36872 | tf_op jit(solution)/shard_map/ppermute | solution.py:210
  25.9 11.7 %collective-permute-start.12 = (bf16[1,48,128]{2,1,0:T(8,128)(2,1)S(1)}, bf16[1,48,128]{2,1,0:T(8,128)(2,1)S(1)}, u32[]{:S(2)}, u32[]{:S(2)}) collective-permute-start(bf16[1,48,128]{2,1,0:T(8,128)(2,1)S(1)} %get-tuple-element.118), channel_id=1, source_target_pairs={{0,32},{1,33},{2,34},{3,35},{4,36},{5,37},{6,38},{7,39},{8,40},{9,... | collective-permute-start | bytes 36872 | tf_op jit(solution)/shard_map/ppermute | solution.py:210
  27.8 12.1 %collective-permute-start.11 = (bf16[1,48,128]{2,1,0:T(8,128)(2,1)S(1)}, bf16[1,48,128]{2,1,0:T(8,128)(2,1)S(1)}, u32[]{:S(2)}, u32[]{:S(2)}) collective-permute-start(bf16[1,48,128]{2,1,0:T(8,128)(2,1)S(1)} %get-tuple-element.118), channel_id=1, source_target_pairs={{0,64},{1,65},{2,66},{3,67},{4,68},{5,69},{6,70},{7,71},{8,72},{9,... | collective-permute-start | bytes 36872 | tf_op jit(solution)/shard_map/ppermute | solution.py:210
  34.2 12.8 %collective-permute-start.25 = (bf16[4,32,128]{2,1,0:T(8,128)(2,1)S(1)}, bf16[4,32,128]{2,1,0:T(8,128)(2,1)S(1)}, u32[]{:S(2)}, u32[]{:S(2)}) collective-permute-start(bf16[4,32,128]{2,1,0:T(8,128)(2,1)S(1)} %pad_maximum_fusion.4), channel_id=1, source_target_pairs={{0,32},{1,33},{2,34},{3,35},{4,36},{5,37},{6,38},{7,39},{8,40},{9,... | collective-permute-start | bytes 98312 | tf_op jit(solution)/shard_map/ppermute | solution.py:210
  39.9 12.6 %collective-permute-start.5 = (bf16[4,48,128]{2,1,0:T(8,128)(2,1)S(1)}, bf16[4,48,128]{2,1,0:T(8,128)(2,1)S(1)}, u32[]{:S(2)}, u32[]{:S(2)}) collective-permute-start(bf16[4,48,128]{2,1,0:T(8,128)(2,1)S(1)} %pad_maximum_fusion.1), channel_id=1, source_target_pairs={{0,16},{1,17},{2,18},{3,19},{4,20},{5,21},{6,22},{7,23},{8,24},{9,... | collective-permute-start | bytes 147464 | tf_op jit(solution)/shard_map/ppermute | solution.py:210
  45.7 13.8 %collective-permute-start.15 = (bf16[4,48,128]{2,1,0:T(8,128)(2,1)S(1)}, bf16[4,48,128]{2,1,0:T(8,128)(2,1)S(1)}, u32[]{:S(2)}, u32[]{:S(2)}) collective-permute-start(bf16[4,48,128]{2,1,0:T(8,128)(2,1)S(1)} %pad_maximum_fusion.2), channel_id=1, source_target_pairs={{0,4},{1,5},{2,6},{3,7},{4,8},{5,9},{6,10},{7,11},{8,12},{9,13},{1... | collective-permute-start | bytes 147464 | tf_op jit(solution)/shard_map/ppermute | solution.py:210
  47.1 11.4 %collective-permute-start.14 = (bf16[4,48,128]{2,1,0:T(8,128)(2,1)S(1)}, bf16[4,48,128]{2,1,0:T(8,128)(2,1)S(1)}, u32[]{:S(2)}, u32[]{:S(2)}) collective-permute-start(bf16[4,48,128]{2,1,0:T(8,128)(2,1)S(1)} %pad_maximum_fusion.2), channel_id=1, source_target_pairs={{0,8},{1,9},{2,10},{3,11},{4,12},{5,13},{6,14},{7,15},{8,0},{9,1},... | collective-permute-start | bytes 147464 | tf_op jit(solution)/shard_map/ppermute | solution.py:210
  51.0 16.5 %collective-permute-start.28 = (bf16[16,32,128]{2,1,0:T(8,128)(2,1)}, bf16[16,32,128]{2,1,0:T(8,128)(2,1)S(1)}, u32[]{:S(2)}, u32[]{:S(2)}) collective-permute-start(bf16[16,32,128]{2,1,0:T(8,128)(2,1)} %get-tuple-element.107), channel_id=1, source_target_pairs={{0,4},{1,5},{2,6},{3,7},{4,8},{5,9},{6,10},{7,11},{8,12},{9,13},{1... | collective-permute-start | bytes 393224 | tf_op jit(solution)/shard_map/ppermute | solution.py:210
  52.5 13.1 %collective-permute-start.27 = (bf16[16,32,128]{2,1,0:T(8,128)(2,1)}, bf16[16,32,128]{2,1,0:T(8,128)(2,1)S(1)}, u32[]{:S(2)}, u32[]{:S(2)}) collective-permute-start(bf16[16,32,128]{2,1,0:T(8,128)(2,1)} %get-tuple-element.107), channel_id=1, source_target_pairs={{0,8},{1,9},{2,10},{3,11},{4,12},{5,13},{6,14},{7,15},{8,0},{9,1},... | collective-permute-start | bytes 393224 | tf_op jit(solution)/shard_map/ppermute | solution.py:210
  58.5 22.4 %collective-permute-start.8 = (bf16[16,48,128]{2,1,0:T(8,128)(2,1)}, bf16[16,48,128]{2,1,0:T(8,128)(2,1)S(1)}, u32[]{:S(2)}, u32[]{:S(2)}) collective-permute-start(bf16[16,48,128]{2,1,0:T(8,128)(2,1)} %get-tuple-element.82), channel_id=1, source_target_pairs={{0,32},{1,33},{2,34},{3,35},{4,36},{5,37},{6,38},{7,39},{8,40},{9,... | collective-permute-start | bytes 589832 | tf_op jit(solution)/shard_map/ppermute | solution.py:210
  59.5 20.5 %collective-permute-start.7 = (bf16[16,48,128]{2,1,0:T(8,128)(2,1)}, bf16[16,48,128]{2,1,0:T(8,128)(2,1)S(1)}, u32[]{:S(2)}, u32[]{:S(2)}) collective-permute-start(bf16[16,48,128]{2,1,0:T(8,128)(2,1)} %get-tuple-element.82), channel_id=1, source_target_pairs={{0,64},{1,65},{2,66},{3,67},{4,68},{5,69},{6,70},{7,71},{8,72},{9,... | collective-permute-start | bytes 589832 | tf_op jit(solution)/shard_map/ppermute | solution.py:210
  62.6 16.7 %collective-permute-start.6 = (bf16[16,48,128]{2,1,0:T(8,128)(2,1)}, bf16[16,48,128]{2,1,0:T(8,128)(2,1)S(1)}, u32[]{:S(2)}, u32[]{:S(2)}) collective-permute-start(bf16[16,48,128]{2,1,0:T(8,128)(2,1)} %get-tuple-element.82), channel_id=1, source_target_pairs={{0,96},{1,97},{2,98},{3,99},{4,100},{5,101},{6,102},{7,103},{8,104... | collective-permute-start | bytes 589832 | tf_op jit(solution)/shard_map/ppermute | solution.py:210
  75.0 12.7 %collective-permute-start.29 = (bf16[64,32,128]{2,1,0:T(8,128)(2,1)}, bf16[64,32,128]{2,1,0:T(8,128)(2,1)}, u32[]{:S(2)}, u32[]{:S(2)}) collective-permute-start(bf16[64,32,128]{2,1,0:T(8,128)(2,1)} %get-tuple-element.68), channel_id=1, source_target_pairs={{0,2},{1,3},{2,0},{3,1},{4,6},{5,7},{6,4},{7,5},{8,10},{9,11},{10,... | collective-permute-start | bytes 1572872 | tf_op jit(solution)/shard_map/ppermute | solution.py:210
  79.3 11.8 %collective-permute-start.19 = (bf16[64,48,128]{2,1,0:T(8,128)(2,1)}, bf16[64,48,128]{2,1,0:T(8,128)(2,1)}, u32[]{:S(2)}, u32[]{:S(2)}) collective-permute-start(bf16[64,48,128]{2,1,0:T(8,128)(2,1)} %get-tuple-element.59), channel_id=1, source_target_pairs={{0,2},{1,3},{2,0},{3,1},{4,6},{5,7},{6,4},{7,5},{8,10},{9,11},{10,... | collective-permute-start | bytes 2359304 | tf_op jit(solution)/shard_map/ppermute | solution.py:210
  123.6 15.4 %collective-permute-start.52 = (bf16[4,4,4,32,128]{4,3,2,1,0:T(8,128)(2,1)}, bf16[4,4,4,32,128]{4,3,2,1,0:T(8,128)(2,1)}, u32[]{:S(2)}, u32[]{:S(2)}) collective-permute-start(bf16[4,4,4,32,128]{4,3,2,1,0:T(8,128)(2,1)} %fusion.3), channel_id=1, source_target_pairs={{0,2},{1,3},{2,0},{3,1},{4,6},{5,7},{6,4},{7,5},{8,10},{9,11},{10,... | collective-permute-start | bytes 1572872 | tf_op jit(solution)/shard_map/ppermute | solution.py:233
  132.6 59.3 %collective-permute-start.30 = (bf16[256,512]{1,0:T(8,128)(2,1)}, bf16[256,512]{1,0:T(8,128)(2,1)}, u32[]{:S(2)}, u32[]{:S(2)}) collective-permute-start(bf16[256,512]{1,0:T(8,128)(2,1)} %reshape.123), channel_id=1, source_target_pairs={{0,1},{1,0},{2,3},{3,2},{4,5},{5,4},{6,7},{7,6},{8,9},{9,8},{10,11... | collective-permute-start | bytes 786440 | tf_op jit(solution)/shard_map/ppermute | solution.py:290
  136.6 64.1 %collective-permute-start.31 = (bf16[256,512]{1,0:T(8,128)(2,1)S(1)}, bf16[256,512]{1,0:T(8,128)(2,1)S(1)}, u32[]{:S(2)}, u32[]{:S(2)}) collective-permute-start(bf16[256,512]{1,0:T(8,128)(2,1)S(1)} %reshape.124), channel_id=1, source_target_pairs={{0,1},{1,0},{2,3},{3,2},{4,5},{5,4},{6,7},{7,6},{8,9},{9,8},{10,11... | collective-permute-start | bytes 786440 | tf_op jit(solution)/shard_map/ppermute | solution.py:290
  141.5 41.6 %collective-permute-start.53 = (bf16[4,4,32,128]{3,2,1,0:T(8,128)(2,1)S(1)}, bf16[4,4,32,128]{3,2,1,0:T(8,128)(2,1)S(1)}, u32[]{:S(2)}, u32[]{:S(2)}) collective-permute-start(bf16[4,4,32,128]{3,2,1,0:T(8,128)(2,1)S(1)} %get-tuple-element.44), channel_id=1, source_target_pairs={{0,4},{1,5},{2,6},{3,7},{4,8},{5,9},{6,10},{7,11},{8,12},{9,13},{1... | collective-permute-start | bytes 393224 | tf_op jit(solution)/shard_map/ppermute | solution.py:233
  183.1 22.7 %collective-permute-start.32 = (bf16[4,4,4,48,128]{4,3,2,1,0:T(8,128)(2,1)S(1)}, bf16[4,4,4,48,128]{4,3,2,1,0:T(8,128)(2,1)S(1)}, u32[]{:S(2)}, u32[]{:S(2)}) collective-permute-start(bf16[4,4,4,48,128]{4,3,2,1,0:T(8,128)(2,1)S(1)} %bitcast.235), channel_id=1, source_target_pairs={{0,2},{1,3},{2,0},{3,1},{4,6},{5,7},{6,4},{7,5},{8,10},{9,11},{10,... | collective-permute-start | bytes 2359304 | tf_op jit(solution)/shard_map/ppermute | solution.py:233
  195.4 14.2 %collective-permute-start.42 = (bf16[4,4,4,48,128]{4,3,2,1,0:T(8,128)(2,1)S(1)}, bf16[4,4,4,48,128]{4,3,2,1,0:T(8,128)(2,1)S(1)}, u32[]{:S(2)}, u32[]{:S(2)}) collective-permute-start(bf16[4,4,4,48,128]{4,3,2,1,0:T(8,128)(2,1)S(1)} %fusion.2), channel_id=1, source_target_pairs={{0,2},{1,3},{2,0},{3,1},{4,6},{5,7},{6,4},{7,5},{8,10},{9,11},{10,... | collective-permute-start | bytes 2359304 | tf_op jit(solution)/shard_map/ppermute | solution.py:233
  (46 other events, 330.4 us)

commit v10 on v8

--- a/solution.py
+++ b/solution.py
@@ -46,7 +46,7 @@
     return jnp.concatenate([kvt_ref[b, first:first + HEAD_DIM, :] for b in blocks], axis=1)
 
 
-def _visit_slots(count_ref, qb, visit, group=4):
+def _visit_slots(count_ref, qb, visit, group=8):
     count = count_ref[qb, 0]
     groups = count // group
 
@@ -58,21 +58,19 @@
 
     lax.fori_loop(0, count_ref.shape[1] // group, body, 0)
     done = groups * group
-    rest = count - done
-
-    @pl.when(rest >= 2)
-    def _():
-        visit((done, done + 1))
-
-    @pl.when(rest % 2 == 1)
-    def _():
-        visit((count - 1,))
+    size = group // 2
+    while size >= 1:
+        @pl.when((count - done) >= size)
+        def _(done=done, size=size):
+            visit(tuple(done + t for t in range(size)))
+        done = done + jnp.where((count - done) >= size, size, 0)
+        size //= 2
 
 
 def _forward_kernel(lists_ref, count_ref, qt_ref, kvt_ref, dot_ref,
                     ot_ref, lse_ref, delta_ref, m_sc, l_sc, acc_sc):
     query_count = lists_ref.shape[0]
-    for qb in range(query_count):
+    def per_query(qb, carry):
         m_sc[...] = jnp.full(m_sc.shape, LOWEST, jnp.float32)
         l_sc[...] = jnp.zeros(l_sc.shape, jnp.float32)
         acc_sc[...] = jnp.zeros(acc_sc.shape, jnp.float32)
@@ -94,13 +92,16 @@
         ot_ref[qb] = out.astype(jnp.bfloat16)
         lse_ref[qb] = m_sc[...] + jnp.log(l_sc[...])
         delta_ref[qb] = jnp.sum(dot_ref[qb].astype(jnp.float32) * out, axis=0, keepdims=True)
+        return carry
+
+    lax.fori_loop(0, query_count, per_query, 0)
 
 
 def _backward_kernel(lists_ref, count_ref, q_ref, qt_ref, kvt_ref, do_ref, dot_ref, lse_ref,
                      delta_ref, dqt_ref, dkvt_ref, dq_sc):
     query_count = lists_ref.shape[0]
     dkvt_ref[...] = jnp.zeros(dkvt_ref.shape, jnp.float32)
-    for qb in range(query_count):
+    def per_query(qb, carry):
         dq_sc[...] = jnp.zeros(dq_sc.shape, jnp.float32)
 
         def visit(slots, qb=qb):
@@ -119,6 +120,9 @@
 
         _visit_slots(count_ref, qb, visit)
         dqt_ref[qb] = (dq_sc[...] * SCALE).astype(jnp.bfloat16)
+        return carry
+
+    lax.fori_loop(0, query_count, per_query, 0)
 
 
 def attend_local(q_rows, do_rows, kv_t, lists, keep):

time: 186 us -> 182 us (0.978)
  Pallas kernels: 59.7 us -> 31.4 us
  starting transfers between devices: 30.3 us -> 55.8 us
  waiting for transfers between devices: 54.3 us -> 52.2 us
    ppermute x10, starting transfers between devices: 12.1 us -> 38.7 us  [scatter_sum(): lax.ppermute(sent, axes, pairs(axis, shift)).astype(jnp.float32)]
    pallas_call x1, Pallas kernels: 37.7 us -> 20.2 us  [attend_local(): pl.pallas_call(_backward_kernel, out_shape=(jax.ShapeDtypeStruct((query_c...]
    pallas_call x1, Pallas kernels: 22 us -> 11.2 us  [attend_local(): pl.pallas_call(_forward_kernel, out_shape=(jax.ShapeDtypeStruct((query_co...]
    ppermute x10, waiting for transfers between devices: 29.6 us -> 27.1 us  [scatter_sum(): lax.ppermute(sent, axes, pairs(axis, shift)).astype(jnp.float32)]
  transfers between devices with their start and end apart: 22 -> 22, of which waited for: 14 -> 15; matrix products, arithmetic and copies ran while one was open for 15% -> 15% of each run, Pallas kernels for 0% -> 0%
where the time goes in v10:
time: 182 us; the launch traced here: 179 us
  starting transfers between devices  55.8 us (31%)
  waiting for transfers between devices  52.2 us (29%)
  Pallas kernels  31.4 us (17%)
  local copies, waits for them, and re-layouts  24.3 us (13%)
  other arithmetic  15 us (8%)
    ppermute x10, starting transfers between devices, scatter_sum(): lax.ppermute(sent, axes, pairs(axis, shift)).astype(jnp.float32)  38.7 us
    ppermute x10, waiting for transfers between devices, scatter_sum(): lax.ppermute(sent, axes, pairs(axis, shift)).astype(jnp.float32)  27.1 us
    ppermute x10, waiting for transfers between devices, gather_blocks(): pieces.append(lax.ppermute(buf, axes, pairs(axis, size - shift)))  24.7 us
    pallas_call x1, Pallas kernels, attend_local(): pl.pallas_call(_backward_kernel, out_shape=(jax.ShapeDtypeStruct((query_c...  20.2 us
    ppermute x10, starting transfers between devices, gather_blocks(): pieces.append(lax.ppermute(buf, axes, pairs(axis, size - shift)))  14.5 us
    pallas_call x1, Pallas kernels, attend_local(): pl.pallas_call(_forward_kernel, out_shape=(jax.ShapeDtypeStruct((query_co...  11.2 us
    unnamed x24, local copies, waits for them, and re-layouts  7.1 us
    another operation x3, other arithmetic  4.7 us
  transfers between devices with their start and end apart: 22, of which 15 were waited for; matrix products, arithmetic and copies ran while one was open for 15% of the time, Pallas kernels for 0%

profile of v10, /device:TPU:0, one launch (start us, length us, event | category | flops | bytes accessed | tf_op | source)
XLA Modules:
  0.0 179.5 jit_solution(948719518414938902)
XLA Ops:
  1.4 3.1 %collective-permute-start = (bf16[1,128,128]{2,1,0:T(8,128)(2,1)S(1)}, bf16[1,128,128]{2,1,0:T(8,128)(2,1)S(1)}, u32[]{:S(2)}, u32[]{:S(2)}) collective-permute-start(bf16[1,128,128]{2,1,0:T(8,128)(2,1)S(1)} %maximum_bitcast_fusion), channel_id=1, source_target_pairs={{0,12},{1,13},{2,14},{3,15},{4,0},{5,1},{6,2},{7,3},{8,4},{9,5},{1... | collective-permute-start | bytes 98312 | tf_op jit(solution)/shard_map/ppermute | solution.py:203
  7.5 2.4 %collective-permute-done.1 = bf16[1,128,128]{2,1,0:T(8,128)(2,1)S(1)} collective-permute-done((bf16[1,128,128]{2,1,0:T(8,128)(2,1)S(1)}, bf16[1,128,128]{2,1,0:T(8,128)(2,1)S(1)}, u32[]{:S(2)}, u32[]{:S(2)}) %collective-permute-start.1) | collective-permute-done | bytes 32800 | tf_op jit(solution)/shard_map/ppermute | solution.py:203
  10.3 2.8 %collective-permute-start.3 = (bf16[4,128,128]{2,1,0:T(8,128)(2,1)S(1)}, bf16[4,128,128]{2,1,0:T(8,128)(2,1)S(1)}, u32[]{:S(2)}, u32[]{:S(2)}) collective-permute-start(bf16[4,128,128]{2,1,0:T(8,128)(2,1)S(1)} %pad_maximum_fusion), channel_id=1, source_target_pairs={{0,17},{1,16},{2,19},{3,18},{4,21},{5,20},{6,23},{7,22},{8,25},{9,... | collective-permute-start | bytes 393224 | tf_op jit(solution)/shard_map/ppermute | solution.py:203
  18.2 1.5 collective-permute-done.4
  21.8 4.0 %collective-permute-start.6 = (bf16[16,128,128]{2,1,0:T(8,128)(2,1)S(1)}, bf16[16,128,128]{2,1,0:T(8,128)(2,1)S(1)}, u32[]{:S(2)}, u32[]{:S(2)}) collective-permute-start(bf16[16,128,128]{2,1,0:T(8,128)(2,1)S(1)} %get-tuple-element.39), channel_id=1, source_target_pairs={{0,96},{1,97},{2,98},{3,99},{4,100},{5,101},{6,102},{7,103},{8,104... | collective-permute-start | bytes 1572872 | tf_op jit(solution)/shard_map/ppermute | solution.py:203
  27.1 18.3 %collective-permute-done.6 = bf16[16,128,128]{2,1,0:T(8,128)(2,1)S(1)} collective-permute-done((bf16[16,128,128]{2,1,0:T(8,128)(2,1)S(1)}, bf16[16,128,128]{2,1,0:T(8,128)(2,1)S(1)}, u32[]{:S(2)}, u32[]{:S(2)}) %collective-permute-start.6) | collective-permute-done | bytes 524320 | tf_op jit(solution)/shard_map/ppermute | solution.py:203
  51.5 2.7 %slice_subtract_fusion.3 = (s32[2,48,1]{2,1,0:T(8,128)S(1)}, s32[2,48,1]{2,1,0:T(8,128)S(1)}, s32[2,48,1]{2,1,0:T(8,128)S(1)}, s32[2,48,1]{2,1,0:T(8,128)S(1)}) fusion(s32[2,48,4]{2,1,0:T(8,128)S(1)} %bitcast.93, s32[]{:T(128)} %bitcast.1, s32[]{:T(128)} %bitcast.5, s32[]{:T(128)} %bitcast.3, s32[]{:T(128)} %bitcast.7), kind=kLoop, calls=%fused_computation.56 | loop fusion | flops 384 | bytes 3088 | tf_op jit(solution)/shard_map/sub | solution.py:237
  56.1 1.7 gather_fusion.1
  64.1 11.2 %shard_map.93 = (bf16[2,64,1024]{2,1,0:T(8,128)(2,1)}, f32[2,1,1024]{2,1,0:T(1,128)}, f32[2,1,1024]{2,1,0:T(1,128)}) custom-call(s32[2,48]{1,0:T(2,128)} %and_select_fusion.4.lists_ref, s32[2,48]{1,0:T(2,128)} %broadcast_in_dim.22.count_ref, bf16[2,64,1024]{2,1,0:T(8,128)(2,1)} %bitcast.88, ...), custom_call_target="tpu_custom_call" | custom-call | tf_op jit(solution)/shard_map/pallas_call | solution.py:137
  75.3 20.2 %shard_map.94 = (bf16[2,64,1024]{2,1,0:T(8,128)(2,1)}, f32[128,128,128]{2,1,0:T(8,128)}) custom-call(s32[2,48]{1,0:T(2,128)} %and_select_fusion.4.lists_ref, s32[2,48]{1,0:T(2,128)} %broadcast_in_dim.22.count_ref, bf16[2,1024,64]{2,1,0:T(8,128)(2,1)} %copy-done, bf16[2,64,1024]{2,1,0:T(8,128)(2,1)} %bitcast.89, ...), custom_call_target="tpu_custom_call" | custom-call | tf_op jit(solution)/shard_map/pallas_call | solution.py:153
  95.5 2.6 %slice.179 = bf16[64,128,128]{2,1,0:T(8,128)(2,1)S(1)} slice(f32[128,128,128]{2,1,0:T(8,128)} %get-tuple-element.15), slice={[64:128], [0:128], [0:128]} | slice | bytes 4194304 | tf_op jit(solution)/shard_map/slice | solution.py:212
  98.1 20.3 %collective-permute-start.12 = (bf16[4,4,4,128,128]{4,3,2,1,0:T(8,128)(2,1)S(1)}, bf16[4,4,4,128,128]{4,3,2,1,0:T(8,128)(2,1)S(1)}, u32[]{:S(2)}, u32[]{:S(2)}) collective-permute-start(bf16[4,4,4,128,128]{4,3,2,1,0:T(8,128)(2,1)S(1)} %bitcast.92), channel_id=1, source_target_pairs={{0,2},{1,3},{2,0},{3,1},{4,6},{5,7},{6,4},{7,5},{8,10},{9,11},{10,... | collective-permute-start | bytes 6291464 | tf_op jit(solution)/shard_map/ppermute | solution.py:213
  118.4 2.5 %slice.97 = f32[64,128,128]{2,1,0:T(8,128)S(1)} slice(f32[128,128,128]{2,1,0:T(8,128)} %get-tuple-element.15), slice={[0:64], [0:128], [0:128]} | slice | bytes 8388608 | tf_op jit(solution)/shard_map/slice | solution.py:210
  122.2 3.0 %fusion.28 = (bf16[4,4,4,128,128]{4,3,2,1,0:T(8,128)(2,1)S(1)}, f32[4,4,4,128,128]{4,3,2,1,0:T(8,128)}) fusion(f32[4,4,4,128,128]{4,3,2,1,0:T(8,128)S(1)} %bitcast.87, bf16[4,4,4,128,128]{4,3,2,1,0:T(8,128)(2,1)S(1)} %collective-permute-done.12), kind=kLoop, calls=%fused_computation.103 | loop fusion | flops 3145728 | bytes 12582912 | tf_op jit(solution)/shard_map/convert.9
  125.2 2.2 %collective-permute-start.13 = (bf16[4,4,128,128]{3,2,1,0:T(8,128)(2,1)S(1)}, bf16[4,4,128,128]{3,2,1,0:T(8,128)(2,1)S(1)}, u32[]{:S(2)}, u32[]{:S(2)}) collective-permute-start(bf16[4,4,128,128]{3,2,1,0:T(8,128)(2,1)S(1)} %get-tuple-element.22), channel_id=1, source_target_pairs={{0,32},{1,33},{2,34},{3,35},{4,36},{5,37},{6,38},{7,39},{8,40},{9,... | collective-permute-start | bytes 1572872 | tf_op jit(solution)/shard_map/ppermute | solution.py:213
  127.4 2.8 %collective-permute-start.15 = (bf16[4,4,128,128]{3,2,1,0:T(8,128)(2,1)S(1)}, bf16[4,4,128,128]{3,2,1,0:T(8,128)(2,1)}, u32[]{:S(2)}, u32[]{:S(2)}) collective-permute-start(bf16[4,4,128,128]{3,2,1,0:T(8,128)(2,1)S(1)} %get-tuple-element.23), channel_id=1, source_target_pairs={{0,96},{1,97},{2,98},{3,99},{4,100},{5,101},{6,102},{7,103},{8,104... | collective-permute-start | bytes 1572872 | tf_op jit(solution)/shard_map/ppermute | solution.py:213
  131.7 20.3 %collective-permute-done.13 = bf16[4,4,128,128]{3,2,1,0:T(8,128)(2,1)S(1)} collective-permute-done((bf16[4,4,128,128]{3,2,1,0:T(8,128)(2,1)S(1)}, bf16[4,4,128,128]{3,2,1,0:T(8,128)(2,1)S(1)}, u32[]{:S(2)}, u32[]{:S(2)}) %collective-permute-start.13) | collective-permute-done | bytes 524320 | tf_op jit(solution)/shard_map/ppermute | solution.py:213
  152.7 1.7 fusion.26
  154.4 7.2 %collective-permute-start.16 = (bf16[4,128,128]{2,1,0:T(8,128)(2,1)S(1)}, bf16[4,128,128]{2,1,0:T(8,128)(2,1)S(1)}, u32[]{:S(2)}, u32[]{:S(2)}) collective-permute-start(bf16[4,128,128]{2,1,0:T(8,128)(2,1)S(1)} %get-tuple-element.25), channel_id=1, source_target_pairs={{0,16},{1,17},{2,18},{3,19},{4,20},{5,21},{6,22},{7,23},{8,24},{9,... | collective-permute-start | bytes 393224 | tf_op jit(solution)/shard_map/ppermute | solution.py:213
  161.6 3.0 %collective-permute-start.17 = (bf16[4,128,128]{2,1,0:T(8,128)(2,1)S(1)}, bf16[4,128,128]{2,1,0:T(8,128)(2,1)S(1)}, u32[]{:S(2)}, u32[]{:S(2)}) collective-permute-start(bf16[4,128,128]{2,1,0:T(8,128)(2,1)S(1)} %get-tuple-element.27), channel_id=1, source_target_pairs={{0,1},{1,0},{2,3},{3,2},{4,5},{5,4},{6,7},{7,6},{8,9},{9,8},{10,11... | collective-permute-start | bytes 393224 | tf_op jit(solution)/shard_map/ppermute | solution.py:213
  165.2 1.6 collective-permute-start.10
  166.8 2.0 %maximum_select_fusion.1 = bf16[256,1024]{1,0:T(8,128)(2,1)} fusion(bf16[256,512]{1,0:T(8,128)(2,1)} %collective-permute-done.11, bf16[256,512]{1,0:T(8,128)(2,1)S(1)} %reshape.82, pred[]{:T(512)S(6)} %eq.22), kind=kLoop, calls=%fused_computation.12 | loop fusion | flops 2359296 | bytes 1048577 | tf_op jit(solution)/shard_map/jit(_where)/select_n | solution.py:253
  168.8 2.9 %collective-permute-done.17 = bf16[4,128,128]{2,1,0:T(8,128)(2,1)S(1)} collective-permute-done((bf16[4,128,128]{2,1,0:T(8,128)(2,1)S(1)}, bf16[4,128,128]{2,1,0:T(8,128)(2,1)S(1)}, u32[]{:S(2)}, u32[]{:S(2)}) %collective-permute-start.17) | collective-permute-done | bytes 131104 | tf_op jit(solution)/shard_map/ppermute | solution.py:213
  172.3 2.8 %collective-permute-start.21 = (bf16[128,128]{1,0:T(8,128)(2,1)S(1)}, bf16[128,128]{1,0:T(8,128)(2,1)S(1)}, u32[]{:S(2)}, u32[]{:S(2)}) collective-permute-start(bf16[128,128]{1,0:T(8,128)(2,1)S(1)} %get-tuple-element.35), channel_id=1, source_target_pairs={{0,12},{1,13},{2,14},{3,15},{4,0},{5,1},{6,2},{7,3},{8,4},{9,5},{1... | collective-permute-start | bytes 98312 | tf_op jit(solution)/shard_map/ppermute | solution.py:213
  (94 shorter events, 35.9 us)
Async XLA Ops:
  0.6 49.6 %copy-start.2 = (s32[128,4]{1,0:T(8,128)S(1)}, s32[128,4]{1,0:T(8,128)}, u32[]{:S(2)}) copy-start(s32[128,4]{1,0:T(8,128)} %constant.80.clone) | copy-start | bytes 6148
  0.6 49.5 %copy-start.5 = (s32[2,48]{1,0:T(2,128)S(1)}, s32[2,48]{1,0:T(2,128)}, u32[]{:S(2)}) copy-start(s32[2,48]{1,0:T(2,128)} %param.10) | copy-start | bytes 1156
  1.4 6.1 %collective-permute-start = (bf16[1,128,128]{2,1,0:T(8,128)(2,1)S(1)}, bf16[1,128,128]{2,1,0:T(8,128)(2,1)S(1)}, u32[]{:S(2)}, u32[]{:S(2)}) collective-permute-start(bf16[1,128,128]{2,1,0:T(8,128)(2,1)S(1)} %maximum_bitcast_fusion), channel_id=1, source_target_pairs={{0,12},{1,13},{2,14},{3,15},{4,0},{5,1},{6,2},{7,3},{8,4},{9,5},{1... | collective-permute-start | bytes 98312 | tf_op jit(solution)/shard_map/ppermute | solution.py:203
  4.6 5.4 %collective-permute-start.1 = (bf16[1,128,128]{2,1,0:T(8,128)(2,1)S(1)}, bf16[1,128,128]{2,1,0:T(8,128)(2,1)S(1)}, u32[]{:S(2)}, u32[]{:S(2)}) collective-permute-start(bf16[1,128,128]{2,1,0:T(8,128)(2,1)S(1)} %maximum_bitcast_fusion), channel_id=1, source_target_pairs={{0,8},{1,9},{2,10},{3,11},{4,12},{5,13},{6,14},{7,15},{8,0},{9,1},... | collective-permute-start | bytes 98312 | tf_op jit(solution)/shard_map/ppermute | solution.py:203
  5.2 5.1 %collective-permute-start.2 = (bf16[1,128,128]{2,1,0:T(8,128)(2,1)S(1)}, bf16[1,128,128]{2,1,0:T(8,128)(2,1)S(1)}, u32[]{:S(2)}, u32[]{:S(2)}) collective-permute-start(bf16[1,128,128]{2,1,0:T(8,128)(2,1)S(1)} %maximum_bitcast_fusion), channel_id=1, source_target_pairs={{0,4},{1,5},{2,6},{3,7},{4,8},{5,9},{6,10},{7,11},{8,12},{9,13},{1... | collective-permute-start | bytes 98312 | tf_op jit(solution)/shard_map/ppermute | solution.py:203
  10.3 7.1 %collective-permute-start.3 = (bf16[4,128,128]{2,1,0:T(8,128)(2,1)S(1)}, bf16[4,128,128]{2,1,0:T(8,128)(2,1)S(1)}, u32[]{:S(2)}, u32[]{:S(2)}) collective-permute-start(bf16[4,128,128]{2,1,0:T(8,128)(2,1)S(1)} %pad_maximum_fusion), channel_id=1, source_target_pairs={{0,17},{1,16},{2,19},{3,18},{4,21},{5,20},{6,23},{7,22},{8,25},{9,... | collective-permute-start | bytes 393224 | tf_op jit(solution)/shard_map/ppermute | solution.py:203
  13.2 6.6 %collective-permute-start.4 = (bf16[4,128,128]{2,1,0:T(8,128)(2,1)S(1)}, bf16[4,128,128]{2,1,0:T(8,128)(2,1)S(1)}, u32[]{:S(2)}, u32[]{:S(2)}) collective-permute-start(bf16[4,128,128]{2,1,0:T(8,128)(2,1)S(1)} %pad_maximum_fusion), channel_id=1, source_target_pairs={{0,1},{1,0},{2,3},{3,2},{4,5},{5,4},{6,7},{7,6},{8,9},{9,8},{10,11... | collective-permute-start | bytes 393224 | tf_op jit(solution)/shard_map/ppermute | solution.py:203
  14.0 7.1 %collective-permute-start.5 = (bf16[4,128,128]{2,1,0:T(8,128)(2,1)S(1)}, bf16[4,128,128]{2,1,0:T(8,128)(2,1)S(1)}, u32[]{:S(2)}, u32[]{:S(2)}) collective-permute-start(bf16[4,128,128]{2,1,0:T(8,128)(2,1)S(1)} %pad_maximum_fusion), channel_id=1, source_target_pairs={{0,16},{1,17},{2,18},{3,19},{4,20},{5,21},{6,22},{7,23},{8,24},{9,... | collective-permute-start | bytes 393224 | tf_op jit(solution)/shard_map/ppermute | solution.py:203
  21.8 23.6 %collective-permute-start.6 = (bf16[16,128,128]{2,1,0:T(8,128)(2,1)S(1)}, bf16[16,128,128]{2,1,0:T(8,128)(2,1)S(1)}, u32[]{:S(2)}, u32[]{:S(2)}) collective-permute-start(bf16[16,128,128]{2,1,0:T(8,128)(2,1)S(1)} %get-tuple-element.39), channel_id=1, source_target_pairs={{0,96},{1,97},{2,98},{3,99},{4,100},{5,101},{6,102},{7,103},{8,104... | collective-permute-start | bytes 1572872 | tf_op jit(solution)/shard_map/ppermute | solution.py:203
  25.9 20.8 %collective-permute-start.7 = (bf16[16,128,128]{2,1,0:T(8,128)(2,1)S(1)}, bf16[16,128,128]{2,1,0:T(8,128)(2,1)S(1)}, u32[]{:S(2)}, u32[]{:S(2)}) collective-permute-start(bf16[16,128,128]{2,1,0:T(8,128)(2,1)S(1)} %get-tuple-element.39), channel_id=1, source_target_pairs={{0,64},{1,65},{2,66},{3,67},{4,68},{5,69},{6,70},{7,71},{8,72},{9,... | collective-permute-start | bytes 1572872 | tf_op jit(solution)/shard_map/ppermute | solution.py:203
  25.9 23.0 %collective-permute-start.8 = (bf16[16,128,128]{2,1,0:T(8,128)(2,1)S(1)}, bf16[16,128,128]{2,1,0:T(8,128)(2,1)S(1)}, u32[]{:S(2)}, u32[]{:S(2)}) collective-permute-start(bf16[16,128,128]{2,1,0:T(8,128)(2,1)S(1)} %get-tuple-element.39), channel_id=1, source_target_pairs={{0,32},{1,33},{2,34},{3,35},{4,36},{5,37},{6,38},{7,39},{8,40},{9,... | collective-permute-start | bytes 1572872 | tf_op jit(solution)/shard_map/ppermute | solution.py:203
  50.1 11.8 %collective-permute-start.9 = (bf16[64,128,128]{2,1,0:T(8,128)(2,1)}, bf16[64,128,128]{2,1,0:T(8,128)(2,1)S(1)}, u32[]{:S(2)}, u32[]{:S(2)}) collective-permute-start(bf16[64,128,128]{2,1,0:T(8,128)(2,1)} %get-tuple-element.28), channel_id=1, source_target_pairs={{0,2},{1,3},{2,0},{3,1},{4,6},{5,7},{6,4},{7,5},{8,10},{9,11},{10,... | collective-permute-start | bytes 6291464 | tf_op jit(solution)/shard_map/ppermute | solution.py:203
  98.1 24.1 %collective-permute-start.12 = (bf16[4,4,4,128,128]{4,3,2,1,0:T(8,128)(2,1)S(1)}, bf16[4,4,4,128,128]{4,3,2,1,0:T(8,128)(2,1)S(1)}, u32[]{:S(2)}, u32[]{:S(2)}) collective-permute-start(bf16[4,4,4,128,128]{4,3,2,1,0:T(8,128)(2,1)S(1)} %bitcast.92), channel_id=1, source_target_pairs={{0,2},{1,3},{2,0},{3,1},{4,6},{5,7},{6,4},{7,5},{8,10},{9,11},{10,... | collective-permute-start | bytes 6291464 | tf_op jit(solution)/shard_map/ppermute | solution.py:213
  125.2 26.7 %collective-permute-start.13 = (bf16[4,4,128,128]{3,2,1,0:T(8,128)(2,1)S(1)}, bf16[4,4,128,128]{3,2,1,0:T(8,128)(2,1)S(1)}, u32[]{:S(2)}, u32[]{:S(2)}) collective-permute-start(bf16[4,4,128,128]{3,2,1,0:T(8,128)(2,1)S(1)} %get-tuple-element.22), channel_id=1, source_target_pairs={{0,32},{1,33},{2,34},{3,35},{4,36},{5,37},{6,38},{7,39},{8,40},{9,... | collective-permute-start | bytes 1572872 | tf_op jit(solution)/shard_map/ppermute | solution.py:213
  127.4 24.6 %collective-permute-start.14 = (bf16[4,4,128,128]{3,2,1,0:T(8,128)(2,1)S(1)}, bf16[4,4,128,128]{3,2,1,0:T(8,128)(2,1)S(1)}, u32[]{:S(2)}, u32[]{:S(2)}) collective-permute-start(bf16[4,4,128,128]{3,2,1,0:T(8,128)(2,1)S(1)} %get-tuple-element.24), channel_id=1, source_target_pairs={{0,64},{1,65},{2,66},{3,67},{4,68},{5,69},{6,70},{7,71},{8,72},{9,... | collective-permute-start | bytes 1572872 | tf_op jit(solution)/shard_map/ppermute | solution.py:213
  127.4 25.3 %collective-permute-start.15 = (bf16[4,4,128,128]{3,2,1,0:T(8,128)(2,1)S(1)}, bf16[4,4,128,128]{3,2,1,0:T(8,128)(2,1)}, u32[]{:S(2)}, u32[]{:S(2)}) collective-permute-start(bf16[4,4,128,128]{3,2,1,0:T(8,128)(2,1)S(1)} %get-tuple-element.23), channel_id=1, source_target_pairs={{0,96},{1,97},{2,98},{3,99},{4,100},{5,101},{6,102},{7,103},{8,104... | collective-permute-start | bytes 1572872 | tf_op jit(solution)/shard_map/ppermute | solution.py:213
  130.8 36.1 %collective-permute-start.11 = (bf16[256,512]{1,0:T(8,128)(2,1)S(1)}, bf16[256,512]{1,0:T(8,128)(2,1)}, u32[]{:S(2)}, u32[]{:S(2)}) collective-permute-start(bf16[256,512]{1,0:T(8,128)(2,1)S(1)} %reshape.82), channel_id=1, source_target_pairs={{0,1},{1,0},{2,3},{3,2},{4,5},{5,4},{6,7},{7,6},{8,9},{9,8},{10,11... | collective-permute-start | bytes 786440 | tf_op jit(solution)/shard_map/ppermute | solution.py:252
  154.4 14.4 %collective-permute-start.16 = (bf16[4,128,128]{2,1,0:T(8,128)(2,1)S(1)}, bf16[4,128,128]{2,1,0:T(8,128)(2,1)S(1)}, u32[]{:S(2)}, u32[]{:S(2)}) collective-permute-start(bf16[4,128,128]{2,1,0:T(8,128)(2,1)S(1)} %get-tuple-element.25), channel_id=1, source_target_pairs={{0,16},{1,17},{2,18},{3,19},{4,20},{5,21},{6,22},{7,23},{8,24},{9,... | collective-permute-start | bytes 393224 | tf_op jit(solution)/shard_map/ppermute | solution.py:213
  161.6 10.2 %collective-permute-start.17 = (bf16[4,128,128]{2,1,0:T(8,128)(2,1)S(1)}, bf16[4,128,128]{2,1,0:T(8,128)(2,1)S(1)}, u32[]{:S(2)}, u32[]{:S(2)}) collective-permute-start(bf16[4,128,128]{2,1,0:T(8,128)(2,1)S(1)} %get-tuple-element.27), channel_id=1, source_target_pairs={{0,1},{1,0},{2,3},{3,2},{4,5},{5,4},{6,7},{7,6},{8,9},{9,8},{10,11... | collective-permute-start | bytes 393224 | tf_op jit(solution)/shard_map/ppermute | solution.py:213
  164.6 7.2 %collective-permute-start.18 = (bf16[4,128,128]{2,1,0:T(8,128)(2,1)S(1)}, bf16[4,128,128]{2,1,0:T(8,128)(2,1)S(1)}, u32[]{:S(2)}, u32[]{:S(2)}) collective-permute-start(bf16[4,128,128]{2,1,0:T(8,128)(2,1)S(1)} %get-tuple-element.26), channel_id=1, source_target_pairs={{0,17},{1,16},{2,19},{3,18},{4,21},{5,20},{6,23},{7,22},{8,25},{9,... | collective-permute-start | bytes 393224 | tf_op jit(solution)/shard_map/ppermute | solution.py:213
  165.2 10.2 %collective-permute-start.10 = (bf16[256,512]{1,0:T(8,128)(2,1)S(1)}, bf16[256,512]{1,0:T(8,128)(2,1)S(1)}, u32[]{:S(2)}, u32[]{:S(2)}) collective-permute-start(bf16[256,512]{1,0:T(8,128)(2,1)S(1)} %reshape.81), channel_id=1, source_target_pairs={{0,1},{1,0},{2,3},{3,2},{4,5},{5,4},{6,7},{7,6},{8,9},{9,8},{10,11... | collective-permute-start | bytes 786440 | tf_op jit(solution)/shard_map/ppermute | solution.py:252
  171.8 5.2 %collective-permute-start.19 = (bf16[128,128]{1,0:T(8,128)(2,1)S(1)}, bf16[128,128]{1,0:T(8,128)(2,1)S(1)}, u32[]{:S(2)}, u32[]{:S(2)}) collective-permute-start(bf16[128,128]{1,0:T(8,128)(2,1)S(1)} %get-tuple-element.34), channel_id=1, source_target_pairs={{0,4},{1,5},{2,6},{3,7},{4,8},{5,9},{6,10},{7,11},{8,12},{9,13},{1... | collective-permute-start | bytes 98312 | tf_op jit(solution)/shard_map/ppermute | solution.py:213
  171.9 5.5 %collective-permute-start.20 = (bf16[128,128]{1,0:T(8,128)(2,1)S(1)}, bf16[128,128]{1,0:T(8,128)(2,1)S(1)}, u32[]{:S(2)}, u32[]{:S(2)}) collective-permute-start(bf16[128,128]{1,0:T(8,128)(2,1)S(1)} %get-tuple-element.36), channel_id=1, source_target_pairs={{0,8},{1,9},{2,10},{3,11},{4,12},{5,13},{6,14},{7,15},{8,0},{9,1},... | collective-permute-start | bytes 98312 | tf_op jit(solution)/shard_map/ppermute | solution.py:213
  172.3 5.9 %collective-permute-start.21 = (bf16[128,128]{1,0:T(8,128)(2,1)S(1)}, bf16[128,128]{1,0:T(8,128)(2,1)S(1)}, u32[]{:S(2)}, u32[]{:S(2)}) collective-permute-start(bf16[128,128]{1,0:T(8,128)(2,1)S(1)} %get-tuple-element.35), channel_id=1, source_target_pairs={{0,12},{1,13},{2,14},{3,15},{4,0},{5,1},{6,2},{7,3},{8,4},{9,5},{1... | collective-permute-start | bytes 98312 | tf_op jit(solution)/shard_map/ppermute | solution.py:213
  (4 other events, 51.4 us)

commit v11 on v10

--- a/solution.py
+++ b/solution.py
@@ -98,7 +98,7 @@
 
 
 def _backward_kernel(lists_ref, count_ref, q_ref, qt_ref, kvt_ref, do_ref, dot_ref, lse_ref,
-                     delta_ref, dqt_ref, dkvt_ref, dq_sc):
+                     delta_ref, dqt_ref, own_ref, send_ref, dq_sc, dkvt_ref):
     query_count = lists_ref.shape[0]
     dkvt_ref[...] = jnp.zeros(dkvt_ref.shape, jnp.float32)
     def per_query(qb, carry):
@@ -123,9 +123,18 @@
         return carry
 
     lax.fori_loop(0, query_count, per_query, 0)
-
-
-def attend_local(q_rows, do_rows, kv_t, lists, keep):
+    held = own_ref.shape[0]
+
+    def hand_over(i, carry):
+        own_ref[i] = dkvt_ref[i]
+        for part in range(send_ref.shape[0]):
+            send_ref[part, i] = dkvt_ref[(part + 1) * held + i].astype(jnp.bfloat16)
+        return carry
+
+    lax.fori_loop(0, held, hand_over, 0)
+
+
+def attend_local(q_rows, do_rows, kv_t, lists, keep, outer):
     order = jnp.argsort(1 - keep, axis=1, stable=True)
     lists = jnp.take_along_axis(lists, order, axis=1)
     keep = jnp.broadcast_to(jnp.sum(keep, axis=1, keepdims=True), lists.shape).astype(jnp.int32)
@@ -150,18 +159,23 @@
         ],
         compiler_params=pltpu.CompilerParams(vmem_limit_bytes=VMEM_LIMIT),
     )(lists, keep, q_t, kv_t, do_t)
-    dq_t, dkv_t = pl.pallas_call(
+    held = block_total // outer
+    dq_t, own, send = pl.pallas_call(
         _backward_kernel,
         out_shape=(
             jax.ShapeDtypeStruct((query_count, HEAD_DIM, rows), jnp.bfloat16),
-            jax.ShapeDtypeStruct((block_total, 2 * HEAD_DIM, BLOCK), f32),
+            jax.ShapeDtypeStruct((held, 2 * HEAD_DIM, BLOCK), f32),
+            jax.ShapeDtypeStruct((outer - 1, held, 2 * HEAD_DIM, BLOCK), jnp.bfloat16),
         ),
         in_specs=[_smem(), _smem()] + [_vmem()] * 7,
-        out_specs=(_vmem(), _vmem()),
-        scratch_shapes=[pltpu.VMEM((HEAD_DIM, rows), f32)],
+        out_specs=(_vmem(), _vmem(), _vmem()),
+        scratch_shapes=[
+            pltpu.VMEM((HEAD_DIM, rows), f32),
+            pltpu.VMEM((block_total, 2 * HEAD_DIM, BLOCK), f32),
+        ],
         compiler_params=pltpu.CompilerParams(vmem_limit_bytes=VMEM_LIMIT),
     )(lists, keep, q_rows, q_t, kv_t, do_rows, do_t, lse, delta)
-    return jnp.swapaxes(o_t, 1, 2), jnp.swapaxes(dq_t, 1, 2), dkv_t
+    return jnp.swapaxes(o_t, 1, 2), jnp.swapaxes(dq_t, 1, 2), (own, send)
 
 
 def first_occurrence(block_lists):
@@ -204,9 +218,15 @@
             buf = jnp.concatenate(pieces, axis=0)
         return buf
 
-    def scatter_sum(part, piece_shape):
-        part = part.reshape(tuple(size for _, size in reversed(stages)) + piece_shape)
-        for axis, size in reversed(stages):
+    def scatter_sum(own, sent_first, piece_shape):
+        later = list(reversed(stages))
+        first_axis, first_size = later.pop(0)
+        part = own
+        for shift in range(1, first_size):
+            part = part + lax.ppermute(
+                sent_first[shift - 1], axes, pairs(first_axis, shift)).astype(jnp.float32)
+        part = part.reshape(tuple(size for _, size in later) + piece_shape)
+        for axis, size in later:
             total = part[0]
             for shift in range(1, size):
                 sent = part[shift].astype(jnp.bfloat16)
@@ -245,7 +265,7 @@
         lists = block_lists.astype(jnp.int32)
         keep = first_occurrence(lists)
         o_rows, dq_rows, dkv_t = attend_local(
-            my_heads(queries), my_heads(out_grad), kv_t, held_at(lists), keep)
+            my_heads(queries), my_heads(out_grad), kv_t, held_at(lists), keep, stages[-1][1])
 
         def join_halves(rows):
             mine = rows.reshape(token_rows, width)
@@ -256,7 +276,7 @@
 
         attended = join_halves(o_rows)
         query_grad = join_halves(dq_rows)
-        owned = scatter_sum(dkv_t, (2 * HEAD_DIM, BLOCK))
+        owned = scatter_sum(*dkv_t, (2 * HEAD_DIM, BLOCK))
         key_grad = (owned[:HEAD_DIM].T * SCALE).astype(jnp.bfloat16)
         value_grad = owned[HEAD_DIM:].T.astype(jnp.bfloat16)
         return (attended, query_grad, key_grad, value_grad)

time: 182 us -> 183 us (level)
  starting transfers between devices: 55.8 us -> 66.3 us
  Pallas kernels: 31.4 us -> 21.1 us
  local copies, waits for them, and re-layouts: 24.3 us -> 20.6 us
  waiting for transfers between devices: 52.2 us -> 55.9 us
  other arithmetic: 15 us -> 17.1 us
    ppermute x0 -> x1, starting transfers between devices: none -> 13.4 us  [scatter_sum(): lax.ppermute(sent_first[shift - 1], axes, pairs(first_axis, shift))]
    pallas_call x1, Pallas kernels: 20.2 us -> 13.5 us  [attend_local(): pl.pallas_call(_backward_kernel, out_shape=(jax.ShapeDtypeStruct((query_c...]
    ppermute x10 -> x9, starting transfers between devices: 38.7 us -> 34.6 us  [scatter_sum(): lax.ppermute(sent, axes, pairs(axis, shift)).astype(jnp.float32)]
    ppermute x0 -> x1, waiting for transfers between devices: none -> 4 us  [scatter_sum(): lax.ppermute(sent_first[shift - 1], axes, pairs(first_axis, shift))]
    pallas_call x1, Pallas kernels: 11.2 us -> 7.65 us  [attend_local(): pl.pallas_call(_forward_kernel, out_shape=(jax.ShapeDtypeStruct((query_co...]
    slice x1, local copies, waits for them, and re-layouts: 2.55 us -> 0.1 us  [scatter_sum(): sent = part[shift].astype(jnp.bfloat16)]
    another operation x3, other arithmetic: 4.7 us -> 6.77 us
    ppermute x10 -> x9, waiting for transfers between devices: 27.1 us -> 27.2 us  [scatter_sum(): lax.ppermute(sent, axes, pairs(axis, shift)).astype(jnp.float32)]
  transfers between devices with their start and end apart: 22 -> 22, of which waited for: 15 -> 12; matrix products, arithmetic and copies ran while one was open for 15% -> 14% of each run, Pallas kernels for 0% -> 0%
where the time goes in v11:
time: 183 us; the launch traced here: 182 us
  starting transfers between devices  66.3 us (36%)
  waiting for transfers between devices  55.9 us (31%)
  Pallas kernels  21.1 us (12%)
  local copies, waits for them, and re-layouts  20.6 us (11%)
  other arithmetic  17.1 us (9%)
    ppermute x9, starting transfers between devices, scatter_sum(): lax.ppermute(sent, axes, pairs(axis, shift)).astype(jnp.float32)  34.6 us
    ppermute x9, waiting for transfers between devices, scatter_sum(): lax.ppermute(sent, axes, pairs(axis, shift)).astype(jnp.float32)  27.2 us
    ppermute x10, waiting for transfers between devices, gather_blocks(): pieces.append(lax.ppermute(buf, axes, pairs(axis, size - shift)))  24.7 us
    ppermute x10, starting transfers between devices, gather_blocks(): pieces.append(lax.ppermute(buf, axes, pairs(axis, size - shift)))  14.5 us
    pallas_call x1, Pallas kernels, attend_local(): pl.pallas_call(_backward_kernel, out_shape=(jax.ShapeDtypeStruct((query_c...  13.5 us
    ppermute x1, starting transfers between devices, scatter_sum(): lax.ppermute(sent_first[shift - 1], axes, pairs(first_axis, shift))  13.4 us
    pallas_call x1, Pallas kernels, attend_local(): pl.pallas_call(_forward_kernel, out_shape=(jax.ShapeDtypeStruct((query_co...  7.65 us
    unnamed x24, local copies, waits for them, and re-layouts  7.16 us
  transfers between devices with their start and end apart: 22, of which 12 were waited for; matrix products, arithmetic and copies ran while one was open for 14% of the time, Pallas kernels for 0%

profile of v11, /device:TPU:0, one launch (start us, length us, event | category | flops | bytes accessed | tf_op | source)
XLA Modules:
  0.0 182.0 jit_solution(15036261062485187263)
XLA Ops:
  1.4 3.1 %collective-permute-start = (bf16[1,128,128]{2,1,0:T(8,128)(2,1)S(1)}, bf16[1,128,128]{2,1,0:T(8,128)(2,1)S(1)}, u32[]{:S(2)}, u32[]{:S(2)}) collective-permute-start(bf16[1,128,128]{2,1,0:T(8,128)(2,1)S(1)} %maximum_bitcast_fusion), channel_id=1, source_target_pairs={{0,12},{1,13},{2,14},{3,15},{4,0},{5,1},{6,2},{7,3},{8,4},{9,5},{1... | collective-permute-start | bytes 98312 | tf_op jit(solution)/shard_map/ppermute | solution.py:217
  7.5 2.4 %collective-permute-done.1 = bf16[1,128,128]{2,1,0:T(8,128)(2,1)S(1)} collective-permute-done((bf16[1,128,128]{2,1,0:T(8,128)(2,1)S(1)}, bf16[1,128,128]{2,1,0:T(8,128)(2,1)S(1)}, u32[]{:S(2)}, u32[]{:S(2)}) %collective-permute-start.1) | collective-permute-done | bytes 32800 | tf_op jit(solution)/shard_map/ppermute | solution.py:217
  10.3 2.8 %collective-permute-start.3 = (bf16[4,128,128]{2,1,0:T(8,128)(2,1)S(1)}, bf16[4,128,128]{2,1,0:T(8,128)(2,1)S(1)}, u32[]{:S(2)}, u32[]{:S(2)}) collective-permute-start(bf16[4,128,128]{2,1,0:T(8,128)(2,1)S(1)} %pad_maximum_fusion), channel_id=1, source_target_pairs={{0,17},{1,16},{2,19},{3,18},{4,21},{5,20},{6,23},{7,22},{8,25},{9,... | collective-permute-start | bytes 393224 | tf_op jit(solution)/shard_map/ppermute | solution.py:217
  21.8 4.0 %collective-permute-start.6 = (bf16[16,128,128]{2,1,0:T(8,128)(2,1)S(1)}, bf16[16,128,128]{2,1,0:T(8,128)(2,1)S(1)}, u32[]{:S(2)}, u32[]{:S(2)}) collective-permute-start(bf16[16,128,128]{2,1,0:T(8,128)(2,1)S(1)} %get-tuple-element.41), channel_id=1, source_target_pairs={{0,96},{1,97},{2,98},{3,99},{4,100},{5,101},{6,102},{7,103},{8,104... | collective-permute-start | bytes 1572872 | tf_op jit(solution)/shard_map/ppermute | solution.py:217
  27.1 18.3 %collective-permute-done.6 = bf16[16,128,128]{2,1,0:T(8,128)(2,1)S(1)} collective-permute-done((bf16[16,128,128]{2,1,0:T(8,128)(2,1)S(1)}, bf16[16,128,128]{2,1,0:T(8,128)(2,1)S(1)}, u32[]{:S(2)}, u32[]{:S(2)}) %collective-permute-start.6) | collective-permute-done | bytes 524320 | tf_op jit(solution)/shard_map/ppermute | solution.py:217
  51.5 2.7 %slice_subtract_fusion.3 = (s32[2,48,1]{2,1,0:T(8,128)S(1)}, s32[2,48,1]{2,1,0:T(8,128)S(1)}, s32[2,48,1]{2,1,0:T(8,128)S(1)}, s32[2,48,1]{2,1,0:T(8,128)S(1)}) fusion(s32[2,48,4]{2,1,0:T(8,128)S(1)} %bitcast.80, s32[]{:T(128)} %bitcast.1, s32[]{:T(128)} %bitcast.5, s32[]{:T(128)} %bitcast.3, s32[]{:T(128)} %bitcast.7), kind=kLoop, calls=%fused_computation.49 | loop fusion | flops 384 | bytes 3088 | tf_op jit(solution)/shard_map/sub | solution.py:257
  56.1 1.7 gather_fusion.1
  62.0 1.5 constant_dynamic-update-slice_fusion.17.kvt_ref
  64.2 7.7 %shard_map.93 = (bf16[2,64,1024]{2,1,0:T(8,128)(2,1)}, f32[2,1,1024]{2,1,0:T(1,128)}, f32[2,1,1024]{2,1,0:T(1,128)}) custom-call(s32[2,48]{1,0:T(2,128)} %and_select_fusion.4.lists_ref, s32[2,48]{1,0:T(2,128)} %broadcast_in_dim.22.count_ref, bf16[2,64,1024]{2,1,0:T(8,128)(2,1)} %bitcast.76, ...), custom_call_target="tpu_custom_call" | custom-call | tf_op jit(solution)/shard_map/pallas_call | solution.py:146
  71.8 13.5 %shard_map.94 = (bf16[2,64,1024]{2,1,0:T(8,128)(2,1)}, f32[64,128,128]{2,1,0:T(8,128)}, bf16[1,64,128,128]{3,2,1,0:T(8,128)(2,1)}) custom-call(s32[2,48]{1,0:T(2,128)} %and_select_fusion.4.lists_ref, s32[2,48]{1,0:T(2,128)} %broadcast_in_dim.22.count_ref, bf16[2,1024,64]{2,1,0:T(8,128)(2,1)} %copy-done, bf16[2,64,1024]{2,1,0:T(8,128)(2,1)} %bitcast.77, ...), custom_call_target="tpu_custom_call" | custom-call | tf_op jit(solution)/shard_map/pallas_call | solution.py:163
  85.3 13.4 %collective-permute-start.12 = (bf16[64,128,128]{2,1,0:T(8,128)(2,1)}, bf16[64,128,128]{2,1,0:T(8,128)(2,1)S(1)}, u32[]{:S(2)}, u32[]{:S(2)}) collective-permute-start(bf16[64,128,128]{2,1,0:T(8,128)(2,1)} %bitcast.90), channel_id=1, source_target_pairs={{0,2},{1,3},{2,0},{3,1},{4,6},{5,7},{6,4},{7,5},{8,10},{9,11},{10,... | collective-permute-start | bytes 6291464 | tf_op jit(solution)/shard_map/ppermute | solution.py:226
  98.8 4.0 %collective-permute-done.12 = bf16[64,128,128]{2,1,0:T(8,128)(2,1)S(1)} collective-permute-done((bf16[64,128,128]{2,1,0:T(8,128)(2,1)}, bf16[64,128,128]{2,1,0:T(8,128)(2,1)S(1)}, u32[]{:S(2)}, u32[]{:S(2)}) %collective-permute-start.12) | collective-permute-done | bytes 2097184 | tf_op jit(solution)/shard_map/ppermute | solution.py:226
  102.8 5.3 %fusion.24 = (bf16[64,128,128]{2,1,0:T(8,128)(2,1)S(1)}, f32[64,128,128]{2,1,0:T(8,128)}) fusion(f32[64,128,128]{2,1,0:T(8,128)} %get-tuple-element.16, bf16[64,128,128]{2,1,0:T(8,128)(2,1)S(1)} %collective-permute-done.12), kind=kLoop, calls=%fused_computation.96 | loop fusion | flops 3145728 | bytes 12582912 | tf_op jit(solution)/shard_map/convert.9
  108.2 14.8 %collective-permute-start.13 = (bf16[4,4,128,128]{3,2,1,0:T(8,128)(2,1)S(1)}, bf16[4,4,128,128]{3,2,1,0:T(8,128)(2,1)S(1)}, u32[]{:S(2)}, u32[]{:S(2)}) collective-permute-start(bf16[4,4,128,128]{3,2,1,0:T(8,128)(2,1)S(1)} %bitcast.83), channel_id=1, source_target_pairs={{0,32},{1,33},{2,34},{3,35},{4,36},{5,37},{6,38},{7,39},{8,40},{9,... | collective-permute-start | bytes 1572872 | tf_op jit(solution)/shard_map/ppermute | solution.py:233
  123.0 7.2 %collective-permute-start.14 = (bf16[4,4,128,128]{3,2,1,0:T(8,128)(2,1)S(1)}, bf16[4,4,128,128]{3,2,1,0:T(8,128)(2,1)S(1)}, u32[]{:S(2)}, u32[]{:S(2)}) collective-permute-start(bf16[4,4,128,128]{3,2,1,0:T(8,128)(2,1)S(1)} %bitcast.82), channel_id=1, source_target_pairs={{0,64},{1,65},{2,66},{3,67},{4,68},{5,69},{6,70},{7,71},{8,72},{9,... | collective-permute-start | bytes 1572872 | tf_op jit(solution)/shard_map/ppermute | solution.py:233
  130.2 2.5 %collective-permute-start.15 = (bf16[4,4,128,128]{3,2,1,0:T(8,128)(2,1)S(1)}, bf16[4,4,128,128]{3,2,1,0:T(8,128)(2,1)}, u32[]{:S(2)}, u32[]{:S(2)}) collective-permute-start(bf16[4,4,128,128]{3,2,1,0:T(8,128)(2,1)S(1)} %bitcast.81), channel_id=1, source_target_pairs={{0,96},{1,97},{2,98},{3,99},{4,100},{5,101},{6,102},{7,103},{8,104... | collective-permute-start | bytes 1572872 | tf_op jit(solution)/shard_map/ppermute | solution.py:233
  135.6 18.2 %collective-permute-done.14 = bf16[4,4,128,128]{3,2,1,0:T(8,128)(2,1)S(1)} collective-permute-done((bf16[4,4,128,128]{3,2,1,0:T(8,128)(2,1)S(1)}, bf16[4,4,128,128]{3,2,1,0:T(8,128)(2,1)S(1)}, u32[]{:S(2)}, u32[]{:S(2)}) %collective-permute-start.14) | collective-permute-done | bytes 524320 | tf_op jit(solution)/shard_map/ppermute | solution.py:233
  156.3 2.4 %collective-permute-start.18 = (bf16[4,128,128]{2,1,0:T(8,128)(2,1)S(1)}, bf16[4,128,128]{2,1,0:T(8,128)(2,1)S(1)}, u32[]{:S(2)}, u32[]{:S(2)}) collective-permute-start(bf16[4,128,128]{2,1,0:T(8,128)(2,1)S(1)} %get-tuple-element.28), channel_id=1, source_target_pairs={{0,17},{1,16},{2,19},{3,18},{4,21},{5,20},{6,23},{7,22},{8,25},{9,... | collective-permute-start | bytes 393224 | tf_op jit(solution)/shard_map/ppermute | solution.py:233
  159.4 2.8 %collective-permute-start.10 = (bf16[256,512]{1,0:T(8,128)(2,1)S(1)}, bf16[256,512]{1,0:T(8,128)(2,1)S(1)}, u32[]{:S(2)}, u32[]{:S(2)}) collective-permute-start(bf16[256,512]{1,0:T(8,128)(2,1)S(1)} %reshape.84), channel_id=1, source_target_pairs={{0,1},{1,0},{2,3},{3,2},{4,5},{5,4},{6,7},{7,6},{8,9},{9,8},{10,11... | collective-permute-start | bytes 786440 | tf_op jit(solution)/shard_map/ppermute | solution.py:272
  162.2 2.0 %maximum_select_fusion.1 = bf16[256,1024]{1,0:T(8,128)(2,1)} fusion(bf16[256,512]{1,0:T(8,128)(2,1)} %collective-permute-done.11, bf16[256,512]{1,0:T(8,128)(2,1)S(1)} %reshape.85, pred[]{:T(512)S(6)} %eq.22), kind=kLoop, calls=%fused_computation.5 | loop fusion | flops 2359296 | bytes 1048577 | tf_op jit(solution)/shard_map/jit(_where)/select_n | solution.py:273
  164.1 6.0 %collective-permute-done.16 = bf16[4,128,128]{2,1,0:T(8,128)(2,1)S(1)} collective-permute-done((bf16[4,128,128]{2,1,0:T(8,128)(2,1)S(1)}, bf16[4,128,128]{2,1,0:T(8,128)(2,1)S(1)}, u32[]{:S(2)}, u32[]{:S(2)}) %collective-permute-start.16) | collective-permute-done | bytes 131104 | tf_op jit(solution)/shard_map/ppermute | solution.py:233
  170.2 2.3 %collective-permute-start.19 = (bf16[128,128]{1,0:T(8,128)(2,1)S(1)}, bf16[128,128]{1,0:T(8,128)(2,1)S(1)}, u32[]{:S(2)}, u32[]{:S(2)}) collective-permute-start(bf16[128,128]{1,0:T(8,128)(2,1)S(1)} %get-tuple-element.36), channel_id=1, source_target_pairs={{0,4},{1,5},{2,6},{3,7},{4,8},{5,9},{6,10},{7,11},{8,12},{9,13},{1... | collective-permute-start | bytes 98312 | tf_op jit(solution)/shard_map/ppermute | solution.py:233
  172.6 4.2 %collective-permute-start.20 = (bf16[128,128]{1,0:T(8,128)(2,1)S(1)}, bf16[128,128]{1,0:T(8,128)(2,1)S(1)}, u32[]{:S(2)}, u32[]{:S(2)}) collective-permute-start(bf16[128,128]{1,0:T(8,128)(2,1)S(1)} %get-tuple-element.38), channel_id=1, source_target_pairs={{0,8},{1,9},{2,10},{3,11},{4,12},{5,13},{6,14},{7,15},{8,0},{9,1},... | collective-permute-start | bytes 98312 | tf_op jit(solution)/shard_map/ppermute | solution.py:233
  179.0 1.7 collective-permute-done.21
  (93 shorter events, 36.3 us)
Async XLA Ops:
  0.6 49.6 %copy-start.2 = (s32[128,4]{1,0:T(8,128)S(1)}, s32[128,4]{1,0:T(8,128)}, u32[]{:S(2)}) copy-start(s32[128,4]{1,0:T(8,128)} %constant.80.clone) | copy-start | bytes 6148
  0.6 49.5 %copy-start.5 = (s32[2,48]{1,0:T(2,128)S(1)}, s32[2,48]{1,0:T(2,128)}, u32[]{:S(2)}) copy-start(s32[2,48]{1,0:T(2,128)} %param.10) | copy-start | bytes 1156
  1.4 6.1 %collective-permute-start = (bf16[1,128,128]{2,1,0:T(8,128)(2,1)S(1)}, bf16[1,128,128]{2,1,0:T(8,128)(2,1)S(1)}, u32[]{:S(2)}, u32[]{:S(2)}) collective-permute-start(bf16[1,128,128]{2,1,0:T(8,128)(2,1)S(1)} %maximum_bitcast_fusion), channel_id=1, source_target_pairs={{0,12},{1,13},{2,14},{3,15},{4,0},{5,1},{6,2},{7,3},{8,4},{9,5},{1... | collective-permute-start | bytes 98312 | tf_op jit(solution)/shard_map/ppermute | solution.py:217
  4.6 5.4 %collective-permute-start.1 = (bf16[1,128,128]{2,1,0:T(8,128)(2,1)S(1)}, bf16[1,128,128]{2,1,0:T(8,128)(2,1)S(1)}, u32[]{:S(2)}, u32[]{:S(2)}) collective-permute-start(bf16[1,128,128]{2,1,0:T(8,128)(2,1)S(1)} %maximum_bitcast_fusion), channel_id=1, source_target_pairs={{0,8},{1,9},{2,10},{3,11},{4,12},{5,13},{6,14},{7,15},{8,0},{9,1},... | collective-permute-start | bytes 98312 | tf_op jit(solution)/shard_map/ppermute | solution.py:217
  5.2 5.1 %collective-permute-start.2 = (bf16[1,128,128]{2,1,0:T(8,128)(2,1)S(1)}, bf16[1,128,128]{2,1,0:T(8,128)(2,1)S(1)}, u32[]{:S(2)}, u32[]{:S(2)}) collective-permute-start(bf16[1,128,128]{2,1,0:T(8,128)(2,1)S(1)} %maximum_bitcast_fusion), channel_id=1, source_target_pairs={{0,4},{1,5},{2,6},{3,7},{4,8},{5,9},{6,10},{7,11},{8,12},{9,13},{1... | collective-permute-start | bytes 98312 | tf_op jit(solution)/shard_map/ppermute | solution.py:217
  10.3 7.1 %collective-permute-start.3 = (bf16[4,128,128]{2,1,0:T(8,128)(2,1)S(1)}, bf16[4,128,128]{2,1,0:T(8,128)(2,1)S(1)}, u32[]{:S(2)}, u32[]{:S(2)}) collective-permute-start(bf16[4,128,128]{2,1,0:T(8,128)(2,1)S(1)} %pad_maximum_fusion), channel_id=1, source_target_pairs={{0,17},{1,16},{2,19},{3,18},{4,21},{5,20},{6,23},{7,22},{8,25},{9,... | collective-permute-start | bytes 393224 | tf_op jit(solution)/shard_map/ppermute | solution.py:217
  13.2 6.6 %collective-permute-start.4 = (bf16[4,128,128]{2,1,0:T(8,128)(2,1)S(1)}, bf16[4,128,128]{2,1,0:T(8,128)(2,1)S(1)}, u32[]{:S(2)}, u32[]{:S(2)}) collective-permute-start(bf16[4,128,128]{2,1,0:T(8,128)(2,1)S(1)} %pad_maximum_fusion), channel_id=1, source_target_pairs={{0,1},{1,0},{2,3},{3,2},{4,5},{5,4},{6,7},{7,6},{8,9},{9,8},{10,11... | collective-permute-start | bytes 393224 | tf_op jit(solution)/shard_map/ppermute | solution.py:217
  14.0 7.1 %collective-permute-start.5 = (bf16[4,128,128]{2,1,0:T(8,128)(2,1)S(1)}, bf16[4,128,128]{2,1,0:T(8,128)(2,1)S(1)}, u32[]{:S(2)}, u32[]{:S(2)}) collective-permute-start(bf16[4,128,128]{2,1,0:T(8,128)(2,1)S(1)} %pad_maximum_fusion), channel_id=1, source_target_pairs={{0,16},{1,17},{2,18},{3,19},{4,20},{5,21},{6,22},{7,23},{8,24},{9,... | collective-permute-start | bytes 393224 | tf_op jit(solution)/shard_map/ppermute | solution.py:217
  21.8 23.6 %collective-permute-start.6 = (bf16[16,128,128]{2,1,0:T(8,128)(2,1)S(1)}, bf16[16,128,128]{2,1,0:T(8,128)(2,1)S(1)}, u32[]{:S(2)}, u32[]{:S(2)}) collective-permute-start(bf16[16,128,128]{2,1,0:T(8,128)(2,1)S(1)} %get-tuple-element.41), channel_id=1, source_target_pairs={{0,96},{1,97},{2,98},{3,99},{4,100},{5,101},{6,102},{7,103},{8,104... | collective-permute-start | bytes 1572872 | tf_op jit(solution)/shard_map/ppermute | solution.py:217
  25.9 20.8 %collective-permute-start.7 = (bf16[16,128,128]{2,1,0:T(8,128)(2,1)S(1)}, bf16[16,128,128]{2,1,0:T(8,128)(2,1)S(1)}, u32[]{:S(2)}, u32[]{:S(2)}) collective-permute-start(bf16[16,128,128]{2,1,0:T(8,128)(2,1)S(1)} %get-tuple-element.41), channel_id=1, source_target_pairs={{0,64},{1,65},{2,66},{3,67},{4,68},{5,69},{6,70},{7,71},{8,72},{9,... | collective-permute-start | bytes 1572872 | tf_op jit(solution)/shard_map/ppermute | solution.py:217
  25.9 23.0 %collective-permute-start.8 = (bf16[16,128,128]{2,1,0:T(8,128)(2,1)S(1)}, bf16[16,128,128]{2,1,0:T(8,128)(2,1)S(1)}, u32[]{:S(2)}, u32[]{:S(2)}) collective-permute-start(bf16[16,128,128]{2,1,0:T(8,128)(2,1)S(1)} %get-tuple-element.41), channel_id=1, source_target_pairs={{0,32},{1,33},{2,34},{3,35},{4,36},{5,37},{6,38},{7,39},{8,40},{9,... | collective-permute-start | bytes 1572872 | tf_op jit(solution)/shard_map/ppermute | solution.py:217
  50.1 11.8 %collective-permute-start.9 = (bf16[64,128,128]{2,1,0:T(8,128)(2,1)}, bf16[64,128,128]{2,1,0:T(8,128)(2,1)S(1)}, u32[]{:S(2)}, u32[]{:S(2)}) collective-permute-start(bf16[64,128,128]{2,1,0:T(8,128)(2,1)} %get-tuple-element.30), channel_id=1, source_target_pairs={{0,2},{1,3},{2,0},{3,1},{4,6},{5,7},{6,4},{7,5},{8,10},{9,11},{10,... | collective-permute-start | bytes 6291464 | tf_op jit(solution)/shard_map/ppermute | solution.py:217
  85.3 17.4 %collective-permute-start.12 = (bf16[64,128,128]{2,1,0:T(8,128)(2,1)}, bf16[64,128,128]{2,1,0:T(8,128)(2,1)S(1)}, u32[]{:S(2)}, u32[]{:S(2)}) collective-permute-start(bf16[64,128,128]{2,1,0:T(8,128)(2,1)} %bitcast.90), channel_id=1, source_target_pairs={{0,2},{1,3},{2,0},{3,1},{4,6},{5,7},{6,4},{7,5},{8,10},{9,11},{10,... | collective-permute-start | bytes 6291464 | tf_op jit(solution)/shard_map/ppermute | solution.py:226
  108.2 27.4 %collective-permute-start.13 = (bf16[4,4,128,128]{3,2,1,0:T(8,128)(2,1)S(1)}, bf16[4,4,128,128]{3,2,1,0:T(8,128)(2,1)S(1)}, u32[]{:S(2)}, u32[]{:S(2)}) collective-permute-start(bf16[4,4,128,128]{3,2,1,0:T(8,128)(2,1)S(1)} %bitcast.83), channel_id=1, source_target_pairs={{0,32},{1,33},{2,34},{3,35},{4,36},{5,37},{6,38},{7,39},{8,40},{9,... | collective-permute-start | bytes 1572872 | tf_op jit(solution)/shard_map/ppermute | solution.py:233
  123.0 30.9 %collective-permute-start.14 = (bf16[4,4,128,128]{3,2,1,0:T(8,128)(2,1)S(1)}, bf16[4,4,128,128]{3,2,1,0:T(8,128)(2,1)S(1)}, u32[]{:S(2)}, u32[]{:S(2)}) collective-permute-start(bf16[4,4,128,128]{3,2,1,0:T(8,128)(2,1)S(1)} %bitcast.82), channel_id=1, source_target_pairs={{0,64},{1,65},{2,66},{3,67},{4,68},{5,69},{6,70},{7,71},{8,72},{9,... | collective-permute-start | bytes 1572872 | tf_op jit(solution)/shard_map/ppermute | solution.py:233
  130.2 23.6 %collective-permute-start.15 = (bf16[4,4,128,128]{3,2,1,0:T(8,128)(2,1)S(1)}, bf16[4,4,128,128]{3,2,1,0:T(8,128)(2,1)}, u32[]{:S(2)}, u32[]{:S(2)}) collective-permute-start(bf16[4,4,128,128]{3,2,1,0:T(8,128)(2,1)S(1)} %bitcast.81), channel_id=1, source_target_pairs={{0,96},{1,97},{2,98},{3,99},{4,100},{5,101},{6,102},{7,103},{8,104... | collective-permute-start | bytes 1572872 | tf_op jit(solution)/shard_map/ppermute | solution.py:233
  133.4 28.8 %collective-permute-start.11 = (bf16[256,512]{1,0:T(8,128)(2,1)S(1)}, bf16[256,512]{1,0:T(8,128)(2,1)}, u32[]{:S(2)}, u32[]{:S(2)}) collective-permute-start(bf16[256,512]{1,0:T(8,128)(2,1)S(1)} %reshape.85), channel_id=1, source_target_pairs={{0,1},{1,0},{2,3},{3,2},{4,5},{5,4},{6,7},{7,6},{8,9},{9,8},{10,11... | collective-permute-start | bytes 786440 | tf_op jit(solution)/shard_map/ppermute | solution.py:272
  155.2 14.9 %collective-permute-start.16 = (bf16[4,128,128]{2,1,0:T(8,128)(2,1)S(1)}, bf16[4,128,128]{2,1,0:T(8,128)(2,1)S(1)}, u32[]{:S(2)}, u32[]{:S(2)}) collective-permute-start(bf16[4,128,128]{2,1,0:T(8,128)(2,1)S(1)} %get-tuple-element.27), channel_id=1, source_target_pairs={{0,16},{1,17},{2,18},{3,19},{4,20},{5,21},{6,22},{7,23},{8,24},{9,... | collective-permute-start | bytes 393224 | tf_op jit(solution)/shard_map/ppermute | solution.py:233
  155.3 14.8 %collective-permute-start.17 = (bf16[4,128,128]{2,1,0:T(8,128)(2,1)S(1)}, bf16[4,128,128]{2,1,0:T(8,128)(2,1)S(1)}, u32[]{:S(2)}, u32[]{:S(2)}) collective-permute-start(bf16[4,128,128]{2,1,0:T(8,128)(2,1)S(1)} %get-tuple-element.29), channel_id=1, source_target_pairs={{0,1},{1,0},{2,3},{3,2},{4,5},{5,4},{6,7},{7,6},{8,9},{9,8},{10,11... | collective-permute-start | bytes 393224 | tf_op jit(solution)/shard_map/ppermute | solution.py:233
  156.3 13.8 %collective-permute-start.18 = (bf16[4,128,128]{2,1,0:T(8,128)(2,1)S(1)}, bf16[4,128,128]{2,1,0:T(8,128)(2,1)S(1)}, u32[]{:S(2)}, u32[]{:S(2)}) collective-permute-start(bf16[4,128,128]{2,1,0:T(8,128)(2,1)S(1)} %get-tuple-element.28), channel_id=1, source_target_pairs={{0,17},{1,16},{2,19},{3,18},{4,21},{5,20},{6,23},{7,22},{8,25},{9,... | collective-permute-start | bytes 393224 | tf_op jit(solution)/shard_map/ppermute | solution.py:233
  159.4 17.4 %collective-permute-start.10 = (bf16[256,512]{1,0:T(8,128)(2,1)S(1)}, bf16[256,512]{1,0:T(8,128)(2,1)S(1)}, u32[]{:S(2)}, u32[]{:S(2)}) collective-permute-start(bf16[256,512]{1,0:T(8,128)(2,1)S(1)} %reshape.84), channel_id=1, source_target_pairs={{0,1},{1,0},{2,3},{3,2},{4,5},{5,4},{6,7},{7,6},{8,9},{9,8},{10,11... | collective-permute-start | bytes 786440 | tf_op jit(solution)/shard_map/ppermute | solution.py:272
  170.2 7.5 %collective-permute-start.19 = (bf16[128,128]{1,0:T(8,128)(2,1)S(1)}, bf16[128,128]{1,0:T(8,128)(2,1)S(1)}, u32[]{:S(2)}, u32[]{:S(2)}) collective-permute-start(bf16[128,128]{1,0:T(8,128)(2,1)S(1)} %get-tuple-element.36), channel_id=1, source_target_pairs={{0,4},{1,5},{2,6},{3,7},{4,8},{5,9},{6,10},{7,11},{8,12},{9,13},{1... | collective-permute-start | bytes 98312 | tf_op jit(solution)/shard_map/ppermute | solution.py:233
  172.6 6.5 %collective-permute-start.20 = (bf16[128,128]{1,0:T(8,128)(2,1)S(1)}, bf16[128,128]{1,0:T(8,128)(2,1)S(1)}, u32[]{:S(2)}, u32[]{:S(2)}) collective-permute-start(bf16[128,128]{1,0:T(8,128)(2,1)S(1)} %get-tuple-element.38), channel_id=1, source_target_pairs={{0,8},{1,9},{2,10},{3,11},{4,12},{5,13},{6,14},{7,15},{8,0},{9,1},... | collective-permute-start | bytes 98312 | tf_op jit(solution)/shard_map/ppermute | solution.py:233
  176.8 3.9 %collective-permute-start.21 = (bf16[128,128]{1,0:T(8,128)(2,1)S(1)}, bf16[128,128]{1,0:T(8,128)(2,1)S(1)}, u32[]{:S(2)}, u32[]{:S(2)}) collective-permute-start(bf16[128,128]{1,0:T(8,128)(2,1)S(1)} %get-tuple-element.37), channel_id=1, source_target_pairs={{0,12},{1,13},{2,14},{3,15},{4,0},{5,1},{6,2},{7,3},{8,4},{9,5},{1... | collective-permute-start | bytes 98312 | tf_op jit(solution)/shard_map/ppermute | solution.py:233
  (4 other events, 77.1 us)

commit v12 on v11

--- a/solution.py
+++ b/solution.py
@@ -77,7 +77,7 @@
 
         def visit(slots, qb=qb):
             blocks = [lists_ref[qb, j] for j in slots]
-            st = _nn(_pair_rows(kvt_ref, blocks, 0), qt_ref[qb]) * SCALE
+            st = _nn(_pair_rows(kvt_ref, blocks, 0), qt_ref[qb])
             m_prev = m_sc[...]
             m_new = jnp.maximum(m_prev, jnp.max(st, axis=0, keepdims=True))
             alpha = jnp.exp(m_prev - m_new)
@@ -106,7 +106,7 @@
 
         def visit(slots, qb=qb):
             blocks = [lists_ref[qb, j] for j in slots]
-            st = _nn(_pair_rows(kvt_ref, blocks, 0), qt_ref[qb]) * SCALE
+            st = _nn(_pair_rows(kvt_ref, blocks, 0), qt_ref[qb])
             pt = jnp.exp(st - lse_ref[qb])
             dvt = jnp.transpose(_nn(pt.astype(jnp.bfloat16), do_ref[qb]))
             dpt = _nn(_pair_rows(kvt_ref, blocks, HEAD_DIM), dot_ref[qb])
@@ -142,7 +142,7 @@
     block_total = kv_t.shape[0]
     f32 = jnp.float32
     do_t = jnp.swapaxes(do_rows, 1, 2)
-    q_t = jnp.swapaxes(q_rows, 1, 2)
+    q_t = jnp.swapaxes(q_rows, 1, 2) * jnp.asarray(SCALE, q_rows.dtype)
     o_t, lse, delta = pl.pallas_call(
         _forward_kernel,
         out_shape=(

time: 183 us -> 183 us (level)
  waiting for transfers between devices: 55.9 us -> 53.7 us
    ppermute x1, starting transfers between devices: 13.4 us -> 18 us  [scatter_sum(): lax.ppermute(sent_first[shift - 1], axes, pairs(first_axis, shift))]
    ppermute x9, starting transfers between devices: 34.6 us -> 32.4 us  [scatter_sum(): lax.ppermute(sent, axes, pairs(axis, shift)).astype(jnp.float32)]
    ppermute x9, waiting for transfers between devices: 27.2 us -> 25 us  [scatter_sum(): lax.ppermute(sent, axes, pairs(axis, shift)).astype(jnp.float32)]
    unnamed x24 -> x28, local copies, waits for them, and re-layouts: 7.16 us -> 7.15 us
  transfers between devices with their start and end apart: 22 -> 22, of which waited for: 12 -> 12; matrix products, arithmetic and copies ran while one was open for 14% -> 15% of each run, Pallas kernels for 0% -> 0%
where the time goes in v12:
time: 183 us
  starting transfers between devices  67.4 us (37%)
  waiting for transfers between devices  53.7 us (29%)
  Pallas kernels  22.3 us (12%)
  local copies, waits for them, and re-layouts  20.5 us (11%)
  other arithmetic  17.8 us (10%)
    ppermute x9, starting transfers between devices, scatter_sum(): lax.ppermute(sent, axes, pairs(axis, shift)).astype(jnp.float32)  32.4 us
    ppermute x9, waiting for transfers between devices, scatter_sum(): lax.ppermute(sent, axes, pairs(axis, shift)).astype(jnp.float32)  25 us
    ppermute x10, waiting for transfers between devices, gather_blocks(): pieces.append(lax.ppermute(buf, axes, pairs(axis, size - shift)))  24.7 us
    ppermute x1, starting transfers between devices, scatter_sum(): lax.ppermute(sent_first[shift - 1], axes, pairs(first_axis, shift))  18 us
    ppermute x10, starting transfers between devices, gather_blocks(): pieces.append(lax.ppermute(buf, axes, pairs(axis, size - shift)))  14.5 us
    pallas_call x1, Pallas kernels, attend_local(): pl.pallas_call(_backward_kernel, out_shape=(jax.ShapeDtypeStruct((query_c...  14.3 us
    pallas_call x1, Pallas kernels, attend_local(): pl.pallas_call(_forward_kernel, out_shape=(jax.ShapeDtypeStruct((query_co...  8.07 us
    unnamed x28, local copies, waits for them, and re-layouts  7.15 us
  transfers between devices with their start and end apart: 22, of which 12 were waited for; matrix products, arithmetic and copies ran while one was open for 15% of the time, Pallas kernels for 0%

profile of v12, /device:TPU:0, one launch (start us, length us, event | category | flops | bytes accessed | tf_op | source)
XLA Modules:
  0.0 182.7 jit_solution(12272067974289638531)
XLA Ops:
  1.4 3.1 %collective-permute-start = (bf16[1,128,128]{2,1,0:T(8,128)(2,1)S(1)}, bf16[1,128,128]{2,1,0:T(8,128)(2,1)S(1)}, u32[]{:S(2)}, u32[]{:S(2)}) collective-permute-start(bf16[1,128,128]{2,1,0:T(8,128)(2,1)S(1)} %maximum_bitcast_fusion), channel_id=1, source_target_pairs={{0,12},{1,13},{2,14},{3,15},{4,0},{5,1},{6,2},{7,3},{8,4},{9,5},{1... | collective-permute-start | bytes 98312 | tf_op jit(solution)/shard_map/ppermute | solution.py:217
  7.5 2.4 %collective-permute-done.1 = bf16[1,128,128]{2,1,0:T(8,128)(2,1)S(1)} collective-permute-done((bf16[1,128,128]{2,1,0:T(8,128)(2,1)S(1)}, bf16[1,128,128]{2,1,0:T(8,128)(2,1)S(1)}, u32[]{:S(2)}, u32[]{:S(2)}) %collective-permute-start.1) | collective-permute-done | bytes 32800 | tf_op jit(solution)/shard_map/ppermute | solution.py:217
  10.3 2.8 %collective-permute-start.3 = (bf16[4,128,128]{2,1,0:T(8,128)(2,1)S(1)}, bf16[4,128,128]{2,1,0:T(8,128)(2,1)S(1)}, u32[]{:S(2)}, u32[]{:S(2)}) collective-permute-start(bf16[4,128,128]{2,1,0:T(8,128)(2,1)S(1)} %pad_maximum_fusion), channel_id=1, source_target_pairs={{0,17},{1,16},{2,19},{3,18},{4,21},{5,20},{6,23},{7,22},{8,25},{9,... | collective-permute-start | bytes 393224 | tf_op jit(solution)/shard_map/ppermute | solution.py:217
  21.8 4.0 %collective-permute-start.6 = (bf16[16,128,128]{2,1,0:T(8,128)(2,1)S(1)}, bf16[16,128,128]{2,1,0:T(8,128)(2,1)S(1)}, u32[]{:S(2)}, u32[]{:S(2)}) collective-permute-start(bf16[16,128,128]{2,1,0:T(8,128)(2,1)S(1)} %get-tuple-element.41), channel_id=1, source_target_pairs={{0,96},{1,97},{2,98},{3,99},{4,100},{5,101},{6,102},{7,103},{8,104... | collective-permute-start | bytes 1572872 | tf_op jit(solution)/shard_map/ppermute | solution.py:217
  27.1 18.3 %collective-permute-done.6 = bf16[16,128,128]{2,1,0:T(8,128)(2,1)S(1)} collective-permute-done((bf16[16,128,128]{2,1,0:T(8,128)(2,1)S(1)}, bf16[16,128,128]{2,1,0:T(8,128)(2,1)S(1)}, u32[]{:S(2)}, u32[]{:S(2)}) %collective-permute-start.6) | collective-permute-done | bytes 524320 | tf_op jit(solution)/shard_map/ppermute | solution.py:217
  51.5 2.7 %slice_subtract_fusion.3 = (s32[2,48,1]{2,1,0:T(8,128)S(1)}, s32[2,48,1]{2,1,0:T(8,128)S(1)}, s32[2,48,1]{2,1,0:T(8,128)S(1)}, s32[2,48,1]{2,1,0:T(8,128)S(1)}) fusion(s32[2,48,4]{2,1,0:T(8,128)S(1)} %bitcast.79, s32[]{:T(128)} %bitcast.1, s32[]{:T(128)} %bitcast.5, s32[]{:T(128)} %bitcast.3, s32[]{:T(128)} %bitcast.7), kind=kLoop, calls=%fused_computation.50 | loop fusion | flops 384 | bytes 3088 | tf_op jit(solution)/shard_map/sub | solution.py:257
  56.1 1.7 gather_fusion.1
  64.8 8.1 %shard_map.93 = (bf16[2,64,1024]{2,1,0:T(8,128)(2,1)}, f32[2,1,1024]{2,1,0:T(1,128)}, f32[2,1,1024]{2,1,0:T(1,128)}) custom-call(s32[2,48]{1,0:T(2,128)} %and_select_fusion.4.lists_ref, s32[2,48]{1,0:T(2,128)} %broadcast_in_dim.22.count_ref, bf16[2,64,1024]{2,1,0:T(8,128)(2,1)} %multiply_bitcast_fusion.qt_ref, ...), custom_call_target="tpu_custom_call" | custom-call | tf_op jit(solution)/shard_map/pallas_call | solution.py:146
  72.9 14.3 %shard_map.94 = (bf16[2,64,1024]{2,1,0:T(8,128)(2,1)}, f32[64,128,128]{2,1,0:T(8,128)}, bf16[1,64,128,128]{3,2,1,0:T(8,128)(2,1)}) custom-call(s32[2,48]{1,0:T(2,128)} %and_select_fusion.4.lists_ref, s32[2,48]{1,0:T(2,128)} %broadcast_in_dim.22.count_ref, bf16[2,1024,64]{2,1,0:T(8,128)(2,1)} %copy-done, bf16[2,64,1024]{2,1,0:T(8,128)(2,1)} %multiply_bitcast_fusion.qt_ref, ...), custom_call_target="tpu_custom_call" | custom-call | tf_op jit(solution)/shard_map/pallas_call | solution.py:163
  87.2 18.0 %collective-permute-start.12 = (bf16[64,128,128]{2,1,0:T(8,128)(2,1)}, bf16[64,128,128]{2,1,0:T(8,128)(2,1)S(1)}, u32[]{:S(2)}, u32[]{:S(2)}) collective-permute-start(bf16[64,128,128]{2,1,0:T(8,128)(2,1)} %bitcast.89), channel_id=1, source_target_pairs={{0,2},{1,3},{2,0},{3,1},{4,6},{5,7},{6,4},{7,5},{8,10},{9,11},{10,... | collective-permute-start | bytes 6291464 | tf_op jit(solution)/shard_map/ppermute | solution.py:226
  105.2 4.0 %collective-permute-done.12 = bf16[64,128,128]{2,1,0:T(8,128)(2,1)S(1)} collective-permute-done((bf16[64,128,128]{2,1,0:T(8,128)(2,1)}, bf16[64,128,128]{2,1,0:T(8,128)(2,1)S(1)}, u32[]{:S(2)}, u32[]{:S(2)}) %collective-permute-start.12) | collective-permute-done | bytes 2097184 | tf_op jit(solution)/shard_map/ppermute | solution.py:226
  109.2 5.3 %fusion.24 = (bf16[64,128,128]{2,1,0:T(8,128)(2,1)S(1)}, f32[64,128,128]{2,1,0:T(8,128)}) fusion(f32[64,128,128]{2,1,0:T(8,128)} %get-tuple-element.16, bf16[64,128,128]{2,1,0:T(8,128)(2,1)S(1)} %collective-permute-done.12), kind=kLoop, calls=%fused_computation.97 | loop fusion | flops 3145728 | bytes 12582912 | tf_op jit(solution)/shard_map/convert.9
  114.6 4.5 %collective-permute-start.13 = (bf16[4,4,128,128]{3,2,1,0:T(8,128)(2,1)S(1)}, bf16[4,4,128,128]{3,2,1,0:T(8,128)(2,1)S(1)}, u32[]{:S(2)}, u32[]{:S(2)}) collective-permute-start(bf16[4,4,128,128]{3,2,1,0:T(8,128)(2,1)S(1)} %bitcast.82), channel_id=1, source_target_pairs={{0,32},{1,33},{2,34},{3,35},{4,36},{5,37},{6,38},{7,39},{8,40},{9,... | collective-permute-start | bytes 1572872 | tf_op jit(solution)/shard_map/ppermute | solution.py:233
  119.1 5.1 %collective-permute-start.14 = (bf16[4,4,128,128]{3,2,1,0:T(8,128)(2,1)S(1)}, bf16[4,4,128,128]{3,2,1,0:T(8,128)(2,1)S(1)}, u32[]{:S(2)}, u32[]{:S(2)}) collective-permute-start(bf16[4,4,128,128]{3,2,1,0:T(8,128)(2,1)S(1)} %bitcast.81), channel_id=1, source_target_pairs={{0,64},{1,65},{2,66},{3,67},{4,68},{5,69},{6,70},{7,71},{8,72},{9,... | collective-permute-start | bytes 1572872 | tf_op jit(solution)/shard_map/ppermute | solution.py:233
  127.0 8.0 %collective-permute-done.13 = bf16[4,4,128,128]{3,2,1,0:T(8,128)(2,1)S(1)} collective-permute-done((bf16[4,4,128,128]{3,2,1,0:T(8,128)(2,1)S(1)}, bf16[4,4,128,128]{3,2,1,0:T(8,128)(2,1)S(1)}, u32[]{:S(2)}, u32[]{:S(2)}) %collective-permute-start.13) | collective-permute-done | bytes 524320 | tf_op jit(solution)/shard_map/ppermute | solution.py:233
  135.0 12.4 %collective-permute-done.14 = bf16[4,4,128,128]{3,2,1,0:T(8,128)(2,1)S(1)} collective-permute-done((bf16[4,4,128,128]{3,2,1,0:T(8,128)(2,1)S(1)}, bf16[4,4,128,128]{3,2,1,0:T(8,128)(2,1)S(1)}, u32[]{:S(2)}, u32[]{:S(2)}) %collective-permute-start.14) | collective-permute-done | bytes 524320 | tf_op jit(solution)/shard_map/ppermute | solution.py:233
  148.8 7.2 %collective-permute-start.16 = (bf16[4,128,128]{2,1,0:T(8,128)(2,1)S(1)}, bf16[4,128,128]{2,1,0:T(8,128)(2,1)S(1)}, u32[]{:S(2)}, u32[]{:S(2)}) collective-permute-start(bf16[4,128,128]{2,1,0:T(8,128)(2,1)S(1)} %get-tuple-element.27), channel_id=1, source_target_pairs={{0,16},{1,17},{2,18},{3,19},{4,20},{5,21},{6,22},{7,23},{8,24},{9,... | collective-permute-start | bytes 393224 | tf_op jit(solution)/shard_map/ppermute | solution.py:233
  156.1 3.0 %collective-permute-start.17 = (bf16[4,128,128]{2,1,0:T(8,128)(2,1)S(1)}, bf16[4,128,128]{2,1,0:T(8,128)(2,1)S(1)}, u32[]{:S(2)}, u32[]{:S(2)}) collective-permute-start(bf16[4,128,128]{2,1,0:T(8,128)(2,1)S(1)} %get-tuple-element.29), channel_id=1, source_target_pairs={{0,1},{1,0},{2,3},{3,2},{4,5},{5,4},{6,7},{7,6},{8,9},{9,8},{10,11... | collective-permute-start | bytes 393224 | tf_op jit(solution)/shard_map/ppermute | solution.py:233
  159.7 1.6 collective-permute-start.10
  161.3 2.0 %maximum_select_fusion.1 = bf16[256,1024]{1,0:T(8,128)(2,1)} fusion(bf16[256,512]{1,0:T(8,128)(2,1)} %collective-permute-done.11, bf16[256,512]{1,0:T(8,128)(2,1)S(1)} %reshape.85, pred[]{:T(512)S(6)} %eq.22), kind=kLoop, calls=%fused_computation.5 | loop fusion | flops 2359296 | bytes 1048577 | tf_op jit(solution)/shard_map/jit(_where)/select_n | solution.py:273
  163.3 2.9 %collective-permute-done.17 = bf16[4,128,128]{2,1,0:T(8,128)(2,1)S(1)} collective-permute-done((bf16[4,128,128]{2,1,0:T(8,128)(2,1)S(1)}, bf16[4,128,128]{2,1,0:T(8,128)(2,1)S(1)}, u32[]{:S(2)}, u32[]{:S(2)}) %collective-permute-start.17) | collective-permute-done | bytes 131104 | tf_op jit(solution)/shard_map/ppermute | solution.py:233
  166.3 9.8 %collective-permute-start.19 = (bf16[128,128]{1,0:T(8,128)(2,1)S(1)}, bf16[128,128]{1,0:T(8,128)(2,1)S(1)}, u32[]{:S(2)}, u32[]{:S(2)}) collective-permute-start(bf16[128,128]{1,0:T(8,128)(2,1)S(1)} %get-tuple-element.36), channel_id=1, source_target_pairs={{0,4},{1,5},{2,6},{3,7},{4,8},{5,9},{6,10},{7,11},{8,12},{9,13},{1... | collective-permute-start | bytes 98312 | tf_op jit(solution)/shard_map/ppermute | solution.py:233
  177.2 1.6 collective-permute-start.21
  179.7 1.7 collective-permute-done.20
  (98 shorter events, 37.2 us)
Async XLA Ops:
  0.6 49.6 %copy-start.2 = (s32[128,4]{1,0:T(8,128)S(1)}, s32[128,4]{1,0:T(8,128)}, u32[]{:S(2)}) copy-start(s32[128,4]{1,0:T(8,128)} %constant.82.clone) | copy-start | bytes 6148
  0.6 49.5 %copy-start.7 = (s32[2,48]{1,0:T(2,128)S(1)}, s32[2,48]{1,0:T(2,128)}, u32[]{:S(2)}) copy-start(s32[2,48]{1,0:T(2,128)} %param.10) | copy-start | bytes 1156
  1.4 6.1 %collective-permute-start = (bf16[1,128,128]{2,1,0:T(8,128)(2,1)S(1)}, bf16[1,128,128]{2,1,0:T(8,128)(2,1)S(1)}, u32[]{:S(2)}, u32[]{:S(2)}) collective-permute-start(bf16[1,128,128]{2,1,0:T(8,128)(2,1)S(1)} %maximum_bitcast_fusion), channel_id=1, source_target_pairs={{0,12},{1,13},{2,14},{3,15},{4,0},{5,1},{6,2},{7,3},{8,4},{9,5},{1... | collective-permute-start | bytes 98312 | tf_op jit(solution)/shard_map/ppermute | solution.py:217
  4.6 5.4 %collective-permute-start.1 = (bf16[1,128,128]{2,1,0:T(8,128)(2,1)S(1)}, bf16[1,128,128]{2,1,0:T(8,128)(2,1)S(1)}, u32[]{:S(2)}, u32[]{:S(2)}) collective-permute-start(bf16[1,128,128]{2,1,0:T(8,128)(2,1)S(1)} %maximum_bitcast_fusion), channel_id=1, source_target_pairs={{0,8},{1,9},{2,10},{3,11},{4,12},{5,13},{6,14},{7,15},{8,0},{9,1},... | collective-permute-start | bytes 98312 | tf_op jit(solution)/shard_map/ppermute | solution.py:217
  5.2 5.1 %collective-permute-start.2 = (bf16[1,128,128]{2,1,0:T(8,128)(2,1)S(1)}, bf16[1,128,128]{2,1,0:T(8,128)(2,1)S(1)}, u32[]{:S(2)}, u32[]{:S(2)}) collective-permute-start(bf16[1,128,128]{2,1,0:T(8,128)(2,1)S(1)} %maximum_bitcast_fusion), channel_id=1, source_target_pairs={{0,4},{1,5},{2,6},{3,7},{4,8},{5,9},{6,10},{7,11},{8,12},{9,13},{1... | collective-permute-start | bytes 98312 | tf_op jit(solution)/shard_map/ppermute | solution.py:217
  10.3 7.1 %collective-permute-start.3 = (bf16[4,128,128]{2,1,0:T(8,128)(2,1)S(1)}, bf16[4,128,128]{2,1,0:T(8,128)(2,1)S(1)}, u32[]{:S(2)}, u32[]{:S(2)}) collective-permute-start(bf16[4,128,128]{2,1,0:T(8,128)(2,1)S(1)} %pad_maximum_fusion), channel_id=1, source_target_pairs={{0,17},{1,16},{2,19},{3,18},{4,21},{5,20},{6,23},{7,22},{8,25},{9,... | collective-permute-start | bytes 393224 | tf_op jit(solution)/shard_map/ppermute | solution.py:217
  13.2 6.6 %collective-permute-start.4 = (bf16[4,128,128]{2,1,0:T(8,128)(2,1)S(1)}, bf16[4,128,128]{2,1,0:T(8,128)(2,1)S(1)}, u32[]{:S(2)}, u32[]{:S(2)}) collective-permute-start(bf16[4,128,128]{2,1,0:T(8,128)(2,1)S(1)} %pad_maximum_fusion), channel_id=1, source_target_pairs={{0,1},{1,0},{2,3},{3,2},{4,5},{5,4},{6,7},{7,6},{8,9},{9,8},{10,11... | collective-permute-start | bytes 393224 | tf_op jit(solution)/shard_map/ppermute | solution.py:217
  14.0 7.1 %collective-permute-start.5 = (bf16[4,128,128]{2,1,0:T(8,128)(2,1)S(1)}, bf16[4,128,128]{2,1,0:T(8,128)(2,1)S(1)}, u32[]{:S(2)}, u32[]{:S(2)}) collective-permute-start(bf16[4,128,128]{2,1,0:T(8,128)(2,1)S(1)} %pad_maximum_fusion), channel_id=1, source_target_pairs={{0,16},{1,17},{2,18},{3,19},{4,20},{5,21},{6,22},{7,23},{8,24},{9,... | collective-permute-start | bytes 393224 | tf_op jit(solution)/shard_map/ppermute | solution.py:217
  21.8 23.6 %collective-permute-start.6 = (bf16[16,128,128]{2,1,0:T(8,128)(2,1)S(1)}, bf16[16,128,128]{2,1,0:T(8,128)(2,1)S(1)}, u32[]{:S(2)}, u32[]{:S(2)}) collective-permute-start(bf16[16,128,128]{2,1,0:T(8,128)(2,1)S(1)} %get-tuple-element.41), channel_id=1, source_target_pairs={{0,96},{1,97},{2,98},{3,99},{4,100},{5,101},{6,102},{7,103},{8,104... | collective-permute-start | bytes 1572872 | tf_op jit(solution)/shard_map/ppermute | solution.py:217
  25.9 20.9 %collective-permute-start.7 = (bf16[16,128,128]{2,1,0:T(8,128)(2,1)S(1)}, bf16[16,128,128]{2,1,0:T(8,128)(2,1)S(1)}, u32[]{:S(2)}, u32[]{:S(2)}) collective-permute-start(bf16[16,128,128]{2,1,0:T(8,128)(2,1)S(1)} %get-tuple-element.41), channel_id=1, source_target_pairs={{0,64},{1,65},{2,66},{3,67},{4,68},{5,69},{6,70},{7,71},{8,72},{9,... | collective-permute-start | bytes 1572872 | tf_op jit(solution)/shard_map/ppermute | solution.py:217
  25.9 23.0 %collective-permute-start.8 = (bf16[16,128,128]{2,1,0:T(8,128)(2,1)S(1)}, bf16[16,128,128]{2,1,0:T(8,128)(2,1)S(1)}, u32[]{:S(2)}, u32[]{:S(2)}) collective-permute-start(bf16[16,128,128]{2,1,0:T(8,128)(2,1)S(1)} %get-tuple-element.41), channel_id=1, source_target_pairs={{0,32},{1,33},{2,34},{3,35},{4,36},{5,37},{6,38},{7,39},{8,40},{9,... | collective-permute-start | bytes 1572872 | tf_op jit(solution)/shard_map/ppermute | solution.py:217
  50.1 12.5 %collective-permute-start.9 = (bf16[64,128,128]{2,1,0:T(8,128)(2,1)}, bf16[64,128,128]{2,1,0:T(8,128)(2,1)S(1)}, u32[]{:S(2)}, u32[]{:S(2)}) collective-permute-start(bf16[64,128,128]{2,1,0:T(8,128)(2,1)} %get-tuple-element.30), channel_id=1, source_target_pairs={{0,2},{1,3},{2,0},{3,1},{4,6},{5,7},{6,4},{7,5},{8,10},{9,11},{10,... | collective-permute-start | bytes 6291464 | tf_op jit(solution)/shard_map/ppermute | solution.py:217
  87.2 22.0 %collective-permute-start.12 = (bf16[64,128,128]{2,1,0:T(8,128)(2,1)}, bf16[64,128,128]{2,1,0:T(8,128)(2,1)S(1)}, u32[]{:S(2)}, u32[]{:S(2)}) collective-permute-start(bf16[64,128,128]{2,1,0:T(8,128)(2,1)} %bitcast.89), channel_id=1, source_target_pairs={{0,2},{1,3},{2,0},{3,1},{4,6},{5,7},{6,4},{7,5},{8,10},{9,11},{10,... | collective-permute-start | bytes 6291464 | tf_op jit(solution)/shard_map/ppermute | solution.py:226
  114.6 20.4 %collective-permute-start.13 = (bf16[4,4,128,128]{3,2,1,0:T(8,128)(2,1)S(1)}, bf16[4,4,128,128]{3,2,1,0:T(8,128)(2,1)S(1)}, u32[]{:S(2)}, u32[]{:S(2)}) collective-permute-start(bf16[4,4,128,128]{3,2,1,0:T(8,128)(2,1)S(1)} %bitcast.82), channel_id=1, source_target_pairs={{0,32},{1,33},{2,34},{3,35},{4,36},{5,37},{6,38},{7,39},{8,40},{9,... | collective-permute-start | bytes 1572872 | tf_op jit(solution)/shard_map/ppermute | solution.py:233
  119.1 28.3 %collective-permute-start.14 = (bf16[4,4,128,128]{3,2,1,0:T(8,128)(2,1)S(1)}, bf16[4,4,128,128]{3,2,1,0:T(8,128)(2,1)S(1)}, u32[]{:S(2)}, u32[]{:S(2)}) collective-permute-start(bf16[4,4,128,128]{3,2,1,0:T(8,128)(2,1)S(1)} %bitcast.81), channel_id=1, source_target_pairs={{0,64},{1,65},{2,66},{3,67},{4,68},{5,69},{6,70},{7,71},{8,72},{9,... | collective-permute-start | bytes 1572872 | tf_op jit(solution)/shard_map/ppermute | solution.py:233
  124.2 23.2 %collective-permute-start.15 = (bf16[4,4,128,128]{3,2,1,0:T(8,128)(2,1)S(1)}, bf16[4,4,128,128]{3,2,1,0:T(8,128)(2,1)}, u32[]{:S(2)}, u32[]{:S(2)}) collective-permute-start(bf16[4,4,128,128]{3,2,1,0:T(8,128)(2,1)S(1)} %bitcast.80), channel_id=1, source_target_pairs={{0,96},{1,97},{2,98},{3,99},{4,100},{5,101},{6,102},{7,103},{8,104... | collective-permute-start | bytes 1572872 | tf_op jit(solution)/shard_map/ppermute | solution.py:233
  124.9 36.4 %collective-permute-start.11 = (bf16[256,512]{1,0:T(8,128)(2,1)S(1)}, bf16[256,512]{1,0:T(8,128)(2,1)}, u32[]{:S(2)}, u32[]{:S(2)}) collective-permute-start(bf16[256,512]{1,0:T(8,128)(2,1)S(1)} %reshape.85), channel_id=1, source_target_pairs={{0,1},{1,0},{2,3},{3,2},{4,5},{5,4},{6,7},{7,6},{8,9},{9,8},{10,11... | collective-permute-start | bytes 786440 | tf_op jit(solution)/shard_map/ppermute | solution.py:272
  148.8 14.4 %collective-permute-start.16 = (bf16[4,128,128]{2,1,0:T(8,128)(2,1)S(1)}, bf16[4,128,128]{2,1,0:T(8,128)(2,1)S(1)}, u32[]{:S(2)}, u32[]{:S(2)}) collective-permute-start(bf16[4,128,128]{2,1,0:T(8,128)(2,1)S(1)} %get-tuple-element.27), channel_id=1, source_target_pairs={{0,16},{1,17},{2,18},{3,19},{4,20},{5,21},{6,22},{7,23},{8,24},{9,... | collective-permute-start | bytes 393224 | tf_op jit(solution)/shard_map/ppermute | solution.py:233
  156.1 10.1 %collective-permute-start.17 = (bf16[4,128,128]{2,1,0:T(8,128)(2,1)S(1)}, bf16[4,128,128]{2,1,0:T(8,128)(2,1)S(1)}, u32[]{:S(2)}, u32[]{:S(2)}) collective-permute-start(bf16[4,128,128]{2,1,0:T(8,128)(2,1)S(1)} %get-tuple-element.29), channel_id=1, source_target_pairs={{0,1},{1,0},{2,3},{3,2},{4,5},{5,4},{6,7},{7,6},{8,9},{9,8},{10,11... | collective-permute-start | bytes 393224 | tf_op jit(solution)/shard_map/ppermute | solution.py:233
  159.0 7.2 %collective-permute-start.18 = (bf16[4,128,128]{2,1,0:T(8,128)(2,1)S(1)}, bf16[4,128,128]{2,1,0:T(8,128)(2,1)S(1)}, u32[]{:S(2)}, u32[]{:S(2)}) collective-permute-start(bf16[4,128,128]{2,1,0:T(8,128)(2,1)S(1)} %get-tuple-element.28), channel_id=1, source_target_pairs={{0,17},{1,16},{2,19},{3,18},{4,21},{5,20},{6,23},{7,22},{8,25},{9,... | collective-permute-start | bytes 393224 | tf_op jit(solution)/shard_map/ppermute | solution.py:233
  159.7 19.2 %collective-permute-start.10 = (bf16[256,512]{1,0:T(8,128)(2,1)S(1)}, bf16[256,512]{1,0:T(8,128)(2,1)S(1)}, u32[]{:S(2)}, u32[]{:S(2)}) collective-permute-start(bf16[256,512]{1,0:T(8,128)(2,1)S(1)} %reshape.84), channel_id=1, source_target_pairs={{0,1},{1,0},{2,3},{3,2},{4,5},{5,4},{6,7},{7,6},{8,9},{9,8},{10,11... | collective-permute-start | bytes 786440 | tf_op jit(solution)/shard_map/ppermute | solution.py:272
  166.3 13.5 %collective-permute-start.19 = (bf16[128,128]{1,0:T(8,128)(2,1)S(1)}, bf16[128,128]{1,0:T(8,128)(2,1)S(1)}, u32[]{:S(2)}, u32[]{:S(2)}) collective-permute-start(bf16[128,128]{1,0:T(8,128)(2,1)S(1)} %get-tuple-element.36), channel_id=1, source_target_pairs={{0,4},{1,5},{2,6},{3,7},{4,8},{5,9},{6,10},{7,11},{8,12},{9,13},{1... | collective-permute-start | bytes 98312 | tf_op jit(solution)/shard_map/ppermute | solution.py:233
  176.0 5.4 %collective-permute-start.20 = (bf16[128,128]{1,0:T(8,128)(2,1)S(1)}, bf16[128,128]{1,0:T(8,128)(2,1)S(1)}, u32[]{:S(2)}, u32[]{:S(2)}) collective-permute-start(bf16[128,128]{1,0:T(8,128)(2,1)S(1)} %get-tuple-element.38), channel_id=1, source_target_pairs={{0,8},{1,9},{2,10},{3,11},{4,12},{5,13},{6,14},{7,15},{8,0},{9,1},... | collective-permute-start | bytes 98312 | tf_op jit(solution)/shard_map/ppermute | solution.py:233
  177.2 4.2 %collective-permute-start.21 = (bf16[128,128]{1,0:T(8,128)(2,1)S(1)}, bf16[128,128]{1,0:T(8,128)(2,1)S(1)}, u32[]{:S(2)}, u32[]{:S(2)}) collective-permute-start(bf16[128,128]{1,0:T(8,128)(2,1)S(1)} %get-tuple-element.37), channel_id=1, source_target_pairs={{0,12},{1,13},{2,14},{3,15},{4,0},{5,1},{6,2},{7,3},{8,4},{9,5},{1... | collective-permute-start | bytes 98312 | tf_op jit(solution)/shard_map/ppermute | solution.py:233
  (6 other events, 144.9 us)

commit v13 on v11

--- a/solution.py
+++ b/solution.py
@@ -67,7 +67,7 @@
         size //= 2
 
 
-def _forward_kernel(lists_ref, count_ref, qt_ref, kvt_ref, dot_ref,
+def _forward_kernel(lists_ref, count_ref, pos_ref, qt_ref, kvt_ref, dot_ref,
                     ot_ref, lse_ref, delta_ref, m_sc, l_sc, acc_sc):
     query_count = lists_ref.shape[0]
     def per_query(qb, carry):
@@ -76,7 +76,7 @@
         acc_sc[...] = jnp.zeros(acc_sc.shape, jnp.float32)
 
         def visit(slots, qb=qb):
-            blocks = [lists_ref[qb, j] for j in slots]
+            blocks = [pos_ref[lists_ref[qb, j]] for j in slots]
             st = _nn(_pair_rows(kvt_ref, blocks, 0), qt_ref[qb]) * SCALE
             m_prev = m_sc[...]
             m_new = jnp.maximum(m_prev, jnp.max(st, axis=0, keepdims=True))
@@ -97,7 +97,7 @@
     lax.fori_loop(0, query_count, per_query, 0)
 
 
-def _backward_kernel(lists_ref, count_ref, q_ref, qt_ref, kvt_ref, do_ref, dot_ref, lse_ref,
+def _backward_kernel(lists_ref, count_ref, pos_ref, q_ref, qt_ref, kvt_ref, do_ref, dot_ref, lse_ref,
                      delta_ref, dqt_ref, own_ref, send_ref, dq_sc, dkvt_ref):
     query_count = lists_ref.shape[0]
     dkvt_ref[...] = jnp.zeros(dkvt_ref.shape, jnp.float32)
@@ -105,7 +105,7 @@
         dq_sc[...] = jnp.zeros(dq_sc.shape, jnp.float32)
 
         def visit(slots, qb=qb):
-            blocks = [lists_ref[qb, j] for j in slots]
+            blocks = [pos_ref[lists_ref[qb, j]] for j in slots]
             st = _nn(_pair_rows(kvt_ref, blocks, 0), qt_ref[qb]) * SCALE
             pt = jnp.exp(st - lse_ref[qb])
             dvt = jnp.transpose(_nn(pt.astype(jnp.bfloat16), do_ref[qb]))
@@ -134,9 +134,11 @@
     lax.fori_loop(0, held, hand_over, 0)
 
 
-def attend_local(q_rows, do_rows, kv_t, lists, keep, outer):
-    order = jnp.argsort(1 - keep, axis=1, stable=True)
-    lists = jnp.take_along_axis(lists, order, axis=1)
+def attend_local(q_rows, do_rows, kv_t, lists, keep, outer, positions):
+    slots = lists.shape[1]
+    rank = jnp.cumsum(keep, axis=1) - 1
+    hit = (rank[:, :, None] == jnp.arange(slots, dtype=jnp.int32)[None, None, :]) & (keep[:, :, None] == 1)
+    lists = jnp.sum(jnp.where(hit, lists[:, :, None], 0), axis=1).astype(jnp.int32)
     keep = jnp.broadcast_to(jnp.sum(keep, axis=1, keepdims=True), lists.shape).astype(jnp.int32)
     query_count, rows, _ = q_rows.shape
     block_total = kv_t.shape[0]
@@ -150,7 +152,7 @@
             jax.ShapeDtypeStruct((query_count, 1, rows), f32),
             jax.ShapeDtypeStruct((query_count, 1, rows), f32),
         ),
-        in_specs=[_smem(), _smem(), _vmem(), _vmem(), _vmem()],
+        in_specs=[_smem(), _smem(), _smem(), _vmem(), _vmem(), _vmem()],
         out_specs=(_vmem(), _vmem(), _vmem()),
         scratch_shapes=[
             pltpu.VMEM((1, rows), f32),
@@ -158,7 +160,7 @@
             pltpu.VMEM((HEAD_DIM, rows), f32),
         ],
         compiler_params=pltpu.CompilerParams(vmem_limit_bytes=VMEM_LIMIT),
-    )(lists, keep, q_t, kv_t, do_t)
+    )(lists, keep, positions, q_t, kv_t, do_t)
     held = block_total // outer
     dq_t, own, send = pl.pallas_call(
         _backward_kernel,
@@ -167,14 +169,14 @@
             jax.ShapeDtypeStruct((held, 2 * HEAD_DIM, BLOCK), f32),
             jax.ShapeDtypeStruct((outer - 1, held, 2 * HEAD_DIM, BLOCK), jnp.bfloat16),
         ),
-        in_specs=[_smem(), _smem()] + [_vmem()] * 7,
+        in_specs=[_smem(), _smem(), _smem()] + [_vmem()] * 7,
         out_specs=(_vmem(), _vmem(), _vmem()),
         scratch_shapes=[
             pltpu.VMEM((HEAD_DIM, rows), f32),
             pltpu.VMEM((block_total, 2 * HEAD_DIM, BLOCK), f32),
         ],
         compiler_params=pltpu.CompilerParams(vmem_limit_bytes=VMEM_LIMIT),
-    )(lists, keep, q_rows, q_t, kv_t, do_rows, do_t, lse, delta)
+    )(lists, keep, positions, q_rows, q_t, kv_t, do_rows, do_t, lse, delta)
     return jnp.swapaxes(o_t, 1, 2), jnp.swapaxes(dq_t, 1, 2), (own, send)
 
 
@@ -265,7 +267,8 @@
         lists = block_lists.astype(jnp.int32)
         keep = first_occurrence(lists)
         o_rows, dq_rows, dkv_t = attend_local(
-            my_heads(queries), my_heads(out_grad), kv_t, held_at(lists), keep, stages[-1][1])
+            my_heads(queries), my_heads(out_grad), kv_t, lists, keep, stages[-1][1],
+            held_at(jnp.arange(block_total, dtype=jnp.int32)))
 
         def join_halves(rows):
             mine = rows.reshape(token_rows, width)

time: 183 us -> 182 us (level)
  starting transfers between devices: 66.3 us -> 42 us
  Pallas kernels: 21.1 us -> 44.8 us
  waiting for transfers between devices: 55.9 us -> 58.4 us
  local copies, waits for them, and re-layouts: 20.6 us -> 18.2 us
    pallas_call x1, Pallas kernels: 13.5 us -> 28.9 us  [attend_local(): pl.pallas_call(_backward_kernel, out_shape=(jax.ShapeDtypeStruct((query_c...]
    ppermute x1, starting transfers between devices: 13.4 us -> 0.01 us  [scatter_sum(): lax.ppermute(sent_first[shift - 1], axes, pairs(first_axis, shift))]
    ppermute x9, starting transfers between devices: 34.6 us -> 23.8 us  [scatter_sum(): lax.ppermute(sent, axes, pairs(axis, shift)).astype(jnp.float32)]
    pallas_call x1, Pallas kernels: 7.65 us -> 16 us  [attend_local(): pl.pallas_call(_forward_kernel, out_shape=(jax.ShapeDtypeStruct((query_co...]
    add x1, other arithmetic: 0.02 us -> 3.18 us  [held_at(): position = position + (coords[..., axis] - own[axis]) % size * stride]
    sub x1, other arithmetic: 2.69 us -> 0.01 us  [attend_local(): rank = jnp.cumsum(keep, axis=1) - 1]
    gather x4 -> x0, local copies, waits for them, and re-layouts: 2.49 us -> none  [the longest x3 1.87 us: attend_local(): lists = jnp.take_along_axis(lists, order, axis=1)]
    ppermute x9, waiting for transfers between devices: 27.2 us -> 29.2 us  [scatter_sum(): lax.ppermute(sent, axes, pairs(axis, shift)).astype(jnp.float32)]
  transfers between devices with their start and end apart: 22 -> 22, of which waited for: 12 -> 13; matrix products, arithmetic and copies ran while one was open for 14% -> 13% of each run, Pallas kernels for 0% -> 0%
where the time goes in v13:
time: 182 us; the launch traced here: 181 us
  waiting for transfers between devices  58.4 us (32%)
  Pallas kernels  44.8 us (25%)
  starting transfers between devices  42 us (23%)
  local copies, waits for them, and re-layouts  18.2 us (10%)
  other arithmetic  16.9 us (9%)
    ppermute x9, waiting for transfers between devices, scatter_sum(): lax.ppermute(sent, axes, pairs(axis, shift)).astype(jnp.float32)  29.2 us
    pallas_call x1, Pallas kernels, attend_local(): pl.pallas_call(_backward_kernel, out_shape=(jax.ShapeDtypeStruct((query_c...  28.9 us
    ppermute x10, waiting for transfers between devices, gather_blocks(): pieces.append(lax.ppermute(buf, axes, pairs(axis, size - shift)))  24.8 us
    ppermute x9, starting transfers between devices, scatter_sum(): lax.ppermute(sent, axes, pairs(axis, shift)).astype(jnp.float32)  23.8 us
    pallas_call x1, Pallas kernels, attend_local(): pl.pallas_call(_forward_kernel, out_shape=(jax.ShapeDtypeStruct((query_co...  16 us
    ppermute x10, starting transfers between devices, gather_blocks(): pieces.append(lax.ppermute(buf, axes, pairs(axis, size - shift)))  14.5 us
    another operation x3, other arithmetic  6.78 us
    unnamed x28, local copies, waits for them, and re-layouts  6.74 us
  transfers between devices with their start and end apart: 22, of which 13 were waited for; matrix products, arithmetic and copies ran while one was open for 13% of the time, Pallas kernels for 0%

profile of v13, /device:TPU:0, one launch (start us, length us, event | category | flops | bytes accessed | tf_op | source)
XLA Modules:
  0.0 181.1 jit_solution(17695918914633156657)
XLA Ops:
  1.4 3.1 %collective-permute-start = (bf16[1,128,128]{2,1,0:T(8,128)(2,1)S(1)}, bf16[1,128,128]{2,1,0:T(8,128)(2,1)S(1)}, u32[]{:S(2)}, u32[]{:S(2)}) collective-permute-start(bf16[1,128,128]{2,1,0:T(8,128)(2,1)S(1)} %maximum_bitcast_fusion), channel_id=1, source_target_pairs={{0,12},{1,13},{2,14},{3,15},{4,0},{5,1},{6,2},{7,3},{8,4},{9,5},{1... | collective-permute-start | bytes 98312 | tf_op jit(solution)/shard_map/ppermute | solution.py:219
  6.2 1.4 constant_dynamic-update-slice_fusion.16
  7.5 2.5 %collective-permute-done.1 = bf16[1,128,128]{2,1,0:T(8,128)(2,1)S(1)} collective-permute-done((bf16[1,128,128]{2,1,0:T(8,128)(2,1)S(1)}, bf16[1,128,128]{2,1,0:T(8,128)(2,1)S(1)}, u32[]{:S(2)}, u32[]{:S(2)}) %collective-permute-start.1) | collective-permute-done | bytes 32800 | tf_op jit(solution)/shard_map/ppermute | solution.py:219
  10.4 2.8 %collective-permute-start.3 = (bf16[4,128,128]{2,1,0:T(8,128)(2,1)S(1)}, bf16[4,128,128]{2,1,0:T(8,128)(2,1)S(1)}, u32[]{:S(2)}, u32[]{:S(2)}) collective-permute-start(bf16[4,128,128]{2,1,0:T(8,128)(2,1)S(1)} %pad_maximum_fusion), channel_id=1, source_target_pairs={{0,17},{1,16},{2,19},{3,18},{4,21},{5,20},{6,23},{7,22},{8,25},{9,... | collective-permute-start | bytes 393224 | tf_op jit(solution)/shard_map/ppermute | solution.py:219
  18.2 1.5 collective-permute-done.4
  21.8 4.0 %collective-permute-start.6 = (bf16[16,128,128]{2,1,0:T(8,128)(2,1)S(1)}, bf16[16,128,128]{2,1,0:T(8,128)(2,1)S(1)}, u32[]{:S(2)}, u32[]{:S(2)}) collective-permute-start(bf16[16,128,128]{2,1,0:T(8,128)(2,1)S(1)} %get-tuple-element.39), channel_id=1, source_target_pairs={{0,96},{1,97},{2,98},{3,99},{4,100},{5,101},{6,102},{7,103},{8,104... | collective-permute-start | bytes 1572872 | tf_op jit(solution)/shard_map/ppermute | solution.py:219
  27.1 18.3 %collective-permute-done.6 = bf16[16,128,128]{2,1,0:T(8,128)(2,1)S(1)} collective-permute-done((bf16[16,128,128]{2,1,0:T(8,128)(2,1)S(1)}, bf16[16,128,128]{2,1,0:T(8,128)(2,1)S(1)}, u32[]{:S(2)}, u32[]{:S(2)}) %collective-permute-start.6) | collective-permute-done | bytes 524320 | tf_op jit(solution)/shard_map/ppermute | solution.py:219
  56.1 3.2 %fusion.15.pos_ref = s32[128]{0:T(128)} fusion(s32[128,1]{0,1:T(1,128)S(1)} %copy-done.9, s32[128,1]{0,1:T(1,128)S(1)} %copy-done.8, s32[128,1]{0,1:T(1,128)S(1)} %copy-done.7, s32[128,1]{0,1:T(1,128)S(1)} %copy-done.6, s32[]{:T(128)} %bitcast.6, s32[]{:T(128)} %bitcast.4, s32[]{:T(128)} %bitcast.2, s32[]{:T(128)} %bitcast), kind=kLoop, calls=%fused_computation.79 | loop fusion | flops 6912 | bytes 2576 | tf_op jit(solution)/shard_map/add | solution.py:259
  59.3 1.6 constant_dynamic-update-slice_fusion.17.kvt_ref
  61.5 16.0 %shard_map.93 = (bf16[2,64,1024]{2,1,0:T(8,128)(2,1)}, f32[2,1,1024]{2,1,0:T(1,128)}, f32[2,1,1024]{2,1,0:T(1,128)}) custom-call(s32[2,48]{1,0:T(2,128)} %select_reduce_fusion.lists_ref, s32[2,48]{1,0:T(2,128)} %broadcast_in_dim.11.count_ref, s32[128]{0:T(128)} %fusion.15.pos_ref, bf16[2,64,1024]{2,1,0:T(8,128)(2,1)} %bitcast.73, ...), custom_call_target="tpu_custom_call" | custom-call | tf_op jit(solution)/shard_map/pallas_call | solution.py:148
  77.5 28.9 %shard_map.94 = (bf16[2,64,1024]{2,1,0:T(8,128)(2,1)}, f32[64,128,128]{2,1,0:T(8,128)}, bf16[1,64,128,128]{3,2,1,0:T(8,128)(2,1)}) custom-call(s32[2,48]{1,0:T(2,128)} %select_reduce_fusion.lists_ref, s32[2,48]{1,0:T(2,128)} %broadcast_in_dim.11.count_ref, s32[128]{0:T(128)} %fusion.15.pos_ref, bf16[2,1024,64]{2,1,0:T(8,128)(2,1)} %copy-done.1, ...), custom_call_target="tpu_custom_call" | custom-call | tf_op jit(solution)/shard_map/pallas_call | solution.py:165
  106.4 4.4 %collective-permute-done.12 = bf16[64,128,128]{2,1,0:T(8,128)(2,1)S(1)} collective-permute-done((bf16[64,128,128]{2,1,0:T(8,128)(2,1)}, bf16[64,128,128]{2,1,0:T(8,128)(2,1)S(1)}, u32[]{:S(2)}, u32[]{:S(2)}) %collective-permute-start.12) | collective-permute-done | bytes 2097184 | tf_op jit(solution)/shard_map/ppermute | solution.py:228
  110.8 5.4 %fusion.24 = (bf16[64,128,128]{2,1,0:T(8,128)(2,1)S(1)}, f32[64,128,128]{2,1,0:T(8,128)}) fusion(f32[64,128,128]{2,1,0:T(8,128)} %get-tuple-element.14, bf16[64,128,128]{2,1,0:T(8,128)(2,1)S(1)} %collective-permute-done.12), kind=kLoop, calls=%fused_computation.89 | loop fusion | flops 3145728 | bytes 12582912 | tf_op jit(solution)/shard_map/convert.9
  116.3 13.7 %collective-permute-start.14 = (bf16[4,4,128,128]{3,2,1,0:T(8,128)(2,1)S(1)}, bf16[4,4,128,128]{3,2,1,0:T(8,128)(2,1)S(1)}, u32[]{:S(2)}, u32[]{:S(2)}) collective-permute-start(bf16[4,4,128,128]{3,2,1,0:T(8,128)(2,1)S(1)} %bitcast.76), channel_id=1, source_target_pairs={{0,64},{1,65},{2,66},{3,67},{4,68},{5,69},{6,70},{7,71},{8,72},{9,... | collective-permute-start | bytes 1572872 | tf_op jit(solution)/shard_map/ppermute | solution.py:235
  131.6 1.3 slice.106
  132.9 8.1 %collective-permute-done.13 = bf16[4,4,128,128]{3,2,1,0:T(8,128)(2,1)S(1)} collective-permute-done((bf16[4,4,128,128]{3,2,1,0:T(8,128)(2,1)S(1)}, bf16[4,4,128,128]{3,2,1,0:T(8,128)(2,1)S(1)}, u32[]{:S(2)}, u32[]{:S(2)}) %collective-permute-start.13) | collective-permute-done | bytes 524320 | tf_op jit(solution)/shard_map/ppermute | solution.py:235
  141.0 12.4 %collective-permute-done.14 = bf16[4,4,128,128]{3,2,1,0:T(8,128)(2,1)S(1)} collective-permute-done((bf16[4,4,128,128]{3,2,1,0:T(8,128)(2,1)S(1)}, bf16[4,4,128,128]{3,2,1,0:T(8,128)(2,1)S(1)}, u32[]{:S(2)}, u32[]{:S(2)}) %collective-permute-start.14) | collective-permute-done | bytes 524320 | tf_op jit(solution)/shard_map/ppermute | solution.py:235
  153.4 1.4 fusion.23
  156.1 2.2 %collective-permute-start.18 = (bf16[4,128,128]{2,1,0:T(8,128)(2,1)S(1)}, bf16[4,128,128]{2,1,0:T(8,128)(2,1)S(1)}, u32[]{:S(2)}, u32[]{:S(2)}) collective-permute-start(bf16[4,128,128]{2,1,0:T(8,128)(2,1)S(1)} %get-tuple-element.26), channel_id=1, source_target_pairs={{0,17},{1,16},{2,19},{3,18},{4,21},{5,20},{6,23},{7,22},{8,25},{9,... | collective-permute-start | bytes 393224 | tf_op jit(solution)/shard_map/ppermute | solution.py:235
  158.9 2.8 %collective-permute-start.10 = (bf16[256,512]{1,0:T(8,128)(2,1)S(1)}, bf16[256,512]{1,0:T(8,128)(2,1)S(1)}, u32[]{:S(2)}, u32[]{:S(2)}) collective-permute-start(bf16[256,512]{1,0:T(8,128)(2,1)S(1)} %reshape.90), channel_id=1, source_target_pairs={{0,1},{1,0},{2,3},{3,2},{4,5},{5,4},{6,7},{7,6},{8,9},{9,8},{10,11... | collective-permute-start | bytes 786440 | tf_op jit(solution)/shard_map/ppermute | solution.py:275
  161.7 2.0 %maximum_select_fusion.1 = bf16[256,1024]{1,0:T(8,128)(2,1)} fusion(bf16[256,512]{1,0:T(8,128)(2,1)} %collective-permute-done.11, bf16[256,512]{1,0:T(8,128)(2,1)S(1)} %reshape.91, pred[]{:T(512)S(6)} %eq.46), kind=kLoop, calls=%fused_computation.3 | loop fusion | flops 2359296 | bytes 1048577 | tf_op jit(solution)/shard_map/jit(_where)/select_n | solution.py:276
  163.7 5.7 %collective-permute-done.16 = bf16[4,128,128]{2,1,0:T(8,128)(2,1)S(1)} collective-permute-done((bf16[4,128,128]{2,1,0:T(8,128)(2,1)S(1)}, bf16[4,128,128]{2,1,0:T(8,128)(2,1)S(1)}, u32[]{:S(2)}, u32[]{:S(2)}) %collective-permute-start.16) | collective-permute-done | bytes 131104 | tf_op jit(solution)/shard_map/ppermute | solution.py:235
  169.9 6.1 %collective-permute-start.20 = (bf16[128,128]{1,0:T(8,128)(2,1)S(1)}, bf16[128,128]{1,0:T(8,128)(2,1)S(1)}, u32[]{:S(2)}, u32[]{:S(2)}) collective-permute-start(bf16[128,128]{1,0:T(8,128)(2,1)S(1)} %get-tuple-element.36), channel_id=1, source_target_pairs={{0,8},{1,9},{2,10},{3,11},{4,12},{5,13},{6,14},{7,15},{8,0},{9,1},... | collective-permute-start | bytes 98312 | tf_op jit(solution)/shard_map/ppermute | solution.py:235
  178.2 1.7 collective-permute-done.21
  (87 shorter events, 30.0 us)
Async XLA Ops:
  0.6 49.5 %copy-start.4 = (bf16[256,1024]{1,0:T(8,128)(2,1)S(1)}, bf16[256,1024]{1,0:T(8,128)(2,1)}, u32[]{:S(2)}) copy-start(bf16[256,1024]{1,0:T(8,128)(2,1)} %param.6) | copy-start | bytes 1572868
  1.4 6.1 %collective-permute-start = (bf16[1,128,128]{2,1,0:T(8,128)(2,1)S(1)}, bf16[1,128,128]{2,1,0:T(8,128)(2,1)S(1)}, u32[]{:S(2)}, u32[]{:S(2)}) collective-permute-start(bf16[1,128,128]{2,1,0:T(8,128)(2,1)S(1)} %maximum_bitcast_fusion), channel_id=1, source_target_pairs={{0,12},{1,13},{2,14},{3,15},{4,0},{5,1},{6,2},{7,3},{8,4},{9,5},{1... | collective-permute-start | bytes 98312 | tf_op jit(solution)/shard_map/ppermute | solution.py:219
  4.6 5.4 %collective-permute-start.1 = (bf16[1,128,128]{2,1,0:T(8,128)(2,1)S(1)}, bf16[1,128,128]{2,1,0:T(8,128)(2,1)S(1)}, u32[]{:S(2)}, u32[]{:S(2)}) collective-permute-start(bf16[1,128,128]{2,1,0:T(8,128)(2,1)S(1)} %maximum_bitcast_fusion), channel_id=1, source_target_pairs={{0,8},{1,9},{2,10},{3,11},{4,12},{5,13},{6,14},{7,15},{8,0},{9,1},... | collective-permute-start | bytes 98312 | tf_op jit(solution)/shard_map/ppermute | solution.py:219
  5.2 5.1 %collective-permute-start.2 = (bf16[1,128,128]{2,1,0:T(8,128)(2,1)S(1)}, bf16[1,128,128]{2,1,0:T(8,128)(2,1)S(1)}, u32[]{:S(2)}, u32[]{:S(2)}) collective-permute-start(bf16[1,128,128]{2,1,0:T(8,128)(2,1)S(1)} %maximum_bitcast_fusion), channel_id=1, source_target_pairs={{0,4},{1,5},{2,6},{3,7},{4,8},{5,9},{6,10},{7,11},{8,12},{9,13},{1... | collective-permute-start | bytes 98312 | tf_op jit(solution)/shard_map/ppermute | solution.py:219
  10.4 7.1 %collective-permute-start.3 = (bf16[4,128,128]{2,1,0:T(8,128)(2,1)S(1)}, bf16[4,128,128]{2,1,0:T(8,128)(2,1)S(1)}, u32[]{:S(2)}, u32[]{:S(2)}) collective-permute-start(bf16[4,128,128]{2,1,0:T(8,128)(2,1)S(1)} %pad_maximum_fusion), channel_id=1, source_target_pairs={{0,17},{1,16},{2,19},{3,18},{4,21},{5,20},{6,23},{7,22},{8,25},{9,... | collective-permute-start | bytes 393224 | tf_op jit(solution)/shard_map/ppermute | solution.py:219
  13.2 6.6 %collective-permute-start.4 = (bf16[4,128,128]{2,1,0:T(8,128)(2,1)S(1)}, bf16[4,128,128]{2,1,0:T(8,128)(2,1)S(1)}, u32[]{:S(2)}, u32[]{:S(2)}) collective-permute-start(bf16[4,128,128]{2,1,0:T(8,128)(2,1)S(1)} %pad_maximum_fusion), channel_id=1, source_target_pairs={{0,1},{1,0},{2,3},{3,2},{4,5},{5,4},{6,7},{7,6},{8,9},{9,8},{10,11... | collective-permute-start | bytes 393224 | tf_op jit(solution)/shard_map/ppermute | solution.py:219
  14.0 7.1 %collective-permute-start.5 = (bf16[4,128,128]{2,1,0:T(8,128)(2,1)S(1)}, bf16[4,128,128]{2,1,0:T(8,128)(2,1)S(1)}, u32[]{:S(2)}, u32[]{:S(2)}) collective-permute-start(bf16[4,128,128]{2,1,0:T(8,128)(2,1)S(1)} %pad_maximum_fusion), channel_id=1, source_target_pairs={{0,16},{1,17},{2,18},{3,19},{4,20},{5,21},{6,22},{7,23},{8,24},{9,... | collective-permute-start | bytes 393224 | tf_op jit(solution)/shard_map/ppermute | solution.py:219
  21.8 23.6 %collective-permute-start.6 = (bf16[16,128,128]{2,1,0:T(8,128)(2,1)S(1)}, bf16[16,128,128]{2,1,0:T(8,128)(2,1)S(1)}, u32[]{:S(2)}, u32[]{:S(2)}) collective-permute-start(bf16[16,128,128]{2,1,0:T(8,128)(2,1)S(1)} %get-tuple-element.39), channel_id=1, source_target_pairs={{0,96},{1,97},{2,98},{3,99},{4,100},{5,101},{6,102},{7,103},{8,104... | collective-permute-start | bytes 1572872 | tf_op jit(solution)/shard_map/ppermute | solution.py:219
  25.9 20.9 %collective-permute-start.7 = (bf16[16,128,128]{2,1,0:T(8,128)(2,1)S(1)}, bf16[16,128,128]{2,1,0:T(8,128)(2,1)S(1)}, u32[]{:S(2)}, u32[]{:S(2)}) collective-permute-start(bf16[16,128,128]{2,1,0:T(8,128)(2,1)S(1)} %get-tuple-element.39), channel_id=1, source_target_pairs={{0,64},{1,65},{2,66},{3,67},{4,68},{5,69},{6,70},{7,71},{8,72},{9,... | collective-permute-start | bytes 1572872 | tf_op jit(solution)/shard_map/ppermute | solution.py:219
  25.9 23.0 %collective-permute-start.8 = (bf16[16,128,128]{2,1,0:T(8,128)(2,1)S(1)}, bf16[16,128,128]{2,1,0:T(8,128)(2,1)S(1)}, u32[]{:S(2)}, u32[]{:S(2)}) collective-permute-start(bf16[16,128,128]{2,1,0:T(8,128)(2,1)S(1)} %get-tuple-element.39), channel_id=1, source_target_pairs={{0,32},{1,33},{2,34},{3,35},{4,36},{5,37},{6,38},{7,39},{8,40},{9,... | collective-permute-start | bytes 1572872 | tf_op jit(solution)/shard_map/ppermute | solution.py:219
  50.1 9.2 %collective-permute-start.9 = (bf16[64,128,128]{2,1,0:T(8,128)(2,1)}, bf16[64,128,128]{2,1,0:T(8,128)(2,1)S(1)}, u32[]{:S(2)}, u32[]{:S(2)}) collective-permute-start(bf16[64,128,128]{2,1,0:T(8,128)(2,1)} %get-tuple-element.28), channel_id=1, source_target_pairs={{0,2},{1,3},{2,0},{3,1},{4,6},{5,7},{6,4},{7,5},{8,10},{9,11},{10,... | collective-permute-start | bytes 6291464 | tf_op jit(solution)/shard_map/ppermute | solution.py:219
  51.4 26.1 %copy-start = (bf16[2,1024,64]{2,1,0:T(8,128)(2,1)}, bf16[2,1024,64]{2,1,0:T(8,128)(2,1)S(1)}, u32[]{:S(2)}) copy-start(bf16[2,1024,64]{2,1,0:T(8,128)(2,1)S(1)} %reshape.89.do_ref) | copy-start | bytes 786436
  106.4 4.4 %collective-permute-start.12 = (bf16[64,128,128]{2,1,0:T(8,128)(2,1)}, bf16[64,128,128]{2,1,0:T(8,128)(2,1)S(1)}, u32[]{:S(2)}, u32[]{:S(2)}) collective-permute-start(bf16[64,128,128]{2,1,0:T(8,128)(2,1)} %bitcast.84), channel_id=1, source_target_pairs={{0,2},{1,3},{2,0},{3,1},{4,6},{5,7},{6,4},{7,5},{8,10},{9,11},{10,... | collective-permute-start | bytes 6291464 | tf_op jit(solution)/shard_map/ppermute | solution.py:228
  116.2 24.8 %collective-permute-start.13 = (bf16[4,4,128,128]{3,2,1,0:T(8,128)(2,1)S(1)}, bf16[4,4,128,128]{3,2,1,0:T(8,128)(2,1)S(1)}, u32[]{:S(2)}, u32[]{:S(2)}) collective-permute-start(bf16[4,4,128,128]{3,2,1,0:T(8,128)(2,1)S(1)} %bitcast.77), channel_id=1, source_target_pairs={{0,32},{1,33},{2,34},{3,35},{4,36},{5,37},{6,38},{7,39},{8,40},{9,... | collective-permute-start | bytes 1572872 | tf_op jit(solution)/shard_map/ppermute | solution.py:235
  116.3 37.1 %collective-permute-start.14 = (bf16[4,4,128,128]{3,2,1,0:T(8,128)(2,1)S(1)}, bf16[4,4,128,128]{3,2,1,0:T(8,128)(2,1)S(1)}, u32[]{:S(2)}, u32[]{:S(2)}) collective-permute-start(bf16[4,4,128,128]{3,2,1,0:T(8,128)(2,1)S(1)} %bitcast.76), channel_id=1, source_target_pairs={{0,64},{1,65},{2,66},{3,67},{4,68},{5,69},{6,70},{7,71},{8,72},{9,... | collective-permute-start | bytes 1572872 | tf_op jit(solution)/shard_map/ppermute | solution.py:235
  130.0 23.4 %collective-permute-start.15 = (bf16[4,4,128,128]{3,2,1,0:T(8,128)(2,1)S(1)}, bf16[4,4,128,128]{3,2,1,0:T(8,128)(2,1)}, u32[]{:S(2)}, u32[]{:S(2)}) collective-permute-start(bf16[4,4,128,128]{3,2,1,0:T(8,128)(2,1)S(1)} %bitcast.75), channel_id=1, source_target_pairs={{0,96},{1,97},{2,98},{3,99},{4,100},{5,101},{6,102},{7,103},{8,104... | collective-permute-start | bytes 1572872 | tf_op jit(solution)/shard_map/ppermute | solution.py:235
  130.7 31.1 %collective-permute-start.11 = (bf16[256,512]{1,0:T(8,128)(2,1)S(1)}, bf16[256,512]{1,0:T(8,128)(2,1)}, u32[]{:S(2)}, u32[]{:S(2)}) collective-permute-start(bf16[256,512]{1,0:T(8,128)(2,1)S(1)} %reshape.91), channel_id=1, source_target_pairs={{0,1},{1,0},{2,3},{3,2},{4,5},{5,4},{6,7},{7,6},{8,9},{9,8},{10,11... | collective-permute-start | bytes 786440 | tf_op jit(solution)/shard_map/ppermute | solution.py:275
  154.8 14.6 %collective-permute-start.16 = (bf16[4,128,128]{2,1,0:T(8,128)(2,1)S(1)}, bf16[4,128,128]{2,1,0:T(8,128)(2,1)S(1)}, u32[]{:S(2)}, u32[]{:S(2)}) collective-permute-start(bf16[4,128,128]{2,1,0:T(8,128)(2,1)S(1)} %get-tuple-element.25), channel_id=1, source_target_pairs={{0,16},{1,17},{2,18},{3,19},{4,20},{5,21},{6,22},{7,23},{8,24},{9,... | collective-permute-start | bytes 393224 | tf_op jit(solution)/shard_map/ppermute | solution.py:235
  154.9 14.5 %collective-permute-start.17 = (bf16[4,128,128]{2,1,0:T(8,128)(2,1)S(1)}, bf16[4,128,128]{2,1,0:T(8,128)(2,1)S(1)}, u32[]{:S(2)}, u32[]{:S(2)}) collective-permute-start(bf16[4,128,128]{2,1,0:T(8,128)(2,1)S(1)} %get-tuple-element.27), channel_id=1, source_target_pairs={{0,1},{1,0},{2,3},{3,2},{4,5},{5,4},{6,7},{7,6},{8,9},{9,8},{10,11... | collective-permute-start | bytes 393224 | tf_op jit(solution)/shard_map/ppermute | solution.py:235
  156.1 13.3 %collective-permute-start.18 = (bf16[4,128,128]{2,1,0:T(8,128)(2,1)S(1)}, bf16[4,128,128]{2,1,0:T(8,128)(2,1)S(1)}, u32[]{:S(2)}, u32[]{:S(2)}) collective-permute-start(bf16[4,128,128]{2,1,0:T(8,128)(2,1)S(1)} %get-tuple-element.26), channel_id=1, source_target_pairs={{0,17},{1,16},{2,19},{3,18},{4,21},{5,20},{6,23},{7,22},{8,25},{9,... | collective-permute-start | bytes 393224 | tf_op jit(solution)/shard_map/ppermute | solution.py:235
  158.9 17.1 %collective-permute-start.10 = (bf16[256,512]{1,0:T(8,128)(2,1)S(1)}, bf16[256,512]{1,0:T(8,128)(2,1)S(1)}, u32[]{:S(2)}, u32[]{:S(2)}) collective-permute-start(bf16[256,512]{1,0:T(8,128)(2,1)S(1)} %reshape.90), channel_id=1, source_target_pairs={{0,1},{1,0},{2,3},{3,2},{4,5},{5,4},{6,7},{7,6},{8,9},{9,8},{10,11... | collective-permute-start | bytes 786440 | tf_op jit(solution)/shard_map/ppermute | solution.py:275
  169.5 7.4 %collective-permute-start.19 = (bf16[128,128]{1,0:T(8,128)(2,1)S(1)}, bf16[128,128]{1,0:T(8,128)(2,1)S(1)}, u32[]{:S(2)}, u32[]{:S(2)}) collective-permute-start(bf16[128,128]{1,0:T(8,128)(2,1)S(1)} %get-tuple-element.34), channel_id=1, source_target_pairs={{0,4},{1,5},{2,6},{3,7},{4,8},{5,9},{6,10},{7,11},{8,12},{9,13},{1... | collective-permute-start | bytes 98312 | tf_op jit(solution)/shard_map/ppermute | solution.py:235
  169.9 8.4 %collective-permute-start.20 = (bf16[128,128]{1,0:T(8,128)(2,1)S(1)}, bf16[128,128]{1,0:T(8,128)(2,1)S(1)}, u32[]{:S(2)}, u32[]{:S(2)}) collective-permute-start(bf16[128,128]{1,0:T(8,128)(2,1)S(1)} %get-tuple-element.36), channel_id=1, source_target_pairs={{0,8},{1,9},{2,10},{3,11},{4,12},{5,13},{6,14},{7,15},{8,0},{9,1},... | collective-permute-start | bytes 98312 | tf_op jit(solution)/shard_map/ppermute | solution.py:235
  176.0 3.9 %collective-permute-start.21 = (bf16[128,128]{1,0:T(8,128)(2,1)S(1)}, bf16[128,128]{1,0:T(8,128)(2,1)S(1)}, u32[]{:S(2)}, u32[]{:S(2)}) collective-permute-start(bf16[128,128]{1,0:T(8,128)(2,1)S(1)} %get-tuple-element.35), channel_id=1, source_target_pairs={{0,12},{1,13},{2,14},{3,15},{4,0},{5,1},{6,2},{7,3},{8,4},{9,5},{1... | collective-permute-start | bytes 98312 | tf_op jit(solution)/shard_map/ppermute | solution.py:235
  (8 other events, 112.5 us)

commit v14 on v13

--- a/solution.py
+++ b/solution.py
@@ -211,6 +211,12 @@
     table_np, stages, pairs = device_table(mesh)
     axes = ("blk", "split")
 
+    held_np = np.zeros((table_np.shape[0], table_np.shape[0]), np.int32)
+    stride = 1
+    for axis, size in stages:
+        held_np += ((table_np[None, :, axis] - table_np[:, None, axis]) % size) * stride
+        stride *= size
+
     def gather_blocks(piece):
         buf = piece[None]
         for axis, size in stages:
@@ -268,7 +274,7 @@
         keep = first_occurrence(lists)
         o_rows, dq_rows, dkv_t = attend_local(
             my_heads(queries), my_heads(out_grad), kv_t, lists, keep, stages[-1][1],
-            held_at(jnp.arange(block_total, dtype=jnp.int32)))
+            lax.dynamic_index_in_dim(jnp.asarray(held_np), me, keepdims=False))
 
         def join_halves(rows):
             mine = rows.reshape(token_rows, width)

time: 182 us -> 177 us (0.973)
  starting transfers between devices: 42 us -> 65.1 us
  Pallas kernels: 44.8 us -> 22.5 us
  other arithmetic: 16.9 us -> 13.7 us
    ppermute x1, starting transfers between devices: 0.01 us -> 23.5 us  [scatter_sum(): lax.ppermute(sent_first[shift - 1], axes, pairs(first_axis, shift))]
    pallas_call x1, Pallas kernels: 28.9 us -> 14.3 us  [attend_local(): pl.pallas_call(_backward_kernel, out_shape=(jax.ShapeDtypeStruct((query_c...]
    pallas_call x1, Pallas kernels: 16 us -> 8.2 us  [attend_local(): pl.pallas_call(_forward_kernel, out_shape=(jax.ShapeDtypeStruct((query_co...]
    add x1 -> x0, other arithmetic: 3.18 us -> none  [held_at(): position = position + (coords[..., axis] - own[axis]) % size * stride]
    unnamed x28 -> x20, local copies, waits for them, and re-layouts: 6.74 us -> 6.84 us
  transfers between devices with their start and end apart: 22 -> 22, of which waited for: 13 -> 14; matrix products, arithmetic and copies ran while one was open for 13% -> 11% of each run, Pallas kernels for 0% -> 0%
where the time goes in v14:
time: 177 us
  starting transfers between devices  65.1 us (37%)
  waiting for transfers between devices  56.7 us (32%)
  Pallas kernels  22.5 us (13%)
  local copies, waits for them, and re-layouts  18.2 us (10%)
  other arithmetic  13.7 us (8%)
    ppermute x9, waiting for transfers between devices, scatter_sum(): lax.ppermute(sent, axes, pairs(axis, shift)).astype(jnp.float32)  28 us
    ppermute x10, waiting for transfers between devices, gather_blocks(): pieces.append(lax.ppermute(buf, axes, pairs(axis, size - shift)))  24.7 us
    ppermute x1, starting transfers between devices, scatter_sum(): lax.ppermute(sent_first[shift - 1], axes, pairs(first_axis, shift))  23.5 us
    ppermute x9, starting transfers between devices, scatter_sum(): lax.ppermute(sent, axes, pairs(axis, shift)).astype(jnp.float32)  23.4 us
    ppermute x10, starting transfers between devices, gather_blocks(): pieces.append(lax.ppermute(buf, axes, pairs(axis, size - shift)))  14.5 us
    pallas_call x1, Pallas kernels, attend_local(): pl.pallas_call(_backward_kernel, out_shape=(jax.ShapeDtypeStruct((query_c...  14.3 us
    pallas_call x1, Pallas kernels, attend_local(): pl.pallas_call(_forward_kernel, out_shape=(jax.ShapeDtypeStruct((query_co...  8.2 us
    unnamed x20, local copies, waits for them, and re-layouts  6.84 us
  transfers between devices with their start and end apart: 22, of which 14 were waited for; matrix products, arithmetic and copies ran while one was open for 11% of the time, Pallas kernels for 0%

profile of v14, /device:TPU:0, one launch (start us, length us, event | category | flops | bytes accessed | tf_op | source)
XLA Modules:
  0.0 177.0 jit_solution(10808827337937153805)
XLA Ops:
  1.4 3.1 %collective-permute-start = (bf16[1,128,128]{2,1,0:T(8,128)(2,1)S(1)}, bf16[1,128,128]{2,1,0:T(8,128)(2,1)S(1)}, u32[]{:S(2)}, u32[]{:S(2)}) collective-permute-start(bf16[1,128,128]{2,1,0:T(8,128)(2,1)S(1)} %maximum_bitcast_fusion), channel_id=1, source_target_pairs={{0,12},{1,13},{2,14},{3,15},{4,0},{5,1},{6,2},{7,3},{8,4},{9,5},{1... | collective-permute-start | bytes 98312 | tf_op jit(solution)/shard_map/ppermute | solution.py:225
  6.2 1.4 constant_dynamic-update-slice_fusion.16
  7.5 2.4 %collective-permute-done.1 = bf16[1,128,128]{2,1,0:T(8,128)(2,1)S(1)} collective-permute-done((bf16[1,128,128]{2,1,0:T(8,128)(2,1)S(1)}, bf16[1,128,128]{2,1,0:T(8,128)(2,1)S(1)}, u32[]{:S(2)}, u32[]{:S(2)}) %collective-permute-start.1) | collective-permute-done | bytes 32800 | tf_op jit(solution)/shard_map/ppermute | solution.py:225
  10.4 2.8 %collective-permute-start.3 = (bf16[4,128,128]{2,1,0:T(8,128)(2,1)S(1)}, bf16[4,128,128]{2,1,0:T(8,128)(2,1)S(1)}, u32[]{:S(2)}, u32[]{:S(2)}) collective-permute-start(bf16[4,128,128]{2,1,0:T(8,128)(2,1)S(1)} %pad_maximum_fusion), channel_id=1, source_target_pairs={{0,17},{1,16},{2,19},{3,18},{4,21},{5,20},{6,23},{7,22},{8,25},{9,... | collective-permute-start | bytes 393224 | tf_op jit(solution)/shard_map/ppermute | solution.py:225
  18.2 1.5 collective-permute-done.4
  21.9 4.0 %collective-permute-start.6 = (bf16[16,128,128]{2,1,0:T(8,128)(2,1)S(1)}, bf16[16,128,128]{2,1,0:T(8,128)(2,1)S(1)}, u32[]{:S(2)}, u32[]{:S(2)}) collective-permute-start(bf16[16,128,128]{2,1,0:T(8,128)(2,1)S(1)} %get-tuple-element.39), channel_id=1, source_target_pairs={{0,96},{1,97},{2,98},{3,99},{4,100},{5,101},{6,102},{7,103},{8,104... | collective-permute-start | bytes 1572872 | tf_op jit(solution)/shard_map/ppermute | solution.py:225
  27.2 18.3 %collective-permute-done.6 = bf16[16,128,128]{2,1,0:T(8,128)(2,1)S(1)} collective-permute-done((bf16[16,128,128]{2,1,0:T(8,128)(2,1)S(1)}, bf16[16,128,128]{2,1,0:T(8,128)(2,1)S(1)}, u32[]{:S(2)}, u32[]{:S(2)}) %collective-permute-start.6) | collective-permute-done | bytes 524320 | tf_op jit(solution)/shard_map/ppermute | solution.py:225
  48.9 1.3 constant_dynamic-update-slice_fusion.7
  56.1 1.5 constant_dynamic-update-slice_fusion.17.kvt_ref
  58.3 8.2 %shard_map.93 = (bf16[2,64,1024]{2,1,0:T(8,128)(2,1)}, f32[2,1,1024]{2,1,0:T(1,128)}, f32[2,1,1024]{2,1,0:T(1,128)}) custom-call(s32[2,48]{1,0:T(2,128)} %select_reduce_fusion.lists_ref, s32[2,48]{1,0:T(2,128)} %broadcast_in_dim.11.count_ref, s32[128]{0:T(128)} %fusion.10.pos_ref, bf16[2,64,1024]{2,1,0:T(8,128)(2,1)} %bitcast.55, ...), custom_call_target="tpu_custom_call" | custom-call | tf_op jit(solution)/shard_map/pallas_call | solution.py:148
  66.5 14.3 %shard_map.94 = (bf16[2,64,1024]{2,1,0:T(8,128)(2,1)}, f32[64,128,128]{2,1,0:T(8,128)}, bf16[1,64,128,128]{3,2,1,0:T(8,128)(2,1)}) custom-call(s32[2,48]{1,0:T(2,128)} %select_reduce_fusion.lists_ref, s32[2,48]{1,0:T(2,128)} %broadcast_in_dim.11.count_ref, s32[128]{0:T(128)} %fusion.10.pos_ref, bf16[2,1024,64]{2,1,0:T(8,128)(2,1)} %copy-done, ...), custom_call_target="tpu_custom_call" | custom-call | tf_op jit(solution)/shard_map/pallas_call | solution.py:165
  80.8 23.5 %collective-permute-start.12 = (bf16[64,128,128]{2,1,0:T(8,128)(2,1)}, bf16[64,128,128]{2,1,0:T(8,128)(2,1)S(1)}, u32[]{:S(2)}, u32[]{:S(2)}) collective-permute-start(bf16[64,128,128]{2,1,0:T(8,128)(2,1)} %bitcast.68), channel_id=1, source_target_pairs={{0,2},{1,3},{2,0},{3,1},{4,6},{5,7},{6,4},{7,5},{8,10},{9,11},{10,... | collective-permute-start | bytes 6291464 | tf_op jit(solution)/shard_map/ppermute | solution.py:234
  104.3 4.0 %collective-permute-done.12 = bf16[64,128,128]{2,1,0:T(8,128)(2,1)S(1)} collective-permute-done((bf16[64,128,128]{2,1,0:T(8,128)(2,1)}, bf16[64,128,128]{2,1,0:T(8,128)(2,1)S(1)}, u32[]{:S(2)}, u32[]{:S(2)}) %collective-permute-start.12) | collective-permute-done | bytes 2097184 | tf_op jit(solution)/shard_map/ppermute | solution.py:234
  108.3 5.3 %fusion.15 = (bf16[64,128,128]{2,1,0:T(8,128)(2,1)S(1)}, f32[64,128,128]{2,1,0:T(8,128)}) fusion(f32[64,128,128]{2,1,0:T(8,128)} %get-tuple-element.14, bf16[64,128,128]{2,1,0:T(8,128)(2,1)S(1)} %collective-permute-done.12), kind=kLoop, calls=%fused_computation.68 | loop fusion | flops 3145728 | bytes 12582912 | tf_op jit(solution)/shard_map/convert.9
  113.8 16.5 %collective-permute-start.14 = (bf16[4,4,128,128]{3,2,1,0:T(8,128)(2,1)S(1)}, bf16[4,4,128,128]{3,2,1,0:T(8,128)(2,1)S(1)}, u32[]{:S(2)}, u32[]{:S(2)}) collective-permute-start(bf16[4,4,128,128]{3,2,1,0:T(8,128)(2,1)S(1)} %bitcast.60), channel_id=1, source_target_pairs={{0,64},{1,65},{2,66},{3,67},{4,68},{5,69},{6,70},{7,71},{8,72},{9,... | collective-permute-start | bytes 1572872 | tf_op jit(solution)/shard_map/ppermute | solution.py:241
  131.8 1.3 slice.70
  133.1 8.0 %collective-permute-done.13 = bf16[4,4,128,128]{3,2,1,0:T(8,128)(2,1)S(1)} collective-permute-done((bf16[4,4,128,128]{3,2,1,0:T(8,128)(2,1)S(1)}, bf16[4,4,128,128]{3,2,1,0:T(8,128)(2,1)S(1)}, u32[]{:S(2)}, u32[]{:S(2)}) %collective-permute-start.13) | collective-permute-done | bytes 524320 | tf_op jit(solution)/shard_map/ppermute | solution.py:241
  141.1 12.4 %collective-permute-done.14 = bf16[4,4,128,128]{3,2,1,0:T(8,128)(2,1)S(1)} collective-permute-done((bf16[4,4,128,128]{3,2,1,0:T(8,128)(2,1)S(1)}, bf16[4,4,128,128]{3,2,1,0:T(8,128)(2,1)S(1)}, u32[]{:S(2)}, u32[]{:S(2)}) %collective-permute-start.14) | collective-permute-done | bytes 524320 | tf_op jit(solution)/shard_map/ppermute | solution.py:241
  153.5 1.4 fusion.14
  155.9 2.5 %collective-permute-start.18 = (bf16[4,128,128]{2,1,0:T(8,128)(2,1)S(1)}, bf16[4,128,128]{2,1,0:T(8,128)(2,1)S(1)}, u32[]{:S(2)}, u32[]{:S(2)}) collective-permute-start(bf16[4,128,128]{2,1,0:T(8,128)(2,1)S(1)} %get-tuple-element.26), channel_id=1, source_target_pairs={{0,17},{1,16},{2,19},{3,18},{4,21},{5,20},{6,23},{7,22},{8,25},{9,... | collective-permute-start | bytes 393224 | tf_op jit(solution)/shard_map/ppermute | solution.py:241
  159.0 2.8 %collective-permute-start.10 = (bf16[256,512]{1,0:T(8,128)(2,1)S(1)}, bf16[256,512]{1,0:T(8,128)(2,1)S(1)}, u32[]{:S(2)}, u32[]{:S(2)}) collective-permute-start(bf16[256,512]{1,0:T(8,128)(2,1)S(1)} %reshape.74), channel_id=1, source_target_pairs={{0,1},{1,0},{2,3},{3,2},{4,5},{5,4},{6,7},{7,6},{8,9},{9,8},{10,11... | collective-permute-start | bytes 786440 | tf_op jit(solution)/shard_map/ppermute | solution.py:281
  161.8 2.0 %maximum_select_fusion.1 = bf16[256,1024]{1,0:T(8,128)(2,1)} fusion(bf16[256,512]{1,0:T(8,128)(2,1)} %collective-permute-done.11, bf16[256,512]{1,0:T(8,128)(2,1)S(1)} %reshape.75, pred[]{:T(512)S(6)} %eq.41), kind=kLoop, calls=%fused_computation.3 | loop fusion | flops 2359296 | bytes 1048577 | tf_op jit(solution)/shard_map/jit(_where)/select_n | solution.py:282
  163.8 5.5 %collective-permute-done.16 = bf16[4,128,128]{2,1,0:T(8,128)(2,1)S(1)} collective-permute-done((bf16[4,128,128]{2,1,0:T(8,128)(2,1)S(1)}, bf16[4,128,128]{2,1,0:T(8,128)(2,1)S(1)}, u32[]{:S(2)}, u32[]{:S(2)}) %collective-permute-start.16) | collective-permute-done | bytes 131104 | tf_op jit(solution)/shard_map/ppermute | solution.py:241
  169.6 3.1 %collective-permute-start.21 = (bf16[128,128]{1,0:T(8,128)(2,1)S(1)}, bf16[128,128]{1,0:T(8,128)(2,1)S(1)}, u32[]{:S(2)}, u32[]{:S(2)}) collective-permute-start(bf16[128,128]{1,0:T(8,128)(2,1)S(1)} %get-tuple-element.35), channel_id=1, source_target_pairs={{0,12},{1,13},{2,14},{3,15},{4,0},{5,1},{6,2},{7,3},{8,4},{9,5},{1... | collective-permute-start | bytes 98312 | tf_op jit(solution)/shard_map/ppermute | solution.py:241
  (77 shorter events, 28.9 us)
Async XLA Ops:
  0.6 49.5 %copy-start.4 = (bf16[256,1024]{1,0:T(8,128)(2,1)S(1)}, bf16[256,1024]{1,0:T(8,128)(2,1)}, u32[]{:S(2)}) copy-start(bf16[256,1024]{1,0:T(8,128)(2,1)} %param.6) | copy-start | bytes 1572868
  1.4 6.1 %collective-permute-start = (bf16[1,128,128]{2,1,0:T(8,128)(2,1)S(1)}, bf16[1,128,128]{2,1,0:T(8,128)(2,1)S(1)}, u32[]{:S(2)}, u32[]{:S(2)}) collective-permute-start(bf16[1,128,128]{2,1,0:T(8,128)(2,1)S(1)} %maximum_bitcast_fusion), channel_id=1, source_target_pairs={{0,12},{1,13},{2,14},{3,15},{4,0},{5,1},{6,2},{7,3},{8,4},{9,5},{1... | collective-permute-start | bytes 98312 | tf_op jit(solution)/shard_map/ppermute | solution.py:225
  4.6 5.4 %collective-permute-start.1 = (bf16[1,128,128]{2,1,0:T(8,128)(2,1)S(1)}, bf16[1,128,128]{2,1,0:T(8,128)(2,1)S(1)}, u32[]{:S(2)}, u32[]{:S(2)}) collective-permute-start(bf16[1,128,128]{2,1,0:T(8,128)(2,1)S(1)} %maximum_bitcast_fusion), channel_id=1, source_target_pairs={{0,8},{1,9},{2,10},{3,11},{4,12},{5,13},{6,14},{7,15},{8,0},{9,1},... | collective-permute-start | bytes 98312 | tf_op jit(solution)/shard_map/ppermute | solution.py:225
  5.2 5.1 %collective-permute-start.2 = (bf16[1,128,128]{2,1,0:T(8,128)(2,1)S(1)}, bf16[1,128,128]{2,1,0:T(8,128)(2,1)S(1)}, u32[]{:S(2)}, u32[]{:S(2)}) collective-permute-start(bf16[1,128,128]{2,1,0:T(8,128)(2,1)S(1)} %maximum_bitcast_fusion), channel_id=1, source_target_pairs={{0,4},{1,5},{2,6},{3,7},{4,8},{5,9},{6,10},{7,11},{8,12},{9,13},{1... | collective-permute-start | bytes 98312 | tf_op jit(solution)/shard_map/ppermute | solution.py:225
  10.4 7.1 %collective-permute-start.3 = (bf16[4,128,128]{2,1,0:T(8,128)(2,1)S(1)}, bf16[4,128,128]{2,1,0:T(8,128)(2,1)S(1)}, u32[]{:S(2)}, u32[]{:S(2)}) collective-permute-start(bf16[4,128,128]{2,1,0:T(8,128)(2,1)S(1)} %pad_maximum_fusion), channel_id=1, source_target_pairs={{0,17},{1,16},{2,19},{3,18},{4,21},{5,20},{6,23},{7,22},{8,25},{9,... | collective-permute-start | bytes 393224 | tf_op jit(solution)/shard_map/ppermute | solution.py:225
  13.2 6.6 %collective-permute-start.4 = (bf16[4,128,128]{2,1,0:T(8,128)(2,1)S(1)}, bf16[4,128,128]{2,1,0:T(8,128)(2,1)S(1)}, u32[]{:S(2)}, u32[]{:S(2)}) collective-permute-start(bf16[4,128,128]{2,1,0:T(8,128)(2,1)S(1)} %pad_maximum_fusion), channel_id=1, source_target_pairs={{0,1},{1,0},{2,3},{3,2},{4,5},{5,4},{6,7},{7,6},{8,9},{9,8},{10,11... | collective-permute-start | bytes 393224 | tf_op jit(solution)/shard_map/ppermute | solution.py:225
  14.0 7.1 %collective-permute-start.5 = (bf16[4,128,128]{2,1,0:T(8,128)(2,1)S(1)}, bf16[4,128,128]{2,1,0:T(8,128)(2,1)S(1)}, u32[]{:S(2)}, u32[]{:S(2)}) collective-permute-start(bf16[4,128,128]{2,1,0:T(8,128)(2,1)S(1)} %pad_maximum_fusion), channel_id=1, source_target_pairs={{0,16},{1,17},{2,18},{3,19},{4,20},{5,21},{6,22},{7,23},{8,24},{9,... | collective-permute-start | bytes 393224 | tf_op jit(solution)/shard_map/ppermute | solution.py:225
  21.9 23.6 %collective-permute-start.6 = (bf16[16,128,128]{2,1,0:T(8,128)(2,1)S(1)}, bf16[16,128,128]{2,1,0:T(8,128)(2,1)S(1)}, u32[]{:S(2)}, u32[]{:S(2)}) collective-permute-start(bf16[16,128,128]{2,1,0:T(8,128)(2,1)S(1)} %get-tuple-element.39), channel_id=1, source_target_pairs={{0,96},{1,97},{2,98},{3,99},{4,100},{5,101},{6,102},{7,103},{8,104... | collective-permute-start | bytes 1572872 | tf_op jit(solution)/shard_map/ppermute | solution.py:225
  25.9 20.8 %collective-permute-start.7 = (bf16[16,128,128]{2,1,0:T(8,128)(2,1)S(1)}, bf16[16,128,128]{2,1,0:T(8,128)(2,1)S(1)}, u32[]{:S(2)}, u32[]{:S(2)}) collective-permute-start(bf16[16,128,128]{2,1,0:T(8,128)(2,1)S(1)} %get-tuple-element.39), channel_id=1, source_target_pairs={{0,64},{1,65},{2,66},{3,67},{4,68},{5,69},{6,70},{7,71},{8,72},{9,... | collective-permute-start | bytes 1572872 | tf_op jit(solution)/shard_map/ppermute | solution.py:225
  25.9 23.0 %collective-permute-start.8 = (bf16[16,128,128]{2,1,0:T(8,128)(2,1)S(1)}, bf16[16,128,128]{2,1,0:T(8,128)(2,1)S(1)}, u32[]{:S(2)}, u32[]{:S(2)}) collective-permute-start(bf16[16,128,128]{2,1,0:T(8,128)(2,1)S(1)} %get-tuple-element.39), channel_id=1, source_target_pairs={{0,32},{1,33},{2,34},{3,35},{4,36},{5,37},{6,38},{7,39},{8,40},{9,... | collective-permute-start | bytes 1572872 | tf_op jit(solution)/shard_map/ppermute | solution.py:225
  50.2 5.9 %collective-permute-start.9 = (bf16[64,128,128]{2,1,0:T(8,128)(2,1)}, bf16[64,128,128]{2,1,0:T(8,128)(2,1)S(1)}, u32[]{:S(2)}, u32[]{:S(2)}) collective-permute-start(bf16[64,128,128]{2,1,0:T(8,128)(2,1)} %get-tuple-element.28), channel_id=1, source_target_pairs={{0,2},{1,3},{2,0},{3,1},{4,6},{5,7},{6,4},{7,5},{8,10},{9,11},{10,... | collective-permute-start | bytes 6291464 | tf_op jit(solution)/shard_map/ppermute | solution.py:225
  80.8 27.5 %collective-permute-start.12 = (bf16[64,128,128]{2,1,0:T(8,128)(2,1)}, bf16[64,128,128]{2,1,0:T(8,128)(2,1)S(1)}, u32[]{:S(2)}, u32[]{:S(2)}) collective-permute-start(bf16[64,128,128]{2,1,0:T(8,128)(2,1)} %bitcast.68), channel_id=1, source_target_pairs={{0,2},{1,3},{2,0},{3,1},{4,6},{5,7},{6,4},{7,5},{8,10},{9,11},{10,... | collective-permute-start | bytes 6291464 | tf_op jit(solution)/shard_map/ppermute | solution.py:234
  108.3 22.0 %copy-start.3 = (bf16[2,64,1024]{2,1,0:T(8,128)(2,1)S(1)}, bf16[2,64,1024]{2,1,0:T(8,128)(2,1)}, u32[]{:S(2)}) copy-start(bf16[2,64,1024]{2,1,0:T(8,128)(2,1)} %get-tuple-element.13) | copy-start | bytes 786436
  113.7 27.4 %collective-permute-start.13 = (bf16[4,4,128,128]{3,2,1,0:T(8,128)(2,1)S(1)}, bf16[4,4,128,128]{3,2,1,0:T(8,128)(2,1)S(1)}, u32[]{:S(2)}, u32[]{:S(2)}) collective-permute-start(bf16[4,4,128,128]{3,2,1,0:T(8,128)(2,1)S(1)} %bitcast.61), channel_id=1, source_target_pairs={{0,32},{1,33},{2,34},{3,35},{4,36},{5,37},{6,38},{7,39},{8,40},{9,... | collective-permute-start | bytes 1572872 | tf_op jit(solution)/shard_map/ppermute | solution.py:241
  113.8 39.7 %collective-permute-start.14 = (bf16[4,4,128,128]{3,2,1,0:T(8,128)(2,1)S(1)}, bf16[4,4,128,128]{3,2,1,0:T(8,128)(2,1)S(1)}, u32[]{:S(2)}, u32[]{:S(2)}) collective-permute-start(bf16[4,4,128,128]{3,2,1,0:T(8,128)(2,1)S(1)} %bitcast.60), channel_id=1, source_target_pairs={{0,64},{1,65},{2,66},{3,67},{4,68},{5,69},{6,70},{7,71},{8,72},{9,... | collective-permute-start | bytes 1572872 | tf_op jit(solution)/shard_map/ppermute | solution.py:241
  130.3 23.2 %collective-permute-start.15 = (bf16[4,4,128,128]{3,2,1,0:T(8,128)(2,1)S(1)}, bf16[4,4,128,128]{3,2,1,0:T(8,128)(2,1)}, u32[]{:S(2)}, u32[]{:S(2)}) collective-permute-start(bf16[4,4,128,128]{3,2,1,0:T(8,128)(2,1)S(1)} %bitcast.59), channel_id=1, source_target_pairs={{0,96},{1,97},{2,98},{3,99},{4,100},{5,101},{6,102},{7,103},{8,104... | collective-permute-start | bytes 1572872 | tf_op jit(solution)/shard_map/ppermute | solution.py:241
  130.9 30.9 %collective-permute-start.11 = (bf16[256,512]{1,0:T(8,128)(2,1)S(1)}, bf16[256,512]{1,0:T(8,128)(2,1)}, u32[]{:S(2)}, u32[]{:S(2)}) collective-permute-start(bf16[256,512]{1,0:T(8,128)(2,1)S(1)} %reshape.75), channel_id=1, source_target_pairs={{0,1},{1,0},{2,3},{3,2},{4,5},{5,4},{6,7},{7,6},{8,9},{9,8},{10,11... | collective-permute-start | bytes 786440 | tf_op jit(solution)/shard_map/ppermute | solution.py:281
  154.9 14.4 %collective-permute-start.16 = (bf16[4,128,128]{2,1,0:T(8,128)(2,1)S(1)}, bf16[4,128,128]{2,1,0:T(8,128)(2,1)S(1)}, u32[]{:S(2)}, u32[]{:S(2)}) collective-permute-start(bf16[4,128,128]{2,1,0:T(8,128)(2,1)S(1)} %get-tuple-element.25), channel_id=1, source_target_pairs={{0,16},{1,17},{2,18},{3,19},{4,20},{5,21},{6,22},{7,23},{8,24},{9,... | collective-permute-start | bytes 393224 | tf_op jit(solution)/shard_map/ppermute | solution.py:241
  155.0 14.3 %collective-permute-start.17 = (bf16[4,128,128]{2,1,0:T(8,128)(2,1)S(1)}, bf16[4,128,128]{2,1,0:T(8,128)(2,1)S(1)}, u32[]{:S(2)}, u32[]{:S(2)}) collective-permute-start(bf16[4,128,128]{2,1,0:T(8,128)(2,1)S(1)} %get-tuple-element.27), channel_id=1, source_target_pairs={{0,1},{1,0},{2,3},{3,2},{4,5},{5,4},{6,7},{7,6},{8,9},{9,8},{10,11... | collective-permute-start | bytes 393224 | tf_op jit(solution)/shard_map/ppermute | solution.py:241
  155.9 13.4 %collective-permute-start.18 = (bf16[4,128,128]{2,1,0:T(8,128)(2,1)S(1)}, bf16[4,128,128]{2,1,0:T(8,128)(2,1)S(1)}, u32[]{:S(2)}, u32[]{:S(2)}) collective-permute-start(bf16[4,128,128]{2,1,0:T(8,128)(2,1)S(1)} %get-tuple-element.26), channel_id=1, source_target_pairs={{0,17},{1,16},{2,19},{3,18},{4,21},{5,20},{6,23},{7,22},{8,25},{9,... | collective-permute-start | bytes 393224 | tf_op jit(solution)/shard_map/ppermute | solution.py:241
  159.0 13.7 %collective-permute-start.10 = (bf16[256,512]{1,0:T(8,128)(2,1)S(1)}, bf16[256,512]{1,0:T(8,128)(2,1)S(1)}, u32[]{:S(2)}, u32[]{:S(2)}) collective-permute-start(bf16[256,512]{1,0:T(8,128)(2,1)S(1)} %reshape.74), channel_id=1, source_target_pairs={{0,1},{1,0},{2,3},{3,2},{4,5},{5,4},{6,7},{7,6},{8,9},{9,8},{10,11... | collective-permute-start | bytes 786440 | tf_op jit(solution)/shard_map/ppermute | solution.py:281
  169.4 5.2 %collective-permute-start.19 = (bf16[128,128]{1,0:T(8,128)(2,1)S(1)}, bf16[128,128]{1,0:T(8,128)(2,1)S(1)}, u32[]{:S(2)}, u32[]{:S(2)}) collective-permute-start(bf16[128,128]{1,0:T(8,128)(2,1)S(1)} %get-tuple-element.34), channel_id=1, source_target_pairs={{0,4},{1,5},{2,6},{3,7},{4,8},{5,9},{6,10},{7,11},{8,12},{9,13},{1... | collective-permute-start | bytes 98312 | tf_op jit(solution)/shard_map/ppermute | solution.py:241
  169.5 5.5 %collective-permute-start.20 = (bf16[128,128]{1,0:T(8,128)(2,1)S(1)}, bf16[128,128]{1,0:T(8,128)(2,1)S(1)}, u32[]{:S(2)}, u32[]{:S(2)}) collective-permute-start(bf16[128,128]{1,0:T(8,128)(2,1)S(1)} %get-tuple-element.36), channel_id=1, source_target_pairs={{0,8},{1,9},{2,10},{3,11},{4,12},{5,13},{6,14},{7,15},{8,0},{9,1},... | collective-permute-start | bytes 98312 | tf_op jit(solution)/shard_map/ppermute | solution.py:241
  169.6 6.2 %collective-permute-start.21 = (bf16[128,128]{1,0:T(8,128)(2,1)S(1)}, bf16[128,128]{1,0:T(8,128)(2,1)S(1)}, u32[]{:S(2)}, u32[]{:S(2)}) collective-permute-start(bf16[128,128]{1,0:T(8,128)(2,1)S(1)} %get-tuple-element.35), channel_id=1, source_target_pairs={{0,12},{1,13},{2,14},{3,15},{4,0},{5,1},{6,2},{7,3},{8,4},{9,5},{1... | collective-permute-start | bytes 98312 | tf_op jit(solution)/shard_map/ppermute | solution.py:241
  (4 other events, 54.4 us)

commit v15 on v14

--- a/solution.py
+++ b/solution.py
@@ -217,14 +217,16 @@
         held_np += ((table_np[None, :, axis] - table_np[:, None, axis]) % size) * stride
         stride *= size
 
-    def gather_blocks(piece):
+    def gather_blocks(piece, tie=None):
         buf = piece[None]
-        for axis, size in stages:
+        for number, (axis, size) in enumerate(stages):
+            if number == 1 and tie is not None:
+                buf, tie = lax.optimization_barrier((buf, tie))
             pieces = [buf]
             for shift in range(1, size):
                 pieces.append(lax.ppermute(buf, axes, pairs(axis, size - shift)))
             buf = jnp.concatenate(pieces, axis=0)
-        return buf
+        return buf, tie
 
     def scatter_sum(own, sent_first, piece_shape):
         later = list(reversed(stages))
@@ -254,7 +256,16 @@
         table = jnp.asarray(table_np)
         own = table[me]
 
-        kv_t = gather_blocks(jnp.concatenate([keys.T, values.T], axis=0))
+        def my_heads(x):
+            part = lax.dynamic_slice_in_dim(x, split_place * width, width, axis=1)
+            return part.reshape(query_count, BLOCK * heads_here, HEAD_DIM)
+
+        lists = block_lists.astype(jnp.int32)
+        keep = first_occurrence(lists)
+        prepared = (my_heads(queries), my_heads(out_grad), lists, keep,
+                    lax.dynamic_index_in_dim(jnp.asarray(held_np), me, keepdims=False))
+        kv_t, prepared = gather_blocks(jnp.concatenate([keys.T, values.T], axis=0), prepared)
+        q_mine, do_mine, lists, keep, positions = prepared
         block_total = kv_t.shape[0]
 
         def held_at(block):
@@ -270,11 +281,8 @@
             part = lax.dynamic_slice_in_dim(x, split_place * width, width, axis=1)
             return part.reshape(query_count, BLOCK * heads_here, HEAD_DIM)
 
-        lists = block_lists.astype(jnp.int32)
-        keep = first_occurrence(lists)
         o_rows, dq_rows, dkv_t = attend_local(
-            my_heads(queries), my_heads(out_grad), kv_t, lists, keep, stages[-1][1],
-            lax.dynamic_index_in_dim(jnp.asarray(held_np), me, keepdims=False))
+            q_mine, do_mine, kv_t, lists, keep, stages[-1][1], positions)
 
         def join_halves(rows):
             mine = rows.reshape(token_rows, width)

time: 177 us -> 176 us (level)
  Pallas kernels: 22.5 us -> 53 us
  starting transfers between devices: 65.1 us -> 35.2 us
    ppermute x1, starting transfers between devices: 23.5 us -> 1.5 us  [scatter_sum(): lax.ppermute(sent_first[shift - 1], axes, pairs(first_axis, shift))]
    pallas_call x1, Pallas kernels: 14.3 us -> 33.9 us  [attend_local(): pl.pallas_call(_backward_kernel, out_shape=(jax.ShapeDtypeStruct((query_c...]
    pallas_call x1, Pallas kernels: 8.2 us -> 19 us  [attend_local(): pl.pallas_call(_forward_kernel, out_shape=(jax.ShapeDtypeStruct((query_co...]
    ppermute x9, starting transfers between devices: 23.4 us -> 15.5 us  [scatter_sum(): lax.ppermute(sent, axes, pairs(axis, shift)).astype(jnp.float32)]
    ppermute x9, waiting for transfers between devices: 28 us -> 26.2 us  [scatter_sum(): lax.ppermute(sent, axes, pairs(axis, shift)).astype(jnp.float32)]
    reshape x4 -> x2, local copies, waits for them, and re-layouts: 2.35 us -> 0.54 us  [my_heads(): return part.reshape(query_count, BLOCK * heads_here, HEAD_DIM)]
    optimization_barrier x0 -> x2, local copies, waits for them, and re-layouts: none -> 1.79 us  [gather_blocks(): buf, tie = lax.optimization_barrier((buf, tie))]
    unnamed x20 -> x16, local copies, waits for them, and re-layouts: 6.84 us -> 5.65 us
  transfers between devices with their start and end apart: 22 -> 22, of which waited for: 14 -> 13; matrix products, arithmetic and copies ran while one was open for 11% -> 11% of each run, Pallas kernels for 0% -> 0%
where the time goes in v15:
time: 176 us; the launch traced here: 175 us
  waiting for transfers between devices  56 us (32%)
  Pallas kernels  53 us (30%)
  starting transfers between devices  35.2 us (20%)
  local copies, waits for them, and re-layouts  17 us (10%)
  other arithmetic  13.1 us (7%)
    pallas_call x1, Pallas kernels, attend_local(): pl.pallas_call(_backward_kernel, out_shape=(jax.ShapeDtypeStruct((query_c...  33.9 us
    ppermute x9, waiting for transfers between devices, scatter_sum(): lax.ppermute(sent, axes, pairs(axis, shift)).astype(jnp.float32)  26.2 us
    ppermute x10, waiting for transfers between devices, gather_blocks(): pieces.append(lax.ppermute(buf, axes, pairs(axis, size - shift)))  25.8 us
    pallas_call x1, Pallas kernels, attend_local(): pl.pallas_call(_forward_kernel, out_shape=(jax.ShapeDtypeStruct((query_co...  19 us
    ppermute x9, starting transfers between devices, scatter_sum(): lax.ppermute(sent, axes, pairs(axis, shift)).astype(jnp.float32)  15.5 us
    ppermute x10, starting transfers between devices, gather_blocks(): pieces.append(lax.ppermute(buf, axes, pairs(axis, size - shift)))  14.5 us
    another operation x3, other arithmetic  6.75 us
    unnamed x16, local copies, waits for them, and re-layouts  5.65 us
  transfers between devices with their start and end apart: 22, of which 13 were waited for; matrix products, arithmetic and copies ran while one was open for 11% of the time, Pallas kernels for 0%

profile of v15, /device:TPU:0, one launch (start us, length us, event | category | flops | bytes accessed | tf_op | source)
XLA Modules:
  0.0 175.1 jit_solution(4716398451104169859)
XLA Ops:
  1.4 3.1 %collective-permute-start = (bf16[1,128,128]{2,1,0:T(8,128)(2,1)S(1)}, bf16[1,128,128]{2,1,0:T(8,128)(2,1)S(1)}, u32[]{:S(2)}, u32[]{:S(2)}) collective-permute-start(bf16[1,128,128]{2,1,0:T(8,128)(2,1)S(1)} %maximum_bitcast_fusion), channel_id=1, source_target_pairs={{0,12},{1,13},{2,14},{3,15},{4,0},{5,1},{6,2},{7,3},{8,4},{9,5},{1... | collective-permute-start | bytes 98312 | tf_op jit(solution)/shard_map/ppermute | solution.py:227
  10.3 2.8 %collective-permute-start.3 = (bf16[4,128,128]{2,1,0:T(8,128)(2,1)S(1)}, bf16[4,128,128]{2,1,0:T(8,128)(2,1)S(1)}, u32[]{:S(2)}, u32[]{:S(2)}) collective-permute-start(bf16[4,128,128]{2,1,0:T(8,128)(2,1)S(1)} %pad_maximum_fusion), channel_id=1, source_target_pairs={{0,17},{1,16},{2,19},{3,18},{4,21},{5,20},{6,23},{7,22},{8,25},{9,... | collective-permute-start | bytes 393224 | tf_op jit(solution)/shard_map/ppermute | solution.py:227
  15.6 2.2 %collective-permute-done.3 = bf16[4,128,128]{2,1,0:T(8,128)(2,1)S(1)} collective-permute-done((bf16[4,128,128]{2,1,0:T(8,128)(2,1)S(1)}, bf16[4,128,128]{2,1,0:T(8,128)(2,1)S(1)}, u32[]{:S(2)}, u32[]{:S(2)}) %collective-permute-start.3) | collective-permute-done | bytes 131104 | tf_op jit(solution)/shard_map/ppermute | solution.py:227
  18.5 1.4 collective-permute-done.4
  22.1 4.0 %collective-permute-start.6 = (bf16[16,128,128]{2,1,0:T(8,128)(2,1)S(1)}, bf16[16,128,128]{2,1,0:T(8,128)(2,1)S(1)}, u32[]{:S(2)}, u32[]{:S(2)}) collective-permute-start(bf16[16,128,128]{2,1,0:T(8,128)(2,1)S(1)} %get-tuple-element.51), channel_id=1, source_target_pairs={{0,96},{1,97},{2,98},{3,99},{4,100},{5,101},{6,102},{7,103},{8,104... | collective-permute-start | bytes 1572872 | tf_op jit(solution)/shard_map/ppermute | solution.py:227
  27.4 19.0 %collective-permute-done.6 = bf16[16,128,128]{2,1,0:T(8,128)(2,1)S(1)} collective-permute-done((bf16[16,128,128]{2,1,0:T(8,128)(2,1)S(1)}, bf16[16,128,128]{2,1,0:T(8,128)(2,1)S(1)}, u32[]{:S(2)}, u32[]{:S(2)}) %collective-permute-start.6) | collective-permute-done | bytes 524320 | tf_op jit(solution)/shard_map/ppermute | solution.py:227
  53.9 1.5 collective-permute-done.9
  55.4 1.5 constant_dynamic-update-slice_fusion.11.kvt_ref
  57.6 19.0 %shard_map.93 = (bf16[2,64,1024]{2,1,0:T(8,128)(2,1)}, f32[2,1,1024]{2,1,0:T(1,128)}, f32[2,1,1024]{2,1,0:T(1,128)}) custom-call(s32[2,48]{1,0:T(2,128)} %select_reduce_fusion.lists_ref, s32[2,48]{1,0:T(2,128)} %broadcast_in_dim.19.count_ref, s32[128]{0:T(128)} %fusion.10.pos_ref, bf16[2,64,1024]{2,1,0:T(8,128)(2,1)} %bitcast.49, ...), custom_call_target="tpu_custom_call" | custom-call | tf_op jit(solution)/shard_map/pallas_call | solution.py:148
  76.6 33.9 %shard_map.94 = (bf16[2,64,1024]{2,1,0:T(8,128)(2,1)}, f32[64,128,128]{2,1,0:T(8,128)}, bf16[1,64,128,128]{3,2,1,0:T(8,128)(2,1)}) custom-call(s32[2,48]{1,0:T(2,128)} %select_reduce_fusion.lists_ref, s32[2,48]{1,0:T(2,128)} %broadcast_in_dim.19.count_ref, s32[128]{0:T(128)} %fusion.10.pos_ref, bf16[2,1024,64]{2,1,0:T(8,128)(2,1)} %copy-done, ...), custom_call_target="tpu_custom_call" | custom-call | tf_op jit(solution)/shard_map/pallas_call | solution.py:165
  110.6 1.5 collective-permute-start.12
  112.1 4.0 %collective-permute-done.12 = bf16[64,128,128]{2,1,0:T(8,128)(2,1)S(1)} collective-permute-done((bf16[64,128,128]{2,1,0:T(8,128)(2,1)}, bf16[64,128,128]{2,1,0:T(8,128)(2,1)S(1)}, u32[]{:S(2)}, u32[]{:S(2)}) %collective-permute-start.12) | collective-permute-done | bytes 2097184 | tf_op jit(solution)/shard_map/ppermute | solution.py:236
  116.1 5.3 %fusion.14 = (bf16[64,128,128]{2,1,0:T(8,128)(2,1)S(1)}, f32[64,128,128]{2,1,0:T(8,128)}) fusion(f32[64,128,128]{2,1,0:T(8,128)} %get-tuple-element.26, bf16[64,128,128]{2,1,0:T(8,128)(2,1)S(1)} %collective-permute-done.12), kind=kLoop, calls=%fused_computation.58 | loop fusion | flops 3145728 | bytes 12582912 | tf_op jit(solution)/shard_map/convert.9
  121.5 4.0 %collective-permute-start.13 = (bf16[4,4,128,128]{3,2,1,0:T(8,128)(2,1)S(1)}, bf16[4,4,128,128]{3,2,1,0:T(8,128)(2,1)S(1)}, u32[]{:S(2)}, u32[]{:S(2)}) collective-permute-start(bf16[4,4,128,128]{3,2,1,0:T(8,128)(2,1)S(1)} %bitcast.55), channel_id=1, source_target_pairs={{0,32},{1,33},{2,34},{3,35},{4,36},{5,37},{6,38},{7,39},{8,40},{9,... | collective-permute-start | bytes 1572872 | tf_op jit(solution)/shard_map/ppermute | solution.py:243
  125.5 2.3 %collective-permute-start.14 = (bf16[4,4,128,128]{3,2,1,0:T(8,128)(2,1)S(1)}, bf16[4,4,128,128]{3,2,1,0:T(8,128)(2,1)S(1)}, u32[]{:S(2)}, u32[]{:S(2)}) collective-permute-start(bf16[4,4,128,128]{3,2,1,0:T(8,128)(2,1)S(1)} %bitcast.54), channel_id=1, source_target_pairs={{0,64},{1,65},{2,66},{3,67},{4,68},{5,69},{6,70},{7,71},{8,72},{9,... | collective-permute-start | bytes 1572872 | tf_op jit(solution)/shard_map/ppermute | solution.py:243
  128.9 2.3 %collective-permute-start.11 = (bf16[256,512]{1,0:T(8,128)(2,1)S(1)}, bf16[256,512]{1,0:T(8,128)(2,1)}, u32[]{:S(2)}, u32[]{:S(2)}) collective-permute-start(bf16[256,512]{1,0:T(8,128)(2,1)S(1)} %reshape.69), channel_id=1, source_target_pairs={{0,1},{1,0},{2,3},{3,2},{4,5},{5,4},{6,7},{7,6},{8,9},{9,8},{10,11... | collective-permute-start | bytes 786440 | tf_op jit(solution)/shard_map/ppermute | solution.py:289
  132.5 6.3 %collective-permute-done.13 = bf16[4,4,128,128]{3,2,1,0:T(8,128)(2,1)S(1)} collective-permute-done((bf16[4,4,128,128]{3,2,1,0:T(8,128)(2,1)S(1)}, bf16[4,4,128,128]{3,2,1,0:T(8,128)(2,1)S(1)}, u32[]{:S(2)}, u32[]{:S(2)}) %collective-permute-start.13) | collective-permute-done | bytes 524320 | tf_op jit(solution)/shard_map/ppermute | solution.py:243
  138.9 12.4 %collective-permute-done.14 = bf16[4,4,128,128]{3,2,1,0:T(8,128)(2,1)S(1)} collective-permute-done((bf16[4,4,128,128]{3,2,1,0:T(8,128)(2,1)S(1)}, bf16[4,4,128,128]{3,2,1,0:T(8,128)(2,1)S(1)}, u32[]{:S(2)}, u32[]{:S(2)}) %collective-permute-start.14) | collective-permute-done | bytes 524320 | tf_op jit(solution)/shard_map/ppermute | solution.py:243
  152.8 2.3 %collective-permute-start.17 = (bf16[4,128,128]{2,1,0:T(8,128)(2,1)S(1)}, bf16[4,128,128]{2,1,0:T(8,128)(2,1)S(1)}, u32[]{:S(2)}, u32[]{:S(2)}) collective-permute-start(bf16[4,128,128]{2,1,0:T(8,128)(2,1)S(1)} %get-tuple-element.39), channel_id=1, source_target_pairs={{0,1},{1,0},{2,3},{3,2},{4,5},{5,4},{6,7},{7,6},{8,9},{9,8},{10,11... | collective-permute-start | bytes 393224 | tf_op jit(solution)/shard_map/ppermute | solution.py:243
  155.1 2.5 %collective-permute-start.18 = (bf16[4,128,128]{2,1,0:T(8,128)(2,1)S(1)}, bf16[4,128,128]{2,1,0:T(8,128)(2,1)S(1)}, u32[]{:S(2)}, u32[]{:S(2)}) collective-permute-start(bf16[4,128,128]{2,1,0:T(8,128)(2,1)S(1)} %get-tuple-element.38), channel_id=1, source_target_pairs={{0,17},{1,16},{2,19},{3,18},{4,21},{5,20},{6,23},{7,22},{8,25},{9,... | collective-permute-start | bytes 393224 | tf_op jit(solution)/shard_map/ppermute | solution.py:243
  158.2 1.4 collective-permute-start.10
  159.6 2.0 %maximum_select_fusion.1 = bf16[256,1024]{1,0:T(8,128)(2,1)} fusion(bf16[256,512]{1,0:T(8,128)(2,1)} %collective-permute-done.11, bf16[256,512]{1,0:T(8,128)(2,1)S(1)} %reshape.69, pred[]{:T(512)S(6)} %eq.37), kind=kLoop, calls=%fused_computation.3 | loop fusion | flops 2359296 | bytes 1048577 | tf_op jit(solution)/shard_map/jit(_where)/select_n | solution.py:290
  161.6 5.7 %collective-permute-done.16 = bf16[4,128,128]{2,1,0:T(8,128)(2,1)S(1)} collective-permute-done((bf16[4,128,128]{2,1,0:T(8,128)(2,1)S(1)}, bf16[4,128,128]{2,1,0:T(8,128)(2,1)S(1)}, u32[]{:S(2)}, u32[]{:S(2)}) %collective-permute-start.16) | collective-permute-done | bytes 131104 | tf_op jit(solution)/shard_map/ppermute | solution.py:243
  168.4 2.8 %collective-permute-start.21 = (bf16[128,128]{1,0:T(8,128)(2,1)S(1)}, bf16[128,128]{1,0:T(8,128)(2,1)S(1)}, u32[]{:S(2)}, u32[]{:S(2)}) collective-permute-start(bf16[128,128]{1,0:T(8,128)(2,1)S(1)} %get-tuple-element.47), channel_id=1, source_target_pairs={{0,12},{1,13},{2,14},{3,15},{4,0},{5,1},{6,2},{7,3},{8,4},{9,5},{1... | collective-permute-start | bytes 98312 | tf_op jit(solution)/shard_map/ppermute | solution.py:243
  (73 shorter events, 30.8 us)
Async XLA Ops:
  1.4 8.6 %collective-permute-start = (bf16[1,128,128]{2,1,0:T(8,128)(2,1)S(1)}, bf16[1,128,128]{2,1,0:T(8,128)(2,1)S(1)}, u32[]{:S(2)}, u32[]{:S(2)}) collective-permute-start(bf16[1,128,128]{2,1,0:T(8,128)(2,1)S(1)} %maximum_bitcast_fusion), channel_id=1, source_target_pairs={{0,12},{1,13},{2,14},{3,15},{4,0},{5,1},{6,2},{7,3},{8,4},{9,5},{1... | collective-permute-start | bytes 98312 | tf_op jit(solution)/shard_map/ppermute | solution.py:227
  4.5 5.5 %collective-permute-start.1 = (bf16[1,128,128]{2,1,0:T(8,128)(2,1)S(1)}, bf16[1,128,128]{2,1,0:T(8,128)(2,1)S(1)}, u32[]{:S(2)}, u32[]{:S(2)}) collective-permute-start(bf16[1,128,128]{2,1,0:T(8,128)(2,1)S(1)} %maximum_bitcast_fusion), channel_id=1, source_target_pairs={{0,8},{1,9},{2,10},{3,11},{4,12},{5,13},{6,14},{7,15},{8,0},{9,1},... | collective-permute-start | bytes 98312 | tf_op jit(solution)/shard_map/ppermute | solution.py:227
  5.1 5.1 %collective-permute-start.2 = (bf16[1,128,128]{2,1,0:T(8,128)(2,1)S(1)}, bf16[1,128,128]{2,1,0:T(8,128)(2,1)S(1)}, u32[]{:S(2)}, u32[]{:S(2)}) collective-permute-start(bf16[1,128,128]{2,1,0:T(8,128)(2,1)S(1)} %maximum_bitcast_fusion), channel_id=1, source_target_pairs={{0,4},{1,5},{2,6},{3,7},{4,8},{5,9},{6,10},{7,11},{8,12},{9,13},{1... | collective-permute-start | bytes 98312 | tf_op jit(solution)/shard_map/ppermute | solution.py:227
  10.0 43.2 %copy-start.1 = (bf16[2,1024,64]{2,1,0:T(8,128)(2,1)}, bf16[2,1024,64]{2,1,0:T(8,128)(2,1)S(1)}, u32[]{:S(2)}) copy-start(bf16[2,1024,64]{2,1,0:T(8,128)(2,1)S(1)} %reshape.67.do_ref) | copy-start | bytes 786436
  10.3 42.9 %copy-start.4 = (s32[2,48]{1,0:T(2,128)S(1)}, s32[2,48]{1,0:T(2,128)}, u32[]{:S(2)}) copy-start(s32[2,48]{1,0:T(2,128)} %param.10) | copy-start | bytes 1156
  10.3 7.5 %collective-permute-start.3 = (bf16[4,128,128]{2,1,0:T(8,128)(2,1)S(1)}, bf16[4,128,128]{2,1,0:T(8,128)(2,1)S(1)}, u32[]{:S(2)}, u32[]{:S(2)}) collective-permute-start(bf16[4,128,128]{2,1,0:T(8,128)(2,1)S(1)} %pad_maximum_fusion), channel_id=1, source_target_pairs={{0,17},{1,16},{2,19},{3,18},{4,21},{5,20},{6,23},{7,22},{8,25},{9,... | collective-permute-start | bytes 393224 | tf_op jit(solution)/shard_map/ppermute | solution.py:227
  13.1 6.8 %collective-permute-start.4 = (bf16[4,128,128]{2,1,0:T(8,128)(2,1)S(1)}, bf16[4,128,128]{2,1,0:T(8,128)(2,1)S(1)}, u32[]{:S(2)}, u32[]{:S(2)}) collective-permute-start(bf16[4,128,128]{2,1,0:T(8,128)(2,1)S(1)} %pad_maximum_fusion), channel_id=1, source_target_pairs={{0,1},{1,0},{2,3},{3,2},{4,5},{5,4},{6,7},{7,6},{8,9},{9,8},{10,11... | collective-permute-start | bytes 393224 | tf_op jit(solution)/shard_map/ppermute | solution.py:227
  14.7 6.6 %collective-permute-start.5 = (bf16[4,128,128]{2,1,0:T(8,128)(2,1)S(1)}, bf16[4,128,128]{2,1,0:T(8,128)(2,1)S(1)}, u32[]{:S(2)}, u32[]{:S(2)}) collective-permute-start(bf16[4,128,128]{2,1,0:T(8,128)(2,1)S(1)} %pad_maximum_fusion), channel_id=1, source_target_pairs={{0,16},{1,17},{2,18},{3,19},{4,20},{5,21},{6,22},{7,23},{8,24},{9,... | collective-permute-start | bytes 393224 | tf_op jit(solution)/shard_map/ppermute | solution.py:227
  22.1 24.3 %collective-permute-start.6 = (bf16[16,128,128]{2,1,0:T(8,128)(2,1)S(1)}, bf16[16,128,128]{2,1,0:T(8,128)(2,1)S(1)}, u32[]{:S(2)}, u32[]{:S(2)}) collective-permute-start(bf16[16,128,128]{2,1,0:T(8,128)(2,1)S(1)} %get-tuple-element.51), channel_id=1, source_target_pairs={{0,96},{1,97},{2,98},{3,99},{4,100},{5,101},{6,102},{7,103},{8,104... | collective-permute-start | bytes 1572872 | tf_op jit(solution)/shard_map/ppermute | solution.py:227
  26.1 21.5 %collective-permute-start.7 = (bf16[16,128,128]{2,1,0:T(8,128)(2,1)S(1)}, bf16[16,128,128]{2,1,0:T(8,128)(2,1)S(1)}, u32[]{:S(2)}, u32[]{:S(2)}) collective-permute-start(bf16[16,128,128]{2,1,0:T(8,128)(2,1)S(1)} %get-tuple-element.51), channel_id=1, source_target_pairs={{0,64},{1,65},{2,66},{3,67},{4,68},{5,69},{6,70},{7,71},{8,72},{9,... | collective-permute-start | bytes 1572872 | tf_op jit(solution)/shard_map/ppermute | solution.py:227
  26.2 23.6 %collective-permute-start.8 = (bf16[16,128,128]{2,1,0:T(8,128)(2,1)S(1)}, bf16[16,128,128]{2,1,0:T(8,128)(2,1)S(1)}, u32[]{:S(2)}, u32[]{:S(2)}) collective-permute-start(bf16[16,128,128]{2,1,0:T(8,128)(2,1)S(1)} %get-tuple-element.51), channel_id=1, source_target_pairs={{0,32},{1,33},{2,34},{3,35},{4,36},{5,37},{6,38},{7,39},{8,40},{9,... | collective-permute-start | bytes 1572872 | tf_op jit(solution)/shard_map/ppermute | solution.py:227
  51.1 4.4 %collective-permute-start.9 = (bf16[64,128,128]{2,1,0:T(8,128)(2,1)}, bf16[64,128,128]{2,1,0:T(8,128)(2,1)S(1)}, u32[]{:S(2)}, u32[]{:S(2)}) collective-permute-start(bf16[64,128,128]{2,1,0:T(8,128)(2,1)} %get-tuple-element.40), channel_id=1, source_target_pairs={{0,2},{1,3},{2,0},{3,1},{4,6},{5,7},{6,4},{7,5},{8,10},{9,11},{10,... | collective-permute-start | bytes 6291464 | tf_op jit(solution)/shard_map/ppermute | solution.py:227
  110.6 5.5 %collective-permute-start.12 = (bf16[64,128,128]{2,1,0:T(8,128)(2,1)}, bf16[64,128,128]{2,1,0:T(8,128)(2,1)S(1)}, u32[]{:S(2)}, u32[]{:S(2)}) collective-permute-start(bf16[64,128,128]{2,1,0:T(8,128)(2,1)} %bitcast.60), channel_id=1, source_target_pairs={{0,2},{1,3},{2,0},{3,1},{4,6},{5,7},{6,4},{7,5},{8,10},{9,11},{10,... | collective-permute-start | bytes 6291464 | tf_op jit(solution)/shard_map/ppermute | solution.py:236
  121.5 17.3 %collective-permute-start.13 = (bf16[4,4,128,128]{3,2,1,0:T(8,128)(2,1)S(1)}, bf16[4,4,128,128]{3,2,1,0:T(8,128)(2,1)S(1)}, u32[]{:S(2)}, u32[]{:S(2)}) collective-permute-start(bf16[4,4,128,128]{3,2,1,0:T(8,128)(2,1)S(1)} %bitcast.55), channel_id=1, source_target_pairs={{0,32},{1,33},{2,34},{3,35},{4,36},{5,37},{6,38},{7,39},{8,40},{9,... | collective-permute-start | bytes 1572872 | tf_op jit(solution)/shard_map/ppermute | solution.py:243
  125.5 25.7 %collective-permute-start.14 = (bf16[4,4,128,128]{3,2,1,0:T(8,128)(2,1)S(1)}, bf16[4,4,128,128]{3,2,1,0:T(8,128)(2,1)S(1)}, u32[]{:S(2)}, u32[]{:S(2)}) collective-permute-start(bf16[4,4,128,128]{3,2,1,0:T(8,128)(2,1)S(1)} %bitcast.54), channel_id=1, source_target_pairs={{0,64},{1,65},{2,66},{3,67},{4,68},{5,69},{6,70},{7,71},{8,72},{9,... | collective-permute-start | bytes 1572872 | tf_op jit(solution)/shard_map/ppermute | solution.py:243
  127.9 23.4 %collective-permute-start.15 = (bf16[4,4,128,128]{3,2,1,0:T(8,128)(2,1)S(1)}, bf16[4,4,128,128]{3,2,1,0:T(8,128)(2,1)}, u32[]{:S(2)}, u32[]{:S(2)}) collective-permute-start(bf16[4,4,128,128]{3,2,1,0:T(8,128)(2,1)S(1)} %bitcast.53), channel_id=1, source_target_pairs={{0,96},{1,97},{2,98},{3,99},{4,100},{5,101},{6,102},{7,103},{8,104... | collective-permute-start | bytes 1572872 | tf_op jit(solution)/shard_map/ppermute | solution.py:243
  128.9 30.7 %collective-permute-start.11 = (bf16[256,512]{1,0:T(8,128)(2,1)S(1)}, bf16[256,512]{1,0:T(8,128)(2,1)}, u32[]{:S(2)}, u32[]{:S(2)}) collective-permute-start(bf16[256,512]{1,0:T(8,128)(2,1)S(1)} %reshape.69), channel_id=1, source_target_pairs={{0,1},{1,0},{2,3},{3,2},{4,5},{5,4},{6,7},{7,6},{8,9},{9,8},{10,11... | collective-permute-start | bytes 786440 | tf_op jit(solution)/shard_map/ppermute | solution.py:289
  152.7 14.6 %collective-permute-start.16 = (bf16[4,128,128]{2,1,0:T(8,128)(2,1)S(1)}, bf16[4,128,128]{2,1,0:T(8,128)(2,1)S(1)}, u32[]{:S(2)}, u32[]{:S(2)}) collective-permute-start(bf16[4,128,128]{2,1,0:T(8,128)(2,1)S(1)} %get-tuple-element.37), channel_id=1, source_target_pairs={{0,16},{1,17},{2,18},{3,19},{4,20},{5,21},{6,22},{7,23},{8,24},{9,... | collective-permute-start | bytes 393224 | tf_op jit(solution)/shard_map/ppermute | solution.py:243
  152.8 14.5 %collective-permute-start.17 = (bf16[4,128,128]{2,1,0:T(8,128)(2,1)S(1)}, bf16[4,128,128]{2,1,0:T(8,128)(2,1)S(1)}, u32[]{:S(2)}, u32[]{:S(2)}) collective-permute-start(bf16[4,128,128]{2,1,0:T(8,128)(2,1)S(1)} %get-tuple-element.39), channel_id=1, source_target_pairs={{0,1},{1,0},{2,3},{3,2},{4,5},{5,4},{6,7},{7,6},{8,9},{9,8},{10,11... | collective-permute-start | bytes 393224 | tf_op jit(solution)/shard_map/ppermute | solution.py:243
  155.1 12.2 %collective-permute-start.18 = (bf16[4,128,128]{2,1,0:T(8,128)(2,1)S(1)}, bf16[4,128,128]{2,1,0:T(8,128)(2,1)S(1)}, u32[]{:S(2)}, u32[]{:S(2)}) collective-permute-start(bf16[4,128,128]{2,1,0:T(8,128)(2,1)S(1)} %get-tuple-element.38), channel_id=1, source_target_pairs={{0,17},{1,16},{2,19},{3,18},{4,21},{5,20},{6,23},{7,22},{8,25},{9,... | collective-permute-start | bytes 393224 | tf_op jit(solution)/shard_map/ppermute | solution.py:243
  158.2 13.0 %collective-permute-start.10 = (bf16[256,512]{1,0:T(8,128)(2,1)S(1)}, bf16[256,512]{1,0:T(8,128)(2,1)S(1)}, u32[]{:S(2)}, u32[]{:S(2)}) collective-permute-start(bf16[256,512]{1,0:T(8,128)(2,1)S(1)} %reshape.68), channel_id=1, source_target_pairs={{0,1},{1,0},{2,3},{3,2},{4,5},{5,4},{6,7},{7,6},{8,9},{9,8},{10,11... | collective-permute-start | bytes 786440 | tf_op jit(solution)/shard_map/ppermute | solution.py:289
  167.4 5.2 %collective-permute-start.19 = (bf16[128,128]{1,0:T(8,128)(2,1)S(1)}, bf16[128,128]{1,0:T(8,128)(2,1)S(1)}, u32[]{:S(2)}, u32[]{:S(2)}) collective-permute-start(bf16[128,128]{1,0:T(8,128)(2,1)S(1)} %get-tuple-element.46), channel_id=1, source_target_pairs={{0,4},{1,5},{2,6},{3,7},{4,8},{5,9},{6,10},{7,11},{8,12},{9,13},{1... | collective-permute-start | bytes 98312 | tf_op jit(solution)/shard_map/ppermute | solution.py:243
  168.4 5.4 %collective-permute-start.20 = (bf16[128,128]{1,0:T(8,128)(2,1)S(1)}, bf16[128,128]{1,0:T(8,128)(2,1)S(1)}, u32[]{:S(2)}, u32[]{:S(2)}) collective-permute-start(bf16[128,128]{1,0:T(8,128)(2,1)S(1)} %get-tuple-element.48), channel_id=1, source_target_pairs={{0,8},{1,9},{2,10},{3,11},{4,12},{5,13},{6,14},{7,15},{8,0},{9,1},... | collective-permute-start | bytes 98312 | tf_op jit(solution)/shard_map/ppermute | solution.py:243
  168.4 5.4 %collective-permute-start.21 = (bf16[128,128]{1,0:T(8,128)(2,1)S(1)}, bf16[128,128]{1,0:T(8,128)(2,1)S(1)}, u32[]{:S(2)}, u32[]{:S(2)}) collective-permute-start(bf16[128,128]{1,0:T(8,128)(2,1)S(1)} %get-tuple-element.47), channel_id=1, source_target_pairs={{0,12},{1,13},{2,14},{3,15},{4,0},{5,1},{6,2},{7,3},{8,4},{9,5},{1... | collective-permute-start | bytes 98312 | tf_op jit(solution)/shard_map/ppermute | solution.py:243
  (3 other events, 73.6 us)

commit v16 on v14

--- a/solution.py
+++ b/solution.py
@@ -87,7 +87,7 @@
                 _pair_cols(kvt_ref, blocks, HEAD_DIM), pt.astype(jnp.bfloat16))
             m_sc[...] = m_new
 
-        _visit_slots(count_ref, qb, visit)
+        _visit_slots(count_ref, qb, visit, group=16)
         out = acc_sc[...] / l_sc[...]
         ot_ref[qb] = out.astype(jnp.bfloat16)
         lse_ref[qb] = m_sc[...] + jnp.log(l_sc[...])

time: 177 us -> 174 us (0.983)
  Pallas kernels: 22.5 us -> 32.9 us
  starting transfers between devices: 65.1 us -> 55.8 us
  waiting for transfers between devices: 56.7 us -> 53 us
    ppermute x1, starting transfers between devices: 23.5 us -> 0.01 us  [scatter_sum(): lax.ppermute(sent_first[shift - 1], axes, pairs(first_axis, shift))]
    ppermute x9, starting transfers between devices: 23.4 us -> 38.7 us  [scatter_sum(): lax.ppermute(sent, axes, pairs(axis, shift)).astype(jnp.float32)]
    pallas_call x1, Pallas kernels: 14.3 us -> 21.9 us  [attend_local(): pl.pallas_call(_backward_kernel, out_shape=(jax.ShapeDtypeStruct((query_c...]
    ppermute x9, waiting for transfers between devices: 28 us -> 24 us  [scatter_sum(): lax.ppermute(sent, axes, pairs(axis, shift)).astype(jnp.float32)]
    pallas_call x1, Pallas kernels: 8.2 us -> 11 us  [attend_local(): pl.pallas_call(_forward_kernel, out_shape=(jax.ShapeDtypeStruct((query_co...]
  transfers between devices with their start and end apart: 22 -> 22, of which waited for: 14 -> 12; matrix products, arithmetic and copies ran while one was open for 11% -> 12% of each run, Pallas kernels for 0% -> 0%
where the time goes in v16:
time: 174 us
  starting transfers between devices  55.8 us (32%)
  waiting for transfers between devices  53 us (30%)
  Pallas kernels  32.9 us (19%)
  local copies, waits for them, and re-layouts  18.2 us (10%)
  other arithmetic  13.7 us (8%)
    ppermute x9, starting transfers between devices, scatter_sum(): lax.ppermute(sent, axes, pairs(axis, shift)).astype(jnp.float32)  38.7 us
    ppermute x10, waiting for transfers between devices, gather_blocks(): pieces.append(lax.ppermute(buf, axes, pairs(axis, size - shift)))  24.7 us
    ppermute x9, waiting for transfers between devices, scatter_sum(): lax.ppermute(sent, axes, pairs(axis, shift)).astype(jnp.float32)  24 us
    pallas_call x1, Pallas kernels, attend_local(): pl.pallas_call(_backward_kernel, out_shape=(jax.ShapeDtypeStruct((query_c...  21.9 us
    ppermute x10, starting transfers between devices, gather_blocks(): pieces.append(lax.ppermute(buf, axes, pairs(axis, size - shift)))  14.5 us
    pallas_call x1, Pallas kernels, attend_local(): pl.pallas_call(_forward_kernel, out_shape=(jax.ShapeDtypeStruct((query_co...  11 us
    unnamed x20, local copies, waits for them, and re-layouts  6.84 us
    another operation x3, other arithmetic  6.77 us
  transfers between devices with their start and end apart: 22, of which 12 were waited for; matrix products, arithmetic and copies ran while one was open for 12% of the time, Pallas kernels for 0%

profile of v16, /device:TPU:0, one launch (start us, length us, event | category | flops | bytes accessed | tf_op | source)
XLA Modules:
  0.0 174.4 jit_solution(11424446640039265779)
XLA Ops:
  1.4 3.1 %collective-permute-start = (bf16[1,128,128]{2,1,0:T(8,128)(2,1)S(1)}, bf16[1,128,128]{2,1,0:T(8,128)(2,1)S(1)}, u32[]{:S(2)}, u32[]{:S(2)}) collective-permute-start(bf16[1,128,128]{2,1,0:T(8,128)(2,1)S(1)} %maximum_bitcast_fusion), channel_id=1, source_target_pairs={{0,12},{1,13},{2,14},{3,15},{4,0},{5,1},{6,2},{7,3},{8,4},{9,5},{1... | collective-permute-start | bytes 98312 | tf_op jit(solution)/shard_map/ppermute | solution.py:225
  6.2 1.4 constant_dynamic-update-slice_fusion.16
  7.5 2.4 %collective-permute-done.1 = bf16[1,128,128]{2,1,0:T(8,128)(2,1)S(1)} collective-permute-done((bf16[1,128,128]{2,1,0:T(8,128)(2,1)S(1)}, bf16[1,128,128]{2,1,0:T(8,128)(2,1)S(1)}, u32[]{:S(2)}, u32[]{:S(2)}) %collective-permute-start.1) | collective-permute-done | bytes 32800 | tf_op jit(solution)/shard_map/ppermute | solution.py:225
  10.4 2.8 %collective-permute-start.3 = (bf16[4,128,128]{2,1,0:T(8,128)(2,1)S(1)}, bf16[4,128,128]{2,1,0:T(8,128)(2,1)S(1)}, u32[]{:S(2)}, u32[]{:S(2)}) collective-permute-start(bf16[4,128,128]{2,1,0:T(8,128)(2,1)S(1)} %pad_maximum_fusion), channel_id=1, source_target_pairs={{0,17},{1,16},{2,19},{3,18},{4,21},{5,20},{6,23},{7,22},{8,25},{9,... | collective-permute-start | bytes 393224 | tf_op jit(solution)/shard_map/ppermute | solution.py:225
  18.2 1.5 collective-permute-done.4
  21.9 4.0 %collective-permute-start.6 = (bf16[16,128,128]{2,1,0:T(8,128)(2,1)S(1)}, bf16[16,128,128]{2,1,0:T(8,128)(2,1)S(1)}, u32[]{:S(2)}, u32[]{:S(2)}) collective-permute-start(bf16[16,128,128]{2,1,0:T(8,128)(2,1)S(1)} %get-tuple-element.39), channel_id=1, source_target_pairs={{0,96},{1,97},{2,98},{3,99},{4,100},{5,101},{6,102},{7,103},{8,104... | collective-permute-start | bytes 1572872 | tf_op jit(solution)/shard_map/ppermute | solution.py:225
  27.2 18.3 %collective-permute-done.6 = bf16[16,128,128]{2,1,0:T(8,128)(2,1)S(1)} collective-permute-done((bf16[16,128,128]{2,1,0:T(8,128)(2,1)S(1)}, bf16[16,128,128]{2,1,0:T(8,128)(2,1)S(1)}, u32[]{:S(2)}, u32[]{:S(2)}) %collective-permute-start.6) | collective-permute-done | bytes 524320 | tf_op jit(solution)/shard_map/ppermute | solution.py:225
  56.1 1.5 constant_dynamic-update-slice_fusion.17.kvt_ref
  58.3 11.0 %shard_map.93 = (bf16[2,64,1024]{2,1,0:T(8,128)(2,1)}, f32[2,1,1024]{2,1,0:T(1,128)}, f32[2,1,1024]{2,1,0:T(1,128)}) custom-call(s32[2,48]{1,0:T(2,128)} %select_reduce_fusion.lists_ref, s32[2,48]{1,0:T(2,128)} %broadcast_in_dim.11.count_ref, s32[128]{0:T(128)} %fusion.10.pos_ref, bf16[2,64,1024]{2,1,0:T(8,128)(2,1)} %bitcast.55, ...), custom_call_target="tpu_custom_call" | custom-call | tf_op jit(solution)/shard_map/pallas_call | solution.py:148
  69.3 21.9 %shard_map.94 = (bf16[2,64,1024]{2,1,0:T(8,128)(2,1)}, f32[64,128,128]{2,1,0:T(8,128)}, bf16[1,64,128,128]{3,2,1,0:T(8,128)(2,1)}) custom-call(s32[2,48]{1,0:T(2,128)} %select_reduce_fusion.lists_ref, s32[2,48]{1,0:T(2,128)} %broadcast_in_dim.11.count_ref, s32[128]{0:T(128)} %fusion.10.pos_ref, bf16[2,1024,64]{2,1,0:T(8,128)(2,1)} %copy-done, ...), custom_call_target="tpu_custom_call" | custom-call | tf_op jit(solution)/shard_map/pallas_call | solution.py:165
  91.2 4.4 %collective-permute-done.12 = bf16[64,128,128]{2,1,0:T(8,128)(2,1)S(1)} collective-permute-done((bf16[64,128,128]{2,1,0:T(8,128)(2,1)}, bf16[64,128,128]{2,1,0:T(8,128)(2,1)S(1)}, u32[]{:S(2)}, u32[]{:S(2)}) %collective-permute-start.12) | collective-permute-done | bytes 2097184 | tf_op jit(solution)/shard_map/ppermute | solution.py:234
  95.6 5.3 %fusion.15 = (bf16[64,128,128]{2,1,0:T(8,128)(2,1)S(1)}, f32[64,128,128]{2,1,0:T(8,128)}) fusion(f32[64,128,128]{2,1,0:T(8,128)} %get-tuple-element.14, bf16[64,128,128]{2,1,0:T(8,128)(2,1)S(1)} %collective-permute-done.12), kind=kLoop, calls=%fused_computation.68 | loop fusion | flops 3145728 | bytes 12582912 | tf_op jit(solution)/shard_map/convert.9
  101.1 22.1 %collective-permute-start.13 = (bf16[4,4,128,128]{3,2,1,0:T(8,128)(2,1)S(1)}, bf16[4,4,128,128]{3,2,1,0:T(8,128)(2,1)S(1)}, u32[]{:S(2)}, u32[]{:S(2)}) collective-permute-start(bf16[4,4,128,128]{3,2,1,0:T(8,128)(2,1)S(1)} %bitcast.61), channel_id=1, source_target_pairs={{0,32},{1,33},{2,34},{3,35},{4,36},{5,37},{6,38},{7,39},{8,40},{9,... | collective-permute-start | bytes 1572872 | tf_op jit(solution)/shard_map/ppermute | solution.py:241
  123.1 2.9 %collective-permute-start.14 = (bf16[4,4,128,128]{3,2,1,0:T(8,128)(2,1)S(1)}, bf16[4,4,128,128]{3,2,1,0:T(8,128)(2,1)S(1)}, u32[]{:S(2)}, u32[]{:S(2)}) collective-permute-start(bf16[4,4,128,128]{3,2,1,0:T(8,128)(2,1)S(1)} %bitcast.60), channel_id=1, source_target_pairs={{0,64},{1,65},{2,66},{3,67},{4,68},{5,69},{6,70},{7,71},{8,72},{9,... | collective-permute-start | bytes 1572872 | tf_op jit(solution)/shard_map/ppermute | solution.py:241
  128.9 8.0 %collective-permute-done.13 = bf16[4,4,128,128]{3,2,1,0:T(8,128)(2,1)S(1)} collective-permute-done((bf16[4,4,128,128]{3,2,1,0:T(8,128)(2,1)S(1)}, bf16[4,4,128,128]{3,2,1,0:T(8,128)(2,1)S(1)}, u32[]{:S(2)}, u32[]{:S(2)}) %collective-permute-start.13) | collective-permute-done | bytes 524320 | tf_op jit(solution)/shard_map/ppermute | solution.py:241
  136.8 12.4 %collective-permute-done.14 = bf16[4,4,128,128]{3,2,1,0:T(8,128)(2,1)S(1)} collective-permute-done((bf16[4,4,128,128]{3,2,1,0:T(8,128)(2,1)S(1)}, bf16[4,4,128,128]{3,2,1,0:T(8,128)(2,1)S(1)}, u32[]{:S(2)}, u32[]{:S(2)}) %collective-permute-start.14) | collective-permute-done | bytes 524320 | tf_op jit(solution)/shard_map/ppermute | solution.py:241
  149.2 1.4 fusion.14
  150.6 4.1 %collective-permute-start.16 = (bf16[4,128,128]{2,1,0:T(8,128)(2,1)S(1)}, bf16[4,128,128]{2,1,0:T(8,128)(2,1)S(1)}, u32[]{:S(2)}, u32[]{:S(2)}) collective-permute-start(bf16[4,128,128]{2,1,0:T(8,128)(2,1)S(1)} %get-tuple-element.25), channel_id=1, source_target_pairs={{0,16},{1,17},{2,18},{3,19},{4,20},{5,21},{6,22},{7,23},{8,24},{9,... | collective-permute-start | bytes 393224 | tf_op jit(solution)/shard_map/ppermute | solution.py:241
  154.7 3.0 %collective-permute-start.17 = (bf16[4,128,128]{2,1,0:T(8,128)(2,1)S(1)}, bf16[4,128,128]{2,1,0:T(8,128)(2,1)S(1)}, u32[]{:S(2)}, u32[]{:S(2)}) collective-permute-start(bf16[4,128,128]{2,1,0:T(8,128)(2,1)S(1)} %get-tuple-element.27), channel_id=1, source_target_pairs={{0,1},{1,0},{2,3},{3,2},{4,5},{5,4},{6,7},{7,6},{8,9},{9,8},{10,11... | collective-permute-start | bytes 393224 | tf_op jit(solution)/shard_map/ppermute | solution.py:241
  158.3 1.6 collective-permute-start.10
  160.0 2.0 %maximum_select_fusion.1 = bf16[256,1024]{1,0:T(8,128)(2,1)} fusion(bf16[256,512]{1,0:T(8,128)(2,1)} %collective-permute-done.11, bf16[256,512]{1,0:T(8,128)(2,1)S(1)} %reshape.75, pred[]{:T(512)S(6)} %eq.41), kind=kLoop, calls=%fused_computation.3 | loop fusion | flops 2359296 | bytes 1048577 | tf_op jit(solution)/shard_map/jit(_where)/select_n | solution.py:282
  162.0 2.9 %collective-permute-done.17 = bf16[4,128,128]{2,1,0:T(8,128)(2,1)S(1)} collective-permute-done((bf16[4,128,128]{2,1,0:T(8,128)(2,1)S(1)}, bf16[4,128,128]{2,1,0:T(8,128)(2,1)S(1)}, u32[]{:S(2)}, u32[]{:S(2)}) %collective-permute-start.17) | collective-permute-done | bytes 131104 | tf_op jit(solution)/shard_map/ppermute | solution.py:241
  165.8 3.2 %collective-permute-start.20 = (bf16[128,128]{1,0:T(8,128)(2,1)S(1)}, bf16[128,128]{1,0:T(8,128)(2,1)S(1)}, u32[]{:S(2)}, u32[]{:S(2)}) collective-permute-start(bf16[128,128]{1,0:T(8,128)(2,1)S(1)} %get-tuple-element.36), channel_id=1, source_target_pairs={{0,8},{1,9},{2,10},{3,11},{4,12},{5,13},{6,14},{7,15},{8,0},{9,1},... | collective-permute-start | bytes 98312 | tf_op jit(solution)/shard_map/ppermute | solution.py:241
  169.0 2.5 %collective-permute-start.21 = (bf16[128,128]{1,0:T(8,128)(2,1)S(1)}, bf16[128,128]{1,0:T(8,128)(2,1)S(1)}, u32[]{:S(2)}, u32[]{:S(2)}) collective-permute-start(bf16[128,128]{1,0:T(8,128)(2,1)S(1)} %get-tuple-element.35), channel_id=1, source_target_pairs={{0,12},{1,13},{2,14},{3,15},{4,0},{5,1},{6,2},{7,3},{8,4},{9,5},{1... | collective-permute-start | bytes 98312 | tf_op jit(solution)/shard_map/ppermute | solution.py:241
  (77 shorter events, 29.7 us)
Async XLA Ops:
  0.6 49.5 %copy-start.4 = (bf16[256,1024]{1,0:T(8,128)(2,1)S(1)}, bf16[256,1024]{1,0:T(8,128)(2,1)}, u32[]{:S(2)}) copy-start(bf16[256,1024]{1,0:T(8,128)(2,1)} %param.6) | copy-start | bytes 1572868
  1.4 6.1 %collective-permute-start = (bf16[1,128,128]{2,1,0:T(8,128)(2,1)S(1)}, bf16[1,128,128]{2,1,0:T(8,128)(2,1)S(1)}, u32[]{:S(2)}, u32[]{:S(2)}) collective-permute-start(bf16[1,128,128]{2,1,0:T(8,128)(2,1)S(1)} %maximum_bitcast_fusion), channel_id=1, source_target_pairs={{0,12},{1,13},{2,14},{3,15},{4,0},{5,1},{6,2},{7,3},{8,4},{9,5},{1... | collective-permute-start | bytes 98312 | tf_op jit(solution)/shard_map/ppermute | solution.py:225
  4.6 5.4 %collective-permute-start.1 = (bf16[1,128,128]{2,1,0:T(8,128)(2,1)S(1)}, bf16[1,128,128]{2,1,0:T(8,128)(2,1)S(1)}, u32[]{:S(2)}, u32[]{:S(2)}) collective-permute-start(bf16[1,128,128]{2,1,0:T(8,128)(2,1)S(1)} %maximum_bitcast_fusion), channel_id=1, source_target_pairs={{0,8},{1,9},{2,10},{3,11},{4,12},{5,13},{6,14},{7,15},{8,0},{9,1},... | collective-permute-start | bytes 98312 | tf_op jit(solution)/shard_map/ppermute | solution.py:225
  5.2 5.1 %collective-permute-start.2 = (bf16[1,128,128]{2,1,0:T(8,128)(2,1)S(1)}, bf16[1,128,128]{2,1,0:T(8,128)(2,1)S(1)}, u32[]{:S(2)}, u32[]{:S(2)}) collective-permute-start(bf16[1,128,128]{2,1,0:T(8,128)(2,1)S(1)} %maximum_bitcast_fusion), channel_id=1, source_target_pairs={{0,4},{1,5},{2,6},{3,7},{4,8},{5,9},{6,10},{7,11},{8,12},{9,13},{1... | collective-permute-start | bytes 98312 | tf_op jit(solution)/shard_map/ppermute | solution.py:225
  10.4 7.1 %collective-permute-start.3 = (bf16[4,128,128]{2,1,0:T(8,128)(2,1)S(1)}, bf16[4,128,128]{2,1,0:T(8,128)(2,1)S(1)}, u32[]{:S(2)}, u32[]{:S(2)}) collective-permute-start(bf16[4,128,128]{2,1,0:T(8,128)(2,1)S(1)} %pad_maximum_fusion), channel_id=1, source_target_pairs={{0,17},{1,16},{2,19},{3,18},{4,21},{5,20},{6,23},{7,22},{8,25},{9,... | collective-permute-start | bytes 393224 | tf_op jit(solution)/shard_map/ppermute | solution.py:225
  13.2 6.6 %collective-permute-start.4 = (bf16[4,128,128]{2,1,0:T(8,128)(2,1)S(1)}, bf16[4,128,128]{2,1,0:T(8,128)(2,1)S(1)}, u32[]{:S(2)}, u32[]{:S(2)}) collective-permute-start(bf16[4,128,128]{2,1,0:T(8,128)(2,1)S(1)} %pad_maximum_fusion), channel_id=1, source_target_pairs={{0,1},{1,0},{2,3},{3,2},{4,5},{5,4},{6,7},{7,6},{8,9},{9,8},{10,11... | collective-permute-start | bytes 393224 | tf_op jit(solution)/shard_map/ppermute | solution.py:225
  14.0 7.1 %collective-permute-start.5 = (bf16[4,128,128]{2,1,0:T(8,128)(2,1)S(1)}, bf16[4,128,128]{2,1,0:T(8,128)(2,1)S(1)}, u32[]{:S(2)}, u32[]{:S(2)}) collective-permute-start(bf16[4,128,128]{2,1,0:T(8,128)(2,1)S(1)} %pad_maximum_fusion), channel_id=1, source_target_pairs={{0,16},{1,17},{2,18},{3,19},{4,20},{5,21},{6,22},{7,23},{8,24},{9,... | collective-permute-start | bytes 393224 | tf_op jit(solution)/shard_map/ppermute | solution.py:225
  21.9 23.6 %collective-permute-start.6 = (bf16[16,128,128]{2,1,0:T(8,128)(2,1)S(1)}, bf16[16,128,128]{2,1,0:T(8,128)(2,1)S(1)}, u32[]{:S(2)}, u32[]{:S(2)}) collective-permute-start(bf16[16,128,128]{2,1,0:T(8,128)(2,1)S(1)} %get-tuple-element.39), channel_id=1, source_target_pairs={{0,96},{1,97},{2,98},{3,99},{4,100},{5,101},{6,102},{7,103},{8,104... | collective-permute-start | bytes 1572872 | tf_op jit(solution)/shard_map/ppermute | solution.py:225
  25.9 20.8 %collective-permute-start.7 = (bf16[16,128,128]{2,1,0:T(8,128)(2,1)S(1)}, bf16[16,128,128]{2,1,0:T(8,128)(2,1)S(1)}, u32[]{:S(2)}, u32[]{:S(2)}) collective-permute-start(bf16[16,128,128]{2,1,0:T(8,128)(2,1)S(1)} %get-tuple-element.39), channel_id=1, source_target_pairs={{0,64},{1,65},{2,66},{3,67},{4,68},{5,69},{6,70},{7,71},{8,72},{9,... | collective-permute-start | bytes 1572872 | tf_op jit(solution)/shard_map/ppermute | solution.py:225
  25.9 23.0 %collective-permute-start.8 = (bf16[16,128,128]{2,1,0:T(8,128)(2,1)S(1)}, bf16[16,128,128]{2,1,0:T(8,128)(2,1)S(1)}, u32[]{:S(2)}, u32[]{:S(2)}) collective-permute-start(bf16[16,128,128]{2,1,0:T(8,128)(2,1)S(1)} %get-tuple-element.39), channel_id=1, source_target_pairs={{0,32},{1,33},{2,34},{3,35},{4,36},{5,37},{6,38},{7,39},{8,40},{9,... | collective-permute-start | bytes 1572872 | tf_op jit(solution)/shard_map/ppermute | solution.py:225
  50.2 5.9 %collective-permute-start.9 = (bf16[64,128,128]{2,1,0:T(8,128)(2,1)}, bf16[64,128,128]{2,1,0:T(8,128)(2,1)S(1)}, u32[]{:S(2)}, u32[]{:S(2)}) collective-permute-start(bf16[64,128,128]{2,1,0:T(8,128)(2,1)} %get-tuple-element.28), channel_id=1, source_target_pairs={{0,2},{1,3},{2,0},{3,1},{4,6},{5,7},{6,4},{7,5},{8,10},{9,11},{10,... | collective-permute-start | bytes 6291464 | tf_op jit(solution)/shard_map/ppermute | solution.py:225
  91.2 4.4 %collective-permute-start.12 = (bf16[64,128,128]{2,1,0:T(8,128)(2,1)}, bf16[64,128,128]{2,1,0:T(8,128)(2,1)S(1)}, u32[]{:S(2)}, u32[]{:S(2)}) collective-permute-start(bf16[64,128,128]{2,1,0:T(8,128)(2,1)} %bitcast.68), channel_id=1, source_target_pairs={{0,2},{1,3},{2,0},{3,1},{4,6},{5,7},{6,4},{7,5},{8,10},{9,11},{10,... | collective-permute-start | bytes 6291464 | tf_op jit(solution)/shard_map/ppermute | solution.py:234
  95.6 30.5 %copy-start.3 = (bf16[2,64,1024]{2,1,0:T(8,128)(2,1)S(1)}, bf16[2,64,1024]{2,1,0:T(8,128)(2,1)}, u32[]{:S(2)}) copy-start(bf16[2,64,1024]{2,1,0:T(8,128)(2,1)} %get-tuple-element.13) | copy-start | bytes 786436
  101.1 35.8 %collective-permute-start.13 = (bf16[4,4,128,128]{3,2,1,0:T(8,128)(2,1)S(1)}, bf16[4,4,128,128]{3,2,1,0:T(8,128)(2,1)S(1)}, u32[]{:S(2)}, u32[]{:S(2)}) collective-permute-start(bf16[4,4,128,128]{3,2,1,0:T(8,128)(2,1)S(1)} %bitcast.61), channel_id=1, source_target_pairs={{0,32},{1,33},{2,34},{3,35},{4,36},{5,37},{6,38},{7,39},{8,40},{9,... | collective-permute-start | bytes 1572872 | tf_op jit(solution)/shard_map/ppermute | solution.py:241
  123.1 26.1 %collective-permute-start.14 = (bf16[4,4,128,128]{3,2,1,0:T(8,128)(2,1)S(1)}, bf16[4,4,128,128]{3,2,1,0:T(8,128)(2,1)S(1)}, u32[]{:S(2)}, u32[]{:S(2)}) collective-permute-start(bf16[4,4,128,128]{3,2,1,0:T(8,128)(2,1)S(1)} %bitcast.60), channel_id=1, source_target_pairs={{0,64},{1,65},{2,66},{3,67},{4,68},{5,69},{6,70},{7,71},{8,72},{9,... | collective-permute-start | bytes 1572872 | tf_op jit(solution)/shard_map/ppermute | solution.py:241
  126.1 23.2 %collective-permute-start.15 = (bf16[4,4,128,128]{3,2,1,0:T(8,128)(2,1)S(1)}, bf16[4,4,128,128]{3,2,1,0:T(8,128)(2,1)}, u32[]{:S(2)}, u32[]{:S(2)}) collective-permute-start(bf16[4,4,128,128]{3,2,1,0:T(8,128)(2,1)S(1)} %bitcast.59), channel_id=1, source_target_pairs={{0,96},{1,97},{2,98},{3,99},{4,100},{5,101},{6,102},{7,103},{8,104... | collective-permute-start | bytes 1572872 | tf_op jit(solution)/shard_map/ppermute | solution.py:241
  126.7 33.3 %collective-permute-start.11 = (bf16[256,512]{1,0:T(8,128)(2,1)S(1)}, bf16[256,512]{1,0:T(8,128)(2,1)}, u32[]{:S(2)}, u32[]{:S(2)}) collective-permute-start(bf16[256,512]{1,0:T(8,128)(2,1)S(1)} %reshape.75), channel_id=1, source_target_pairs={{0,1},{1,0},{2,3},{3,2},{4,5},{5,4},{6,7},{7,6},{8,9},{9,8},{10,11... | collective-permute-start | bytes 786440 | tf_op jit(solution)/shard_map/ppermute | solution.py:281
  150.6 11.3 %collective-permute-start.16 = (bf16[4,128,128]{2,1,0:T(8,128)(2,1)S(1)}, bf16[4,128,128]{2,1,0:T(8,128)(2,1)S(1)}, u32[]{:S(2)}, u32[]{:S(2)}) collective-permute-start(bf16[4,128,128]{2,1,0:T(8,128)(2,1)S(1)} %get-tuple-element.25), channel_id=1, source_target_pairs={{0,16},{1,17},{2,18},{3,19},{4,20},{5,21},{6,22},{7,23},{8,24},{9,... | collective-permute-start | bytes 393224 | tf_op jit(solution)/shard_map/ppermute | solution.py:241
  154.7 10.1 %collective-permute-start.17 = (bf16[4,128,128]{2,1,0:T(8,128)(2,1)S(1)}, bf16[4,128,128]{2,1,0:T(8,128)(2,1)S(1)}, u32[]{:S(2)}, u32[]{:S(2)}) collective-permute-start(bf16[4,128,128]{2,1,0:T(8,128)(2,1)S(1)} %get-tuple-element.27), channel_id=1, source_target_pairs={{0,1},{1,0},{2,3},{3,2},{4,5},{5,4},{6,7},{7,6},{8,9},{9,8},{10,11... | collective-permute-start | bytes 393224 | tf_op jit(solution)/shard_map/ppermute | solution.py:241
  157.7 7.2 %collective-permute-start.18 = (bf16[4,128,128]{2,1,0:T(8,128)(2,1)S(1)}, bf16[4,128,128]{2,1,0:T(8,128)(2,1)S(1)}, u32[]{:S(2)}, u32[]{:S(2)}) collective-permute-start(bf16[4,128,128]{2,1,0:T(8,128)(2,1)S(1)} %get-tuple-element.26), channel_id=1, source_target_pairs={{0,17},{1,16},{2,19},{3,18},{4,21},{5,20},{6,23},{7,22},{8,25},{9,... | collective-permute-start | bytes 393224 | tf_op jit(solution)/shard_map/ppermute | solution.py:241
  158.3 13.3 %collective-permute-start.10 = (bf16[256,512]{1,0:T(8,128)(2,1)S(1)}, bf16[256,512]{1,0:T(8,128)(2,1)S(1)}, u32[]{:S(2)}, u32[]{:S(2)}) collective-permute-start(bf16[256,512]{1,0:T(8,128)(2,1)S(1)} %reshape.74), channel_id=1, source_target_pairs={{0,1},{1,0},{2,3},{3,2},{4,5},{5,4},{6,7},{7,6},{8,9},{9,8},{10,11... | collective-permute-start | bytes 786440 | tf_op jit(solution)/shard_map/ppermute | solution.py:281
  165.0 7.6 %collective-permute-start.19 = (bf16[128,128]{1,0:T(8,128)(2,1)S(1)}, bf16[128,128]{1,0:T(8,128)(2,1)S(1)}, u32[]{:S(2)}, u32[]{:S(2)}) collective-permute-start(bf16[128,128]{1,0:T(8,128)(2,1)S(1)} %get-tuple-element.34), channel_id=1, source_target_pairs={{0,4},{1,5},{2,6},{3,7},{4,8},{5,9},{6,10},{7,11},{8,12},{9,13},{1... | collective-permute-start | bytes 98312 | tf_op jit(solution)/shard_map/ppermute | solution.py:241
  165.8 6.7 %collective-permute-start.20 = (bf16[128,128]{1,0:T(8,128)(2,1)S(1)}, bf16[128,128]{1,0:T(8,128)(2,1)S(1)}, u32[]{:S(2)}, u32[]{:S(2)}) collective-permute-start(bf16[128,128]{1,0:T(8,128)(2,1)S(1)} %get-tuple-element.36), channel_id=1, source_target_pairs={{0,8},{1,9},{2,10},{3,11},{4,12},{5,13},{6,14},{7,15},{8,0},{9,1},... | collective-permute-start | bytes 98312 | tf_op jit(solution)/shard_map/ppermute | solution.py:241
  169.0 4.1 %collective-permute-start.21 = (bf16[128,128]{1,0:T(8,128)(2,1)S(1)}, bf16[128,128]{1,0:T(8,128)(2,1)S(1)}, u32[]{:S(2)}, u32[]{:S(2)}) collective-permute-start(bf16[128,128]{1,0:T(8,128)(2,1)S(1)} %get-tuple-element.35), channel_id=1, source_target_pairs={{0,12},{1,13},{2,14},{3,15},{4,0},{5,1},{6,2},{7,3},{8,4},{9,5},{1... | collective-permute-start | bytes 98312 | tf_op jit(solution)/shard_map/ppermute | solution.py:241
  (4 other events, 63.6 us)

commit v17 on v16

--- a/solution.py
+++ b/solution.py
@@ -118,7 +118,7 @@
                 dkvt_ref[b, :HEAD_DIM, :] += dkt[:, cols]
                 dkvt_ref[b, HEAD_DIM:, :] += dvt[:, cols]
 
-        _visit_slots(count_ref, qb, visit)
+        _visit_slots(count_ref, qb, visit, group=16)
         dqt_ref[qb] = (dq_sc[...] * SCALE).astype(jnp.bfloat16)
         return carry
 

time: 174 us -> 175 us (level); the launches traced: 174 us -> 174 us
  starting transfers between devices: 55.8 us -> 51.5 us
  waiting for transfers between devices: 53 us -> 55.3 us
    ppermute x9, starting transfers between devices: 38.7 us -> 34.5 us  [scatter_sum(): lax.ppermute(sent, axes, pairs(axis, shift)).astype(jnp.float32)]
    ppermute x9, waiting for transfers between devices: 24 us -> 26.3 us  [scatter_sum(): lax.ppermute(sent, axes, pairs(axis, shift)).astype(jnp.float32)]
  transfers between devices with their start and end apart: 22 -> 22, of which waited for: 12 -> 13; matrix products, arithmetic and copies ran while one was open for 12% -> 12% of each run, Pallas kernels for 0% -> 0%
where the time goes in v17:
time: 175 us; the launch traced here: 174 us
  waiting for transfers between devices  55.3 us (32%)
  starting transfers between devices  51.5 us (29%)
  Pallas kernels  34 us (19%)
  local copies, waits for them, and re-layouts  18.2 us (10%)
  other arithmetic  13.7 us (8%)
    ppermute x9, starting transfers between devices, scatter_sum(): lax.ppermute(sent, axes, pairs(axis, shift)).astype(jnp.float32)  34.5 us
    ppermute x9, waiting for transfers between devices, scatter_sum(): lax.ppermute(sent, axes, pairs(axis, shift)).astype(jnp.float32)  26.3 us
    ppermute x10, waiting for transfers between devices, gather_blocks(): pieces.append(lax.ppermute(buf, axes, pairs(axis, size - shift)))  24.7 us
    pallas_call x1, Pallas kernels, attend_local(): pl.pallas_call(_backward_kernel, out_shape=(jax.ShapeDtypeStruct((query_c...  21.9 us
    ppermute x10, starting transfers between devices, gather_blocks(): pieces.append(lax.ppermute(buf, axes, pairs(axis, size - shift)))  14.5 us
    pallas_call x1, Pallas kernels, attend_local(): pl.pallas_call(_forward_kernel, out_shape=(jax.ShapeDtypeStruct((query_co...  12.1 us
    unnamed x20, local copies, waits for them, and re-layouts  6.84 us
    another operation x3, other arithmetic  6.77 us
  transfers between devices with their start and end apart: 22, of which 13 were waited for; matrix products, arithmetic and copies ran while one was open for 12% of the time, Pallas kernels for 0%

profile of v17, /device:TPU:0, one launch (start us, length us, event | category | flops | bytes accessed | tf_op | source)
XLA Modules:
  0.0 173.6 jit_solution(1458863528819610684)
XLA Ops:
  1.4 3.1 %collective-permute-start = (bf16[1,128,128]{2,1,0:T(8,128)(2,1)S(1)}, bf16[1,128,128]{2,1,0:T(8,128)(2,1)S(1)}, u32[]{:S(2)}, u32[]{:S(2)}) collective-permute-start(bf16[1,128,128]{2,1,0:T(8,128)(2,1)S(1)} %maximum_bitcast_fusion), channel_id=1, source_target_pairs={{0,12},{1,13},{2,14},{3,15},{4,0},{5,1},{6,2},{7,3},{8,4},{9,5},{1... | collective-permute-start | bytes 98312 | tf_op jit(solution)/shard_map/ppermute | solution.py:225
  6.2 1.4 constant_dynamic-update-slice_fusion.16
  7.5 2.4 %collective-permute-done.1 = bf16[1,128,128]{2,1,0:T(8,128)(2,1)S(1)} collective-permute-done((bf16[1,128,128]{2,1,0:T(8,128)(2,1)S(1)}, bf16[1,128,128]{2,1,0:T(8,128)(2,1)S(1)}, u32[]{:S(2)}, u32[]{:S(2)}) %collective-permute-start.1) | collective-permute-done | bytes 32800 | tf_op jit(solution)/shard_map/ppermute | solution.py:225
  10.4 2.8 %collective-permute-start.3 = (bf16[4,128,128]{2,1,0:T(8,128)(2,1)S(1)}, bf16[4,128,128]{2,1,0:T(8,128)(2,1)S(1)}, u32[]{:S(2)}, u32[]{:S(2)}) collective-permute-start(bf16[4,128,128]{2,1,0:T(8,128)(2,1)S(1)} %pad_maximum_fusion), channel_id=1, source_target_pairs={{0,17},{1,16},{2,19},{3,18},{4,21},{5,20},{6,23},{7,22},{8,25},{9,... | collective-permute-start | bytes 393224 | tf_op jit(solution)/shard_map/ppermute | solution.py:225
  18.2 1.5 collective-permute-done.4
  21.9 4.0 %collective-permute-start.6 = (bf16[16,128,128]{2,1,0:T(8,128)(2,1)S(1)}, bf16[16,128,128]{2,1,0:T(8,128)(2,1)S(1)}, u32[]{:S(2)}, u32[]{:S(2)}) collective-permute-start(bf16[16,128,128]{2,1,0:T(8,128)(2,1)S(1)} %get-tuple-element.39), channel_id=1, source_target_pairs={{0,96},{1,97},{2,98},{3,99},{4,100},{5,101},{6,102},{7,103},{8,104... | collective-permute-start | bytes 1572872 | tf_op jit(solution)/shard_map/ppermute | solution.py:225
  27.2 18.3 %collective-permute-done.6 = bf16[16,128,128]{2,1,0:T(8,128)(2,1)S(1)} collective-permute-done((bf16[16,128,128]{2,1,0:T(8,128)(2,1)S(1)}, bf16[16,128,128]{2,1,0:T(8,128)(2,1)S(1)}, u32[]{:S(2)}, u32[]{:S(2)}) %collective-permute-start.6) | collective-permute-done | bytes 524320 | tf_op jit(solution)/shard_map/ppermute | solution.py:225
  56.1 1.5 constant_dynamic-update-slice_fusion.17.kvt_ref
  58.3 12.1 %shard_map.93 = (bf16[2,64,1024]{2,1,0:T(8,128)(2,1)}, f32[2,1,1024]{2,1,0:T(1,128)}, f32[2,1,1024]{2,1,0:T(1,128)}) custom-call(s32[2,48]{1,0:T(2,128)} %select_reduce_fusion.lists_ref, s32[2,48]{1,0:T(2,128)} %broadcast_in_dim.11.count_ref, s32[128]{0:T(128)} %fusion.10.pos_ref, bf16[2,64,1024]{2,1,0:T(8,128)(2,1)} %bitcast.55, ...), custom_call_target="tpu_custom_call" | custom-call | tf_op jit(solution)/shard_map/pallas_call | solution.py:148
  70.4 21.9 %shard_map.94 = (bf16[2,64,1024]{2,1,0:T(8,128)(2,1)}, f32[64,128,128]{2,1,0:T(8,128)}, bf16[1,64,128,128]{3,2,1,0:T(8,128)(2,1)}) custom-call(s32[2,48]{1,0:T(2,128)} %select_reduce_fusion.lists_ref, s32[2,48]{1,0:T(2,128)} %broadcast_in_dim.11.count_ref, s32[128]{0:T(128)} %fusion.10.pos_ref, bf16[2,1024,64]{2,1,0:T(8,128)(2,1)} %copy-done, ...), custom_call_target="tpu_custom_call" | custom-call | tf_op jit(solution)/shard_map/pallas_call | solution.py:165
  92.3 4.4 %collective-permute-done.12 = bf16[64,128,128]{2,1,0:T(8,128)(2,1)S(1)} collective-permute-done((bf16[64,128,128]{2,1,0:T(8,128)(2,1)}, bf16[64,128,128]{2,1,0:T(8,128)(2,1)S(1)}, u32[]{:S(2)}, u32[]{:S(2)}) %collective-permute-start.12) | collective-permute-done | bytes 2097184 | tf_op jit(solution)/shard_map/ppermute | solution.py:234
  96.7 5.3 %fusion.15 = (bf16[64,128,128]{2,1,0:T(8,128)(2,1)S(1)}, f32[64,128,128]{2,1,0:T(8,128)}) fusion(f32[64,128,128]{2,1,0:T(8,128)} %get-tuple-element.14, bf16[64,128,128]{2,1,0:T(8,128)(2,1)S(1)} %collective-permute-done.12), kind=kLoop, calls=%fused_computation.68 | loop fusion | flops 3145728 | bytes 12582912 | tf_op jit(solution)/shard_map/convert.9
  102.1 8.8 %collective-permute-start.13 = (bf16[4,4,128,128]{3,2,1,0:T(8,128)(2,1)S(1)}, bf16[4,4,128,128]{3,2,1,0:T(8,128)(2,1)S(1)}, u32[]{:S(2)}, u32[]{:S(2)}) collective-permute-start(bf16[4,4,128,128]{3,2,1,0:T(8,128)(2,1)S(1)} %bitcast.61), channel_id=1, source_target_pairs={{0,32},{1,33},{2,34},{3,35},{4,36},{5,37},{6,38},{7,39},{8,40},{9,... | collective-permute-start | bytes 1572872 | tf_op jit(solution)/shard_map/ppermute | solution.py:241
  110.9 14.4 %collective-permute-start.14 = (bf16[4,4,128,128]{3,2,1,0:T(8,128)(2,1)S(1)}, bf16[4,4,128,128]{3,2,1,0:T(8,128)(2,1)S(1)}, u32[]{:S(2)}, u32[]{:S(2)}) collective-permute-start(bf16[4,4,128,128]{3,2,1,0:T(8,128)(2,1)S(1)} %bitcast.60), channel_id=1, source_target_pairs={{0,64},{1,65},{2,66},{3,67},{4,68},{5,69},{6,70},{7,71},{8,72},{9,... | collective-permute-start | bytes 1572872 | tf_op jit(solution)/shard_map/ppermute | solution.py:241
  128.1 8.0 %collective-permute-done.13 = bf16[4,4,128,128]{3,2,1,0:T(8,128)(2,1)S(1)} collective-permute-done((bf16[4,4,128,128]{3,2,1,0:T(8,128)(2,1)S(1)}, bf16[4,4,128,128]{3,2,1,0:T(8,128)(2,1)S(1)}, u32[]{:S(2)}, u32[]{:S(2)}) %collective-permute-start.13) | collective-permute-done | bytes 524320 | tf_op jit(solution)/shard_map/ppermute | solution.py:241
  136.1 12.4 %collective-permute-done.14 = bf16[4,4,128,128]{3,2,1,0:T(8,128)(2,1)S(1)} collective-permute-done((bf16[4,4,128,128]{3,2,1,0:T(8,128)(2,1)S(1)}, bf16[4,4,128,128]{3,2,1,0:T(8,128)(2,1)S(1)}, u32[]{:S(2)}, u32[]{:S(2)}) %collective-permute-start.14) | collective-permute-done | bytes 524320 | tf_op jit(solution)/shard_map/ppermute | solution.py:241
  148.5 1.4 fusion.14
  149.9 1.9 %collective-permute-start.16 = (bf16[4,128,128]{2,1,0:T(8,128)(2,1)S(1)}, bf16[4,128,128]{2,1,0:T(8,128)(2,1)S(1)}, u32[]{:S(2)}, u32[]{:S(2)}) collective-permute-start(bf16[4,128,128]{2,1,0:T(8,128)(2,1)S(1)} %get-tuple-element.25), channel_id=1, source_target_pairs={{0,16},{1,17},{2,18},{3,19},{4,20},{5,21},{6,22},{7,23},{8,24},{9,... | collective-permute-start | bytes 393224 | tf_op jit(solution)/shard_map/ppermute | solution.py:241
  151.8 3.0 %collective-permute-start.17 = (bf16[4,128,128]{2,1,0:T(8,128)(2,1)S(1)}, bf16[4,128,128]{2,1,0:T(8,128)(2,1)S(1)}, u32[]{:S(2)}, u32[]{:S(2)}) collective-permute-start(bf16[4,128,128]{2,1,0:T(8,128)(2,1)S(1)} %get-tuple-element.27), channel_id=1, source_target_pairs={{0,1},{1,0},{2,3},{3,2},{4,5},{5,4},{6,7},{7,6},{8,9},{9,8},{10,11... | collective-permute-start | bytes 393224 | tf_op jit(solution)/shard_map/ppermute | solution.py:241
  155.4 1.6 collective-permute-start.10
  157.0 2.0 %maximum_select_fusion.1 = bf16[256,1024]{1,0:T(8,128)(2,1)} fusion(bf16[256,512]{1,0:T(8,128)(2,1)} %collective-permute-done.11, bf16[256,512]{1,0:T(8,128)(2,1)S(1)} %reshape.75, pred[]{:T(512)S(6)} %eq.41), kind=kLoop, calls=%fused_computation.3 | loop fusion | flops 2359296 | bytes 1048577 | tf_op jit(solution)/shard_map/jit(_where)/select_n | solution.py:282
  159.0 2.9 %collective-permute-done.17 = bf16[4,128,128]{2,1,0:T(8,128)(2,1)S(1)} collective-permute-done((bf16[4,128,128]{2,1,0:T(8,128)(2,1)S(1)}, bf16[4,128,128]{2,1,0:T(8,128)(2,1)S(1)}, u32[]{:S(2)}, u32[]{:S(2)}) %collective-permute-start.17) | collective-permute-done | bytes 131104 | tf_op jit(solution)/shard_map/ppermute | solution.py:241
  162.1 6.4 %collective-permute-start.20 = (bf16[128,128]{1,0:T(8,128)(2,1)S(1)}, bf16[128,128]{1,0:T(8,128)(2,1)S(1)}, u32[]{:S(2)}, u32[]{:S(2)}) collective-permute-start(bf16[128,128]{1,0:T(8,128)(2,1)S(1)} %get-tuple-element.36), channel_id=1, source_target_pairs={{0,8},{1,9},{2,10},{3,11},{4,12},{5,13},{6,14},{7,15},{8,0},{9,1},... | collective-permute-start | bytes 98312 | tf_op jit(solution)/shard_map/ppermute | solution.py:241
  170.7 1.7 collective-permute-done.21
  (77 shorter events, 29.5 us)
Async XLA Ops:
  0.6 49.5 %copy-start.4 = (bf16[256,1024]{1,0:T(8,128)(2,1)S(1)}, bf16[256,1024]{1,0:T(8,128)(2,1)}, u32[]{:S(2)}) copy-start(bf16[256,1024]{1,0:T(8,128)(2,1)} %param.6) | copy-start | bytes 1572868
  1.4 6.1 %collective-permute-start = (bf16[1,128,128]{2,1,0:T(8,128)(2,1)S(1)}, bf16[1,128,128]{2,1,0:T(8,128)(2,1)S(1)}, u32[]{:S(2)}, u32[]{:S(2)}) collective-permute-start(bf16[1,128,128]{2,1,0:T(8,128)(2,1)S(1)} %maximum_bitcast_fusion), channel_id=1, source_target_pairs={{0,12},{1,13},{2,14},{3,15},{4,0},{5,1},{6,2},{7,3},{8,4},{9,5},{1... | collective-permute-start | bytes 98312 | tf_op jit(solution)/shard_map/ppermute | solution.py:225
  4.6 5.4 %collective-permute-start.1 = (bf16[1,128,128]{2,1,0:T(8,128)(2,1)S(1)}, bf16[1,128,128]{2,1,0:T(8,128)(2,1)S(1)}, u32[]{:S(2)}, u32[]{:S(2)}) collective-permute-start(bf16[1,128,128]{2,1,0:T(8,128)(2,1)S(1)} %maximum_bitcast_fusion), channel_id=1, source_target_pairs={{0,8},{1,9},{2,10},{3,11},{4,12},{5,13},{6,14},{7,15},{8,0},{9,1},... | collective-permute-start | bytes 98312 | tf_op jit(solution)/shard_map/ppermute | solution.py:225
  5.2 5.1 %collective-permute-start.2 = (bf16[1,128,128]{2,1,0:T(8,128)(2,1)S(1)}, bf16[1,128,128]{2,1,0:T(8,128)(2,1)S(1)}, u32[]{:S(2)}, u32[]{:S(2)}) collective-permute-start(bf16[1,128,128]{2,1,0:T(8,128)(2,1)S(1)} %maximum_bitcast_fusion), channel_id=1, source_target_pairs={{0,4},{1,5},{2,6},{3,7},{4,8},{5,9},{6,10},{7,11},{8,12},{9,13},{1... | collective-permute-start | bytes 98312 | tf_op jit(solution)/shard_map/ppermute | solution.py:225
  10.4 7.1 %collective-permute-start.3 = (bf16[4,128,128]{2,1,0:T(8,128)(2,1)S(1)}, bf16[4,128,128]{2,1,0:T(8,128)(2,1)S(1)}, u32[]{:S(2)}, u32[]{:S(2)}) collective-permute-start(bf16[4,128,128]{2,1,0:T(8,128)(2,1)S(1)} %pad_maximum_fusion), channel_id=1, source_target_pairs={{0,17},{1,16},{2,19},{3,18},{4,21},{5,20},{6,23},{7,22},{8,25},{9,... | collective-permute-start | bytes 393224 | tf_op jit(solution)/shard_map/ppermute | solution.py:225
  13.2 6.6 %collective-permute-start.4 = (bf16[4,128,128]{2,1,0:T(8,128)(2,1)S(1)}, bf16[4,128,128]{2,1,0:T(8,128)(2,1)S(1)}, u32[]{:S(2)}, u32[]{:S(2)}) collective-permute-start(bf16[4,128,128]{2,1,0:T(8,128)(2,1)S(1)} %pad_maximum_fusion), channel_id=1, source_target_pairs={{0,1},{1,0},{2,3},{3,2},{4,5},{5,4},{6,7},{7,6},{8,9},{9,8},{10,11... | collective-permute-start | bytes 393224 | tf_op jit(solution)/shard_map/ppermute | solution.py:225
  14.0 7.1 %collective-permute-start.5 = (bf16[4,128,128]{2,1,0:T(8,128)(2,1)S(1)}, bf16[4,128,128]{2,1,0:T(8,128)(2,1)S(1)}, u32[]{:S(2)}, u32[]{:S(2)}) collective-permute-start(bf16[4,128,128]{2,1,0:T(8,128)(2,1)S(1)} %pad_maximum_fusion), channel_id=1, source_target_pairs={{0,16},{1,17},{2,18},{3,19},{4,20},{5,21},{6,22},{7,23},{8,24},{9,... | collective-permute-start | bytes 393224 | tf_op jit(solution)/shard_map/ppermute | solution.py:225
  21.9 23.6 %collective-permute-start.6 = (bf16[16,128,128]{2,1,0:T(8,128)(2,1)S(1)}, bf16[16,128,128]{2,1,0:T(8,128)(2,1)S(1)}, u32[]{:S(2)}, u32[]{:S(2)}) collective-permute-start(bf16[16,128,128]{2,1,0:T(8,128)(2,1)S(1)} %get-tuple-element.39), channel_id=1, source_target_pairs={{0,96},{1,97},{2,98},{3,99},{4,100},{5,101},{6,102},{7,103},{8,104... | collective-permute-start | bytes 1572872 | tf_op jit(solution)/shard_map/ppermute | solution.py:225
  25.9 20.8 %collective-permute-start.7 = (bf16[16,128,128]{2,1,0:T(8,128)(2,1)S(1)}, bf16[16,128,128]{2,1,0:T(8,128)(2,1)S(1)}, u32[]{:S(2)}, u32[]{:S(2)}) collective-permute-start(bf16[16,128,128]{2,1,0:T(8,128)(2,1)S(1)} %get-tuple-element.39), channel_id=1, source_target_pairs={{0,64},{1,65},{2,66},{3,67},{4,68},{5,69},{6,70},{7,71},{8,72},{9,... | collective-permute-start | bytes 1572872 | tf_op jit(solution)/shard_map/ppermute | solution.py:225
  25.9 23.0 %collective-permute-start.8 = (bf16[16,128,128]{2,1,0:T(8,128)(2,1)S(1)}, bf16[16,128,128]{2,1,0:T(8,128)(2,1)S(1)}, u32[]{:S(2)}, u32[]{:S(2)}) collective-permute-start(bf16[16,128,128]{2,1,0:T(8,128)(2,1)S(1)} %get-tuple-element.39), channel_id=1, source_target_pairs={{0,32},{1,33},{2,34},{3,35},{4,36},{5,37},{6,38},{7,39},{8,40},{9,... | collective-permute-start | bytes 1572872 | tf_op jit(solution)/shard_map/ppermute | solution.py:225
  50.2 5.9 %collective-permute-start.9 = (bf16[64,128,128]{2,1,0:T(8,128)(2,1)}, bf16[64,128,128]{2,1,0:T(8,128)(2,1)S(1)}, u32[]{:S(2)}, u32[]{:S(2)}) collective-permute-start(bf16[64,128,128]{2,1,0:T(8,128)(2,1)} %get-tuple-element.28), channel_id=1, source_target_pairs={{0,2},{1,3},{2,0},{3,1},{4,6},{5,7},{6,4},{7,5},{8,10},{9,11},{10,... | collective-permute-start | bytes 6291464 | tf_op jit(solution)/shard_map/ppermute | solution.py:225
  92.3 4.4 %collective-permute-start.12 = (bf16[64,128,128]{2,1,0:T(8,128)(2,1)}, bf16[64,128,128]{2,1,0:T(8,128)(2,1)S(1)}, u32[]{:S(2)}, u32[]{:S(2)}) collective-permute-start(bf16[64,128,128]{2,1,0:T(8,128)(2,1)} %bitcast.68), channel_id=1, source_target_pairs={{0,2},{1,3},{2,0},{3,1},{4,6},{5,7},{6,4},{7,5},{8,10},{9,11},{10,... | collective-permute-start | bytes 6291464 | tf_op jit(solution)/shard_map/ppermute | solution.py:234
  96.7 28.7 %copy-start.3 = (bf16[2,64,1024]{2,1,0:T(8,128)(2,1)S(1)}, bf16[2,64,1024]{2,1,0:T(8,128)(2,1)}, u32[]{:S(2)}) copy-start(bf16[2,64,1024]{2,1,0:T(8,128)(2,1)} %get-tuple-element.13) | copy-start | bytes 786436
  102.1 34.0 %collective-permute-start.13 = (bf16[4,4,128,128]{3,2,1,0:T(8,128)(2,1)S(1)}, bf16[4,4,128,128]{3,2,1,0:T(8,128)(2,1)S(1)}, u32[]{:S(2)}, u32[]{:S(2)}) collective-permute-start(bf16[4,4,128,128]{3,2,1,0:T(8,128)(2,1)S(1)} %bitcast.61), channel_id=1, source_target_pairs={{0,32},{1,33},{2,34},{3,35},{4,36},{5,37},{6,38},{7,39},{8,40},{9,... | collective-permute-start | bytes 1572872 | tf_op jit(solution)/shard_map/ppermute | solution.py:241
  110.9 37.6 %collective-permute-start.14 = (bf16[4,4,128,128]{3,2,1,0:T(8,128)(2,1)S(1)}, bf16[4,4,128,128]{3,2,1,0:T(8,128)(2,1)S(1)}, u32[]{:S(2)}, u32[]{:S(2)}) collective-permute-start(bf16[4,4,128,128]{3,2,1,0:T(8,128)(2,1)S(1)} %bitcast.60), channel_id=1, source_target_pairs={{0,64},{1,65},{2,66},{3,67},{4,68},{5,69},{6,70},{7,71},{8,72},{9,... | collective-permute-start | bytes 1572872 | tf_op jit(solution)/shard_map/ppermute | solution.py:241
  125.3 23.2 %collective-permute-start.15 = (bf16[4,4,128,128]{3,2,1,0:T(8,128)(2,1)S(1)}, bf16[4,4,128,128]{3,2,1,0:T(8,128)(2,1)}, u32[]{:S(2)}, u32[]{:S(2)}) collective-permute-start(bf16[4,4,128,128]{3,2,1,0:T(8,128)(2,1)S(1)} %bitcast.59), channel_id=1, source_target_pairs={{0,96},{1,97},{2,98},{3,99},{4,100},{5,101},{6,102},{7,103},{8,104... | collective-permute-start | bytes 1572872 | tf_op jit(solution)/shard_map/ppermute | solution.py:241
  126.0 31.1 %collective-permute-start.11 = (bf16[256,512]{1,0:T(8,128)(2,1)S(1)}, bf16[256,512]{1,0:T(8,128)(2,1)}, u32[]{:S(2)}, u32[]{:S(2)}) collective-permute-start(bf16[256,512]{1,0:T(8,128)(2,1)S(1)} %reshape.75), channel_id=1, source_target_pairs={{0,1},{1,0},{2,3},{3,2},{4,5},{5,4},{6,7},{7,6},{8,9},{9,8},{10,11... | collective-permute-start | bytes 786440 | tf_op jit(solution)/shard_map/ppermute | solution.py:281
  149.9 9.1 %collective-permute-start.16 = (bf16[4,128,128]{2,1,0:T(8,128)(2,1)S(1)}, bf16[4,128,128]{2,1,0:T(8,128)(2,1)S(1)}, u32[]{:S(2)}, u32[]{:S(2)}) collective-permute-start(bf16[4,128,128]{2,1,0:T(8,128)(2,1)S(1)} %get-tuple-element.25), channel_id=1, source_target_pairs={{0,16},{1,17},{2,18},{3,19},{4,20},{5,21},{6,22},{7,23},{8,24},{9,... | collective-permute-start | bytes 393224 | tf_op jit(solution)/shard_map/ppermute | solution.py:241
  151.8 10.1 %collective-permute-start.17 = (bf16[4,128,128]{2,1,0:T(8,128)(2,1)S(1)}, bf16[4,128,128]{2,1,0:T(8,128)(2,1)S(1)}, u32[]{:S(2)}, u32[]{:S(2)}) collective-permute-start(bf16[4,128,128]{2,1,0:T(8,128)(2,1)S(1)} %get-tuple-element.27), channel_id=1, source_target_pairs={{0,1},{1,0},{2,3},{3,2},{4,5},{5,4},{6,7},{7,6},{8,9},{9,8},{10,11... | collective-permute-start | bytes 393224 | tf_op jit(solution)/shard_map/ppermute | solution.py:241
  154.8 7.2 %collective-permute-start.18 = (bf16[4,128,128]{2,1,0:T(8,128)(2,1)S(1)}, bf16[4,128,128]{2,1,0:T(8,128)(2,1)S(1)}, u32[]{:S(2)}, u32[]{:S(2)}) collective-permute-start(bf16[4,128,128]{2,1,0:T(8,128)(2,1)S(1)} %get-tuple-element.26), channel_id=1, source_target_pairs={{0,17},{1,16},{2,19},{3,18},{4,21},{5,20},{6,23},{7,22},{8,25},{9,... | collective-permute-start | bytes 393224 | tf_op jit(solution)/shard_map/ppermute | solution.py:241
  155.4 13.1 %collective-permute-start.10 = (bf16[256,512]{1,0:T(8,128)(2,1)S(1)}, bf16[256,512]{1,0:T(8,128)(2,1)S(1)}, u32[]{:S(2)}, u32[]{:S(2)}) collective-permute-start(bf16[256,512]{1,0:T(8,128)(2,1)S(1)} %reshape.74), channel_id=1, source_target_pairs={{0,1},{1,0},{2,3},{3,2},{4,5},{5,4},{6,7},{7,6},{8,9},{9,8},{10,11... | collective-permute-start | bytes 786440 | tf_op jit(solution)/shard_map/ppermute | solution.py:281
  162.0 7.4 %collective-permute-start.19 = (bf16[128,128]{1,0:T(8,128)(2,1)S(1)}, bf16[128,128]{1,0:T(8,128)(2,1)S(1)}, u32[]{:S(2)}, u32[]{:S(2)}) collective-permute-start(bf16[128,128]{1,0:T(8,128)(2,1)S(1)} %get-tuple-element.34), channel_id=1, source_target_pairs={{0,4},{1,5},{2,6},{3,7},{4,8},{5,9},{6,10},{7,11},{8,12},{9,13},{1... | collective-permute-start | bytes 98312 | tf_op jit(solution)/shard_map/ppermute | solution.py:241
  162.1 8.6 %collective-permute-start.20 = (bf16[128,128]{1,0:T(8,128)(2,1)S(1)}, bf16[128,128]{1,0:T(8,128)(2,1)S(1)}, u32[]{:S(2)}, u32[]{:S(2)}) collective-permute-start(bf16[128,128]{1,0:T(8,128)(2,1)S(1)} %get-tuple-element.36), channel_id=1, source_target_pairs={{0,8},{1,9},{2,10},{3,11},{4,12},{5,13},{6,14},{7,15},{8,0},{9,1},... | collective-permute-start | bytes 98312 | tf_op jit(solution)/shard_map/ppermute | solution.py:241
  168.5 3.9 %collective-permute-start.21 = (bf16[128,128]{1,0:T(8,128)(2,1)S(1)}, bf16[128,128]{1,0:T(8,128)(2,1)S(1)}, u32[]{:S(2)}, u32[]{:S(2)}) collective-permute-start(bf16[128,128]{1,0:T(8,128)(2,1)S(1)} %get-tuple-element.35), channel_id=1, source_target_pairs={{0,12},{1,13},{2,14},{3,15},{4,0},{5,1},{6,2},{7,3},{8,4},{9,5},{1... | collective-permute-start | bytes 98312 | tf_op jit(solution)/shard_map/ppermute | solution.py:241
  (4 other events, 63.5 us)
